TPU v7x, 32 devices: a whole 2x2x4 slice. The times are simulated.
32 devices in a mesh: dp: 4 (over z), fsdp: 2 (over x), rows: 4 (over y, core).
Axes of the slice: x: 2, y: 2, z: 4, core: 2. Of those that a mesh axis runs over, the one named last changes fastest.
Arguments:
- feature_maps: bfloat16 [8, 16, 32, 1536], P(('dp', 'fsdp'), 'rows'), may hold values from -30 to 30
- dw_kernel: float32 [7, 7, 1536], replicated, may hold values from -0.875 to 0.875
- norm_gain: float32 [1536], replicated, may hold values from 0.5 to 1.5
- w_up: bfloat16 [1536, 6144], P(('dp', 'rows'), 'fsdp'), may hold values from -0.15625 to 0.15625
- w_down: bfloat16 [6144, 1536], P('fsdp', ('dp', 'rows')), may hold values from -0.078125 to 0.078125
- layer_scale: float32 [1536], replicated, may hold values from 0.3 to 1.5
- d_out: bfloat16 [8, 16, 32, 1536], P(('dp', 'fsdp'), 'rows'), may hold values from -20 to 20
Outputs:
- result: bfloat16 [8, 16, 32, 1536], P(('dp', 'fsdp'), 'rows')
- grad_x: bfloat16 [8, 16, 32, 1536], P(('dp', 'fsdp'), 'rows')
- grad_up: float32 [1536, 6144], P(('dp', 'rows'), 'fsdp')
- grad_down: float32 [6144, 1536], P('fsdp', ('dp', 'rows'))
- grad_kernel: float32 [7, 7, 1536], replicated
- grad_gain: float32 [1536], replicated
- grad_scale: float32 [1536], replicated
All inputs are finite; a program needn't handle non-finite values.
Results may differ from a plain program's by a relative error of at most 0.0075.
Values may be sent and summed in bfloat16 or wider, within the bound.
No kernel may reach another device: no remote copies, remote signals or barrier semaphores. Data moves between devices by JAX's collectives and lax.ppermute only.
A program may use at most 128 MiB of HBM per device.

v0:
```python
import math

import jax
import jax.numpy as jnp
from jax import lax
from jax.sharding import PartitionSpec as P

KS = 7


norm_eps = 1e-06
inv_root_two = 1.0 / math.sqrt(2.0)
inv_root_two_pi = 1.0 / math.sqrt(2.0 * math.pi)
contract_rows = (((0,), (0,)), ((), ()))
contract_cols = (((1,), (1,)), ((), ()))


def padded_2(x, sides, width):
    for axis, dim in sides:
        devices, length = (lax.axis_size(axis), x.shape[dim])
        up = [(i, (i + 1) % devices) for i in range(devices - 1)]
        down = [(j, i) for i, j in up]
        last = lax.slice_in_dim(x, length - width, length, axis=dim)
        leading = lax.slice_in_dim(x, 0, width, axis=dim)
        before = lax.ppermute(last, axis, up)
        after = lax.ppermute(leading, axis, down)
        x = jnp.concatenate([before, x, after], axis=dim)
    return x


def gelu_exact(values):
    return 0.5 * values * (1.0 + jax.scipy.special.erf(values * inv_root_two))


def gelu_slope(values):
    cdf_part = 0.5 * (1.0 + jax.scipy.special.erf(values * inv_root_two))
    return cdf_part + values * jnp.exp(-0.5 * values * values) * inv_root_two_pi


def reduce_down(down_part):
    return lax.psum_scatter(down_part, ("dp", "rows"), scatter_dimension=1, tiled=True)


def body(feature_maps, dw_kernel, norm_gain, w_up, w_down, layer_scale, d_out):
    scenes, strip, across, width = feature_maps.shape
    cells = scenes * strip * across
    rimmed = padded_2(feature_maps, (("rows", 1),), 3)
    padded = jnp.pad(rimmed.astype(jnp.float32), ((0, 0), (0, 0), (3, 3), (0, 0)))
    filtered = jnp.zeros(feature_maps.shape, jnp.float32)
    for row_off in range(KS):
        for col_off in range(KS):
            filtered = (
                filtered
                + padded[:, row_off : row_off + strip, col_off : col_off + across, :]
                * dw_kernel[row_off, col_off]
            )
    flat = filtered.reshape(cells, width)
    average = jnp.mean(flat, axis=-1, keepdims=True)
    center = flat - average
    variance = jnp.mean(center * center, axis=-1, keepdims=True)
    rstd = lax.rsqrt(variance + norm_eps)
    normed = center * rstd
    scaled = (normed * norm_gain).astype(jnp.bfloat16)
    gathered = lax.all_gather(scaled, "fsdp", axis=0, tiled=True)
    up_full = lax.all_gather(w_up, ("dp", "rows"), axis=0, tiled=True)
    down_full = lax.all_gather(w_down, ("dp", "rows"), axis=1, tiled=True)
    hidden = jnp.dot(gathered, up_full, preferred_element_type=jnp.float32)
    active = gelu_exact(hidden).astype(jnp.bfloat16)
    mlp_terms = jnp.dot(active, down_full, preferred_element_type=jnp.float32)
    branch = lax.psum_scatter(
        mlp_terms.astype(jnp.bfloat16), "fsdp", scatter_dimension=0, tiled=True
    ).astype(jnp.float32)
    resid = feature_maps.reshape(cells, width).astype(jnp.float32)
    result = (resid + layer_scale * branch).astype(jnp.bfloat16).reshape(feature_maps.shape)
    cotan = d_out.reshape(cells, width).astype(jnp.float32)
    scale_part = jnp.sum(cotan * branch, axis=0)
    back = (cotan * layer_scale).astype(jnp.bfloat16)
    back_all = lax.all_gather(back, "fsdp", axis=0, tiled=True)
    down_part = lax.dot_general(active, back_all, contract_rows, preferred_element_type=jnp.float32)
    slope_in = lax.dot_general(
        back_all, down_full, contract_cols, preferred_element_type=jnp.float32
    )
    hidden_grad = (slope_in * gelu_slope(hidden)).astype(jnp.bfloat16)
    up_part = lax.dot_general(
        gathered, hidden_grad, contract_rows, preferred_element_type=jnp.float32
    )
    norm_terms = lax.dot_general(
        hidden_grad, up_full, contract_cols, preferred_element_type=jnp.float32
    )
    norm_grad = lax.psum_scatter(norm_terms, "fsdp", scatter_dimension=0, tiled=True)
    grad_up = lax.psum_scatter(up_part, ("dp", "rows"), scatter_dimension=0, tiled=True)
    grad_down = reduce_down(down_part)
    gain_part = jnp.sum(norm_grad * normed, axis=0)
    scaled_grad = norm_grad * norm_gain
    conv_grad = rstd * (
        scaled_grad
        - jnp.mean(scaled_grad, axis=-1, keepdims=True)
        - normed * jnp.mean(scaled_grad * normed, axis=-1, keepdims=True)
    )
    conv_grad = conv_grad.reshape(feature_maps.shape)
    grad_rim = padded_2(conv_grad.astype(jnp.bfloat16), (("rows", 1),), 3).astype(conv_grad.dtype)
    grad_pad = jnp.pad(grad_rim, ((0, 0), (0, 0), (3, 3), (0, 0)))
    kernel_rows = []
    back_conv = jnp.zeros(feature_maps.shape, jnp.float32)
    for row_off in range(KS):
        for col_off in range(KS):
            window = padded[:, row_off : row_off + strip, col_off : col_off + across, :]
            kernel_rows.append(jnp.sum(window * conv_grad, axis=(0, 1, 2)))
            back_conv = (
                back_conv
                + grad_pad[
                    :, 6 - row_off : 6 - row_off + strip, 6 - col_off : 6 - col_off + across, :
                ]
                * dw_kernel[row_off, col_off]
            )
    kernel_part = jnp.stack(kernel_rows).reshape(KS, KS, width)
    grad_x = (d_out.astype(jnp.float32) + back_conv).astype(jnp.bfloat16)
    grad_kernel, grad_gain, grad_scale = lax.psum(
        (kernel_part, gain_part, scale_part), ("dp", "fsdp", "rows")
    )
    return (result, grad_x, grad_up, grad_down, grad_kernel, grad_gain, grad_scale)


def solution(mesh):
    return jax.shard_map(
        body,
        mesh=mesh,
        in_specs=(
            P(("dp", "fsdp"), "rows", None, None),
            P(),
            P(),
            P(("dp", "rows"), "fsdp"),
            P("fsdp", ("dp", "rows")),
            P(),
            P(("dp", "fsdp"), "rows", None, None),
        ),
        out_specs=(
            P(("dp", "fsdp"), "rows", None, None),
            P(("dp", "fsdp"), "rows", None, None),
            P(("dp", "rows"), "fsdp"),
            P("fsdp", ("dp", "rows")),
            P(),
            P(),
            P(),
        ),
        check_vma=False,
    )
```

profile of v0, /device:TPU:0, one launch (start us, length us, event | category | flops | bytes accessed | tf_op | source)
XLA Modules:
  0.0 797.9 jit_solution(10668589192870983978)
XLA Ops:
  8.7 1.1 fusion.105
  9.8 2.4 collective-permute-start
  12.2 1.3 collective-permute-start.1
  13.5 1.3 slice_reduce_fusion.46
  16.4 1.4 collective-permute-done.1
  18.0 9.5 %fusion.103 = (f32[4,32]{1,0:T(4,128)S(1)}, f32[1,4,32,1536]{3,2,1,0:T(8,128)S(1)}) fusion(f32[1536]{0:T(1024)S(1)} %get-tuple-element.106, f32[1536]{0:T(1024)S(1)} %get-tuple-element.107, f32[1536]{0:T(1024)S(1)} %get-tuple-element.60, f32[1536]{0:T(1024)S(1)} %get-tuple-element.61, f32[1,10,32,1536]{3,2,1,0:T(8,128)S(1)} %maximum_convert_fusion, ...), kind=kLoop, calls=%fused_computation.314 | loop fusion | flops 19267456 | bytes 8641024 | tf_op jit(solution)/shard_map/reduce_sum | solution.py:58
  30.1 8.6 %all_gather.12 = bf16[256,1536]{1,0:T(8,128)(2,1)} all-gather(bf16[128,1536]{1,0:T(8,128)(2,1)S(1)} %multiply_convert_fusion.1), channel_id=1, replica_groups=mesh['dp'=4,'fsdp'=2,'rows'=4] {'fsdp'}, dimensions={0}, use_global_device_ids=true | all-gather | bytes 1179648 | tf_op jit(solution)/shard_map/all_gather | solution.py:64
  38.7 55.8 %all-gather.3.cloned.1.call-done = bf16[1536,3072]{1,0:T(8,128)(2,1)} async-done(((bf16[96,3072]{1,0:T(8,128)(2,1)}), bf16[1536,3072]{1,0:T(8,128)(2,1)}) %all-gather.3.cloned.1.call-update) | async-done | bytes 9437200 | tf_op jit(solution)/shard_map/all_gather | solution.py:65
  94.5 8.2 %fusion.106 = f32[256,3072]{1,0:T(8,128)} fusion(bf16[256,1536]{1,0:T(8,128)(2,1)} %all_gather.12, bf16[1536,3072]{1,0:T(8,128)(2,1)} %all-gather.3.cloned.1.call-done), kind=kOutput, calls=%fused_computation.317 | convolution fusion | flops 2415919104 | bytes 13369344 | tf_op jit(solution)/shard_map/dot_general | solution.py:67
  102.7 73.7 %all-gather.5.cloned.1.call-done = bf16[3072,1536]{0,1:T(8,128)(2,1)} async-done(((bf16[3072,96]{0,1:T(8,128)(2,1)}), bf16[3072,1536]{0,1:T(8,128)(2,1)}) %all-gather.5.cloned.1.call-update) | async-done | bytes 9437200 | tf_op jit(solution)/shard_map/all_gather | solution.py:66
  176.4 8.2 %convolution_convert_fusion = bf16[256,1536]{1,0:T(8,128)(2,1)} fusion(bf16[3072,1536]{0,1:T(8,128)(2,1)} %all-gather.5.cloned.1.call-done, f32[256,3072]{1,0:T(8,128)} %fusion.106), kind=kOutput, calls=%fused_computation.93 | convolution fusion | flops 2420244480 | bytes 13369344 | tf_op jit(solution)/shard_map/dot_general | solution.py:69
  184.6 15.7 %reduce-scatter.5.cloned.1.call-done = bf16[128,1536]{1,0:T(8,128)(2,1)} async-done(((bf16[256,1536]{1,0:T(8,128)(2,1)}), bf16[128,1536]{1,0:T(8,128)(2,1)}) %reduce-scatter.5.cloned.1.call-update) | async-done | bytes 393232 | tf_op jit(solution)/shard_map/reduce_scatter | solution.py:70
  200.3 2.7 fusion.7
  203.0 11.8 %all_gather.15 = bf16[256,1536]{1,0:T(8,128)(2,1)S(1)} all-gather(bf16[128,1536]{1,0:T(8,128)(2,1)S(1)} %get-tuple-element.114), channel_id=1, replica_groups=mesh['dp'=4,'fsdp'=2,'rows'=4] {'fsdp'}, dimensions={0}, use_global_device_ids=true | all-gather | bytes 1179648 | tf_op jit(solution)/shard_map/all_gather | solution.py:78
  215.7 5.5 fusion
  221.3 1.2 copy-done.7
  222.5 3.8 fusion.107
  226.4 26.2 %reduce-scatter.7.cloned.1.call-done = f32[128,1536]{1,0:T(8,128)} async-done(((f32[256,1536]{1,0:T(8,128)}), f32[128,1536]{1,0:T(8,128)}) %reduce-scatter.7.cloned.1.call-update) | async-done | bytes 786448 | tf_op jit(solution)/shard_map/reduce_scatter | solution.py:90
  252.6 2.0 multiply_reduce_fusion
  254.6 3.6 multiply_reduce_fusion.2
  258.2 1.2 multiply_reduce_fusion.3
  259.4 2.0 multiply_reduce_fusion.1
  263.5 11.1 %fusion.102 = f32[3072,1536]{0,1:T(8,128)} fusion(bf16[256,1536]{1,0:T(8,128)(2,1)S(1)} %copy-done.3, f32[256,3072]{1,0:T(8,128)} %fusion.106), kind=kOutput, calls=%fused_computation.313 | convolution fusion | flops 2419851264 | bytes 22806528 | tf_op jit(solution)/shard_map/dot_general | solution.py:79
  276.2 7.9 fusion.108
  284.7 1.9 collective-permute-start.2
  286.5 1.3 collective-permute-start.3
  287.9 42.3 %all-reduce.2 = (f32[1536]{0:T(1024)}, f32[1536]{0:T(1024)}) all-reduce(f32[1536]{0:T(1024)} %get-tuple-element.56, f32[1536]{0:T(1024)} %get-tuple-element.113), channel_id=1, replica_groups=mesh['dp'=4,'fsdp'=2,'rows'=4] {'dp','fsdp','rows'}, use_global_device_ids=true, to_apply=%region_59.60 | all-reduce | flops 3072 | bytes 24576 | tf_op jit(solution)/shard_map/psum | solution.py:118
  330.7 7.5 fusion.95
  338.3 51.2 %all-reduce.5.cloned.1.call-done = f32[7,7,1536]{2,1,0:T(8,128)} async-done(((f32[7,7,1536]{2,1,0:T(8,128)}), f32[7,7,1536]{2,1,0:T(8,128)}) %all-reduce.5.cloned.1.call-update) | async-done | bytes 301072 | tf_op jit(solution)/shard_map/psum | solution.py:118
  389.4 200.8 %reduce-scatter.11.cloned.1.call-done = f32[3072,96]{0,1:T(8,128)} async-done(((f32[3072,1536]{0,1:T(8,128)}), f32[3072,96]{0,1:T(8,128)}) %reduce-scatter.11.cloned.1.call-update) | async-done | bytes 1179664 | tf_op jit(solution)/shard_map/reduce_scatter | solution.py:41
  590.2 199.1 %reduce-scatter.9.cloned.1.call-done = f32[96,3072]{1,0:T(8,128)} async-done(((f32[1536,3072]{1,0:T(8,128)}), f32[96,3072]{1,0:T(8,128)}) %reduce-scatter.9.cloned.1.call-update) | async-done | bytes 1179664 | tf_op jit(solution)/shard_map/reduce_scatter | solution.py:91
  789.3 1.7 copy.15
  (270 shorter events, 10.1 us)
Async XLA Ops:
  7.2 87.3 %all-gather.3.cloned.1.call-start = ((), (), s32[]{:S(2)}) async-start(), calls=%async_computation.4 | async-start | bytes 10027008 | tf_op jit(solution)/shard_map/all_gather | solution.py:65
  7.9 168.5 %all-gather.5.cloned.1.call-start = ((), (), s32[]{:S(2)}) async-start(), calls=%async_computation.5 | async-start | bytes 10027008 | tf_op jit(solution)/shard_map/all_gather | solution.py:66
  8.7 191.6 %reduce-scatter.5.cloned.1.call-start = ((), (), s32[]{:S(2)}) async-start(), calls=%async_computation.6 | async-start | bytes 1179648 | tf_op jit(solution)/shard_map/reduce_scatter | solution.py:70
  9.8 6.6 collective-permute-start
  12.2 5.6 collective-permute-start.1
  102.7 97.6 %copy-start.5 = (bf16[1,4,32,1536]{3,2,1,0:T(8,128)(2,1)S(1)}, bf16[1,4,32,1536]{3,2,1,0:T(8,128)(2,1)}, u32[]{:S(2)}) copy-start(bf16[1,4,32,1536]{3,2,1,0:T(8,128)(2,1)} %param.13) | copy-start | bytes 1179652
  184.6 68.0 %reduce-scatter.7.cloned.1.call-start = ((), (), s32[]{:S(2)}) async-start(), calls=%async_computation.7 | async-start | bytes 2359296 | tf_op jit(solution)/shard_map/reduce_scatter | solution.py:90
  226.3 163.1 %all-reduce.5.cloned.1.call-start = ((), (), s32[]{:S(2)}) async-start(), calls=%async_computation.10 | async-start | bytes 688128 | tf_op jit(solution)/shard_map/psum | solution.py:118
  263.4 326.7 %reduce-scatter.11.cloned.1.call-start = ((), (), s32[]{:S(2)}) async-start(), calls=%async_computation.9 | async-start | bytes 20054016 | tf_op jit(solution)/shard_map/reduce_scatter | solution.py:41
  274.6 514.7 %reduce-scatter.9.cloned.1.call-start = ((), (), s32[]{:S(2)}) async-start(), calls=%async_computation.8 | async-start | bytes 20054016 | tf_op jit(solution)/shard_map/reduce_scatter | solution.py:91
  284.2 46.1 %copy-start.6 = (bf16[1,4,32,1536]{3,2,1,0:T(8,128)(2,1)S(1)}, bf16[1,4,32,1536]{3,2,1,0:T(8,128)(2,1)}, u32[]{:S(2)}) copy-start(bf16[1,4,32,1536]{3,2,1,0:T(8,128)(2,1)} %param.13) | copy-start | bytes 1179652
  284.2 46.1 %copy-start.12 = (f32[1536]{0:T(1024)S(1)}, f32[1536]{0:T(1024)}, u32[]{:S(2)}) copy-start(f32[1536]{0:T(1024)} %copy-done.11) | copy-start | bytes 18436
  284.2 46.1 %copy-start.14 = (f32[1536]{0:T(1024)S(1)}, f32[1536]{0:T(1024)}, u32[]{:S(2)}) copy-start(f32[1536]{0:T(1024)} %copy-done.13) | copy-start | bytes 18436
  284.2 46.1 %copy-start.16 = (f32[1536]{0:T(1024)S(1)}, f32[1536]{0:T(1024)}, u32[]{:S(2)}) copy-start(f32[1536]{0:T(1024)} %copy-done.15) | copy-start | bytes 18436
  284.2 46.1 %copy-start.18 = (f32[1536]{0:T(1024)S(1)}, f32[1536]{0:T(1024)}, u32[]{:S(2)}) copy-start(f32[1536]{0:T(1024)} %copy-done.17) | copy-start | bytes 18436
  284.3 46.1 %copy-start.20 = (f32[1536]{0:T(1024)S(1)}, f32[1536]{0:T(1024)}, u32[]{:S(2)}) copy-start(f32[1536]{0:T(1024)} %copy-done.19) | copy-start | bytes 18436
  284.3 46.1 %copy-start.22 = (f32[1536]{0:T(1024)S(1)}, f32[1536]{0:T(1024)}, u32[]{:S(2)}) copy-start(f32[1536]{0:T(1024)} %copy-done.21) | copy-start | bytes 18436
  284.3 46.1 %copy-start.24 = (f32[1536]{0:T(1024)S(1)}, f32[1536]{0:T(1024)}, u32[]{:S(2)}) copy-start(f32[1536]{0:T(1024)} %copy-done.23) | copy-start | bytes 18436
  284.3 46.1 %copy-start.26 = (f32[1536]{0:T(1024)S(1)}, f32[1536]{0:T(1024)}, u32[]{:S(2)}) copy-start(f32[1536]{0:T(1024)} %copy-done.25) | copy-start | bytes 18436
  284.3 46.1 %copy-start.28 = (f32[1536]{0:T(1024)S(1)}, f32[1536]{0:T(1024)}, u32[]{:S(2)}) copy-start(f32[1536]{0:T(1024)} %copy-done.27) | copy-start | bytes 18436
  284.3 46.1 %copy-start.30 = (f32[1536]{0:T(1024)S(1)}, f32[1536]{0:T(1024)}, u32[]{:S(2)}) copy-start(f32[1536]{0:T(1024)} %copy-done.29) | copy-start | bytes 18436
  284.3 46.1 %copy-start.32 = (f32[1536]{0:T(1024)S(1)}, f32[1536]{0:T(1024)}, u32[]{:S(2)}) copy-start(f32[1536]{0:T(1024)} %copy-done.31) | copy-start | bytes 18436
  284.3 46.1 %copy-start.34 = (f32[1536]{0:T(1024)S(1)}, f32[1536]{0:T(1024)}, u32[]{:S(2)}) copy-start(f32[1536]{0:T(1024)} %copy-done.33) | copy-start | bytes 18436
  284.3 46.1 %copy-start.36 = (f32[1536]{0:T(1024)S(1)}, f32[1536]{0:T(1024)}, u32[]{:S(2)}) copy-start(f32[1536]{0:T(1024)} %copy-done.35) | copy-start | bytes 18436
  284.3 46.1 %copy-start.38 = (f32[1536]{0:T(1024)S(1)}, f32[1536]{0:T(1024)}, u32[]{:S(2)}) copy-start(f32[1536]{0:T(1024)} %copy-done.37) | copy-start | bytes 18436
  284.4 46.1 %copy-start.40 = (f32[1536]{0:T(1024)S(1)}, f32[1536]{0:T(1024)}, u32[]{:S(2)}) copy-start(f32[1536]{0:T(1024)} %copy-done.39) | copy-start | bytes 18436
  284.4 46.1 %copy-start.42 = (f32[1536]{0:T(1024)S(1)}, f32[1536]{0:T(1024)}, u32[]{:S(2)}) copy-start(f32[1536]{0:T(1024)} %copy-done.41) | copy-start | bytes 18436
  284.4 46.1 %copy-start.44 = (f32[1536]{0:T(1024)S(1)}, f32[1536]{0:T(1024)}, u32[]{:S(2)}) copy-start(f32[1536]{0:T(1024)} %copy-done.43) | copy-start | bytes 18436
  284.4 46.1 %copy-start.46 = (f32[1536]{0:T(1024)S(1)}, f32[1536]{0:T(1024)}, u32[]{:S(2)}) copy-start(f32[1536]{0:T(1024)} %copy-done.45) | copy-start | bytes 18436
  284.4 46.1 %copy-start.48 = (f32[1536]{0:T(1024)S(1)}, f32[1536]{0:T(1024)}, u32[]{:S(2)}) copy-start(f32[1536]{0:T(1024)} %copy-done.47) | copy-start | bytes 18436
  284.7 45.5 %collective-permute-start.2 = (bf16[1,3,32,1536]{3,2,1,0:T(8,128)(2,1)S(1)}, bf16[1,3,32,1536]{3,2,1,0:T(8,128)(2,1)S(1)}, u32[]{:S(2)}, u32[]{:S(2)}) collective-permute-start(bf16[1,3,32,1536]{3,2,1,0:T(8,128)(2,1)S(1)} %get-tuple-element.116), channel_id=1, source_target_pairs={{0,1},{1,2},{2,3},{4,5},{5,6},{6,7},{8,9},{9,10},{10,11},{12,13},{... | collective-permute-start | bytes 884744 | tf_op jit(solution)/shard_map/ppermute | solution.py:25
  286.5 43.6 %collective-permute-start.3 = (bf16[1,3,32,1536]{3,2,1,0:T(8,128)(2,1)S(1)}, bf16[1,3,32,1536]{3,2,1,0:T(8,128)(2,1)S(1)}, u32[]{:S(2)}, u32[]{:S(2)}) collective-permute-start(bf16[1,3,32,1536]{3,2,1,0:T(8,128)(2,1)S(1)} %get-tuple-element.117), channel_id=1, source_target_pairs={{1,0},{2,1},{3,2},{5,4},{6,5},{7,6},{9,8},{10,9},{11,10},{13,12},{... | collective-permute-start | bytes 884744 | tf_op jit(solution)/shard_map/ppermute | solution.py:26
  (73 other events, 1542.2 us)
Sparse Core Ops, SparseCore 0:
  10.3 84.1 all-gather.2
  96.8 79.5 all-gather.4
  184.7 15.5 reduce-scatter.4
  226.4 26.0 reduce-scatter.6
  263.6 125.8 all-reduce.4
  394.5 195.6 reduce-scatter.10
  595.4 193.8 reduce-scatter.8
where the time goes:
time: 799 us; the launch traced here: 798 us
  waiting for transfers between devices  625 us (78%)
  blocking collectives  62.7 us (8%)
  matrix products  44.7 us (6%)
  other arithmetic  30 us (4%)
  between operations  16 us (2%)
  local copies, waits for them, and re-layouts  12.1 us (2%)
    reduce_scatter x1, waiting for transfers between devices, reduce_down(): lax.psum_scatter(down_part, ('dp', 'rows'), scatter_dimension=1, tiled=True)  201 us
    reduce_scatter x1, waiting for transfers between devices, body(): lax.psum_scatter(up_part, ('dp', 'rows'), scatter_dimension=0, tiled=True)  199 us
    all_gather x1, waiting for transfers between devices, body(): down_full = lax.all_gather(w_down, ('dp', 'rows'), axis=1, tiled=True)  73.7 us
    all_gather x1, waiting for transfers between devices, body(): up_full = lax.all_gather(w_up, ('dp', 'rows'), axis=0, tiled=True)  55.8 us
    psum x1, waiting for transfers between devices, body(): lax.psum((kernel_part, gain_part, scale_part), ('dp', 'fsdp', 'rows'))  51.2 us
    psum x1, blocking collectives, body(): lax.psum((kernel_part, gain_part, scale_part), ('dp', 'fsdp', 'rows'))  42.3 us
    reduce_scatter x1, waiting for transfers between devices, body(): lax.psum_scatter(norm_terms, 'fsdp', scatter_dimension=0, tiled=True)  26.2 us
  transfers between devices with their start and end apart: 11, of which 8 were waited for; matrix products, arithmetic and copies ran while one was open for 6% of the time, Pallas kernels for 0%

commit v1 on v0

--- a/solution.py
+++ b/solution.py
@@ -37,13 +37,17 @@
     return cdf_part + values * jnp.exp(-0.5 * values * values) * inv_root_two_pi
 
 
-def reduce_down(down_part):
-    return lax.psum_scatter(down_part, ("dp", "rows"), scatter_dimension=1, tiled=True)
-
-
 def body(feature_maps, dw_kernel, norm_gain, w_up, w_down, layer_scale, d_out):
     scenes, strip, across, width = feature_maps.shape
     cells = scenes * strip * across
+    hid_axes = ("fsdp", "rows")
+    up_loc = lax.all_to_all(w_up, "rows", 1, 0, tiled=True)
+    up_loc = lax.all_gather(up_loc, "dp", axis=0, tiled=True)
+    down_loc = lax.all_to_all(w_down, "rows", 0, 1, tiled=True)
+    down_loc = lax.all_gather(down_loc, "dp", axis=1, tiled=True)
+    cotan = d_out.reshape(cells, width).astype(jnp.float32)
+    back = (cotan * layer_scale).astype(jnp.bfloat16)
+    back_all = lax.all_gather(back, hid_axes, axis=0, tiled=True)
     rimmed = padded_2(feature_maps, (("rows", 1),), 3)
     padded = jnp.pad(rimmed.astype(jnp.float32), ((0, 0), (0, 0), (3, 3), (0, 0)))
     filtered = jnp.zeros(feature_maps.shape, jnp.float32)
@@ -61,35 +65,32 @@
     rstd = lax.rsqrt(variance + norm_eps)
     normed = center * rstd
     scaled = (normed * norm_gain).astype(jnp.bfloat16)
-    gathered = lax.all_gather(scaled, "fsdp", axis=0, tiled=True)
-    up_full = lax.all_gather(w_up, ("dp", "rows"), axis=0, tiled=True)
-    down_full = lax.all_gather(w_down, ("dp", "rows"), axis=1, tiled=True)
-    hidden = jnp.dot(gathered, up_full, preferred_element_type=jnp.float32)
+    gathered = lax.all_gather(scaled, hid_axes, axis=0, tiled=True)
+    hidden = jnp.dot(gathered, up_loc, preferred_element_type=jnp.float32)
     active = gelu_exact(hidden).astype(jnp.bfloat16)
-    mlp_terms = jnp.dot(active, down_full, preferred_element_type=jnp.float32)
+    mlp_terms = jnp.dot(active, down_loc, preferred_element_type=jnp.float32)
     branch = lax.psum_scatter(
-        mlp_terms.astype(jnp.bfloat16), "fsdp", scatter_dimension=0, tiled=True
+        mlp_terms.astype(jnp.bfloat16), hid_axes, scatter_dimension=0, tiled=True
     ).astype(jnp.float32)
     resid = feature_maps.reshape(cells, width).astype(jnp.float32)
     result = (resid + layer_scale * branch).astype(jnp.bfloat16).reshape(feature_maps.shape)
-    cotan = d_out.reshape(cells, width).astype(jnp.float32)
     scale_part = jnp.sum(cotan * branch, axis=0)
-    back = (cotan * layer_scale).astype(jnp.bfloat16)
-    back_all = lax.all_gather(back, "fsdp", axis=0, tiled=True)
     down_part = lax.dot_general(active, back_all, contract_rows, preferred_element_type=jnp.float32)
     slope_in = lax.dot_general(
-        back_all, down_full, contract_cols, preferred_element_type=jnp.float32
+        back_all, down_loc, contract_cols, preferred_element_type=jnp.float32
     )
     hidden_grad = (slope_in * gelu_slope(hidden)).astype(jnp.bfloat16)
     up_part = lax.dot_general(
         gathered, hidden_grad, contract_rows, preferred_element_type=jnp.float32
     )
     norm_terms = lax.dot_general(
-        hidden_grad, up_full, contract_cols, preferred_element_type=jnp.float32
+        hidden_grad, up_loc, contract_cols, preferred_element_type=jnp.float32
     )
-    norm_grad = lax.psum_scatter(norm_terms, "fsdp", scatter_dimension=0, tiled=True)
-    grad_up = lax.psum_scatter(up_part, ("dp", "rows"), scatter_dimension=0, tiled=True)
-    grad_down = reduce_down(down_part)
+    norm_grad = lax.psum_scatter(norm_terms, hid_axes, scatter_dimension=0, tiled=True)
+    grad_up = lax.psum_scatter(up_part, "dp", scatter_dimension=0, tiled=True)
+    grad_up = lax.all_to_all(grad_up, "rows", 0, 1, tiled=True)
+    grad_down = lax.psum_scatter(down_part, "dp", scatter_dimension=1, tiled=True)
+    grad_down = lax.all_to_all(grad_down, "rows", 1, 0, tiled=True)
     gain_part = jnp.sum(norm_grad * normed, axis=0)
     scaled_grad = norm_grad * norm_gain
     conv_grad = rstd * (

time: 799 us -> 635 us (0.79)
  waiting for transfers between devices: 625 us -> 426 us
  local copies, waits for them, and re-layouts: 12.1 us -> 30.5 us
  blocking collectives: 62.7 us -> 77.4 us
    reduce_scatter x4, waiting for transfers between devices: 442 us -> 180 us  [the longest x1 65.5 us: body(): lax.psum_scatter(down_part, 'dp', scatter_dimension=1, tiled=True)]
    psum x1, waiting for transfers between devices: 51.2 us -> 111 us  [body(): lax.psum((kernel_part, gain_part, scale_part), ('dp', 'fsdp', 'rows'))]
    all_to_all x0 -> x2, blocking collectives: none -> 29.5 us  [the longest x1 15.8 us: body(): down_loc = lax.all_to_all(w_down, 'rows', 0, 1, tiled=True)]
    all_gather x2 -> x0, blocking collectives: 20.4 us -> none  [the longest x1 11.8 us: body(): back_all = lax.all_gather(back, 'fsdp', axis=0, tiled=True)]
    another operation x50, local copies, waits for them, and re-layouts: 0.83 us -> 15.7 us  [body(): kernel_part = jnp.stack(kernel_rows).reshape(KS, KS, width)]
    all_gather x2 -> x4, waiting for transfers between devices: 129 us -> 128 us  [the longest x1 44.7 us: body(): down_loc = lax.all_gather(down_loc, 'dp', axis=1, tiled=True)]
  transfers between devices with their start and end apart: 11 -> 15, of which waited for: 8 -> 11; matrix products, arithmetic and copies ran while one was open for 6% -> 13% of each run, Pallas kernels for 0% -> 0%
where the time goes in v1:
time: 635 us; the launch traced here: 634 us
  waiting for transfers between devices  426 us (67%)
  blocking collectives  77.4 us (12%)
  matrix products  39.7 us (6%)
  other arithmetic  30.6 us (5%)
  local copies, waits for them, and re-layouts  30.5 us (5%)
  between operations  14.9 us (2%)
  starting transfers between devices  14.6 us (2%)
    psum x1, waiting for transfers between devices, body(): lax.psum((kernel_part, gain_part, scale_part), ('dp', 'fsdp', 'rows'))  111 us
    reduce_scatter x1, waiting for transfers between devices, body(): lax.psum_scatter(down_part, 'dp', scatter_dimension=1, tiled=True)  65.5 us
    reduce_scatter x1, waiting for transfers between devices, body(): lax.psum_scatter(norm_terms, hid_axes, scatter_dimension=0, tiled=True)  58.8 us
    psum x1, blocking collectives, body(): lax.psum((kernel_part, gain_part, scale_part), ('dp', 'fsdp', 'rows'))  48 us
    reduce_scatter x1, waiting for transfers between devices, body(): lax.psum_scatter(mlp_terms.astype(jnp.bfloat16), hid_axes, scatter_dimens...  45.1 us
    all_gather x1, waiting for transfers between devices, body(): down_loc = lax.all_gather(down_loc, 'dp', axis=1, tiled=True)  44.7 us
    all_gather x1, waiting for transfers between devices, body(): gathered = lax.all_gather(scaled, hid_axes, axis=0, tiled=True)  33.6 us
    all_gather x1, waiting for transfers between devices, body(): back_all = lax.all_gather(back, hid_axes, axis=0, tiled=True)  32.2 us
  transfers between devices with their start and end apart: 15, of which 11 were waited for; matrix products, arithmetic and copies ran while one was open for 13% of the time, Pallas kernels for 0%

profile of v1, /device:TPU:0, one launch (start us, length us, event | category | flops | bytes accessed | tf_op | source)
XLA Modules:
  0.0 633.8 jit_solution(6933835637550639418)
XLA Ops:
  8.4 13.7 %all_to_all.76 = bf16[96,4,768]{2,0,1:T(8,128)(2,1)} all-to-all(bf16[96,4,768]{2,0,1:T(8,128)(2,1)S(1)} %bitcast.112), channel_id=1, replica_groups=mesh['dp'=4,'fsdp'=2,'rows'=4] {'rows'}, dimensions={1} | all-to-all | bytes 1179648 | tf_op jit(solution)/shard_map/all_to_all | solution.py:44
  27.8 9.5 %fusion.103 = (f32[4,32]{1,0:T(4,128)S(1)}, f32[1,4,32,1536]{3,2,1,0:T(8,128)S(1)}) fusion(f32[1536]{0:T(1024)S(1)} %get-tuple-element.106, f32[1536]{0:T(1024)S(1)} %get-tuple-element.107, f32[1536]{0:T(1024)S(1)} %get-tuple-element.60, f32[1536]{0:T(1024)S(1)} %get-tuple-element.61, f32[1,10,32,1536]{3,2,1,0:T(8,128)S(1)} %maximum_convert_fusion, ...), kind=kLoop, calls=%fused_computation.315 | loop fusion | flops 19267456 | bytes 8641024 | tf_op jit(solution)/shard_map/reduce_sum | solution.py:62
  40.1 15.8 %all_to_all.77 = bf16[4,768,96]{1,2,0:T(8,128)(2,1)} all-to-all(bf16[4,768,96]{1,2,0:T(8,128)(2,1)S(1)} %bitcast.113), channel_id=1, replica_groups=mesh['dp'=4,'fsdp'=2,'rows'=4] {'rows'}, dimensions={0} | all-to-all | bytes 1179648 | tf_op jit(solution)/shard_map/all_to_all | solution.py:46
  56.0 17.5 %all-gather.7.cloned.1.call-done = bf16[1536,768]{1,0:T(8,128)(2,1)} async-done(((bf16[384,768]{1,0:T(8,128)(2,1)}), bf16[1536,768]{1,0:T(8,128)(2,1)}) %all-gather.7.cloned.1.call-update) | async-done | bytes 2359312 | tf_op jit(solution)/shard_map/all_gather | solution.py:45
  73.5 33.6 %all-gather.5.cloned.1.call-done = bf16[1024,1536]{1,0:T(8,128)(2,1)} async-done(((bf16[128,1536]{1,0:T(8,128)(2,1)}), bf16[1024,1536]{1,0:T(8,128)(2,1)}) %all-gather.5.cloned.1.call-update) | async-done | bytes 3145744 | tf_op jit(solution)/shard_map/all_gather | solution.py:68
  107.1 7.4 %multiply_convert_fusion = (bf16[1024,768]{1,0:T(8,128)(2,1)}, f32[1024,768]{1,0:T(8,128)}) fusion(bf16[1024,1536]{1,0:T(8,128)(2,1)} %all-gather.5.cloned.1.call-done, bf16[1536,768]{1,0:T(8,128)(2,1)} %all-gather.7.cloned.1.call-done), kind=kOutput, calls=%fused_computation.92 | convolution fusion | flops 2419851264 | bytes 10223616 | tf_op jit(solution)/shard_map/dot_general | solution.py:69
  114.5 44.7 %all-gather.9.cloned.1.call-done = bf16[768,1536]{0,1:T(8,128)(2,1)} async-done(((bf16[768,384]{0,1:T(8,128)(2,1)}), bf16[768,1536]{0,1:T(8,128)(2,1)}) %all-gather.9.cloned.1.call-update) | async-done | bytes 2359312 | tf_op jit(solution)/shard_map/all_gather | solution.py:47
  159.2 6.5 %convolution_convert_fusion = bf16[1024,1536]{1,0:T(8,128)(2,1)} fusion(bf16[1024,768]{1,0:T(8,128)(2,1)} %get-tuple-element.120, bf16[768,1536]{0,1:T(8,128)(2,1)} %all-gather.9.cloned.1.call-done), kind=kOutput, calls=%fused_computation.85 | convolution fusion | flops 2417491968 | bytes 7077888 | tf_op jit(solution)/shard_map/dot_general | solution.py:71
  165.7 45.1 %reduce-scatter.5.cloned.1.call-done = bf16[128,1536]{1,0:T(8,128)(2,1)} async-done(((bf16[1024,1536]{1,0:T(8,128)(2,1)}), bf16[128,1536]{1,0:T(8,128)(2,1)}) %reduce-scatter.5.cloned.1.call-update) | async-done | bytes 393232 | tf_op jit(solution)/shard_map/reduce_scatter | solution.py:72
  210.9 2.7 fusion.8
  213.8 32.2 %all-gather.11.cloned.1.call-done = bf16[1024,1536]{1,0:T(8,128)(2,1)} async-done(((bf16[128,1536]{1,0:T(8,128)(2,1)}), bf16[1024,1536]{1,0:T(8,128)(2,1)}) %all-gather.11.cloned.1.call-update) | async-done | bytes 3145744 | tf_op jit(solution)/shard_map/all_gather | solution.py:50
  246.0 7.2 %fusion.108 = f32[768,1536]{1,0:T(8,128)} fusion(bf16[1024,768]{1,0:T(8,128)(2,1)} %get-tuple-element.120, bf16[1024,1536]{1,0:T(8,128)(2,1)} %all-gather.11.cloned.1.call-done), kind=kOutput, calls=%fused_computation.320 | convolution fusion | flops 2415919104 | bytes 9437184 | tf_op jit(solution)/shard_map/dot_general | solution.py:78
  253.3 6.8 %fusion.5 = bf16[1024,768]{1,0:T(8,128)(2,1)S(1)} fusion(f32[1024,768]{1,0:T(8,128)} %get-tuple-element.121, bf16[1024,1536]{1,0:T(8,128)(2,1)} %all-gather.11.cloned.1.call-done, bf16[768,1536]{0,1:T(8,128)(2,1)} %all-gather.9.cloned.1.call-done), kind=kOutput, calls=%fused_computation.91 | convolution fusion | flops 2423783424 | bytes 10223616 | tf_op jit(solution)/shard_map/dot_general | solution.py:79
  261.3 4.6 fusion.106
  265.9 7.2 %fusion.107 = f32[1536,768]{1,0:T(8,128)} fusion(bf16[1024,1536]{1,0:T(8,128)(2,1)} %all-gather.5.cloned.1.call-done, bf16[1024,768]{1,0:T(8,128)(2,1)} %copy-done.49), kind=kOutput, calls=%fused_computation.319 | convolution fusion | flops 2415919104 | bytes 9437184 | tf_op jit(solution)/shard_map/dot_general | solution.py:83
  273.2 65.5 %reduce-scatter.11.cloned.1.call-done = f32[768,384]{1,0:T(8,128)} async-done(((f32[768,1536]{1,0:T(8,128)}), f32[768,384]{1,0:T(8,128)}) %reduce-scatter.11.cloned.1.call-update) | async-done | bytes 1179664 | tf_op jit(solution)/shard_map/reduce_scatter | solution.py:92
  338.7 2.7 copy.26
  341.4 4.3 all-to-all-start.3
  345.9 58.8 %reduce-scatter.7.cloned.1.call-done = f32[128,1536]{1,0:T(8,128)} async-done(((f32[1024,1536]{1,0:T(8,128)}), f32[128,1536]{1,0:T(8,128)}) %reduce-scatter.7.cloned.1.call-update) | async-done | bytes 786448 | tf_op jit(solution)/shard_map/reduce_scatter | solution.py:89
  404.7 2.0 multiply_reduce_fusion
  406.8 3.6 multiply_reduce_fusion.2
  410.4 2.0 multiply_reduce_fusion.1
  424.7 1.7 collective-permute-start.2
  429.3 4.2 stack.199
  434.3 48.0 %all-reduce.2 = (f32[1536]{0:T(1024)}, f32[1536]{0:T(1024)}) all-reduce(f32[1536]{0:T(1024)} %get-tuple-element.56, f32[1536]{0:T(1024)} %get-tuple-element.113), channel_id=1, replica_groups=mesh['dp'=4,'fsdp'=2,'rows'=4] {'dp','fsdp','rows'}, use_global_device_ids=true, to_apply=%region_59.60 | all-reduce | flops 3072 | bytes 24576 | tf_op jit(solution)/shard_map/psum | solution.py:119
  482.5 10.9 %reduce-scatter.9.cloned.1.call-done = f32[384,768]{1,0:T(8,128)} async-done(((f32[1536,768]{1,0:T(8,128)}), f32[384,768]{1,0:T(8,128)}) %reduce-scatter.9.cloned.1.call-update) | async-done | bytes 1179664 | tf_op jit(solution)/shard_map/reduce_scatter | solution.py:90
  493.4 3.5 all-to-all-start.2
  496.9 8.1 %fusion.96 = bf16[1,4,32,1536]{3,2,1,0:T(8,128)(2,1)} fusion(f32[1,10,32,1536]{3,2,1,0:T(8,128)S(1)} %maximum_convert_fusion.1, bf16[1,4,32,1536]{3,2,1,0:T(8,128)(2,1)S(1)} %copy-done.1, f32[1536]{0:T(1024)} %copy-done.13, f32[1536]{0:T(1024)} %copy-done.14, f32[1536]{0:T(1024)} %copy-done.16, f32[1536]{0:T(1024)} %copy-done.17, f32[1536]{0:T(1024)} %copy-done.18, ...), kind=kLoop, calls=%fused_computation.188 | loop fusion | flops 19660800 | bytes 8562688 | tf_op jit(solution)/shard_map/convert_element_type | solution.py:118
  505.0 2.4 copy.31
  507.4 5.8 all-to-all-done.2
  514.4 111.1 %all-reduce.5.cloned.1.call-done = f32[7,7,1536]{2,1,0:T(8,128)} async-done(((f32[7,7,1536]{2,1,0:T(8,128)}), f32[7,7,1536]{2,1,0:T(8,128)}) %all-reduce.5.cloned.1.call-update) | async-done | bytes 301072 | tf_op jit(solution)/shard_map/psum | solution.py:119
  625.5 1.7 copy.37
  (196 shorter events, 28.0 us)
Async XLA Ops:
  7.2 15.0 %copy-start = (bf16[1,4,32,1536]{3,2,1,0:T(8,128)(2,1)S(1)}, bf16[1,4,32,1536]{3,2,1,0:T(8,128)(2,1)}, u32[]{:S(2)}) copy-start(bf16[1,4,32,1536]{3,2,1,0:T(8,128)(2,1)} %param.7) | copy-start | bytes 1179652
  7.2 18.0 %copy-start.2 = (f32[7,7,1536]{2,1,0:T(8,128)S(1)}, f32[7,7,1536]{2,1,0:T(8,128)}, u32[]{:S(2)}) copy-start(f32[7,7,1536]{2,1,0:T(8,128)} %param.8) | copy-start | bytes 903172
  7.2 66.3 %all-gather.7.cloned.1.call-start = ((), (), s32[]{:S(2)}) async-start(), calls=%async_computation.9 | async-start | bytes 2949120 | tf_op jit(solution)/shard_map/all_gather | solution.py:45
  22.1 85.0 %all-gather.5.cloned.1.call-start = ((), (), s32[]{:S(2)}) async-start(), calls=%async_computation.8 | async-start | bytes 3538944 | tf_op jit(solution)/shard_map/all_gather | solution.py:68
  22.2 4.8 collective-permute-start
  23.9 3.7 collective-permute-start.1
  25.4 11.8 %copy-start.4 = (f32[1536]{0:T(1024)}, f32[1536]{0:T(1024)S(1)}, u32[]{:S(2)}) copy-start(f32[1536]{0:T(1024)S(1)} %get-tuple-element.98) | copy-start | bytes 18436
  25.4 11.8 %copy-start.6 = (f32[1536]{0:T(1024)}, f32[1536]{0:T(1024)S(1)}, u32[]{:S(2)}) copy-start(f32[1536]{0:T(1024)S(1)} %get-tuple-element.99) | copy-start | bytes 18436
  25.4 11.8 %copy-start.7 = (f32[1536]{0:T(1024)}, f32[1536]{0:T(1024)S(1)}, u32[]{:S(2)}) copy-start(f32[1536]{0:T(1024)S(1)} %get-tuple-element.100) | copy-start | bytes 18436
  25.4 11.8 %copy-start.8 = (f32[1536]{0:T(1024)}, f32[1536]{0:T(1024)S(1)}, u32[]{:S(2)}) copy-start(f32[1536]{0:T(1024)S(1)} %get-tuple-element.101) | copy-start | bytes 18436
  25.5 11.8 %copy-start.9 = (f32[1536]{0:T(1024)}, f32[1536]{0:T(1024)S(1)}, u32[]{:S(2)}) copy-start(f32[1536]{0:T(1024)S(1)} %get-tuple-element.102) | copy-start | bytes 18436
  25.5 11.8 %copy-start.10 = (f32[1536]{0:T(1024)}, f32[1536]{0:T(1024)S(1)}, u32[]{:S(2)}) copy-start(f32[1536]{0:T(1024)S(1)} %get-tuple-element.103) | copy-start | bytes 18436
  25.5 11.8 %copy-start.11 = (f32[1536]{0:T(1024)}, f32[1536]{0:T(1024)S(1)}, u32[]{:S(2)}) copy-start(f32[1536]{0:T(1024)S(1)} %get-tuple-element.104) | copy-start | bytes 18436
  25.5 11.8 %copy-start.12 = (f32[1536]{0:T(1024)}, f32[1536]{0:T(1024)S(1)}, u32[]{:S(2)}) copy-start(f32[1536]{0:T(1024)S(1)} %get-tuple-element.105) | copy-start | bytes 18436
  25.5 11.8 %copy-start.13 = (f32[1536]{0:T(1024)}, f32[1536]{0:T(1024)S(1)}, u32[]{:S(2)}) copy-start(f32[1536]{0:T(1024)S(1)} %get-tuple-element.106) | copy-start | bytes 18436
  37.7 18.3 %copy-start.44 = (f32[128]{0:T(128)}, f32[128]{0:T(128)S(1)}, u32[]{:S(2)}) copy-start(f32[128]{0:T(128)S(1)} %div.15) | copy-start | bytes 1540
  38.0 76.5 %copy-start.46 = (f32[128]{0:T(128)}, f32[128]{0:T(128)S(1)}, u32[]{:S(2)}) copy-start(f32[128]{0:T(128)S(1)} %rsqrt.12) | copy-start | bytes 1540
  39.0 120.2 %all-gather.9.cloned.1.call-start = ((), (), s32[]{:S(2)}) async-start(), calls=%async_computation.10 | async-start | bytes 2949120 | tf_op jit(solution)/shard_map/all_gather | solution.py:47
  56.0 154.9 %reduce-scatter.5.cloned.1.call-start = ((), (), s32[]{:S(2)}) async-start(), calls=%async_computation.11 | async-start | bytes 3538944 | tf_op jit(solution)/shard_map/reduce_scatter | solution.py:72
  165.7 45.2 %copy-start.1 = (bf16[1,4,32,1536]{3,2,1,0:T(8,128)(2,1)S(1)}, bf16[1,4,32,1536]{3,2,1,0:T(8,128)(2,1)}, u32[]{:S(2)}) copy-start(bf16[1,4,32,1536]{3,2,1,0:T(8,128)(2,1)} %param.13) | copy-start | bytes 1179652
  165.7 80.4 %all-gather.11.cloned.1.call-start = ((), (), s32[]{:S(2)}) async-start(), calls=%async_computation.12 | async-start | bytes 3538944 | tf_op jit(solution)/shard_map/all_gather | solution.py:50
  213.6 125.1 %reduce-scatter.11.cloned.1.call-start = ((), (), s32[]{:S(2)}) async-start(), calls=%async_computation.15 | async-start | bytes 5898240 | tf_op jit(solution)/shard_map/reduce_scatter | solution.py:92
  253.3 151.4 %reduce-scatter.7.cloned.1.call-start = ((), (), s32[]{:S(2)}) async-start(), calls=%async_computation.13 | async-start | bytes 7077888 | tf_op jit(solution)/shard_map/reduce_scatter | solution.py:89
  265.9 227.5 %reduce-scatter.9.cloned.1.call-start = ((), (), s32[]{:S(2)}) async-start(), calls=%async_computation.14 | async-start | bytes 5898240 | tf_op jit(solution)/shard_map/reduce_scatter | solution.py:90
  273.2 131.5 %copy-start.45 = (f32[128]{0:T(128)S(1)}, f32[128]{0:T(128)}, u32[]{:S(2)}) copy-start(f32[128]{0:T(128)} %copy-done.44) | copy-start | bytes 1540
  273.2 131.5 %copy-start.47 = (f32[128]{0:T(128)S(1)}, f32[128]{0:T(128)}, u32[]{:S(2)}) copy-start(f32[128]{0:T(128)} %copy-done.46) | copy-start | bytes 1540
  341.4 152.0 %all-to-all-start.3 = ((f32[768,4,96]{0,2,1:T(8,128)}), f32[768,4,96]{0,2,1:T(8,128)}, u32[]{:S(2)}, u32[]{:S(2)}) async-start(f32[768,4,96]{0,2,1:T(8,128)} %bitcast.108), calls=%async_computation.7 | async-start | bytes 2359296 | tf_op jit(solution)/shard_map/all_to_all | solution.py:93
  345.7 279.8 %all-reduce.5.cloned.1.call-start = ((), (), s32[]{:S(2)}) async-start(), calls=%async_computation.16 | async-start | bytes 688128 | tf_op jit(solution)/shard_map/psum | solution.py:119
  424.7 57.6 %collective-permute-start.2 = (bf16[1,3,32,1536]{3,2,1,0:T(8,128)(2,1)}, bf16[1,3,32,1536]{3,2,1,0:T(8,128)(2,1)S(1)}, u32[]{:S(2)}, u32[]{:S(2)}) collective-permute-start(bf16[1,3,32,1536]{3,2,1,0:T(8,128)(2,1)} %get-tuple-element.116), channel_id=1, source_target_pairs={{0,1},{1,2},{2,3},{4,5},{5,6},{6,7},{8,9},{9,10},{10,11},{12,13},{... | collective-permute-start | bytes 884744 | tf_op jit(solution)/shard_map/ppermute | solution.py:25
  426.5 55.8 %collective-permute-start.3 = (bf16[1,3,32,1536]{3,2,1,0:T(8,128)(2,1)}, bf16[1,3,32,1536]{3,2,1,0:T(8,128)(2,1)S(1)}, u32[]{:S(2)}, u32[]{:S(2)}) collective-permute-start(bf16[1,3,32,1536]{3,2,1,0:T(8,128)(2,1)} %get-tuple-element.117), channel_id=1, source_target_pairs={{1,0},{2,1},{3,2},{5,4},{6,5},{7,6},{9,8},{10,9},{11,10},{13,12},{... | collective-permute-start | bytes 884744 | tf_op jit(solution)/shard_map/ppermute | solution.py:26
  482.3 14.6 %copy-start.5 = (f32[1536]{0:T(1024)S(1)}, f32[1536]{0:T(1024)}, u32[]{:S(2)}) copy-start(f32[1536]{0:T(1024)} %copy-done.4) | copy-start | bytes 18436
  493.4 19.9 %all-to-all-start.2 = ((f32[4,96,768]{2,1,0:T(8,128)}), f32[4,96,768]{2,1,0:T(8,128)S(1)}, u32[]{:S(2)}, u32[]{:S(2)}) async-start(f32[4,96,768]{2,1,0:T(8,128)} %bitcast.115), calls=%async_computation.5 | async-start | bytes 2359296 | tf_op jit(solution)/shard_map/all_to_all | solution.py:91
  (33 other events, 355.0 us)
Sparse Core Ops, SparseCore 0:
  22.2 51.1 all-gather.6
  75.9 31.1 all-gather.4
  108.7 50.4 all-gather.8
  165.8 45.0 reduce-scatter.4
  213.7 32.2 all-gather.10
  253.4 85.2 reduce-scatter.10
  342.5 62.2 reduce-scatter.6
  407.0 86.2 reduce-scatter.8
  499.3 126.1 all-reduce.4

commit v2 on v1

--- a/solution.py
+++ b/solution.py
@@ -35,6 +35,22 @@
 def gelu_slope(values):
     cdf_part = 0.5 * (1.0 + jax.scipy.special.erf(values * inv_root_two))
     return cdf_part + values * jnp.exp(-0.5 * values * values) * inv_root_two_pi
+
+
+def small_sums(kernel_part, gain_part, scale_part, width):
+    every = ("dp", "fsdp", "rows")
+    devices = lax.axis_size(every)
+    packed = jnp.concatenate(
+        [kernel_part.reshape(KS * KS, width), gain_part[None], scale_part[None]], axis=0
+    )
+    count = packed.shape[0]
+    per = -(-count // devices)
+    packed = jnp.pad(packed, ((0, per * devices - count), (0, 0)))
+    mine = lax.all_to_all(packed.reshape(devices, per, width), every, 0, 0, tiled=True).sum(0)
+    spread = jnp.broadcast_to(mine[None], (devices, per, width))
+    total = lax.all_to_all(spread, every, 0, 0, tiled=True).reshape(devices * per, width)
+    kernel_sum = total[: KS * KS].reshape(KS, KS, width)
+    return kernel_sum, total[KS * KS], total[KS * KS + 1]
 
 
 def body(feature_maps, dw_kernel, norm_gain, w_up, w_down, layer_scale, d_out):
@@ -86,11 +102,17 @@
     norm_terms = lax.dot_general(
         hidden_grad, up_loc, contract_cols, preferred_element_type=jnp.float32
     )
-    norm_grad = lax.psum_scatter(norm_terms, hid_axes, scatter_dimension=0, tiled=True)
-    grad_up = lax.psum_scatter(up_part, "dp", scatter_dimension=0, tiled=True)
-    grad_up = lax.all_to_all(grad_up, "rows", 0, 1, tiled=True)
-    grad_down = lax.psum_scatter(down_part, "dp", scatter_dimension=1, tiled=True)
-    grad_down = lax.all_to_all(grad_down, "rows", 1, 0, tiled=True)
+    norm_grad = lax.psum_scatter(
+        norm_terms.astype(jnp.bfloat16), hid_axes, scatter_dimension=0, tiled=True
+    ).astype(jnp.float32)
+    grad_up = lax.psum_scatter(
+        up_part.astype(jnp.bfloat16), "dp", scatter_dimension=0, tiled=True
+    )
+    grad_up = lax.all_to_all(grad_up, "rows", 0, 1, tiled=True).astype(jnp.float32)
+    grad_down = lax.psum_scatter(
+        down_part.astype(jnp.bfloat16), "dp", scatter_dimension=1, tiled=True
+    )
+    grad_down = lax.all_to_all(grad_down, "rows", 1, 0, tiled=True).astype(jnp.float32)
     gain_part = jnp.sum(norm_grad * normed, axis=0)
     scaled_grad = norm_grad * norm_gain
     conv_grad = rstd * (
@@ -116,9 +138,7 @@
             )
     kernel_part = jnp.stack(kernel_rows).reshape(KS, KS, width)
     grad_x = (d_out.astype(jnp.float32) + back_conv).astype(jnp.bfloat16)
-    grad_kernel, grad_gain, grad_scale = lax.psum(
-        (kernel_part, gain_part, scale_part), ("dp", "fsdp", "rows")
-    )
+    grad_kernel, grad_gain, grad_scale = small_sums(kernel_part, gain_part, scale_part, width)
     return (result, grad_x, grad_up, grad_down, grad_kernel, grad_gain, grad_scale)
 
 

time: 635 us -> 454 us (0.71)
  waiting for transfers between devices: 426 us -> 295 us
  blocking collectives: 77.4 us -> 29.5 us
  local copies, waits for them, and re-layouts: 30.5 us -> 19.1 us
  starting transfers between devices: 14.6 us -> 23.4 us
    psum x1 -> x0, waiting for transfers between devices: 111 us -> none  [body(): lax.psum((kernel_part, gain_part, scale_part), ('dp', 'fsdp', 'rows'))]
    reduce_scatter x3 -> x2, waiting for transfers between devices: 135 us -> 75.3 us  [the longest x1 45.1 us: body(): lax.psum_scatter(norm_terms.astype(jnp.bfloat16), hid_axes, scatter_dimen...]
    psum x1 -> x0, blocking collectives: 48 us -> none  [body(): lax.psum((kernel_part, gain_part, scale_part), ('dp', 'fsdp', 'rows'))]
    unnamed x9, waiting for transfers between devices: 0.15 us -> 38.1 us
    another operation x50 -> x49, local copies, waits for them, and re-layouts: 15.7 us -> 0.31 us  [body(): kernel_part = jnp.stack(kernel_rows).reshape(KS, KS, width)]
    all_to_all x2 -> x4, starting transfers between devices: 7.82 us -> 16.4 us  [the longest x1 4.59 us: small_sums(): lax.all_to_all(packed.reshape(devices, per, width), every, 0, 0, tiled=True)]
  transfers between devices with their start and end apart: 15 -> 16, of which waited for: 11 -> 11; matrix products, arithmetic and copies ran while one was open for 13% -> 14% of each run, Pallas kernels for 0% -> 0%
where the time goes in v2:
time: 454 us; the launch traced here: 453 us
  waiting for transfers between devices  295 us (65%)
  matrix products  37.6 us (8%)
  other arithmetic  32.5 us (7%)
  blocking collectives  29.5 us (6%)
  starting transfers between devices  23.4 us (5%)
  local copies, waits for them, and re-layouts  19.1 us (4%)
  between operations  15.9 us (4%)
    reduce_scatter x1, waiting for transfers between devices, body(): lax.psum_scatter(norm_terms.astype(jnp.bfloat16), hid_axes, scatter_dimen...  45.1 us
    reduce_scatter x1, waiting for transfers between devices, body(): lax.psum_scatter(mlp_terms.astype(jnp.bfloat16), hid_axes, scatter_dimens...  45.1 us
    all_gather x1, waiting for transfers between devices, body(): down_loc = lax.all_gather(down_loc, 'dp', axis=1, tiled=True)  44.7 us
    unnamed x9, waiting for transfers between devices  38.1 us
    all_gather x1, waiting for transfers between devices, body(): gathered = lax.all_gather(scaled, hid_axes, axis=0, tiled=True)  33.6 us
    all_gather x1, waiting for transfers between devices, body(): back_all = lax.all_gather(back, hid_axes, axis=0, tiled=True)  32.2 us
    reduce_scatter x1, waiting for transfers between devices, body(): lax.psum_scatter(up_part.astype(jnp.bfloat16), 'dp', scatter_dimension=0,...  30.2 us
    all_gather x1, waiting for transfers between devices, body(): up_loc = lax.all_gather(up_loc, 'dp', axis=0, tiled=True)  17.5 us
  transfers between devices with their start and end apart: 16, of which 11 were waited for; matrix products, arithmetic and copies ran while one was open for 14% of the time, Pallas kernels for 0%

profile of v2, /device:TPU:0, one launch (start us, length us, event | category | flops | bytes accessed | tf_op | source)
XLA Modules:
  0.0 452.6 jit_solution(5773476002915113719)
XLA Ops:
  8.4 13.7 %all_to_all.74 = bf16[96,4,768]{2,0,1:T(8,128)(2,1)} all-to-all(bf16[96,4,768]{2,0,1:T(8,128)(2,1)S(1)} %bitcast.116), channel_id=1, replica_groups=mesh['dp'=4,'fsdp'=2,'rows'=4] {'rows'}, dimensions={1} | all-to-all | bytes 1179648 | tf_op jit(solution)/shard_map/all_to_all | solution.py:60
  22.2 1.7 collective-permute-start
  27.8 9.4 %fusion.111 = (f32[4,32]{1,0:T(4,128)S(1)}, f32[1,4,32,1536]{3,2,1,0:T(8,128)S(1)}) fusion(f32[1536]{0:T(1024)S(1)} %get-tuple-element.108, f32[1536]{0:T(1024)S(1)} %get-tuple-element.109, f32[1536]{0:T(1024)S(1)} %get-tuple-element.62, f32[1536]{0:T(1024)S(1)} %get-tuple-element.63, f32[1,10,32,1536]{3,2,1,0:T(8,128)S(1)} %maximum_convert_fusion, ...), kind=kLoop, calls=%fused_computation.327 | loop fusion | flops 19267456 | bytes 8641024 | tf_op jit(solution)/shard_map/reduce_sum | solution.py:78
  40.1 15.8 %all_to_all.75 = bf16[4,768,96]{1,2,0:T(8,128)(2,1)} all-to-all(bf16[4,768,96]{1,2,0:T(8,128)(2,1)S(1)} %bitcast.117), channel_id=1, replica_groups=mesh['dp'=4,'fsdp'=2,'rows'=4] {'rows'}, dimensions={0} | all-to-all | bytes 1179648 | tf_op jit(solution)/shard_map/all_to_all | solution.py:62
  56.0 17.5 %all-gather.7.cloned.1.call-done = bf16[1536,768]{1,0:T(8,128)(2,1)} async-done(((bf16[384,768]{1,0:T(8,128)(2,1)}), bf16[1536,768]{1,0:T(8,128)(2,1)}) %all-gather.7.cloned.1.call-update) | async-done | bytes 2359312 | tf_op jit(solution)/shard_map/all_gather | solution.py:61
  73.5 33.6 %all-gather.5.cloned.1.call-done = bf16[1024,1536]{1,0:T(8,128)(2,1)} async-done(((bf16[128,1536]{1,0:T(8,128)(2,1)}), bf16[1024,1536]{1,0:T(8,128)(2,1)}) %all-gather.5.cloned.1.call-update) | async-done | bytes 3145744 | tf_op jit(solution)/shard_map/all_gather | solution.py:84
  107.1 7.4 %multiply_convert_fusion = (bf16[1024,768]{1,0:T(8,128)(2,1)}, f32[1024,768]{1,0:T(8,128)}) fusion(bf16[1024,1536]{1,0:T(8,128)(2,1)} %all-gather.5.cloned.1.call-done, bf16[1536,768]{1,0:T(8,128)(2,1)} %all-gather.7.cloned.1.call-done), kind=kOutput, calls=%fused_computation.95 | convolution fusion | flops 2419851264 | bytes 10223616 | tf_op jit(solution)/shard_map/dot_general | solution.py:85
  114.5 44.7 %all-gather.9.cloned.1.call-done = bf16[768,1536]{0,1:T(8,128)(2,1)} async-done(((bf16[768,384]{0,1:T(8,128)(2,1)}), bf16[768,1536]{0,1:T(8,128)(2,1)}) %all-gather.9.cloned.1.call-update) | async-done | bytes 2359312 | tf_op jit(solution)/shard_map/all_gather | solution.py:63
  159.2 6.5 %convolution_convert_fusion.1 = bf16[1024,1536]{1,0:T(8,128)(2,1)} fusion(bf16[1024,768]{1,0:T(8,128)(2,1)} %get-tuple-element.120, bf16[768,1536]{0,1:T(8,128)(2,1)} %all-gather.9.cloned.1.call-done), kind=kOutput, calls=%fused_computation.86 | convolution fusion | flops 2417491968 | bytes 7077888 | tf_op jit(solution)/shard_map/dot_general | solution.py:87
  165.7 45.1 %reduce-scatter.7.cloned.1.call-done = bf16[128,1536]{1,0:T(8,128)(2,1)} async-done(((bf16[1024,1536]{1,0:T(8,128)(2,1)}), bf16[128,1536]{1,0:T(8,128)(2,1)}) %reduce-scatter.7.cloned.1.call-update) | async-done | bytes 393232 | tf_op jit(solution)/shard_map/reduce_scatter | solution.py:88
  210.9 2.7 fusion.11
  213.8 32.2 %all-gather.11.cloned.1.call-done = bf16[1024,1536]{1,0:T(8,128)(2,1)} async-done(((bf16[128,1536]{1,0:T(8,128)(2,1)}), bf16[1024,1536]{1,0:T(8,128)(2,1)}) %all-gather.11.cloned.1.call-update) | async-done | bytes 3145744 | tf_op jit(solution)/shard_map/all_gather | solution.py:66
  246.0 6.8 %fusion.5 = bf16[1024,768]{1,0:T(8,128)(2,1)S(1)} fusion(f32[1024,768]{1,0:T(8,128)} %get-tuple-element.121, bf16[1024,1536]{1,0:T(8,128)(2,1)} %all-gather.11.cloned.1.call-done, bf16[768,1536]{0,1:T(8,128)(2,1)} %all-gather.9.cloned.1.call-done), kind=kOutput, calls=%fused_computation.94 | convolution fusion | flops 2423783424 | bytes 10223616 | tf_op jit(solution)/shard_map/dot_general | solution.py:95
  254.1 4.0 convolution_convert_fusion.3
  258.1 6.4 %convolution_convert_fusion = bf16[1024,1536]{1,0:T(8,128)(2,1)} fusion(bf16[1024,768]{1,0:T(8,128)(2,1)} %copy-done.80, bf16[1536,768]{1,0:T(8,128)(2,1)} %all-gather.7.cloned.1.call-done), kind=kOutput, calls=%fused_computation.85 | convolution fusion | flops 2417491968 | bytes 7077888 | tf_op jit(solution)/shard_map/dot_general | solution.py:102
  264.7 6.5 %convolution_convert_fusion.2 = bf16[768,1536]{1,0:T(8,128)(2,1)} fusion(bf16[1024,768]{1,0:T(8,128)(2,1)} %get-tuple-element.120, bf16[1024,1536]{1,0:T(8,128)(2,1)} %all-gather.11.cloned.1.call-done), kind=kOutput, calls=%fused_computation.87 | convolution fusion | flops 2417098752 | bytes 7077888 | tf_op jit(solution)/shard_map/dot_general | solution.py:94
  271.2 4.3 copy.39
  276.1 30.2 %reduce-scatter.11.cloned.1.call-done = bf16[384,768]{1,0:T(8,128)(2,1)} async-done(((bf16[1536,768]{1,0:T(8,128)(2,1)}), bf16[384,768]{1,0:T(8,128)(2,1)}) %reduce-scatter.11.cloned.1.call-update) | async-done | bytes 589840 | tf_op jit(solution)/shard_map/reduce_scatter | solution.py:108
  306.3 4.4 all-to-all-start.2
  310.7 45.1 %reduce-scatter.9.cloned.1.call-done = bf16[128,1536]{1,0:T(8,128)(2,1)} async-done(((bf16[1024,1536]{1,0:T(8,128)(2,1)}), bf16[128,1536]{1,0:T(8,128)(2,1)}) %reduce-scatter.9.cloned.1.call-update) | async-done | bytes 393232 | tf_op jit(solution)/shard_map/reduce_scatter | solution.py:105
  355.8 1.4 fusion.15
  357.2 3.6 multiply_reduce_fusion.1
  360.8 2.0 multiply_reduce_fusion
  366.3 4.6 %all-to-all-start.4 = ((f32[32,2,1536]{2,1,0:T(2,128)}), f32[32,2,1536]{2,1,0:T(2,128)S(1)}, u32[]{:S(2)}, u32[]{:S(2)}) async-start(f32[32,2,1536]{2,1,0:T(2,128)} %reshape.346), calls=%async_computation.7 | async-start | bytes 786432 | tf_op jit(solution)/shard_map/all_to_all | solution.py:49
  371.0 2.2 collective-permute-start.2
  374.4 38.0 %reduce-scatter.13.cloned.1.call-done = bf16[384,768]{1,0:T(8,128)(2,1)} async-done(((bf16[1536,768]{1,0:T(8,128)(2,1)}), bf16[384,768]{1,0:T(8,128)(2,1)}) %reduce-scatter.13.cloned.1.call-update) | async-done | bytes 589840
  412.4 3.5 all-to-all-start.3
  419.6 5.8 %all-to-all-done.3 = bf16[768,4,96]{0,2,1:T(8,128)(2,1)S(1)} async-done(((bf16[768,4,96]{0,2,1:T(8,128)(2,1)}), bf16[768,4,96]{0,2,1:T(8,128)(2,1)S(1)}, u32[]{:S(2)}, u32[]{:S(2)}) %all-to-all-start.3) | async-done | bytes 589856 | tf_op jit(solution)/shard_map/all_to_all | solution.py:115
  425.4 1.5 broadcast_in_dim.8
  427.0 3.9 all-to-all-start.5
  431.2 7.7 %fusion.103 = bf16[1,4,32,1536]{3,2,1,0:T(8,128)(2,1)} fusion(f32[1,10,32,1536]{3,2,1,0:T(8,128)S(1)} %maximum_convert_fusion.1, bf16[1,4,32,1536]{3,2,1,0:T(8,128)(2,1)S(1)} %copy-done.2, f32[1536]{0:T(1024)S(1)} %copy-done.26, f32[1536]{0:T(1024)S(1)} %copy-done.28, f32[1536]{0:T(1024)S(1)} %copy-done.32, f32[1536]{0:T(1024)S(1)} %copy-done.34, ...), kind=kLoop, calls=%fused_computation.202 | loop fusion | flops 19660800 | bytes 8611840 | tf_op jit(solution)/shard_map/convert_element_type | solution.py:140
  442.3 1.7 all-to-all-done.5
  (268 shorter events, 22.9 us)
Async XLA Ops:
  7.2 15.0 %copy-start = (bf16[1,4,32,1536]{3,2,1,0:T(8,128)(2,1)S(1)}, bf16[1,4,32,1536]{3,2,1,0:T(8,128)(2,1)}, u32[]{:S(2)}) copy-start(bf16[1,4,32,1536]{3,2,1,0:T(8,128)(2,1)} %param.7) | copy-start | bytes 1179652
  7.2 18.0 %copy-start.7 = (f32[7,7,1536]{2,1,0:T(8,128)S(1)}, f32[7,7,1536]{2,1,0:T(8,128)}, u32[]{:S(2)}) copy-start(f32[7,7,1536]{2,1,0:T(8,128)} %param.8) | copy-start | bytes 903172
  7.2 66.3 %all-gather.7.cloned.1.call-start = ((), (), s32[]{:S(2)}) async-start(), calls=%async_computation.11 | async-start | bytes 2949120 | tf_op jit(solution)/shard_map/all_gather | solution.py:61
  22.1 85.0 %all-gather.5.cloned.1.call-start = ((), (), s32[]{:S(2)}) async-start(), calls=%async_computation.10 | async-start | bytes 3538944 | tf_op jit(solution)/shard_map/all_gather | solution.py:84
  22.2 4.8 %collective-permute-start = (bf16[1,3,32,1536]{3,2,1,0:T(8,128)(2,1)S(1)}, bf16[1,3,32,1536]{3,2,1,0:T(8,128)(2,1)S(1)}, u32[]{:S(2)}, u32[]{:S(2)}) collective-permute-start(bf16[1,3,32,1536]{3,2,1,0:T(8,128)(2,1)S(1)} %get-tuple-element.118), channel_id=1, source_target_pairs={{0,1},{1,2},{2,3},{4,5},{5,6},{6,7},{8,9},{9,10},{10,11},{12,13},{... | collective-permute-start | bytes 884744 | tf_op jit(solution)/shard_map/ppermute | solution.py:25
  23.9 3.7 collective-permute-start.1
  37.7 18.3 %copy-start.75 = (f32[128]{0:T(128)}, f32[128]{0:T(128)S(1)}, u32[]{:S(2)}) copy-start(f32[128]{0:T(128)S(1)} %div.15) | copy-start | bytes 1540
  38.0 76.5 %copy-start.77 = (f32[128]{0:T(128)}, f32[128]{0:T(128)S(1)}, u32[]{:S(2)}) copy-start(f32[128]{0:T(128)S(1)} %rsqrt.12) | copy-start | bytes 1540
  39.0 120.2 %all-gather.9.cloned.1.call-start = ((), (), s32[]{:S(2)}) async-start(), calls=%async_computation.12 | async-start | bytes 2949120 | tf_op jit(solution)/shard_map/all_gather | solution.py:63
  55.9 154.9 %reduce-scatter.7.cloned.1.call-start = ((), (), s32[]{:S(2)}) async-start(), calls=%async_computation.13 | async-start | bytes 3538944 | tf_op jit(solution)/shard_map/reduce_scatter | solution.py:88
  165.6 45.2 %copy-start.1 = (bf16[1,4,32,1536]{3,2,1,0:T(8,128)(2,1)S(1)}, bf16[1,4,32,1536]{3,2,1,0:T(8,128)(2,1)}, u32[]{:S(2)}) copy-start(bf16[1,4,32,1536]{3,2,1,0:T(8,128)(2,1)} %param.13) | copy-start | bytes 1179652
  165.7 80.4 %all-gather.11.cloned.1.call-start = ((), (), s32[]{:S(2)}) async-start(), calls=%async_computation.14 | async-start | bytes 3538944 | tf_op jit(solution)/shard_map/all_gather | solution.py:66
  213.6 92.7 %reduce-scatter.11.cloned.1.call-start = ((), (), s32[]{:S(2)}) async-start(), calls=%async_computation.16 | async-start | bytes 2949120 | tf_op jit(solution)/shard_map/reduce_scatter | solution.py:108
  258.1 97.7 %reduce-scatter.9.cloned.1.call-start = ((), (), s32[]{:S(2)}) async-start(), calls=%async_computation.15 | async-start | bytes 3538944 | tf_op jit(solution)/shard_map/reduce_scatter | solution.py:105
  264.6 147.8 %reduce-scatter.13.cloned.1.call-start = ((), (), s32[]{:S(2)}) async-start(), calls=%async_computation.17 | async-start | bytes 2949120
  275.5 80.4 %copy-start.76 = (f32[128]{0:T(128)S(1)}, f32[128]{0:T(128)}, u32[]{:S(2)}) copy-start(f32[128]{0:T(128)} %copy-done.75) | copy-start | bytes 1540
  275.5 80.4 %copy-start.78 = (f32[128]{0:T(128)S(1)}, f32[128]{0:T(128)}, u32[]{:S(2)}) copy-start(f32[128]{0:T(128)} %copy-done.77) | copy-start | bytes 1540
  306.3 60.0 %all-to-all-start.2 = ((bf16[4,96,768]{2,1,0:T(8,128)(2,1)}), bf16[4,96,768]{2,1,0:T(8,128)(2,1)}, u32[]{:S(2)}, u32[]{:S(2)}) async-start(bf16[4,96,768]{2,1,0:T(8,128)(2,1)} %bitcast.124), calls=%async_computation.5 | async-start | bytes 1179648 | tf_op jit(solution)/shard_map/all_to_all | solution.py:111
  366.3 46.1 %all-to-all-start.4 = ((f32[32,2,1536]{2,1,0:T(2,128)}), f32[32,2,1536]{2,1,0:T(2,128)S(1)}, u32[]{:S(2)}, u32[]{:S(2)}) async-start(f32[32,2,1536]{2,1,0:T(2,128)} %reshape.346), calls=%async_computation.7 | async-start | bytes 786432 | tf_op jit(solution)/shard_map/all_to_all | solution.py:49
  371.0 45.3 %collective-permute-start.2 = (bf16[1,3,32,1536]{3,2,1,0:T(8,128)(2,1)S(1)}, bf16[1,3,32,1536]{3,2,1,0:T(8,128)(2,1)S(1)}, u32[]{:S(2)}, u32[]{:S(2)}) collective-permute-start(bf16[1,3,32,1536]{3,2,1,0:T(8,128)(2,1)S(1)} %get-tuple-element.116), channel_id=1, source_target_pairs={{0,1},{1,2},{2,3},{4,5},{5,6},{6,7},{8,9},{9,10},{10,11},{12,13},{... | collective-permute-start | bytes 884744 | tf_op jit(solution)/shard_map/ppermute | solution.py:25
  373.1 43.1 %collective-permute-start.3 = (bf16[1,3,32,1536]{3,2,1,0:T(8,128)(2,1)S(1)}, bf16[1,3,32,1536]{3,2,1,0:T(8,128)(2,1)S(1)}, u32[]{:S(2)}, u32[]{:S(2)}) collective-permute-start(bf16[1,3,32,1536]{3,2,1,0:T(8,128)(2,1)S(1)} %get-tuple-element.117), channel_id=1, source_target_pairs={{1,0},{2,1},{3,2},{5,4},{6,5},{7,6},{9,8},{10,9},{11,10},{13,12},{... | collective-permute-start | bytes 884744 | tf_op jit(solution)/shard_map/ppermute | solution.py:26
  412.4 13.0 %all-to-all-start.3 = ((bf16[768,4,96]{0,2,1:T(8,128)(2,1)}), bf16[768,4,96]{0,2,1:T(8,128)(2,1)S(1)}, u32[]{:S(2)}, u32[]{:S(2)}) async-start(bf16[768,4,96]{0,2,1:T(8,128)(2,1)} %bitcast.123), calls=%async_computation.6 | async-start | bytes 1179648 | tf_op jit(solution)/shard_map/all_to_all | solution.py:115
  416.0 14.9 %copy-start.2 = (bf16[1,4,32,1536]{3,2,1,0:T(8,128)(2,1)S(1)}, bf16[1,4,32,1536]{3,2,1,0:T(8,128)(2,1)}, u32[]{:S(2)}) copy-start(bf16[1,4,32,1536]{3,2,1,0:T(8,128)(2,1)} %param.13) | copy-start | bytes 1179652
  416.0 14.9 %copy-start.10 = (f32[1536]{0:T(1024)S(1)}, f32[1536]{0:T(1024)}, u32[]{:S(2)}) copy-start(f32[1536]{0:T(1024)} %copy-done.9) | copy-start | bytes 18436
  416.0 14.9 %copy-start.12 = (f32[1536]{0:T(1024)S(1)}, f32[1536]{0:T(1024)}, u32[]{:S(2)}) copy-start(f32[1536]{0:T(1024)} %copy-done.11) | copy-start | bytes 18436
  416.0 14.9 %copy-start.14 = (f32[1536]{0:T(1024)S(1)}, f32[1536]{0:T(1024)}, u32[]{:S(2)}) copy-start(f32[1536]{0:T(1024)} %copy-done.13) | copy-start | bytes 18436
  416.0 14.9 %copy-start.16 = (f32[1536]{0:T(1024)S(1)}, f32[1536]{0:T(1024)}, u32[]{:S(2)}) copy-start(f32[1536]{0:T(1024)} %copy-done.15) | copy-start | bytes 18436
  416.0 14.9 %copy-start.18 = (f32[1536]{0:T(1024)S(1)}, f32[1536]{0:T(1024)}, u32[]{:S(2)}) copy-start(f32[1536]{0:T(1024)} %copy-done.17) | copy-start | bytes 18436
  416.0 14.9 %copy-start.20 = (f32[1536]{0:T(1024)S(1)}, f32[1536]{0:T(1024)}, u32[]{:S(2)}) copy-start(f32[1536]{0:T(1024)} %copy-done.19) | copy-start | bytes 18436
  416.0 14.9 %copy-start.22 = (f32[1536]{0:T(1024)S(1)}, f32[1536]{0:T(1024)}, u32[]{:S(2)}) copy-start(f32[1536]{0:T(1024)} %copy-done.21) | copy-start | bytes 18436
  416.0 14.9 %copy-start.24 = (f32[1536]{0:T(1024)S(1)}, f32[1536]{0:T(1024)}, u32[]{:S(2)}) copy-start(f32[1536]{0:T(1024)} %copy-done.23) | copy-start | bytes 18436
  427.0 17.1 %all-to-all-start.5 = ((f32[32,2,1536]{2,1,0:T(2,128)}), f32[32,2,1536]{2,1,0:T(2,128)S(1)}, u32[]{:S(2)}, u32[]{:S(2)}) async-start(f32[32,2,1536]{2,1,0:T(2,128)} %broadcast_in_dim.8), calls=%async_computation.8 | async-start | bytes 786432 | tf_op jit(solution)/shard_map/all_to_all | solution.py:51
  (65 other events, 727.1 us)
Sparse Core Ops, SparseCore 0:
  22.2 51.1 all-gather.6
  75.9 31.1 all-gather.4
  108.6 50.4 all-gather.8
  165.8 45.0 reduce-scatter.6
  213.7 32.2 all-gather.10
  258.2 48.0 reduce-scatter.10
  310.0 45.7 reduce-scatter.8
  358.1 54.2 reduce-scatter.12

commit v3 on v2

--- a/solution.py
+++ b/solution.py
@@ -53,14 +53,43 @@
     return kernel_sum, total[KS * KS], total[KS * KS + 1]
 
 
+def shifts(devices):
+    return [d for d in range(1, devices)] + [-d for d in range(1, devices)]
+
+
+def line_perm(devices, d):
+    return [(i, i + d) for i in range(devices) if 0 <= i + d < devices]
+
+
+def gather_dp(x):
+    devices = lax.axis_size("dp")
+    me = lax.axis_index("dp")
+    got = {d: lax.ppermute(x, "dp", line_perm(devices, d)) for d in shifts(devices)}
+    order = [got[d] for d in range(devices - 1, 0, -1)] + [x] + [got[-d] for d in range(1, devices)]
+    stacked = jnp.stack(order)
+    return lax.dynamic_slice_in_dim(stacked, devices - 1 - me, devices, axis=0)
+
+
+def scatter_sum_dp(parts):
+    devices = lax.axis_size("dp")
+    me = lax.axis_index("dp")
+    sent = parts.astype(jnp.bfloat16)
+    total = lax.dynamic_index_in_dim(parts, me, axis=0, keepdims=False)
+    for d in shifts(devices):
+        target = jnp.clip(me + d, 0, devices - 1)
+        block = lax.dynamic_index_in_dim(sent, target, axis=0, keepdims=False)
+        total = total + lax.ppermute(block, "dp", line_perm(devices, d)).astype(jnp.float32)
+    return total
+
+
 def body(feature_maps, dw_kernel, norm_gain, w_up, w_down, layer_scale, d_out):
     scenes, strip, across, width = feature_maps.shape
     cells = scenes * strip * across
     hid_axes = ("fsdp", "rows")
-    up_loc = lax.all_to_all(w_up, "rows", 1, 0, tiled=True)
-    up_loc = lax.all_gather(up_loc, "dp", axis=0, tiled=True)
-    down_loc = lax.all_to_all(w_down, "rows", 0, 1, tiled=True)
-    down_loc = lax.all_gather(down_loc, "dp", axis=1, tiled=True)
+    up_loc = gather_dp(lax.all_to_all(w_up, "rows", 1, 0, tiled=True))
+    dp_size, block_c, hid_part = up_loc.shape
+    up_loc = up_loc.reshape(dp_size * block_c, hid_part)
+    down3 = gather_dp(lax.all_to_all(w_down, "rows", 0, 1, tiled=True))
     cotan = d_out.reshape(cells, width).astype(jnp.float32)
     back = (cotan * layer_scale).astype(jnp.bfloat16)
     back_all = lax.all_gather(back, hid_axes, axis=0, tiled=True)
@@ -84,16 +113,23 @@
     gathered = lax.all_gather(scaled, hid_axes, axis=0, tiled=True)
     hidden = jnp.dot(gathered, up_loc, preferred_element_type=jnp.float32)
     active = gelu_exact(hidden).astype(jnp.bfloat16)
-    mlp_terms = jnp.dot(active, down_loc, preferred_element_type=jnp.float32)
+    mlp_terms = jnp.einsum(
+        "xh,khj->xkj", active, down3, preferred_element_type=jnp.float32
+    ).reshape(active.shape[0], width)
     branch = lax.psum_scatter(
         mlp_terms.astype(jnp.bfloat16), hid_axes, scatter_dimension=0, tiled=True
     ).astype(jnp.float32)
     resid = feature_maps.reshape(cells, width).astype(jnp.float32)
     result = (resid + layer_scale * branch).astype(jnp.bfloat16).reshape(feature_maps.shape)
     scale_part = jnp.sum(cotan * branch, axis=0)
-    down_part = lax.dot_general(active, back_all, contract_rows, preferred_element_type=jnp.float32)
-    slope_in = lax.dot_general(
-        back_all, down_loc, contract_cols, preferred_element_type=jnp.float32
+    down_part_t = lax.dot_general(
+        back_all, active, contract_rows, preferred_element_type=jnp.float32
+    )
+    slope_in = jnp.einsum(
+        "xkj,khj->xh",
+        back_all.reshape(back_all.shape[0], dp_size, block_c),
+        down3,
+        preferred_element_type=jnp.float32,
     )
     hidden_grad = (slope_in * gelu_slope(hidden)).astype(jnp.bfloat16)
     up_part = lax.dot_general(
@@ -105,14 +141,10 @@
     norm_grad = lax.psum_scatter(
         norm_terms.astype(jnp.bfloat16), hid_axes, scatter_dimension=0, tiled=True
     ).astype(jnp.float32)
-    grad_up = lax.psum_scatter(
-        up_part.astype(jnp.bfloat16), "dp", scatter_dimension=0, tiled=True
-    )
-    grad_up = lax.all_to_all(grad_up, "rows", 0, 1, tiled=True).astype(jnp.float32)
-    grad_down = lax.psum_scatter(
-        down_part.astype(jnp.bfloat16), "dp", scatter_dimension=1, tiled=True
-    )
-    grad_down = lax.all_to_all(grad_down, "rows", 1, 0, tiled=True).astype(jnp.float32)
+    grad_up = scatter_sum_dp(up_part.reshape(dp_size, block_c, hid_part))
+    grad_up = lax.all_to_all(grad_up, "rows", 0, 1, tiled=True)
+    grad_down_t = scatter_sum_dp(down_part_t.reshape(dp_size, block_c, hid_part))
+    grad_down = lax.all_to_all(grad_down_t, "rows", 0, 1, tiled=True).T
     gain_part = jnp.sum(norm_grad * normed, axis=0)
     scaled_grad = norm_grad * norm_gain
     conv_grad = rstd * (

time: 454 us -> 510 us (1.12)
  starting transfers between devices: 23.4 us -> 145 us
  waiting for transfers between devices: 295 us -> 227 us
  local copies, waits for them, and re-layouts: 19.1 us -> 49.6 us
  blocking collectives: 29.5 us -> 0 us
  other arithmetic: 32.5 us -> 38.9 us
  matrix products: 37.6 us -> 32.2 us
    ppermute x0 -> x24, waiting for transfers between devices: none -> 117 us  [the longest x12 68.4 us: gather_dp(): lax.ppermute(x, 'dp', line_perm(devices, d))]
    ppermute x0 -> x24, starting transfers between devices: none -> 113 us  [the longest x12 57.7 us: gather_dp(): lax.ppermute(x, 'dp', line_perm(devices, d))]
    all_gather x2 -> x0, waiting for transfers between devices: 62.2 us -> none  [the longest x1 44.7 us: body(): down_loc = lax.all_gather(down_loc, 'dp', axis=1, tiled=True)]
    reduce_scatter x1, waiting for transfers between devices: 45.1 us -> 0.01 us  [body(): lax.psum_scatter(norm_terms.astype(jnp.bfloat16), hid_axes, scatter_dimen...]
    unnamed x9 -> x4, waiting for transfers between devices: 38.1 us -> 0.07 us
    all_gather x1, waiting for transfers between devices: 33.6 us -> 0.01 us  [body(): gathered = lax.all_gather(scaled, hid_axes, axis=0, tiled=True)]
    reduce_scatter x1 -> x0, waiting for transfers between devices: 30.2 us -> none  [body(): lax.psum_scatter(up_part.astype(jnp.bfloat16), 'dp', scatter_dimension=0,...]
    all_to_all x2 -> x0, blocking collectives: 29.5 us -> none  [the longest x1 15.8 us: body(): down_loc = lax.all_to_all(w_down, 'rows', 0, 1, tiled=True)]
  transfers between devices with their start and end apart: 16 -> 38, of which waited for: 11 -> 18; matrix products, arithmetic and copies ran while one was open for 14% -> 12% of each run, Pallas kernels for 0% -> 0%
where the time goes in v3:
time: 510 us; the launch traced here: 508 us
  waiting for transfers between devices  227 us (45%)
  starting transfers between devices  145 us (28%)
  local copies, waits for them, and re-layouts  49.6 us (10%)
  other arithmetic  38.9 us (8%)
  matrix products  32.2 us (6%)
  between operations  16 us (3%)
    ppermute x12, waiting for transfers between devices, gather_dp(): lax.ppermute(x, 'dp', line_perm(devices, d))  68.4 us
    ppermute x12, starting transfers between devices, gather_dp(): lax.ppermute(x, 'dp', line_perm(devices, d))  57.7 us
    ppermute x12, starting transfers between devices, scatter_sum_dp(): lax.ppermute(block, 'dp', line_perm(devices, d)).astype(jnp.float32)  55.2 us
    ppermute x12, waiting for transfers between devices, scatter_sum_dp(): lax.ppermute(block, 'dp', line_perm(devices, d)).astype(jnp.float32)  48.4 us
    reduce_scatter x1, waiting for transfers between devices, body(): lax.psum_scatter(mlp_terms.astype(jnp.bfloat16), hid_axes, scatter_dimens...  44.7 us
    all_gather x1, waiting for transfers between devices, body(): back_all = lax.all_gather(back, hid_axes, axis=0, tiled=True)  32.2 us
    unnamed x210, local copies, waits for them, and re-layouts  15 us
  transfers between devices with their start and end apart: 38, of which 18 were waited for; matrix products, arithmetic and copies ran while one was open for 12% of the time, Pallas kernels for 0%

profile of v3, /device:TPU:0, one launch (start us, length us, event | category | flops | bytes accessed | tf_op | source)
XLA Modules:
  0.0 508.2 jit_solution(11445574879648555610)
XLA Ops:
  19.2 9.5 %fusion.129 = (f32[4,32]{1,0:T(4,128)S(1)}, f32[1,4,32,1536]{3,2,1,0:T(8,128)S(1)}) fusion(f32[1536]{0:T(1024)S(1)} %get-tuple-element.115, f32[1536]{0:T(1024)S(1)} %get-tuple-element.116, f32[1536]{0:T(1024)S(1)} %get-tuple-element.69, f32[1536]{0:T(1024)S(1)} %get-tuple-element.70, f32[1,10,32,1536]{3,2,1,0:T(8,128)S(1)} %maximum_convert_fusion, ...), kind=kLoop, calls=%fused_computation.368 | loop fusion | flops 19267456 | bytes 8641024 | tf_op jit(solution)/shard_map/reduce_sum | solution.py:107
  31.3 6.1 %all-to-all-start = ((bf16[96,4,768]{2,0,1:T(8,128)(2,1)}), bf16[96,4,768]{2,0,1:T(8,128)(2,1)S(1)}, u32[]{:S(2)}, u32[]{:S(2)}) async-start(bf16[96,4,768]{2,0,1:T(8,128)(2,1)} %bitcast.220), calls=%async_computation | async-start | bytes 1179648 | tf_op jit(solution)/shard_map/all_to_all | solution.py:89
  39.4 9.6 %all-to-all-done = bf16[96,4,768]{2,0,1:T(8,128)(2,1)S(1)} async-done(((bf16[96,4,768]{2,0,1:T(8,128)(2,1)}), bf16[96,4,768]{2,0,1:T(8,128)(2,1)S(1)}, u32[]{:S(2)}, u32[]{:S(2)}) %all-to-all-start) | async-done | bytes 589856 | tf_op jit(solution)/shard_map/all_to_all | solution.py:89
  53.3 6.6 %collective-permute-start.2 = (bf16[384,768]{1,0:T(8,128)(2,1)}, bf16[384,768]{1,0:T(8,128)(2,1)}, u32[]{:S(2)}, u32[]{:S(2)}) collective-permute-start(bf16[384,768]{1,0:T(8,128)(2,1)} %bitcast.212), channel_id=1, source_target_pairs={{0,24},{1,25},{2,26},{3,27},{4,28},{5,29},{6,30},{7,31}} | collective-permute-start | bytes 1769480 | tf_op jit(solution)/shard_map/ppermute | solution.py:67
  59.9 6.8 %all-to-all-done.1 = bf16[4,768,96]{1,2,0:T(8,128)(2,1)S(1)} async-done(((bf16[4,768,96]{1,2,0:T(8,128)(2,1)}), bf16[4,768,96]{1,2,0:T(8,128)(2,1)S(1)}, u32[]{:S(2)}, u32[]{:S(2)}) %all-to-all-start.1) | async-done | bytes 589856 | tf_op jit(solution)/shard_map/all_to_all | solution.py:92
  66.7 7.1 %collective-permute-start.8 = (bf16[768,384]{0,1:T(8,128)(2,1)S(1)}, bf16[768,384]{0,1:T(8,128)(2,1)}, u32[]{:S(2)}, u32[]{:S(2)}) collective-permute-start(bf16[768,384]{0,1:T(8,128)(2,1)S(1)} %bitcast.205), channel_id=1, source_target_pairs={{0,24},{1,25},{2,26},{3,27},{4,28},{5,29},{6,30},{7,31}} | collective-permute-start | bytes 1769480 | tf_op jit(solution)/shard_map/ppermute | solution.py:67
  81.6 5.4 %collective-permute-done.8 = bf16[768,384]{0,1:T(8,128)(2,1)} collective-permute-done((bf16[768,384]{0,1:T(8,128)(2,1)S(1)}, bf16[768,384]{0,1:T(8,128)(2,1)}, u32[]{:S(2)}, u32[]{:S(2)}) %collective-permute-start.8) | collective-permute-done | bytes 589856 | tf_op jit(solution)/shard_map/ppermute | solution.py:67
  90.1 9.5 %collective-permute-done.3 = bf16[384,768]{1,0:T(8,128)(2,1)} collective-permute-done((bf16[384,768]{1,0:T(8,128)(2,1)}, bf16[384,768]{1,0:T(8,128)(2,1)}, u32[]{:S(2)}, u32[]{:S(2)}) %collective-permute-start.3) | collective-permute-done | bytes 589856 | tf_op jit(solution)/shard_map/ppermute | solution.py:67
  99.7 5.3 %collective-permute-start.9 = (bf16[768,384]{0,1:T(8,128)(2,1)S(1)}, bf16[768,384]{0,1:T(8,128)(2,1)S(1)}, u32[]{:S(2)}, u32[]{:S(2)}) collective-permute-start(bf16[768,384]{0,1:T(8,128)(2,1)S(1)} %bitcast.206), channel_id=1, source_target_pairs={{0,16},{8,24},{1,17},{9,25},{2,18},{10,26},{3,19},{11,27},{4,20},{... | collective-permute-start | bytes 1769480 | tf_op jit(solution)/shard_map/ppermute | solution.py:67
  106.1 6.2 %collective-permute-done.4 = bf16[384,768]{1,0:T(8,128)(2,1)S(1)} collective-permute-done((bf16[384,768]{1,0:T(8,128)(2,1)}, bf16[384,768]{1,0:T(8,128)(2,1)S(1)}, u32[]{:S(2)}, u32[]{:S(2)}) %collective-permute-start.4) | collective-permute-done | bytes 589856 | tf_op jit(solution)/shard_map/ppermute | solution.py:67
  112.3 27.0 %collective-permute-start.10 = (bf16[768,384]{0,1:T(8,128)(2,1)S(1)}, bf16[768,384]{0,1:T(8,128)(2,1)S(1)}, u32[]{:S(2)}, u32[]{:S(2)}) collective-permute-start(bf16[768,384]{0,1:T(8,128)(2,1)S(1)} %bitcast.207), channel_id=1, source_target_pairs={{0,8},{8,16},{16,24},{1,9},{9,17},{17,25},{2,10},{10,18},{18,26},{... | collective-permute-start | bytes 1769480 | tf_op jit(solution)/shard_map/ppermute | solution.py:67
  144.4 7.5 %collective-permute-done.10 = bf16[768,384]{0,1:T(8,128)(2,1)S(1)} collective-permute-done((bf16[768,384]{0,1:T(8,128)(2,1)S(1)}, bf16[768,384]{0,1:T(8,128)(2,1)S(1)}, u32[]{:S(2)}, u32[]{:S(2)}) %collective-permute-start.10) | collective-permute-done | bytes 589856 | tf_op jit(solution)/shard_map/ppermute | solution.py:67
  157.7 38.1 %collective-permute-done.12 = bf16[768,384]{0,1:T(8,128)(2,1)S(1)} collective-permute-done((bf16[768,384]{0,1:T(8,128)(2,1)S(1)}, bf16[768,384]{0,1:T(8,128)(2,1)S(1)}, u32[]{:S(2)}, u32[]{:S(2)}) %collective-permute-start.12) | collective-permute-done | bytes 589856 | tf_op jit(solution)/shard_map/ppermute | solution.py:67
  197.7 6.9 %multiply_convert_fusion = (bf16[1024,768]{1,0:T(8,128)(2,1)S(1)}, f32[1024,768]{1,0:T(8,128)}) fusion(bf16[1024,1536]{1,0:T(8,128)(2,1)} %all-gather.3.cloned.1.call-done, bf16[1536,768]{1,0:T(8,128)(2,1)} %bitcast.203), kind=kOutput, calls=%fused_computation.92 | convolution fusion | flops 2419851264 | bytes 10223616 | tf_op jit(solution)/shard_map/dot_general | solution.py:114
  204.5 6.3 %convolution_convert_fusion.1 = bf16[1024,4,384]{0,2,1:T(8,128)(2,1)} fusion(bf16[7,768,384]{1,2,0:T(8,128)(2,1)} %bitcast_dynamic-update-slice_fusion.1, s32[]{:T(128)S(6)} %select_n.22, bf16[1024,768]{1,0:T(8,128)(2,1)S(1)} %get-tuple-element.139), kind=kOutput, calls=%fused_computation.94 | convolution fusion | flops 2417491968 | bytes 7077892 | tf_op jit(solution)/shard_map/xh,khj->xkj/dot_general | solution.py:116
  210.9 4.6 copy.53
  215.6 44.7 %reduce-scatter.3.cloned.1.call-done = bf16[128,1536]{1,0:T(8,128)(2,1)} async-done(((bf16[1024,1536]{1,0:T(8,128)(2,1)}), bf16[128,1536]{1,0:T(8,128)(2,1)}) %reduce-scatter.3.cloned.1.call-update) | async-done | bytes 393232 | tf_op jit(solution)/shard_map/reduce_scatter | solution.py:119
  263.3 32.2 %all-gather.5.cloned.1.call-done = bf16[1024,1536]{1,0:T(8,128)(2,1)} async-done(((bf16[128,1536]{1,0:T(8,128)(2,1)}), bf16[1024,1536]{1,0:T(8,128)(2,1)}) %all-gather.5.cloned.1.call-update) | async-done | bytes 3145744 | tf_op jit(solution)/shard_map/all_gather | solution.py:95
  295.5 4.7 copy.54
  300.2 7.2 %fusion.5 = bf16[1024,768]{1,0:T(8,128)(2,1)S(1)} fusion(f32[1024,768]{1,0:T(8,128)} %get-tuple-element.140, bf16[1024,4,384]{0,2,1:T(8,128)(2,1)} %bitcast.201, bf16[7,768,384]{1,2,0:T(8,128)(2,1)} %bitcast_dynamic-update-slice_fusion.1, s32[]{:T(128)S(6)} %select_n.22), kind=kOutput, calls=%fused_computation.91 | convolution fusion | flops 2423783424 | bytes 10223620 | tf_op jit(solution)/shard_map/xkj,khj->xh/dot_general | solution.py:128
  312.7 5.0 fusion.133
  325.0 5.1 %collective-permute-start.23 = (bf16[384,768]{1,0:T(8,128)(2,1)S(1)}, bf16[384,768]{1,0:T(8,128)(2,1)}, u32[]{:S(2)}, u32[]{:S(2)}) collective-permute-start(bf16[384,768]{1,0:T(8,128)(2,1)S(1)} %get-tuple-element.125), channel_id=1, source_target_pairs={{0,16},{8,24},{1,17},{9,25},{2,18},{10,26},{3,19},{11,27},{4,20},{... | collective-permute-start | bytes 1769480 | tf_op jit(solution)/shard_map/ppermute | solution.py:81
  343.0 8.2 %collective-permute-done.23 = bf16[384,768]{1,0:T(8,128)(2,1)} collective-permute-done((bf16[384,768]{1,0:T(8,128)(2,1)S(1)}, bf16[384,768]{1,0:T(8,128)(2,1)}, u32[]{:S(2)}, u32[]{:S(2)}) %collective-permute-start.23) | collective-permute-done | bytes 589856 | tf_op jit(solution)/shard_map/ppermute | solution.py:81
  351.3 28.8 %collective-permute-start.16 = (bf16[384,768]{1,0:T(8,128)(2,1)}, bf16[384,768]{1,0:T(8,128)(2,1)}, u32[]{:S(2)}, u32[]{:S(2)}) collective-permute-start(bf16[384,768]{1,0:T(8,128)(2,1)} %get-tuple-element.126), channel_id=1, source_target_pairs={{0,8},{8,16},{16,24},{1,9},{9,17},{17,25},{2,10},{10,18},{18,26},{... | collective-permute-start | bytes 1769480 | tf_op jit(solution)/shard_map/ppermute | solution.py:81
  380.0 5.4 %collective-permute-start.17 = (bf16[384,768]{1,0:T(8,128)(2,1)}, bf16[384,768]{1,0:T(8,128)(2,1)}, u32[]{:S(2)}, u32[]{:S(2)}) collective-permute-start(bf16[384,768]{1,0:T(8,128)(2,1)} %get-tuple-element.131), channel_id=1, source_target_pairs={{0,16},{8,24},{1,17},{9,25},{2,18},{10,26},{3,19},{11,27},{4,20},{... | collective-permute-start | bytes 1769480 | tf_op jit(solution)/shard_map/ppermute | solution.py:81
  398.4 4.3 all-to-all-start.3
  406.0 11.1 %collective-permute-done.18 = bf16[384,768]{1,0:T(8,128)(2,1)} collective-permute-done((bf16[384,768]{1,0:T(8,128)(2,1)}, bf16[384,768]{1,0:T(8,128)(2,1)}, u32[]{:S(2)}, u32[]{:S(2)}) %collective-permute-start.18) | collective-permute-done | bytes 589856 | tf_op jit(solution)/shard_map/ppermute | solution.py:81
  417.1 23.2 %collective-permute-done.20 = bf16[384,768]{1,0:T(8,128)(2,1)} collective-permute-done((bf16[384,768]{1,0:T(8,128)(2,1)}, bf16[384,768]{1,0:T(8,128)(2,1)}, u32[]{:S(2)}, u32[]{:S(2)}) %collective-permute-start.20) | collective-permute-done | bytes 589856 | tf_op jit(solution)/shard_map/ppermute | solution.py:81
  459.5 6.8 %all-to-all-done.2 = f32[4,96,768]{2,1,0:T(8,128)} async-done(((f32[4,96,768]{2,1,0:T(8,128)}), f32[4,96,768]{2,1,0:T(8,128)}, u32[]{:S(2)}, u32[]{:S(2)}) %all-to-all-start.2) | async-done | bytes 1179680 | tf_op jit(solution)/shard_map/all_to_all | solution.py:145
  477.7 4.4 all-to-all-done.4
  487.2 7.4 %fusion.119 = bf16[1,4,32,1536]{3,2,1,0:T(8,128)(2,1)} fusion(f32[1,10,32,1536]{3,2,1,0:T(8,128)S(1)} %maximum_convert_fusion.1, bf16[1,4,32,1536]{3,2,1,0:T(8,128)(2,1)S(1)} %copy-done.7, f32[1536]{0:T(1024)S(1)} %copy-done.27, f32[1536]{0:T(1024)S(1)} %copy-done.29, f32[1536]{0:T(1024)S(1)} %copy-done.33, f32[1536]{0:T(1024)S(1)} %copy-done.35, ...), kind=kLoop, calls=%fused_computation.214 | loop fusion | flops 19660800 | bytes 8640512 | tf_op jit(solution)/shard_map/convert_element_type | solution.py:172
  494.6 5.4 %all-to-all-done.5 = f32[32,2,1536]{2,1,0:T(2,128)S(1)} async-done(((f32[32,2,1536]{2,1,0:T(2,128)}), f32[32,2,1536]{2,1,0:T(2,128)S(1)}, u32[]{:S(2)}, u32[]{:S(2)}) %all-to-all-start.5) | async-done | bytes 393248 | tf_op jit(solution)/shard_map/all_to_all | solution.py:51
  (362 shorter events, 125.7 us)
Async XLA Ops:
  7.2 190.5 %all-gather.3.cloned.1.call-start = ((), (), s32[]{:S(2)}) async-start(), calls=%async_computation.8 | async-start | bytes 3538944 | tf_op jit(solution)/shard_map/all_gather | solution.py:113
  31.3 17.7 %all-to-all-start = ((bf16[96,4,768]{2,0,1:T(8,128)(2,1)}), bf16[96,4,768]{2,0,1:T(8,128)(2,1)S(1)}, u32[]{:S(2)}, u32[]{:S(2)}) async-start(bf16[96,4,768]{2,0,1:T(8,128)(2,1)} %bitcast.220), calls=%async_computation | async-start | bytes 1179648 | tf_op jit(solution)/shard_map/all_to_all | solution.py:89
  49.8 17.0 %all-to-all-start.1 = ((bf16[4,768,96]{1,2,0:T(8,128)(2,1)}), bf16[4,768,96]{1,2,0:T(8,128)(2,1)S(1)}, u32[]{:S(2)}, u32[]{:S(2)}) async-start(bf16[4,768,96]{1,2,0:T(8,128)(2,1)} %bitcast.219), calls=%async_computation.1 | async-start | bytes 1179648 | tf_op jit(solution)/shard_map/all_to_all | solution.py:92
  53.3 207.0 %reduce-scatter.3.cloned.1.call-start = ((), (), s32[]{:S(2)}) async-start(), calls=%async_computation.9 | async-start | bytes 3538944 | tf_op jit(solution)/shard_map/reduce_scatter | solution.py:119
  53.3 25.8 %collective-permute-start.2 = (bf16[384,768]{1,0:T(8,128)(2,1)}, bf16[384,768]{1,0:T(8,128)(2,1)}, u32[]{:S(2)}, u32[]{:S(2)}) collective-permute-start(bf16[384,768]{1,0:T(8,128)(2,1)} %bitcast.212), channel_id=1, source_target_pairs={{0,24},{1,25},{2,26},{3,27},{4,28},{5,29},{6,30},{7,31}} | collective-permute-start | bytes 1769480 | tf_op jit(solution)/shard_map/ppermute | solution.py:67
  66.7 20.2 %collective-permute-start.8 = (bf16[768,384]{0,1:T(8,128)(2,1)S(1)}, bf16[768,384]{0,1:T(8,128)(2,1)}, u32[]{:S(2)}, u32[]{:S(2)}) collective-permute-start(bf16[768,384]{0,1:T(8,128)(2,1)S(1)} %bitcast.205), channel_id=1, source_target_pairs={{0,24},{1,25},{2,26},{3,27},{4,28},{5,29},{6,30},{7,31}} | collective-permute-start | bytes 1769480 | tf_op jit(solution)/shard_map/ppermute | solution.py:67
  73.9 25.8 %collective-permute-start.3 = (bf16[384,768]{1,0:T(8,128)(2,1)}, bf16[384,768]{1,0:T(8,128)(2,1)}, u32[]{:S(2)}, u32[]{:S(2)}) collective-permute-start(bf16[384,768]{1,0:T(8,128)(2,1)} %bitcast.213), channel_id=1, source_target_pairs={{0,16},{8,24},{1,17},{9,25},{2,18},{10,26},{3,19},{11,27},{4,20},{... | collective-permute-start | bytes 1769480 | tf_op jit(solution)/shard_map/ppermute | solution.py:67
  76.0 36.3 %collective-permute-start.4 = (bf16[384,768]{1,0:T(8,128)(2,1)}, bf16[384,768]{1,0:T(8,128)(2,1)S(1)}, u32[]{:S(2)}, u32[]{:S(2)}) collective-permute-start(bf16[384,768]{1,0:T(8,128)(2,1)} %bitcast.214), channel_id=1, source_target_pairs={{0,8},{8,16},{16,24},{1,9},{9,17},{17,25},{2,10},{10,18},{18,26},{... | collective-permute-start | bytes 1769480 | tf_op jit(solution)/shard_map/ppermute | solution.py:67
  77.8 61.6 %collective-permute-start.5 = (bf16[384,768]{1,0:T(8,128)(2,1)}, bf16[384,768]{1,0:T(8,128)(2,1)S(1)}, u32[]{:S(2)}, u32[]{:S(2)}) collective-permute-start(bf16[384,768]{1,0:T(8,128)(2,1)} %bitcast.215), channel_id=1, source_target_pairs={{8,0},{16,8},{24,16},{9,1},{17,9},{25,17},{10,2},{18,10},{26,18},{... | collective-permute-start | bytes 1769480 | tf_op jit(solution)/shard_map/ppermute | solution.py:67
  79.1 61.6 %collective-permute-start.6 = (bf16[384,768]{1,0:T(8,128)(2,1)}, bf16[384,768]{1,0:T(8,128)(2,1)S(1)}, u32[]{:S(2)}, u32[]{:S(2)}) collective-permute-start(bf16[384,768]{1,0:T(8,128)(2,1)} %bitcast.216), channel_id=1, source_target_pairs={{16,0},{24,8},{17,1},{25,9},{18,2},{26,10},{19,3},{27,11},{20,4},{... | collective-permute-start | bytes 1769480 | tf_op jit(solution)/shard_map/ppermute | solution.py:67
  86.9 55.2 %collective-permute-start.7 = (bf16[384,768]{1,0:T(8,128)(2,1)}, bf16[384,768]{1,0:T(8,128)(2,1)S(1)}, u32[]{:S(2)}, u32[]{:S(2)}) collective-permute-start(bf16[384,768]{1,0:T(8,128)(2,1)} %bitcast.217), channel_id=1, source_target_pairs={{24,0},{25,1},{26,2},{27,3},{28,4},{29,5},{30,6},{31,7}} | collective-permute-start | bytes 1769480 | tf_op jit(solution)/shard_map/ppermute | solution.py:67
  99.7 43.8 %collective-permute-start.9 = (bf16[768,384]{0,1:T(8,128)(2,1)S(1)}, bf16[768,384]{0,1:T(8,128)(2,1)S(1)}, u32[]{:S(2)}, u32[]{:S(2)}) collective-permute-start(bf16[768,384]{0,1:T(8,128)(2,1)S(1)} %bitcast.206), channel_id=1, source_target_pairs={{0,16},{8,24},{1,17},{9,25},{2,18},{10,26},{3,19},{11,27},{4,20},{... | collective-permute-start | bytes 1769480 | tf_op jit(solution)/shard_map/ppermute | solution.py:67
  112.3 39.6 %collective-permute-start.10 = (bf16[768,384]{0,1:T(8,128)(2,1)S(1)}, bf16[768,384]{0,1:T(8,128)(2,1)S(1)}, u32[]{:S(2)}, u32[]{:S(2)}) collective-permute-start(bf16[768,384]{0,1:T(8,128)(2,1)S(1)} %bitcast.207), channel_id=1, source_target_pairs={{0,8},{8,16},{16,24},{1,9},{9,17},{17,25},{2,10},{10,18},{18,26},{... | collective-permute-start | bytes 1769480 | tf_op jit(solution)/shard_map/ppermute | solution.py:67
  139.4 17.5 %collective-permute-start.11 = (bf16[768,384]{0,1:T(8,128)(2,1)S(1)}, bf16[768,384]{0,1:T(8,128)(2,1)S(1)}, u32[]{:S(2)}, u32[]{:S(2)}) collective-permute-start(bf16[768,384]{0,1:T(8,128)(2,1)S(1)} %bitcast.208), channel_id=1, source_target_pairs={{8,0},{16,8},{24,16},{9,1},{17,9},{25,17},{10,2},{18,10},{26,18},{... | collective-permute-start | bytes 1769480 | tf_op jit(solution)/shard_map/ppermute | solution.py:67
  140.8 55.1 %collective-permute-start.12 = (bf16[768,384]{0,1:T(8,128)(2,1)S(1)}, bf16[768,384]{0,1:T(8,128)(2,1)S(1)}, u32[]{:S(2)}, u32[]{:S(2)}) collective-permute-start(bf16[768,384]{0,1:T(8,128)(2,1)S(1)} %bitcast.209), channel_id=1, source_target_pairs={{16,0},{24,8},{17,1},{25,9},{18,2},{26,10},{19,3},{27,11},{20,4},{... | collective-permute-start | bytes 1769480 | tf_op jit(solution)/shard_map/ppermute | solution.py:67
  142.1 54.6 %collective-permute-start.13 = (bf16[768,384]{0,1:T(8,128)(2,1)S(1)}, bf16[768,384]{0,1:T(8,128)(2,1)S(1)}, u32[]{:S(2)}, u32[]{:S(2)}) collective-permute-start(bf16[768,384]{0,1:T(8,128)(2,1)S(1)} %bitcast.210), channel_id=1, source_target_pairs={{24,0},{25,1},{26,2},{27,3},{28,4},{29,5},{30,6},{31,7}} | collective-permute-start | bytes 1769480 | tf_op jit(solution)/shard_map/ppermute | solution.py:67
  215.5 80.0 %all-gather.5.cloned.1.call-start = ((), (), s32[]{:S(2)}) async-start(), calls=%async_computation.10 | async-start | bytes 3538944 | tf_op jit(solution)/shard_map/all_gather | solution.py:95
  263.0 181.1 %reduce-scatter.5.cloned.1.call-start = ((), (), s32[]{:S(2)}) async-start(), calls=%async_computation.11 | async-start | bytes 3538944 | tf_op jit(solution)/shard_map/reduce_scatter | solution.py:141
  321.3 20.3 %collective-permute-start.22 = (bf16[384,768]{1,0:T(8,128)(2,1)S(1)}, bf16[384,768]{1,0:T(8,128)(2,1)S(1)}, u32[]{:S(2)}, u32[]{:S(2)}) collective-permute-start(bf16[384,768]{1,0:T(8,128)(2,1)S(1)} %get-tuple-element.120), channel_id=1, source_target_pairs={{0,8},{8,16},{16,24},{1,9},{9,17},{17,25},{2,10},{10,18},{18,26},{... | collective-permute-start | bytes 1769480 | tf_op jit(solution)/shard_map/ppermute | solution.py:81
  325.0 26.3 %collective-permute-start.23 = (bf16[384,768]{1,0:T(8,128)(2,1)S(1)}, bf16[384,768]{1,0:T(8,128)(2,1)}, u32[]{:S(2)}, u32[]{:S(2)}) collective-permute-start(bf16[384,768]{1,0:T(8,128)(2,1)S(1)} %get-tuple-element.125), channel_id=1, source_target_pairs={{0,16},{8,24},{1,17},{9,25},{2,18},{10,26},{3,19},{11,27},{4,20},{... | collective-permute-start | bytes 1769480 | tf_op jit(solution)/shard_map/ppermute | solution.py:81
  330.1 50.0 %collective-permute-start.24 = (bf16[384,768]{1,0:T(8,128)(2,1)}, bf16[384,768]{1,0:T(8,128)(2,1)}, u32[]{:S(2)}, u32[]{:S(2)}) collective-permute-start(bf16[384,768]{1,0:T(8,128)(2,1)} %get-tuple-element.124), channel_id=1, source_target_pairs={{0,24},{1,25},{2,26},{3,27},{4,28},{5,29},{6,30},{7,31}} | collective-permute-start | bytes 1769480 | tf_op jit(solution)/shard_map/ppermute | solution.py:81
  332.2 53.3 %collective-permute-start.25 = (bf16[384,768]{1,0:T(8,128)(2,1)}, bf16[384,768]{1,0:T(8,128)(2,1)}, u32[]{:S(2)}, u32[]{:S(2)}) collective-permute-start(bf16[384,768]{1,0:T(8,128)(2,1)} %get-tuple-element.123), channel_id=1, source_target_pairs={{8,0},{16,8},{24,16},{9,1},{17,9},{25,17},{10,2},{18,10},{26,18},{... | collective-permute-start | bytes 1769480 | tf_op jit(solution)/shard_map/ppermute | solution.py:81
  333.5 54.1 %collective-permute-start.26 = (bf16[384,768]{1,0:T(8,128)(2,1)}, bf16[384,768]{1,0:T(8,128)(2,1)}, u32[]{:S(2)}, u32[]{:S(2)}) collective-permute-start(bf16[384,768]{1,0:T(8,128)(2,1)} %get-tuple-element.122), channel_id=1, source_target_pairs={{16,0},{24,8},{17,1},{25,9},{18,2},{26,10},{19,3},{27,11},{20,4},{... | collective-permute-start | bytes 1769480 | tf_op jit(solution)/shard_map/ppermute | solution.py:81
  341.5 47.3 %collective-permute-start.27 = (bf16[384,768]{1,0:T(8,128)(2,1)}, bf16[384,768]{1,0:T(8,128)(2,1)}, u32[]{:S(2)}, u32[]{:S(2)}) collective-permute-start(bf16[384,768]{1,0:T(8,128)(2,1)} %get-tuple-element.121), channel_id=1, source_target_pairs={{24,0},{25,1},{26,2},{27,3},{28,4},{29,5},{30,6},{31,7}} | collective-permute-start | bytes 1769480 | tf_op jit(solution)/shard_map/ppermute | solution.py:81
  351.3 42.0 %collective-permute-start.16 = (bf16[384,768]{1,0:T(8,128)(2,1)}, bf16[384,768]{1,0:T(8,128)(2,1)}, u32[]{:S(2)}, u32[]{:S(2)}) collective-permute-start(bf16[384,768]{1,0:T(8,128)(2,1)} %get-tuple-element.126), channel_id=1, source_target_pairs={{0,8},{8,16},{16,24},{1,9},{9,17},{17,25},{2,10},{10,18},{18,26},{... | collective-permute-start | bytes 1769480 | tf_op jit(solution)/shard_map/ppermute | solution.py:81
  380.0 25.9 %collective-permute-start.17 = (bf16[384,768]{1,0:T(8,128)(2,1)}, bf16[384,768]{1,0:T(8,128)(2,1)}, u32[]{:S(2)}, u32[]{:S(2)}) collective-permute-start(bf16[384,768]{1,0:T(8,128)(2,1)} %get-tuple-element.131), channel_id=1, source_target_pairs={{0,16},{8,24},{1,17},{9,25},{2,18},{10,26},{3,19},{11,27},{4,20},{... | collective-permute-start | bytes 1769480 | tf_op jit(solution)/shard_map/ppermute | solution.py:81
  385.5 31.6 %collective-permute-start.18 = (bf16[384,768]{1,0:T(8,128)(2,1)}, bf16[384,768]{1,0:T(8,128)(2,1)}, u32[]{:S(2)}, u32[]{:S(2)}) collective-permute-start(bf16[384,768]{1,0:T(8,128)(2,1)} %get-tuple-element.130), channel_id=1, source_target_pairs={{0,24},{1,25},{2,26},{3,27},{4,28},{5,29},{6,30},{7,31}} | collective-permute-start | bytes 1769480 | tf_op jit(solution)/shard_map/ppermute | solution.py:81
  387.6 29.5 %collective-permute-start.19 = (bf16[384,768]{1,0:T(8,128)(2,1)}, bf16[384,768]{1,0:T(8,128)(2,1)}, u32[]{:S(2)}, u32[]{:S(2)}) collective-permute-start(bf16[384,768]{1,0:T(8,128)(2,1)} %get-tuple-element.129), channel_id=1, source_target_pairs={{8,0},{16,8},{24,16},{9,1},{17,9},{25,17},{10,2},{18,10},{26,18},{... | collective-permute-start | bytes 1769480 | tf_op jit(solution)/shard_map/ppermute | solution.py:81
  388.9 51.4 %collective-permute-start.20 = (bf16[384,768]{1,0:T(8,128)(2,1)}, bf16[384,768]{1,0:T(8,128)(2,1)}, u32[]{:S(2)}, u32[]{:S(2)}) collective-permute-start(bf16[384,768]{1,0:T(8,128)(2,1)} %get-tuple-element.128), channel_id=1, source_target_pairs={{16,0},{24,8},{17,1},{25,9},{18,2},{26,10},{19,3},{27,11},{20,4},{... | collective-permute-start | bytes 1769480 | tf_op jit(solution)/shard_map/ppermute | solution.py:81
  393.3 47.0 %collective-permute-start.21 = (bf16[384,768]{1,0:T(8,128)(2,1)}, bf16[384,768]{1,0:T(8,128)(2,1)}, u32[]{:S(2)}, u32[]{:S(2)}) collective-permute-start(bf16[384,768]{1,0:T(8,128)(2,1)} %get-tuple-element.127), channel_id=1, source_target_pairs={{24,0},{25,1},{26,2},{27,3},{28,4},{29,5},{30,6},{31,7}} | collective-permute-start | bytes 1769480 | tf_op jit(solution)/shard_map/ppermute | solution.py:81
  398.4 47.7 %all-to-all-start.3 = ((f32[4,96,768]{2,1,0:T(8,128)}), f32[4,96,768]{2,1,0:T(8,128)}, u32[]{:S(2)}, u32[]{:S(2)}) async-start(f32[4,96,768]{2,1,0:T(8,128)} %bitcast.200), calls=%async_computation.5 | async-start | bytes 2359296 | tf_op jit(solution)/shard_map/all_to_all | solution.py:147
  446.1 20.2 %all-to-all-start.2 = ((f32[4,96,768]{2,1,0:T(8,128)}), f32[4,96,768]{2,1,0:T(8,128)}, u32[]{:S(2)}, u32[]{:S(2)}) async-start(f32[4,96,768]{2,1,0:T(8,128)} %bitcast.199), calls=%async_computation.4 | async-start | bytes 2359296 | tf_op jit(solution)/shard_map/all_to_all | solution.py:145
  (105 other events, 1300.3 us)
Sparse Core Ops, SparseCore 0:
  30.6 42.2 all-gather.2
  215.7 44.5 reduce-scatter.2
  263.1 32.2 all-gather.4
  312.8 46.2 reduce-scatter.4

commit v4 on v2

--- a/solution.py
+++ b/solution.py
@@ -57,10 +57,10 @@
     scenes, strip, across, width = feature_maps.shape
     cells = scenes * strip * across
     hid_axes = ("fsdp", "rows")
-    up_loc = lax.all_to_all(w_up, "rows", 1, 0, tiled=True)
-    up_loc = lax.all_gather(up_loc, "dp", axis=0, tiled=True)
-    down_loc = lax.all_to_all(w_down, "rows", 0, 1, tiled=True)
-    down_loc = lax.all_gather(down_loc, "dp", axis=1, tiled=True)
+    up_mine = lax.all_to_all(w_up, "rows", 1, 0, tiled=True)
+    down_mine = lax.all_to_all(w_down, "rows", 0, 1, tiled=True)
+    both = lax.all_gather(jnp.stack([up_mine, down_mine.T]), "dp", axis=1, tiled=True)
+    up_loc, down_t = both[0], both[1]
     cotan = d_out.reshape(cells, width).astype(jnp.float32)
     back = (cotan * layer_scale).astype(jnp.bfloat16)
     back_all = lax.all_gather(back, hid_axes, axis=0, tiled=True)
@@ -84,17 +84,19 @@
     gathered = lax.all_gather(scaled, hid_axes, axis=0, tiled=True)
     hidden = jnp.dot(gathered, up_loc, preferred_element_type=jnp.float32)
     active = gelu_exact(hidden).astype(jnp.bfloat16)
-    mlp_terms = jnp.dot(active, down_loc, preferred_element_type=jnp.float32)
+    mlp_terms = lax.dot_general(
+        active, down_t, contract_cols, preferred_element_type=jnp.float32
+    )
     branch = lax.psum_scatter(
         mlp_terms.astype(jnp.bfloat16), hid_axes, scatter_dimension=0, tiled=True
     ).astype(jnp.float32)
     resid = feature_maps.reshape(cells, width).astype(jnp.float32)
     result = (resid + layer_scale * branch).astype(jnp.bfloat16).reshape(feature_maps.shape)
     scale_part = jnp.sum(cotan * branch, axis=0)
-    down_part = lax.dot_general(active, back_all, contract_rows, preferred_element_type=jnp.float32)
-    slope_in = lax.dot_general(
-        back_all, down_loc, contract_cols, preferred_element_type=jnp.float32
+    down_part_t = lax.dot_general(
+        back_all, active, contract_rows, preferred_element_type=jnp.float32
     )
+    slope_in = jnp.dot(back_all, down_t, preferred_element_type=jnp.float32)
     hidden_grad = (slope_in * gelu_slope(hidden)).astype(jnp.bfloat16)
     up_part = lax.dot_general(
         gathered, hidden_grad, contract_rows, preferred_element_type=jnp.float32
@@ -105,14 +107,13 @@
     norm_grad = lax.psum_scatter(
         norm_terms.astype(jnp.bfloat16), hid_axes, scatter_dimension=0, tiled=True
     ).astype(jnp.float32)
-    grad_up = lax.psum_scatter(
-        up_part.astype(jnp.bfloat16), "dp", scatter_dimension=0, tiled=True
-    )
-    grad_up = lax.all_to_all(grad_up, "rows", 0, 1, tiled=True).astype(jnp.float32)
-    grad_down = lax.psum_scatter(
-        down_part.astype(jnp.bfloat16), "dp", scatter_dimension=1, tiled=True
-    )
-    grad_down = lax.all_to_all(grad_down, "rows", 1, 0, tiled=True).astype(jnp.float32)
+    dp_size = lax.axis_size("dp")
+    grad_parts = jnp.stack([up_part, down_part_t]).astype(jnp.bfloat16)
+    grad_parts = grad_parts.reshape(2, dp_size, -1, grad_parts.shape[-1])
+    grad_sums = lax.all_to_all(grad_parts, "dp", 1, 1, tiled=True)
+    grad_sums = grad_sums.astype(jnp.float32).sum(1)
+    grad_up = lax.all_to_all(grad_sums[0], "rows", 0, 1, tiled=True)
+    grad_down = lax.all_to_all(grad_sums[1], "rows", 0, 1, tiled=True).T
     gain_part = jnp.sum(norm_grad * normed, axis=0)
     scaled_grad = norm_grad * norm_gain
     conv_grad = rstd * (

time: 454 us -> 521 us (1.15)
  waiting for transfers between devices: 295 us -> 356 us
  blocking collectives: 29.5 us -> 14.9 us
  starting transfers between devices: 23.4 us -> 35.6 us
  other arithmetic: 32.5 us -> 39.2 us
    all_to_all x2 -> x4, waiting for transfers between devices: 5.77 us -> 127 us  [the longest x1 104 us: body(): grad_sums = lax.all_to_all(grad_parts, 'dp', 1, 1, tiled=True)]
    unnamed x9 -> x5, waiting for transfers between devices: 38.1 us -> 0.08 us
    reduce_scatter x1 -> x0, waiting for transfers between devices: 30.2 us -> none  [body(): lax.psum_scatter(up_part.astype(jnp.bfloat16), 'dp', scatter_dimension=0,...]
    all_gather x2 -> x1, waiting for transfers between devices: 62.2 us -> 92.2 us  [body(): lax.all_gather(jnp.stack([up_mine, down_mine.T]), 'dp', axis=1, tiled=True)]
    all_gather x1, waiting for transfers between devices: 33.6 us -> 4.88 us  [body(): gathered = lax.all_gather(scaled, hid_axes, axis=0, tiled=True)]
    all_to_all x2 -> x1, blocking collectives: 29.5 us -> 14.9 us  [body(): down_mine = lax.all_to_all(w_down, 'rows', 0, 1, tiled=True)]
    all_to_all x2 -> x4, starting transfers between devices: 7.88 us -> 20.2 us  [the longest x1 6.13 us: body(): up_mine = lax.all_to_all(w_up, 'rows', 1, 0, tiled=True)]
    all_to_all x1, waiting for transfers between devices: 1.74 us -> 8.23 us  [small_sums(): lax.all_to_all(spread, every, 0, 0, tiled=True)]
  transfers between devices with their start and end apart: 16 -> 15, of which waited for: 11 -> 12; matrix products, arithmetic and copies ran while one was open for 14% -> 8% of each run, Pallas kernels for 0% -> 0%
where the time goes in v4:
time: 521 us; the launch traced here: 520 us
  waiting for transfers between devices  356 us (68%)
  other arithmetic  39.2 us (8%)
  starting transfers between devices  35.6 us (7%)
  matrix products  35.3 us (7%)
  local copies, waits for them, and re-layouts  23.5 us (5%)
  between operations  15.1 us (3%)
  blocking collectives  14.9 us (3%)
    all_to_all x1, waiting for transfers between devices, body(): grad_sums = lax.all_to_all(grad_parts, 'dp', 1, 1, tiled=True)  104 us
    all_gather x1, waiting for transfers between devices, body(): lax.all_gather(jnp.stack([up_mine, down_mine.T]), 'dp', axis=1, tiled=True)  92.2 us
    reduce_scatter x1, waiting for transfers between devices, body(): lax.psum_scatter(mlp_terms.astype(jnp.bfloat16), hid_axes, scatter_dimens...  44.8 us
    reduce_scatter x1, waiting for transfers between devices, body(): lax.psum_scatter(norm_terms.astype(jnp.bfloat16), hid_axes, scatter_dimen...  38.7 us
    all_gather x1, waiting for transfers between devices, body(): back_all = lax.all_gather(back, hid_axes, axis=0, tiled=True)  32.2 us
    all_to_all x1, blocking collectives, body(): down_mine = lax.all_to_all(w_down, 'rows', 0, 1, tiled=True)  14.9 us
    all_to_all x1, waiting for transfers between devices, body(): up_mine = lax.all_to_all(w_up, 'rows', 1, 0, tiled=True)  11.3 us
  transfers between devices with their start and end apart: 15, of which 12 were waited for; matrix products, arithmetic and copies ran while one was open for 8% of the time, Pallas kernels for 0%

profile of v4, /device:TPU:0, one launch (start us, length us, event | category | flops | bytes accessed | tf_op | source)
XLA Modules:
  0.0 519.7 jit_solution(10892718375282407475)
XLA Ops:
  15.8 2.5 slice_reduce_fusion.49
  19.9 9.4 %fusion.113 = (f32[4,32]{1,0:T(4,128)S(1)}, f32[1,4,32,1536]{3,2,1,0:T(8,128)S(1)}) fusion(f32[1536]{0:T(1024)S(1)} %get-tuple-element.108, f32[1536]{0:T(1024)S(1)} %get-tuple-element.109, f32[1536]{0:T(1024)S(1)} %get-tuple-element.62, f32[1536]{0:T(1024)S(1)} %get-tuple-element.63, f32[1,10,32,1536]{3,2,1,0:T(8,128)S(1)} %maximum_convert_fusion, ...), kind=kLoop, calls=%fused_computation.332 | loop fusion | flops 19267456 | bytes 8641024 | tf_op jit(solution)/shard_map/reduce_sum | solution.py:78
  31.6 6.1 %all-to-all-start = ((bf16[96,4,768]{2,0,1:T(8,128)(2,1)}), bf16[96,4,768]{2,0,1:T(8,128)(2,1)}, u32[]{:S(2)}, u32[]{:S(2)}) async-start(bf16[96,4,768]{2,0,1:T(8,128)(2,1)} %bitcast.126), calls=%async_computation | async-start | bytes 1179648 | tf_op jit(solution)/shard_map/all_to_all | solution.py:60
  38.8 11.3 %all-to-all-done = bf16[96,4,768]{2,0,1:T(8,128)(2,1)} async-done(((bf16[96,4,768]{2,0,1:T(8,128)(2,1)}), bf16[96,4,768]{2,0,1:T(8,128)(2,1)}, u32[]{:S(2)}, u32[]{:S(2)}) %all-to-all-start) | async-done | bytes 589856 | tf_op jit(solution)/shard_map/all_to_all | solution.py:60
  50.1 14.9 %all_to_all.88 = bf16[4,768,96]{1,2,0:T(8,128)(2,1)S(1)} all-to-all(bf16[4,768,96]{1,2,0:T(8,128)(2,1)S(1)} %bitcast.130), channel_id=1, replica_groups=mesh['dp'=4,'fsdp'=2,'rows'=4] {'rows'}, dimensions={0} | all-to-all | bytes 1179648 | tf_op jit(solution)/shard_map/all_to_all | solution.py:61
  67.2 4.9 all-gather.4.cloned.1.call-done
  72.1 92.2 %all-gather.6.cloned.1.call-done = bf16[2,1536,768]{2,1,0:T(8,128)(2,1)} async-done(((bf16[2,384,768]{2,1,0:T(8,128)(2,1)}), bf16[2,1536,768]{2,1,0:T(8,128)(2,1)}) %all-gather.6.cloned.1.call-update) | async-done | bytes 4718608 | tf_op jit(solution)/shard_map/all_gather | solution.py:62
  164.3 7.2 %multiply_convert_fusion = (bf16[1024,768]{1,0:T(8,128)(2,1)S(1)}, f32[1024,768]{1,0:T(8,128)}) fusion(bf16[1024,1536]{1,0:T(8,128)(2,1)} %all-gather.4.cloned.1.call-done, bf16[2,1536,768]{2,1,0:T(8,128)(2,1)} %all-gather.6.cloned.1.call-done), kind=kOutput, calls=%fused_computation.97 | convolution fusion | flops 2419851264 | bytes 10223616 | tf_op jit(solution)/shard_map/dot_general | solution.py:85
  172.6 4.1 convolution_convert_fusion.1
  176.8 44.8 %reduce-scatter.3.cloned.1.call-done = bf16[128,1536]{1,0:T(8,128)(2,1)} async-done(((bf16[1024,1536]{1,0:T(8,128)(2,1)}), bf16[128,1536]{1,0:T(8,128)(2,1)}) %reduce-scatter.3.cloned.1.call-update) | async-done | bytes 393232 | tf_op jit(solution)/shard_map/reduce_scatter | solution.py:90
  221.6 2.7 fusion.13
  224.5 32.2 %all-gather.8.cloned.1.call-done = bf16[1024,1536]{1,0:T(8,128)(2,1)} async-done(((bf16[128,1536]{1,0:T(8,128)(2,1)}), bf16[1024,1536]{1,0:T(8,128)(2,1)}) %all-gather.8.cloned.1.call-update) | async-done | bytes 3145744 | tf_op jit(solution)/shard_map/all_gather | solution.py:66
  256.8 6.6 %fusion.5 = bf16[1024,768]{1,0:T(8,128)(2,1)S(1)} fusion(f32[1024,768]{1,0:T(8,128)} %get-tuple-element.123, bf16[1024,1536]{1,0:T(8,128)(2,1)} %all-gather.8.cloned.1.call-done, bf16[2,1536,768]{2,1,0:T(8,128)(2,1)} %all-gather.6.cloned.1.call-done), kind=kOutput, calls=%fused_computation.96 | convolution fusion | flops 2423783424 | bytes 10223616 | tf_op jit(solution)/shard_map/dot_general | solution.py:99
  264.6 5.7 %convolution_convert_fusion = bf16[1024,1536]{1,0:T(8,128)(2,1)} fusion(bf16[1024,768]{1,0:T(8,128)(2,1)S(1)} %fusion.5, bf16[2,1536,768]{2,1,0:T(8,128)(2,1)} %all-gather.6.cloned.1.call-done), kind=kOutput, calls=%fused_computation.87 | convolution fusion | flops 2417491968 | bytes 7077888 | tf_op jit(solution)/shard_map/dot_general | solution.py:104
  271.6 6.5 %convolution_convert_fusion.2 = bf16[1536,768]{1,0:T(8,128)(2,1)} fusion(bf16[1024,1536]{1,0:T(8,128)(2,1)} %all-gather.8.cloned.1.call-done, bf16[1024,768]{1,0:T(8,128)(2,1)} %copy-done.55), kind=kOutput, calls=%fused_computation.89 | convolution fusion | flops 2417098752 | bytes 7077888 | tf_op jit(solution)/shard_map/dot_general | solution.py:96
  278.0 38.7 %reduce-scatter.5.cloned.1.call-done = bf16[128,1536]{1,0:T(8,128)(2,1)} async-done(((bf16[1024,1536]{1,0:T(8,128)(2,1)}), bf16[128,1536]{1,0:T(8,128)(2,1)}) %reduce-scatter.5.cloned.1.call-update) | async-done | bytes 393232 | tf_op jit(solution)/shard_map/reduce_scatter | solution.py:107
  318.1 3.6 multiply_reduce_fusion.1
  327.2 4.8 all-to-all-start.5
  332.0 5.2 convolution_convert_fusion.3
  337.2 2.6 pad_maximum_fusion
  339.8 5.2 all-to-all-done.5
  344.9 4.9 all-to-all-start.2
  350.0 104.1 %all-to-all-done.2 = bf16[2,4,384,768]{3,2,0,1:T(8,128)(2,1)} async-done(((bf16[2,4,384,768]{3,2,0,1:T(8,128)(2,1)}), bf16[2,4,384,768]{3,2,0,1:T(8,128)(2,1)}, u32[]{:S(2)}, u32[]{:S(2)}) %all-to-all-start.2) | async-done | bytes 4718624 | tf_op jit(solution)/shard_map/all_to_all | solution.py:113
  455.0 2.9 all-to-all-start.6
  458.0 3.3 convert_reduce_fusion
  462.9 8.2 %all-to-all-done.6 = f32[32,2,1536]{2,1,0:T(2,128)S(1)} async-done(((f32[32,2,1536]{2,1,0:T(2,128)}), f32[32,2,1536]{2,1,0:T(2,128)S(1)}, u32[]{:S(2)}, u32[]{:S(2)}) %all-to-all-start.6) | async-done | bytes 393248 | tf_op jit(solution)/shard_map/all_to_all | solution.py:51
  471.1 4.3 all-to-all-start.3
  479.2 3.2 collective-permute-done.3
  482.6 8.7 %all-to-all-done.3 = f32[4,96,768]{2,1,0:T(8,128)} async-done(((f32[4,96,768]{2,1,0:T(8,128)}), f32[4,96,768]{2,1,0:T(8,128)}, u32[]{:S(2)}, u32[]{:S(2)}) %all-to-all-start.3) | async-done | bytes 1179680 | tf_op jit(solution)/shard_map/all_to_all | solution.py:115
  491.3 4.9 all-to-all-start.4
  496.2 8.1 %fusion.105 = bf16[1,4,32,1536]{3,2,1,0:T(8,128)(2,1)} fusion(f32[1,10,32,1536]{3,2,1,0:T(8,128)S(1)} %maximum_convert_fusion.1, bf16[1,4,32,1536]{3,2,1,0:T(8,128)(2,1)S(1)} %copy-done.3, f32[1536]{0:T(1024)} %copy-done.16, f32[1536]{0:T(1024)} %copy-done.17, f32[1536]{0:T(1024)} %copy-done.19, f32[1536]{0:T(1024)} %copy-done.20, f32[1536]{0:T(1024)} %copy-done.21, ...), kind=kLoop, calls=%fused_computation.207 | loop fusion | flops 19660800 | bytes 8562688 | tf_op jit(solution)/shard_map/convert_element_type | solution.py:141
  509.4 2.7 all-to-all-done.4
  (213 shorter events, 38.2 us)
Async XLA Ops:
  7.2 64.9 %all-gather.4.cloned.1.call-start = ((), (), s32[]{:S(2)}) async-start(), calls=%async_computation.9 | async-start | bytes 3538944 | tf_op jit(solution)/shard_map/all_gather | solution.py:84
  8.3 10.0 %collective-permute-start = (bf16[1,3,32,1536]{3,2,1,0:T(8,128)(2,1)S(1)}, bf16[1,3,32,1536]{3,2,1,0:T(8,128)(2,1)S(1)}, u32[]{:S(2)}, u32[]{:S(2)}) collective-permute-start(bf16[1,3,32,1536]{3,2,1,0:T(8,128)(2,1)S(1)} %get-tuple-element.120), channel_id=1, source_target_pairs={{0,1},{1,2},{2,3},{4,5},{5,6},{6,7},{8,9},{9,10},{10,11},{12,13},{... | collective-permute-start | bytes 884744 | tf_op jit(solution)/shard_map/ppermute | solution.py:25
  10.7 7.6 %collective-permute-start.1 = (bf16[1,3,32,1536]{3,2,1,0:T(8,128)(2,1)S(1)}, bf16[1,3,32,1536]{3,2,1,0:T(8,128)(2,1)S(1)}, u32[]{:S(2)}, u32[]{:S(2)}) collective-permute-start(bf16[1,3,32,1536]{3,2,1,0:T(8,128)(2,1)S(1)} %get-tuple-element.121), channel_id=1, source_target_pairs={{1,0},{2,1},{3,2},{5,4},{6,5},{7,6},{9,8},{10,9},{11,10},{13,12},{... | collective-permute-start | bytes 884744 | tf_op jit(solution)/shard_map/ppermute | solution.py:26
  13.4 6.1 %copy-start.7 = (f32[1536]{0:T(1024)}, f32[1536]{0:T(1024)S(1)}, u32[]{:S(2)}) copy-start(f32[1536]{0:T(1024)S(1)} %get-tuple-element.100) | copy-start | bytes 18436
  13.4 6.1 %copy-start.9 = (f32[1536]{0:T(1024)}, f32[1536]{0:T(1024)S(1)}, u32[]{:S(2)}) copy-start(f32[1536]{0:T(1024)S(1)} %get-tuple-element.101) | copy-start | bytes 18436
  13.4 6.1 %copy-start.10 = (f32[1536]{0:T(1024)}, f32[1536]{0:T(1024)S(1)}, u32[]{:S(2)}) copy-start(f32[1536]{0:T(1024)S(1)} %get-tuple-element.102) | copy-start | bytes 18436
  13.4 6.1 %copy-start.11 = (f32[1536]{0:T(1024)}, f32[1536]{0:T(1024)S(1)}, u32[]{:S(2)}) copy-start(f32[1536]{0:T(1024)S(1)} %get-tuple-element.103) | copy-start | bytes 18436
  13.4 6.1 %copy-start.12 = (f32[1536]{0:T(1024)}, f32[1536]{0:T(1024)S(1)}, u32[]{:S(2)}) copy-start(f32[1536]{0:T(1024)S(1)} %get-tuple-element.104) | copy-start | bytes 18436
  13.4 6.1 %copy-start.13 = (f32[1536]{0:T(1024)}, f32[1536]{0:T(1024)S(1)}, u32[]{:S(2)}) copy-start(f32[1536]{0:T(1024)S(1)} %get-tuple-element.105) | copy-start | bytes 18436
  19.9 9.9 %copy-start.6 = (f32[1536]{0:T(1024)S(1)}, f32[1536]{0:T(1024)}, u32[]{:S(2)}) copy-start(f32[1536]{0:T(1024)} %param.9) | copy-start | bytes 18436
  29.4 9.4 %copy-start.49 = (f32[128]{0:T(128)}, f32[128]{0:T(128)S(1)}, u32[]{:S(2)}) copy-start(f32[128]{0:T(128)S(1)} %div.15) | copy-start | bytes 1540
  29.7 9.1 %copy-start.51 = (f32[128]{0:T(128)}, f32[128]{0:T(128)S(1)}, u32[]{:S(2)}) copy-start(f32[128]{0:T(128)S(1)} %rsqrt.12) | copy-start | bytes 1540
  31.6 18.5 %all-to-all-start = ((bf16[96,4,768]{2,0,1:T(8,128)(2,1)}), bf16[96,4,768]{2,0,1:T(8,128)(2,1)}, u32[]{:S(2)}, u32[]{:S(2)}) async-start(bf16[96,4,768]{2,0,1:T(8,128)(2,1)} %bitcast.126), calls=%async_computation | async-start | bytes 1179648 | tf_op jit(solution)/shard_map/all_to_all | solution.py:60
  37.7 126.6 %all-gather.6.cloned.1.call-start = ((), (), s32[]{:S(2)}) async-start(), calls=%async_computation.10 | async-start | bytes 5898240 | tf_op jit(solution)/shard_map/all_gather | solution.py:62
  67.2 154.4 %reduce-scatter.3.cloned.1.call-start = ((), (), s32[]{:S(2)}) async-start(), calls=%async_computation.11 | async-start | bytes 3538944 | tf_op jit(solution)/shard_map/reduce_scatter | solution.py:90
  164.3 8.3 %copy-start.53 = (bf16[2,1536,768]{2,1,0:T(8,128)(2,1)S(1)}, bf16[2,1536,768]{2,1,0:T(8,128)(2,1)}, u32[]{:S(2)}) copy-start(bf16[2,1536,768]{2,1,0:T(8,128)(2,1)} %all-gather.6.cloned.1.call-done) | copy-start | bytes 14155780
  176.7 44.8 %copy-start = (bf16[1,4,32,1536]{3,2,1,0:T(8,128)(2,1)S(1)}, bf16[1,4,32,1536]{3,2,1,0:T(8,128)(2,1)}, u32[]{:S(2)}) copy-start(bf16[1,4,32,1536]{3,2,1,0:T(8,128)(2,1)} %param.7) | copy-start | bytes 1179652
  176.7 44.8 %copy-start.2 = (bf16[1,4,32,1536]{3,2,1,0:T(8,128)(2,1)S(1)}, bf16[1,4,32,1536]{3,2,1,0:T(8,128)(2,1)}, u32[]{:S(2)}) copy-start(bf16[1,4,32,1536]{3,2,1,0:T(8,128)(2,1)} %param.13) | copy-start | bytes 1179652
  176.7 80.0 %all-gather.8.cloned.1.call-start = ((), (), s32[]{:S(2)}) async-start(), calls=%async_computation.12 | async-start | bytes 3538944 | tf_op jit(solution)/shard_map/all_gather | solution.py:66
  224.3 92.4 %reduce-scatter.5.cloned.1.call-start = ((), (), s32[]{:S(2)}) async-start(), calls=%async_computation.13 | async-start | bytes 3538944 | tf_op jit(solution)/shard_map/reduce_scatter | solution.py:107
  271.6 45.2 %copy-start.50 = (f32[128]{0:T(128)S(1)}, f32[128]{0:T(128)}, u32[]{:S(2)}) copy-start(f32[128]{0:T(128)} %copy-done.49) | copy-start | bytes 1540
  271.6 45.2 %copy-start.52 = (f32[128]{0:T(128)S(1)}, f32[128]{0:T(128)}, u32[]{:S(2)}) copy-start(f32[128]{0:T(128)} %copy-done.51) | copy-start | bytes 1540
  327.2 17.8 %all-to-all-start.5 = ((f32[32,2,1536]{2,1,0:T(2,128)}), f32[32,2,1536]{2,1,0:T(2,128)S(1)}, u32[]{:S(2)}, u32[]{:S(2)}) async-start(f32[32,2,1536]{2,1,0:T(2,128)} %reshape.352), calls=%async_computation.7 | async-start | bytes 786432 | tf_op jit(solution)/shard_map/all_to_all | solution.py:49
  344.9 109.2 %all-to-all-start.2 = ((bf16[2,4,384,768]{3,2,0,1:T(8,128)(2,1)}), bf16[2,4,384,768]{3,2,0,1:T(8,128)(2,1)}, u32[]{:S(2)}, u32[]{:S(2)}) async-start(bf16[2,4,384,768]{3,2,0,1:T(8,128)(2,1)} %pad_maximum_fusion), calls=%async_computation.4 | async-start | bytes 9437184 | tf_op jit(solution)/shard_map/all_to_all | solution.py:113
  455.0 16.1 %all-to-all-start.6 = ((f32[32,2,1536]{2,1,0:T(2,128)}), f32[32,2,1536]{2,1,0:T(2,128)S(1)}, u32[]{:S(2)}, u32[]{:S(2)}) async-start(f32[32,2,1536]{2,1,0:T(2,128)} %broadcast_in_dim.8), calls=%async_computation.8 | async-start | bytes 786432 | tf_op jit(solution)/shard_map/all_to_all | solution.py:51
  471.1 11.5 %copy-start.4 = (f32[32,2,1536]{2,1,0:T(2,128)}, f32[32,2,1536]{2,1,0:T(2,128)S(1)}, u32[]{:S(2)}) copy-start(f32[32,2,1536]{2,1,0:T(2,128)S(1)} %all-to-all-done.6) | copy-start | bytes 1179652
  471.1 20.2 %all-to-all-start.3 = ((f32[4,96,768]{2,1,0:T(8,128)}), f32[4,96,768]{2,1,0:T(8,128)}, u32[]{:S(2)}, u32[]{:S(2)}) async-start(f32[4,96,768]{2,1,0:T(8,128)} %bitcast.18), calls=%async_computation.5 | async-start | bytes 2359296 | tf_op jit(solution)/shard_map/all_to_all | solution.py:115
  475.5 3.7 collective-permute-start.2
  477.8 4.6 collective-permute-start.3
  482.4 13.8 %copy-start.3 = (bf16[1,4,32,1536]{3,2,1,0:T(8,128)(2,1)S(1)}, bf16[1,4,32,1536]{3,2,1,0:T(8,128)(2,1)}, u32[]{:S(2)}) copy-start(bf16[1,4,32,1536]{3,2,1,0:T(8,128)(2,1)} %param.13) | copy-start | bytes 1179652
  482.4 13.8 %copy-start.8 = (f32[1536]{0:T(1024)S(1)}, f32[1536]{0:T(1024)}, u32[]{:S(2)}) copy-start(f32[1536]{0:T(1024)} %copy-done.7) | copy-start | bytes 18436
  491.3 20.7 %all-to-all-start.4 = ((f32[4,96,768]{2,1,0:T(8,128)}), f32[4,96,768]{2,1,0:T(8,128)S(1)}, u32[]{:S(2)}, u32[]{:S(2)}) async-start(f32[4,96,768]{2,1,0:T(8,128)} %bitcast.129), calls=%async_computation.6 | async-start | bytes 2359296 | tf_op jit(solution)/shard_map/all_to_all | solution.py:116
  (39 other events, 128.4 us)
Sparse Core Ops, SparseCore 0:
  30.8 41.2 all-gather.3
  74.2 90.0 all-gather.5
  176.9 44.6 reduce-scatter.2
  224.4 32.2 all-gather.7
  270.4 46.2 reduce-scatter.4

commit v5 on v4

--- a/solution.py
+++ b/solution.py
@@ -107,13 +107,10 @@
     norm_grad = lax.psum_scatter(
         norm_terms.astype(jnp.bfloat16), hid_axes, scatter_dimension=0, tiled=True
     ).astype(jnp.float32)
-    dp_size = lax.axis_size("dp")
     grad_parts = jnp.stack([up_part, down_part_t]).astype(jnp.bfloat16)
-    grad_parts = grad_parts.reshape(2, dp_size, -1, grad_parts.shape[-1])
-    grad_sums = lax.all_to_all(grad_parts, "dp", 1, 1, tiled=True)
-    grad_sums = grad_sums.astype(jnp.float32).sum(1)
-    grad_up = lax.all_to_all(grad_sums[0], "rows", 0, 1, tiled=True)
-    grad_down = lax.all_to_all(grad_sums[1], "rows", 0, 1, tiled=True).T
+    grad_sums = lax.psum_scatter(grad_parts, "dp", scatter_dimension=1, tiled=True)
+    grad_up = lax.all_to_all(grad_sums[0], "rows", 0, 1, tiled=True).astype(jnp.float32)
+    grad_down = lax.all_to_all(grad_sums[1], "rows", 0, 1, tiled=True).T.astype(jnp.float32)
     gain_part = jnp.sum(norm_grad * normed, axis=0)
     scaled_grad = norm_grad * norm_gain
     conv_grad = rstd * (

time: 521 us -> 460 us (0.88)
  waiting for transfers between devices: 356 us -> 280 us
  blocking collectives: 14.9 us -> 42.1 us
  starting transfers between devices: 35.6 us -> 24.5 us
    all_to_all x4 -> x2, waiting for transfers between devices: 121 us -> 6.43 us  [the longest x1 6.43 us: body(): lax.all_to_all(grad_sums[1], 'rows', 0, 1, tiled=True).T.astype(jnp.float32)]
    reduce_scatter x0 -> x1, waiting for transfers between devices: none -> 54.3 us  [body(): lax.psum_scatter(grad_parts, 'dp', scatter_dimension=1, tiled=True)]
    all_to_all x0 -> x1, blocking collectives: none -> 27.3 us  [small_sums(): lax.all_to_all(packed.reshape(devices, per, width), every, 0, 0, tiled=True)]
    all_to_all x4 -> x2, starting transfers between devices: 18.9 us -> 7.18 us  [the longest x1 3.7 us: body(): lax.all_to_all(grad_sums[0], 'rows', 0, 1, tiled=True).astype(jnp.float32)]
    all_to_all x1, waiting for transfers between devices: 8.23 us -> 0.01 us  [small_sums(): lax.all_to_all(spread, every, 0, 0, tiled=True)]
  transfers between devices with their start and end apart: 15 -> 14, of which waited for: 12 -> 8; matrix products, arithmetic and copies ran while one was open for 8% -> 10% of each run, Pallas kernels for 0% -> 0%
where the time goes in v5:
time: 460 us; the launch traced here: 456 us
  waiting for transfers between devices  280 us (61%)
  blocking collectives  42.1 us (9%)
  other arithmetic  36.4 us (8%)
  matrix products  31.7 us (7%)
  starting transfers between devices  24.5 us (5%)
  local copies, waits for them, and re-layouts  24.4 us (5%)
  between operations  16.1 us (4%)
    all_gather x1, waiting for transfers between devices, body(): lax.all_gather(jnp.stack([up_mine, down_mine.T]), 'dp', axis=1, tiled=True)  92.2 us
    reduce_scatter x1, waiting for transfers between devices, body(): lax.psum_scatter(grad_parts, 'dp', scatter_dimension=1, tiled=True)  54.3 us
    reduce_scatter x1, waiting for transfers between devices, body(): lax.psum_scatter(mlp_terms.astype(jnp.bfloat16), hid_axes, scatter_dimens...  44.8 us
    reduce_scatter x1, waiting for transfers between devices, body(): lax.psum_scatter(norm_terms.astype(jnp.bfloat16), hid_axes, scatter_dimen...  34.3 us
    all_gather x1, waiting for transfers between devices, body(): back_all = lax.all_gather(back, hid_axes, axis=0, tiled=True)  32.2 us
    all_to_all x1, blocking collectives, small_sums(): lax.all_to_all(packed.reshape(devices, per, width), every, 0, 0, tiled=True)  27.3 us
    all_to_all x1, blocking collectives, body(): down_mine = lax.all_to_all(w_down, 'rows', 0, 1, tiled=True)  14.9 us
    all_to_all x1, waiting for transfers between devices, body(): up_mine = lax.all_to_all(w_up, 'rows', 1, 0, tiled=True)  11.3 us
  transfers between devices with their start and end apart: 14, of which 8 were waited for; matrix products, arithmetic and copies ran while one was open for 10% of the time, Pallas kernels for 0%

profile of v5, /device:TPU:0, one launch (start us, length us, event | category | flops | bytes accessed | tf_op | source)
XLA Modules:
  0.0 455.7 jit_solution(2944048798734324605)
XLA Ops:
  8.3 2.4 collective-permute-start
  13.5 2.1 slice_reduce_fusion.50
  15.8 2.5 slice_reduce_fusion.49
  19.9 9.4 %fusion.115 = (f32[4,32]{1,0:T(4,128)S(1)}, f32[1,4,32,1536]{3,2,1,0:T(8,128)S(1)}) fusion(f32[1536]{0:T(1024)S(1)} %get-tuple-element.108, f32[1536]{0:T(1024)S(1)} %get-tuple-element.109, f32[1536]{0:T(1024)S(1)} %get-tuple-element.62, f32[1536]{0:T(1024)S(1)} %get-tuple-element.63, f32[1,10,32,1536]{3,2,1,0:T(8,128)S(1)} %maximum_convert_fusion, ...), kind=kLoop, calls=%fused_computation.335 | loop fusion | flops 19267456 | bytes 8641024 | tf_op jit(solution)/shard_map/reduce_sum | solution.py:78
  31.6 6.1 %all-to-all-start = ((bf16[96,4,768]{2,0,1:T(8,128)(2,1)}), bf16[96,4,768]{2,0,1:T(8,128)(2,1)}, u32[]{:S(2)}, u32[]{:S(2)}) async-start(bf16[96,4,768]{2,0,1:T(8,128)(2,1)} %bitcast.126), calls=%async_computation | async-start | bytes 1179648 | tf_op jit(solution)/shard_map/all_to_all | solution.py:60
  38.8 11.3 %all-to-all-done = bf16[96,4,768]{2,0,1:T(8,128)(2,1)} async-done(((bf16[96,4,768]{2,0,1:T(8,128)(2,1)}), bf16[96,4,768]{2,0,1:T(8,128)(2,1)}, u32[]{:S(2)}, u32[]{:S(2)}) %all-to-all-start) | async-done | bytes 589856 | tf_op jit(solution)/shard_map/all_to_all | solution.py:60
  50.1 14.9 %all_to_all.71 = bf16[4,768,96]{1,2,0:T(8,128)(2,1)S(1)} all-to-all(bf16[4,768,96]{1,2,0:T(8,128)(2,1)S(1)} %bitcast.128), channel_id=1, replica_groups=mesh['dp'=4,'fsdp'=2,'rows'=4] {'rows'}, dimensions={0} | all-to-all | bytes 1179648 | tf_op jit(solution)/shard_map/all_to_all | solution.py:61
  65.0 2.2 pad_maximum_fusion.1
  67.2 4.9 %all-gather.4.cloned.1.call-done = bf16[1024,1536]{1,0:T(8,128)(2,1)} async-done(((bf16[128,1536]{1,0:T(8,128)(2,1)}), bf16[1024,1536]{1,0:T(8,128)(2,1)}) %all-gather.4.cloned.1.call-update) | async-done | bytes 3145744 | tf_op jit(solution)/shard_map/all_gather | solution.py:84
  72.1 92.2 %all-gather.6.cloned.1.call-done = bf16[2,1536,768]{2,1,0:T(8,128)(2,1)} async-done(((bf16[2,384,768]{2,1,0:T(8,128)(2,1)}), bf16[2,1536,768]{2,1,0:T(8,128)(2,1)}) %all-gather.6.cloned.1.call-update) | async-done | bytes 4718608 | tf_op jit(solution)/shard_map/all_gather | solution.py:62
  164.3 7.1 %multiply_convert_fusion = (bf16[1024,768]{1,0:T(8,128)(2,1)S(1)}, f32[1024,768]{1,0:T(8,128)}) fusion(bf16[1024,1536]{1,0:T(8,128)(2,1)} %all-gather.4.cloned.1.call-done, bf16[2,1536,768]{2,1,0:T(8,128)(2,1)} %all-gather.6.cloned.1.call-done), kind=kOutput, calls=%fused_computation.96 | convolution fusion | flops 2419851264 | bytes 10223616 | tf_op jit(solution)/shard_map/dot_general | solution.py:85
  172.6 4.0 convolution_convert_fusion.1
  176.8 44.8 %reduce-scatter.4.cloned.1.call-done = bf16[128,1536]{1,0:T(8,128)(2,1)} async-done(((bf16[1024,1536]{1,0:T(8,128)(2,1)}), bf16[128,1536]{1,0:T(8,128)(2,1)}) %reduce-scatter.4.cloned.1.call-update) | async-done | bytes 393232 | tf_op jit(solution)/shard_map/reduce_scatter | solution.py:90
  221.6 2.7 fusion.15
  224.5 32.2 %all-gather.8.cloned.1.call-done = bf16[1024,1536]{1,0:T(8,128)(2,1)} async-done(((bf16[128,1536]{1,0:T(8,128)(2,1)}), bf16[1024,1536]{1,0:T(8,128)(2,1)}) %all-gather.8.cloned.1.call-update) | async-done | bytes 3145744 | tf_op jit(solution)/shard_map/all_gather | solution.py:66
  256.8 6.6 %fusion.5 = bf16[1024,768]{1,0:T(8,128)(2,1)S(1)} fusion(f32[1024,768]{1,0:T(8,128)} %get-tuple-element.123, bf16[1024,1536]{1,0:T(8,128)(2,1)} %all-gather.8.cloned.1.call-done, bf16[2,1536,768]{2,1,0:T(8,128)(2,1)} %all-gather.6.cloned.1.call-done), kind=kOutput, calls=%fused_computation.95 | convolution fusion | flops 2423783424 | bytes 10223616 | tf_op jit(solution)/shard_map/dot_general | solution.py:99
  264.6 5.8 %convolution_convert_fusion = bf16[1024,1536]{1,0:T(8,128)(2,1)} fusion(bf16[1024,768]{1,0:T(8,128)(2,1)S(1)} %fusion.5, bf16[2,1536,768]{2,1,0:T(8,128)(2,1)} %all-gather.6.cloned.1.call-done), kind=kOutput, calls=%fused_computation.86 | convolution fusion | flops 2417491968 | bytes 7077888 | tf_op jit(solution)/shard_map/dot_general | solution.py:104
  270.4 5.2 %fusion.7 = bf16[1,1536,768]{2,1,0:T(8,128)(2,1)S(1)} fusion(bf16[1024,1536]{1,0:T(8,128)(2,1)} %all-gather.8.cloned.1.call-done, bf16[1024,768]{1,0:T(8,128)(2,1)} %copy-done.94), kind=kOutput, calls=%fused_computation.99 | convolution fusion | flops 2417098752 | bytes 7077888 | tf_op jit(solution)/shard_map/dot_general | solution.py:96
  275.6 3.0 fusion.6
  278.6 2.6 pad_maximum_fusion
  282.5 34.3 %reduce-scatter.6.cloned.1.call-done = bf16[128,1536]{1,0:T(8,128)(2,1)} async-done(((bf16[1024,1536]{1,0:T(8,128)(2,1)}), bf16[128,1536]{1,0:T(8,128)(2,1)}) %reduce-scatter.6.cloned.1.call-update) | async-done | bytes 393232 | tf_op jit(solution)/shard_map/reduce_scatter | solution.py:107
  318.7 3.6 multiply_reduce_fusion.1
  322.6 2.0 multiply_reduce_fusion
  327.1 27.3 %all_to_all.72 = f32[32,2,1536]{2,1,0:T(2,128)S(1)} all-to-all(f32[32,2,1536]{2,1,0:T(2,128)S(1)} %reshape.349), channel_id=1, replica_groups=mesh['dp'=4,'fsdp'=2,'rows'=4] {'dp','fsdp','rows'}, dimensions={0} | all-to-all | bytes 786432 | tf_op jit(solution)/shard_map/all_to_all | solution.py:49
  355.3 3.7 all-to-all-start.5
  359.1 2.2 collective-permute-start.2
  362.6 54.3 %reduce-scatter.8.cloned.1.call-done = bf16[2,384,768]{2,1,0:T(8,128)(2,1)} async-done(((bf16[2,1536,768]{2,1,0:T(8,128)(2,1)}), bf16[2,384,768]{2,1,0:T(8,128)(2,1)}) %reduce-scatter.8.cloned.1.call-update) | async-done | bytes 1179664 | tf_op jit(solution)/shard_map/reduce_scatter | solution.py:111
  416.8 2.3 fusion.116
  419.2 3.5 all-to-all-start.3
  425.7 6.4 %all-to-all-done.3 = bf16[4,96,768]{2,1,0:T(8,128)(2,1)S(1)} async-done(((bf16[4,96,768]{2,1,0:T(8,128)(2,1)}), bf16[4,96,768]{2,1,0:T(8,128)(2,1)S(1)}, u32[]{:S(2)}, u32[]{:S(2)}) %all-to-all-start.3) | async-done | bytes 589856 | tf_op jit(solution)/shard_map/all_to_all | solution.py:113
  432.2 3.7 all-to-all-start.2
  436.2 7.5 %fusion.107 = bf16[1,4,32,1536]{3,2,1,0:T(8,128)(2,1)} fusion(f32[1,10,32,1536]{3,2,1,0:T(8,128)S(1)} %maximum_convert_fusion.1, bf16[1,4,32,1536]{3,2,1,0:T(8,128)(2,1)} %param.13, f32[1536]{0:T(1024)S(1)} %copy-done.24, f32[1536]{0:T(1024)S(1)} %copy-done.26, f32[1536]{0:T(1024)S(1)} %copy-done.30, f32[1536]{0:T(1024)S(1)} %copy-done.32, ...), kind=kLoop, calls=%fused_computation.210 | loop fusion | flops 19660800 | bytes 8640512 | tf_op jit(solution)/shard_map/convert_element_type | solution.py:138
  (296 shorter events, 27.0 us)
Async XLA Ops:
  7.2 64.9 %all-gather.4.cloned.1.call-start = ((), (), s32[]{:S(2)}) async-start(), calls=%async_computation.9 | async-start | bytes 3538944 | tf_op jit(solution)/shard_map/all_gather | solution.py:84
  8.3 10.0 %collective-permute-start = (bf16[1,3,32,1536]{3,2,1,0:T(8,128)(2,1)S(1)}, bf16[1,3,32,1536]{3,2,1,0:T(8,128)(2,1)S(1)}, u32[]{:S(2)}, u32[]{:S(2)}) collective-permute-start(bf16[1,3,32,1536]{3,2,1,0:T(8,128)(2,1)S(1)} %get-tuple-element.120), channel_id=1, source_target_pairs={{0,1},{1,2},{2,3},{4,5},{5,6},{6,7},{8,9},{9,10},{10,11},{12,13},{... | collective-permute-start | bytes 884744 | tf_op jit(solution)/shard_map/ppermute | solution.py:25
  10.7 7.6 %collective-permute-start.1 = (bf16[1,3,32,1536]{3,2,1,0:T(8,128)(2,1)S(1)}, bf16[1,3,32,1536]{3,2,1,0:T(8,128)(2,1)S(1)}, u32[]{:S(2)}, u32[]{:S(2)}) collective-permute-start(bf16[1,3,32,1536]{3,2,1,0:T(8,128)(2,1)S(1)} %get-tuple-element.121), channel_id=1, source_target_pairs={{1,0},{2,1},{3,2},{5,4},{6,5},{7,6},{9,8},{10,9},{11,10},{13,12},{... | collective-permute-start | bytes 884744 | tf_op jit(solution)/shard_map/ppermute | solution.py:26
  31.6 18.5 %all-to-all-start = ((bf16[96,4,768]{2,0,1:T(8,128)(2,1)}), bf16[96,4,768]{2,0,1:T(8,128)(2,1)}, u32[]{:S(2)}, u32[]{:S(2)}) async-start(bf16[96,4,768]{2,0,1:T(8,128)(2,1)} %bitcast.126), calls=%async_computation | async-start | bytes 1179648 | tf_op jit(solution)/shard_map/all_to_all | solution.py:60
  37.7 126.6 %all-gather.6.cloned.1.call-start = ((), (), s32[]{:S(2)}) async-start(), calls=%async_computation.10 | async-start | bytes 5898240 | tf_op jit(solution)/shard_map/all_gather | solution.py:62
  67.2 154.4 %reduce-scatter.4.cloned.1.call-start = ((), (), s32[]{:S(2)}) async-start(), calls=%async_computation.11 | async-start | bytes 3538944 | tf_op jit(solution)/shard_map/reduce_scatter | solution.py:90
  176.7 44.9 %copy-start = (bf16[1,4,32,1536]{3,2,1,0:T(8,128)(2,1)S(1)}, bf16[1,4,32,1536]{3,2,1,0:T(8,128)(2,1)}, u32[]{:S(2)}) copy-start(bf16[1,4,32,1536]{3,2,1,0:T(8,128)(2,1)} %param.7) | copy-start | bytes 1179652
  176.7 44.9 %copy-start.1 = (bf16[1,4,32,1536]{3,2,1,0:T(8,128)(2,1)S(1)}, bf16[1,4,32,1536]{3,2,1,0:T(8,128)(2,1)}, u32[]{:S(2)}) copy-start(bf16[1,4,32,1536]{3,2,1,0:T(8,128)(2,1)} %param.13) | copy-start | bytes 1179652
  176.7 80.0 %all-gather.8.cloned.1.call-start = ((), (), s32[]{:S(2)}) async-start(), calls=%async_computation.12 | async-start | bytes 3538944 | tf_op jit(solution)/shard_map/all_gather | solution.py:66
  224.3 92.5 %reduce-scatter.6.cloned.1.call-start = ((), (), s32[]{:S(2)}) async-start(), calls=%async_computation.13 | async-start | bytes 3538944 | tf_op jit(solution)/shard_map/reduce_scatter | solution.py:107
  270.3 146.5 %reduce-scatter.8.cloned.1.call-start = ((), (), s32[]{:S(2)}) async-start(), calls=%async_computation.14 | async-start | bytes 5898240 | tf_op jit(solution)/shard_map/reduce_scatter | solution.py:111
  281.2 35.6 %copy-start.89 = (f32[128]{0:T(128)S(1)}, f32[128]{0:T(128)}, u32[]{:S(2)}) copy-start(f32[128]{0:T(128)} %copy-done.88) | copy-start | bytes 1540
  281.2 35.6 %copy-start.91 = (f32[128]{0:T(128)S(1)}, f32[128]{0:T(128)}, u32[]{:S(2)}) copy-start(f32[128]{0:T(128)} %copy-done.90) | copy-start | bytes 1540
  355.3 63.9 %all-to-all-start.5 = ((f32[32,2,1536]{2,1,0:T(2,128)}), f32[32,2,1536]{2,1,0:T(2,128)S(1)}, u32[]{:S(2)}, u32[]{:S(2)}) async-start(f32[32,2,1536]{2,1,0:T(2,128)} %broadcast_in_dim.8), calls=%async_computation.8 | async-start | bytes 786432 | tf_op jit(solution)/shard_map/all_to_all | solution.py:51
  359.1 64.0 %collective-permute-start.2 = (bf16[1,3,32,1536]{3,2,1,0:T(8,128)(2,1)S(1)}, bf16[1,3,32,1536]{3,2,1,0:T(8,128)(2,1)S(1)}, u32[]{:S(2)}, u32[]{:S(2)}) collective-permute-start(bf16[1,3,32,1536]{3,2,1,0:T(8,128)(2,1)S(1)} %get-tuple-element.118), channel_id=1, source_target_pairs={{0,1},{1,2},{2,3},{4,5},{5,6},{6,7},{8,9},{9,10},{10,11},{12,13},{... | collective-permute-start | bytes 884744 | tf_op jit(solution)/shard_map/ppermute | solution.py:25
  361.3 61.8 %collective-permute-start.3 = (bf16[1,3,32,1536]{3,2,1,0:T(8,128)(2,1)S(1)}, bf16[1,3,32,1536]{3,2,1,0:T(8,128)(2,1)S(1)}, u32[]{:S(2)}, u32[]{:S(2)}) collective-permute-start(bf16[1,3,32,1536]{3,2,1,0:T(8,128)(2,1)S(1)} %get-tuple-element.119), channel_id=1, source_target_pairs={{1,0},{2,1},{3,2},{5,4},{6,5},{7,6},{9,8},{10,9},{11,10},{13,12},{... | collective-permute-start | bytes 884744 | tf_op jit(solution)/shard_map/ppermute | solution.py:26
  419.2 13.0 %all-to-all-start.3 = ((bf16[4,96,768]{2,1,0:T(8,128)(2,1)}), bf16[4,96,768]{2,1,0:T(8,128)(2,1)S(1)}, u32[]{:S(2)}, u32[]{:S(2)}) async-start(bf16[4,96,768]{2,1,0:T(8,128)(2,1)} %bitcast.18), calls=%async_computation.6 | async-start | bytes 1179648 | tf_op jit(solution)/shard_map/all_to_all | solution.py:113
  422.6 13.2 %copy-start.8 = (f32[1536]{0:T(1024)S(1)}, f32[1536]{0:T(1024)}, u32[]{:S(2)}) copy-start(f32[1536]{0:T(1024)} %copy-done.7) | copy-start | bytes 18436
  422.6 13.2 %copy-start.10 = (f32[1536]{0:T(1024)S(1)}, f32[1536]{0:T(1024)}, u32[]{:S(2)}) copy-start(f32[1536]{0:T(1024)} %copy-done.9) | copy-start | bytes 18436
  422.7 13.2 %copy-start.12 = (f32[1536]{0:T(1024)S(1)}, f32[1536]{0:T(1024)}, u32[]{:S(2)}) copy-start(f32[1536]{0:T(1024)} %copy-done.11) | copy-start | bytes 18436
  422.7 13.2 %copy-start.14 = (f32[1536]{0:T(1024)S(1)}, f32[1536]{0:T(1024)}, u32[]{:S(2)}) copy-start(f32[1536]{0:T(1024)} %copy-done.13) | copy-start | bytes 18436
  422.7 13.2 %copy-start.16 = (f32[1536]{0:T(1024)S(1)}, f32[1536]{0:T(1024)}, u32[]{:S(2)}) copy-start(f32[1536]{0:T(1024)} %copy-done.15) | copy-start | bytes 18436
  422.7 13.2 %copy-start.18 = (f32[1536]{0:T(1024)S(1)}, f32[1536]{0:T(1024)}, u32[]{:S(2)}) copy-start(f32[1536]{0:T(1024)} %copy-done.17) | copy-start | bytes 18436
  422.7 13.2 %copy-start.20 = (f32[1536]{0:T(1024)S(1)}, f32[1536]{0:T(1024)}, u32[]{:S(2)}) copy-start(f32[1536]{0:T(1024)} %copy-done.19) | copy-start | bytes 18436
  422.7 13.2 %copy-start.22 = (f32[1536]{0:T(1024)S(1)}, f32[1536]{0:T(1024)}, u32[]{:S(2)}) copy-start(f32[1536]{0:T(1024)} %copy-done.21) | copy-start | bytes 18436
  422.7 13.2 %copy-start.24 = (f32[1536]{0:T(1024)S(1)}, f32[1536]{0:T(1024)}, u32[]{:S(2)}) copy-start(f32[1536]{0:T(1024)} %copy-done.23) | copy-start | bytes 18436
  422.7 13.2 %copy-start.26 = (f32[1536]{0:T(1024)S(1)}, f32[1536]{0:T(1024)}, u32[]{:S(2)}) copy-start(f32[1536]{0:T(1024)} %copy-done.25) | copy-start | bytes 18436
  422.7 13.2 %copy-start.28 = (f32[1536]{0:T(1024)S(1)}, f32[1536]{0:T(1024)}, u32[]{:S(2)}) copy-start(f32[1536]{0:T(1024)} %copy-done.27) | copy-start | bytes 18436
  422.7 13.2 %copy-start.30 = (f32[1536]{0:T(1024)S(1)}, f32[1536]{0:T(1024)}, u32[]{:S(2)}) copy-start(f32[1536]{0:T(1024)} %copy-done.29) | copy-start | bytes 18436
  422.8 13.2 %copy-start.32 = (f32[1536]{0:T(1024)S(1)}, f32[1536]{0:T(1024)}, u32[]{:S(2)}) copy-start(f32[1536]{0:T(1024)} %copy-done.31) | copy-start | bytes 18436
  422.8 13.2 %copy-start.34 = (f32[1536]{0:T(1024)S(1)}, f32[1536]{0:T(1024)}, u32[]{:S(2)}) copy-start(f32[1536]{0:T(1024)} %copy-done.33) | copy-start | bytes 18436
  432.2 15.5 %all-to-all-start.2 = ((bf16[4,96,768]{2,1,0:T(8,128)(2,1)}), bf16[4,96,768]{2,1,0:T(8,128)(2,1)S(1)}, u32[]{:S(2)}, u32[]{:S(2)}) async-start(bf16[4,96,768]{2,1,0:T(8,128)(2,1)} %bitcast.129), calls=%async_computation.5 | async-start | bytes 1179648 | tf_op jit(solution)/shard_map/all_to_all | solution.py:112
  (79 other events, 542.7 us)
Sparse Core Ops, SparseCore 0:
  30.8 41.2 all-gather.3
  74.3 89.9 all-gather.5
  176.8 44.6 reduce-scatter.3
  224.4 32.2 all-gather.7
  270.5 46.2 reduce-scatter.5
  318.9 97.8 reduce-scatter.7

commit v6 on v5

--- a/solution.py
+++ b/solution.py
@@ -57,9 +57,12 @@
     scenes, strip, across, width = feature_maps.shape
     cells = scenes * strip * across
     hid_axes = ("fsdp", "rows")
-    up_mine = lax.all_to_all(w_up, "rows", 1, 0, tiled=True)
-    down_mine = lax.all_to_all(w_down, "rows", 0, 1, tiled=True)
-    both = lax.all_gather(jnp.stack([up_mine, down_mine.T]), "dp", axis=1, tiled=True)
+    dp_size, row_size = lax.axis_size("dp"), lax.axis_size("rows")
+    block_c, hid_f = w_up.shape
+    both = lax.all_gather(jnp.stack([w_up, w_down.T]), "dp", axis=1, tiled=True)
+    both = lax.all_to_all(both, "rows", 2, 1, tiled=True)
+    both = both.reshape(2, row_size, dp_size, block_c, hid_f // row_size)
+    both = both.transpose(0, 2, 1, 3, 4).reshape(2, dp_size * row_size * block_c, hid_f // row_size)
     up_loc, down_t = both[0], both[1]
     cotan = d_out.reshape(cells, width).astype(jnp.float32)
     back = (cotan * layer_scale).astype(jnp.bfloat16)

time: 460 us -> 494 us (1.074)
  blocking collectives: 42.1 us -> 93.3 us
  waiting for transfers between devices: 280 us -> 246 us
  local copies, waits for them, and re-layouts: 24.4 us -> 50.4 us
  starting transfers between devices: 24.5 us -> 18.4 us
    all_to_all x1, blocking collectives: 14.9 us -> 66 us  [body(): both = lax.all_to_all(both, 'rows', 2, 1, tiled=True)]
    all_gather x1, waiting for transfers between devices: 92.2 us -> 72.7 us  [body(): both = lax.all_gather(jnp.stack([w_up, w_down.T]), 'dp', axis=1, tiled=True)]
    all_gather x0 -> x1, local copies, waits for them, and re-layouts: none -> 16.1 us  [body(): both = lax.all_gather(jnp.stack([w_up, w_down.T]), 'dp', axis=1, tiled=True)]
    all_to_all x1 -> x0, waiting for transfers between devices: 11.3 us -> none  [body(): up_mine = lax.all_to_all(w_up, 'rows', 1, 0, tiled=True)]
    all_to_all x2, local copies, waits for them, and re-layouts: 1.96 us -> 9.35 us  [body(): both = lax.all_to_all(both, 'rows', 2, 1, tiled=True)]
    all_to_all x1 -> x0, starting transfers between devices: 6.13 us -> none  [body(): up_mine = lax.all_to_all(w_up, 'rows', 1, 0, tiled=True)]
    slice x0 -> x3, local copies, waits for them, and re-layouts: none -> 5.86 us  [body(): up_loc, down_t = (both[0], both[1])]
  transfers between devices with their start and end apart: 14 -> 13, of which waited for: 8 -> 7; matrix products, arithmetic and copies ran while one was open for 10% -> 17% of each run, Pallas kernels for 0% -> 0%
where the time goes in v6:
time: 494 us; the launch traced here: 489 us
  waiting for transfers between devices  246 us (50%)
  blocking collectives  93.3 us (19%)
  local copies, waits for them, and re-layouts  50.4 us (10%)
  other arithmetic  34.6 us (7%)
  matrix products  30.1 us (6%)
  starting transfers between devices  18.4 us (4%)
  between operations  16.1 us (3%)
    all_gather x1, waiting for transfers between devices, body(): both = lax.all_gather(jnp.stack([w_up, w_down.T]), 'dp', axis=1, tiled=True)  72.7 us
    all_to_all x1, blocking collectives, body(): both = lax.all_to_all(both, 'rows', 2, 1, tiled=True)  66 us
    reduce_scatter x1, waiting for transfers between devices, body(): lax.psum_scatter(grad_parts, 'dp', scatter_dimension=1, tiled=True)  54.3 us
    reduce_scatter x1, waiting for transfers between devices, body(): lax.psum_scatter(mlp_terms.astype(jnp.bfloat16), hid_axes, scatter_dimens...  43.7 us
    reduce_scatter x1, waiting for transfers between devices, body(): lax.psum_scatter(norm_terms.astype(jnp.bfloat16), hid_axes, scatter_dimen...  34.3 us
    all_gather x1, waiting for transfers between devices, body(): back_all = lax.all_gather(back, hid_axes, axis=0, tiled=True)  32.4 us
    all_to_all x1, blocking collectives, small_sums(): lax.all_to_all(packed.reshape(devices, per, width), every, 0, 0, tiled=True)  27.3 us
    all_gather x1, local copies, waits for them, and re-layouts, body(): both = lax.all_gather(jnp.stack([w_up, w_down.T]), 'dp', axis=1, tiled=True)  16.1 us
  transfers between devices with their start and end apart: 13, of which 7 were waited for; matrix products, arithmetic and copies ran while one was open for 17% of the time, Pallas kernels for 0%

profile of v6, /device:TPU:0, one launch (start us, length us, event | category | flops | bytes accessed | tf_op | source)
XLA Modules:
  0.0 489.4 jit_solution(3732843747266746847)
XLA Ops:
  8.6 2.2 copy.52
  11.0 2.4 collective-permute-start
  16.5 2.5 collective-permute-done.1
  19.1 9.5 %fusion.113 = (f32[4,32]{1,0:T(4,128)S(1)}, f32[1,4,32,1536]{3,2,1,0:T(8,128)S(1)}) fusion(f32[1536]{0:T(1024)S(1)} %get-tuple-element.108, f32[1536]{0:T(1024)S(1)} %get-tuple-element.109, f32[1536]{0:T(1024)S(1)} %get-tuple-element.62, f32[1536]{0:T(1024)S(1)} %get-tuple-element.63, f32[1,10,32,1536]{3,2,1,0:T(8,128)S(1)} %maximum_convert_fusion, ...), kind=kLoop, calls=%fused_computation.329 | loop fusion | flops 19267456 | bytes 8641024 | tf_op jit(solution)/shard_map/reduce_sum | solution.py:81
  30.4 72.7 %all-gather.6.cloned.1.call-done = bf16[2,384,3072]{2,0,1:T(2,128)(2,1)} async-done(((bf16[2,96,3072]{2,0,1:T(2,128)(2,1)}), bf16[2,384,3072]{2,0,1:T(2,128)(2,1)}) %all-gather.6.cloned.1.call-update) | async-done | bytes 4718608 | tf_op jit(solution)/shard_map/all_gather | solution.py:62
  103.2 16.1 %copy.53 = bf16[2,384,3072]{1,0,2:T(2,128)(2,1)} copy(bf16[2,384,3072]{2,0,1:T(2,128)(2,1)} %all-gather.6.cloned.1.call-done) | data formatting | bytes 9437184 | tf_op jit(solution)/shard_map/all_gather | solution.py:62
  119.3 66.0 %all_to_all.51 = bf16[2,384,3072]{1,0,2:T(2,128)(2,1)S(1)} all-to-all(bf16[2,384,3072]{1,0,2:T(2,128)(2,1)} %copy.53), channel_id=1, replica_groups=mesh['dp'=4,'fsdp'=2,'rows'=4] {'rows'}, dimensions={2} | all-to-all | bytes 9437184 | tf_op jit(solution)/shard_map/all_to_all | solution.py:63
  185.3 2.7 copy.54
  188.0 6.6 %copy.55 = bf16[2,4,384,768]{3,2,1,0:T(8,128)(2,1)} copy(bf16[2,4,384,768]{2,3,1,0:T(8,128)(2,1)} %bitcast.115) | data formatting | bytes 9437184 | tf_op jit(solution)/shard_map/all_to_all | solution.py:63
  194.7 2.7 fusion.114
  200.5 7.1 %multiply_convert_fusion = (bf16[1024,768]{1,0:T(8,128)(2,1)S(1)}, f32[1024,768]{1,0:T(8,128)}) fusion(bf16[1024,1536]{1,0:T(8,128)(2,1)} %all-gather.4.cloned.1.call-done, bf16[1536,768]{1,0:T(8,128)(2,1)} %bitcast.118), kind=kOutput, calls=%fused_computation.96 | convolution fusion | flops 2419851264 | bytes 10223616 | tf_op jit(solution)/shard_map/dot_general | solution.py:88
  208.8 4.0 convolution_convert_fusion.1
  213.1 43.7 %reduce-scatter.4.cloned.1.call-done = bf16[128,1536]{1,0:T(8,128)(2,1)} async-done(((bf16[1024,1536]{1,0:T(8,128)(2,1)}), bf16[128,1536]{1,0:T(8,128)(2,1)}) %reduce-scatter.4.cloned.1.call-update) | async-done | bytes 393232 | tf_op jit(solution)/shard_map/reduce_scatter | solution.py:93
  256.8 2.7 fusion.13
  259.6 32.4 %all-gather.8.cloned.1.call-done = bf16[1024,1536]{1,0:T(8,128)(2,1)} async-done(((bf16[128,1536]{1,0:T(8,128)(2,1)}), bf16[1024,1536]{1,0:T(8,128)(2,1)}) %all-gather.8.cloned.1.call-update) | async-done | bytes 3145744 | tf_op jit(solution)/shard_map/all_gather | solution.py:69
  292.0 6.8 %fusion.5 = bf16[1024,768]{1,0:T(8,128)(2,1)S(1)} fusion(f32[1024,768]{1,0:T(8,128)} %get-tuple-element.125, bf16[1024,1536]{1,0:T(8,128)(2,1)} %all-gather.8.cloned.1.call-done, bf16[1536,768]{1,0:T(8,128)(2,1)} %bitcast.116), kind=kOutput, calls=%fused_computation.95 | convolution fusion | flops 2423783424 | bytes 10223616 | tf_op jit(solution)/shard_map/dot_general | solution.py:102
  299.9 4.0 convolution_convert_fusion
  304.1 5.2 %fusion.7 = bf16[1,1536,768]{2,1,0:T(8,128)(2,1)S(1)} fusion(bf16[1024,1536]{1,0:T(8,128)(2,1)} %all-gather.8.cloned.1.call-done, bf16[1024,768]{1,0:T(8,128)(2,1)} %copy-done.95), kind=kOutput, calls=%fused_computation.99 | convolution fusion | flops 2417098752 | bytes 7077888 | tf_op jit(solution)/shard_map/dot_general | solution.py:99
  309.3 3.0 fusion.6
  312.2 2.5 pad_maximum_fusion
  316.1 34.3 %reduce-scatter.6.cloned.1.call-done = bf16[128,1536]{1,0:T(8,128)(2,1)} async-done(((bf16[1024,1536]{1,0:T(8,128)(2,1)}), bf16[128,1536]{1,0:T(8,128)(2,1)}) %reduce-scatter.6.cloned.1.call-update) | async-done | bytes 393232 | tf_op jit(solution)/shard_map/reduce_scatter | solution.py:110
  352.4 3.6 multiply_reduce_fusion.1
  356.2 2.0 multiply_reduce_fusion
  360.7 27.3 %all_to_all.52 = f32[32,2,1536]{2,1,0:T(2,128)S(1)} all-to-all(f32[32,2,1536]{2,1,0:T(2,128)S(1)} %reshape.352), channel_id=1, replica_groups=mesh['dp'=4,'fsdp'=2,'rows'=4] {'dp','fsdp','rows'}, dimensions={0} | all-to-all | bytes 786432 | tf_op jit(solution)/shard_map/all_to_all | solution.py:49
  389.0 3.7 all-to-all-start.4
  392.7 2.2 collective-permute-start.2
  396.2 54.3 %reduce-scatter.8.cloned.1.call-done = bf16[2,384,768]{2,1,0:T(8,128)(2,1)} async-done(((bf16[2,1536,768]{2,1,0:T(8,128)(2,1)}), bf16[2,384,768]{2,1,0:T(8,128)(2,1)}) %reduce-scatter.8.cloned.1.call-update) | async-done | bytes 1179664 | tf_op jit(solution)/shard_map/reduce_scatter | solution.py:114
  450.5 2.3 fusion.115
  452.8 3.5 all-to-all-start.2
  459.4 6.4 %all-to-all-done.2 = bf16[4,96,768]{2,1,0:T(8,128)(2,1)S(1)} async-done(((bf16[4,96,768]{2,1,0:T(8,128)(2,1)}), bf16[4,96,768]{2,1,0:T(8,128)(2,1)S(1)}, u32[]{:S(2)}, u32[]{:S(2)}) %all-to-all-start.2) | async-done | bytes 589856 | tf_op jit(solution)/shard_map/all_to_all | solution.py:116
  465.8 3.7 all-to-all-start.1
  469.9 7.5 %fusion.105 = bf16[1,4,32,1536]{3,2,1,0:T(8,128)(2,1)} fusion(f32[1,10,32,1536]{3,2,1,0:T(8,128)S(1)} %maximum_convert_fusion.1, bf16[1,4,32,1536]{3,2,1,0:T(8,128)(2,1)} %param.13, f32[1536]{0:T(1024)S(1)} %copy-done.26, f32[1536]{0:T(1024)S(1)} %copy-done.28, f32[1536]{0:T(1024)S(1)} %copy-done.32, f32[1536]{0:T(1024)S(1)} %copy-done.34, ...), kind=kLoop, calls=%fused_computation.206 | loop fusion | flops 19660800 | bytes 8640512 | tf_op jit(solution)/shard_map/convert_element_type | solution.py:141
  (301 shorter events, 27.6 us)
Async XLA Ops:
  7.2 96.0 %all-gather.6.cloned.1.call-start = ((), (), s32[]{:S(2)}) async-start(), calls=%async_computation.9 | async-start | bytes 5898240 | tf_op jit(solution)/shard_map/all_gather | solution.py:62
  10.9 189.6 %all-gather.4.cloned.1.call-start = ((), (), s32[]{:S(2)}) async-start(), calls=%async_computation.8 | async-start | bytes 3538944 | tf_op jit(solution)/shard_map/all_gather | solution.py:87
  11.0 5.5 %collective-permute-start = (bf16[1,3,32,1536]{3,2,1,0:T(8,128)(2,1)S(1)}, bf16[1,3,32,1536]{3,2,1,0:T(8,128)(2,1)S(1)}, u32[]{:S(2)}, u32[]{:S(2)}) collective-permute-start(bf16[1,3,32,1536]{3,2,1,0:T(8,128)(2,1)S(1)} %get-tuple-element.122), channel_id=1, source_target_pairs={{0,1},{1,2},{2,3},{4,5},{5,6},{6,7},{8,9},{9,10},{10,11},{12,13},{... | collective-permute-start | bytes 884744 | tf_op jit(solution)/shard_map/ppermute | solution.py:25
  13.4 5.6 %collective-permute-start.1 = (bf16[1,3,32,1536]{3,2,1,0:T(8,128)(2,1)S(1)}, bf16[1,3,32,1536]{3,2,1,0:T(8,128)(2,1)S(1)}, u32[]{:S(2)}, u32[]{:S(2)}) collective-permute-start(bf16[1,3,32,1536]{3,2,1,0:T(8,128)(2,1)S(1)} %get-tuple-element.123), channel_id=1, source_target_pairs={{1,0},{2,1},{3,2},{5,4},{6,5},{7,6},{9,8},{10,9},{11,10},{13,12},{... | collective-permute-start | bytes 884744 | tf_op jit(solution)/shard_map/ppermute | solution.py:26
  14.9 13.7 %copy-start.9 = (f32[1536]{0:T(1024)}, f32[1536]{0:T(1024)S(1)}, u32[]{:S(2)}) copy-start(f32[1536]{0:T(1024)S(1)} %get-tuple-element.100) | copy-start | bytes 18436
  14.9 13.7 %copy-start.11 = (f32[1536]{0:T(1024)}, f32[1536]{0:T(1024)S(1)}, u32[]{:S(2)}) copy-start(f32[1536]{0:T(1024)S(1)} %get-tuple-element.101) | copy-start | bytes 18436
  14.9 13.7 %copy-start.13 = (f32[1536]{0:T(1024)}, f32[1536]{0:T(1024)S(1)}, u32[]{:S(2)}) copy-start(f32[1536]{0:T(1024)S(1)} %get-tuple-element.102) | copy-start | bytes 18436
  14.9 13.7 %copy-start.15 = (f32[1536]{0:T(1024)}, f32[1536]{0:T(1024)S(1)}, u32[]{:S(2)}) copy-start(f32[1536]{0:T(1024)S(1)} %get-tuple-element.103) | copy-start | bytes 18436
  14.9 13.7 %copy-start.17 = (f32[1536]{0:T(1024)}, f32[1536]{0:T(1024)S(1)}, u32[]{:S(2)}) copy-start(f32[1536]{0:T(1024)S(1)} %get-tuple-element.104) | copy-start | bytes 18436
  14.9 13.7 %copy-start.19 = (f32[1536]{0:T(1024)}, f32[1536]{0:T(1024)S(1)}, u32[]{:S(2)}) copy-start(f32[1536]{0:T(1024)S(1)} %get-tuple-element.105) | copy-start | bytes 18436
  14.9 13.7 %copy-start.21 = (f32[1536]{0:T(1024)}, f32[1536]{0:T(1024)S(1)}, u32[]{:S(2)}) copy-start(f32[1536]{0:T(1024)S(1)} %get-tuple-element.106) | copy-start | bytes 18436
  15.0 13.7 %copy-start.23 = (f32[1536]{0:T(1024)}, f32[1536]{0:T(1024)S(1)}, u32[]{:S(2)}) copy-start(f32[1536]{0:T(1024)S(1)} %get-tuple-element.107) | copy-start | bytes 18436
  15.0 13.7 %copy-start.25 = (f32[1536]{0:T(1024)}, f32[1536]{0:T(1024)S(1)}, u32[]{:S(2)}) copy-start(f32[1536]{0:T(1024)S(1)} %get-tuple-element.108) | copy-start | bytes 18436
  15.0 13.7 %copy-start.27 = (f32[1536]{0:T(1024)}, f32[1536]{0:T(1024)S(1)}, u32[]{:S(2)}) copy-start(f32[1536]{0:T(1024)S(1)} %get-tuple-element.109) | copy-start | bytes 18436
  15.3 13.4 %copy-start.29 = (f32[1536]{0:T(1024)}, f32[1536]{0:T(1024)S(1)}, u32[]{:S(2)}) copy-start(f32[1536]{0:T(1024)S(1)} %get-tuple-element.61) | copy-start | bytes 18436
  15.3 13.4 %copy-start.31 = (f32[1536]{0:T(1024)}, f32[1536]{0:T(1024)S(1)}, u32[]{:S(2)}) copy-start(f32[1536]{0:T(1024)S(1)} %get-tuple-element.62) | copy-start | bytes 18436
  15.3 13.4 %copy-start.33 = (f32[1536]{0:T(1024)}, f32[1536]{0:T(1024)S(1)}, u32[]{:S(2)}) copy-start(f32[1536]{0:T(1024)S(1)} %get-tuple-element.63) | copy-start | bytes 18436
  15.3 13.4 %copy-start.35 = (f32[1536]{0:T(1024)}, f32[1536]{0:T(1024)S(1)}, u32[]{:S(2)}) copy-start(f32[1536]{0:T(1024)S(1)} %get-tuple-element.64) | copy-start | bytes 18436
  29.1 90.2 %copy-start.90 = (f32[128]{0:T(128)}, f32[128]{0:T(128)S(1)}, u32[]{:S(2)}) copy-start(f32[128]{0:T(128)S(1)} %div.15) | copy-start | bytes 1540
  29.4 89.9 %copy-start.92 = (f32[128]{0:T(128)}, f32[128]{0:T(128)S(1)}, u32[]{:S(2)}) copy-start(f32[128]{0:T(128)S(1)} %rsqrt.12) | copy-start | bytes 1540
  30.4 226.4 %reduce-scatter.4.cloned.1.call-start = ((), (), s32[]{:S(2)}) async-start(), calls=%async_computation.10 | async-start | bytes 3538944 | tf_op jit(solution)/shard_map/reduce_scatter | solution.py:93
  212.8 44.0 %copy-start.3 = (bf16[1,4,32,1536]{3,2,1,0:T(8,128)(2,1)S(1)}, bf16[1,4,32,1536]{3,2,1,0:T(8,128)(2,1)}, u32[]{:S(2)}) copy-start(bf16[1,4,32,1536]{3,2,1,0:T(8,128)(2,1)} %param.13) | copy-start | bytes 1179652
  212.9 79.1 %all-gather.8.cloned.1.call-start = ((), (), s32[]{:S(2)}) async-start(), calls=%async_computation.11 | async-start | bytes 3538944 | tf_op jit(solution)/shard_map/all_gather | solution.py:69
  259.5 90.9 %reduce-scatter.6.cloned.1.call-start = ((), (), s32[]{:S(2)}) async-start(), calls=%async_computation.12 | async-start | bytes 3538944 | tf_op jit(solution)/shard_map/reduce_scatter | solution.py:110
  304.0 146.5 %reduce-scatter.8.cloned.1.call-start = ((), (), s32[]{:S(2)}) async-start(), calls=%async_computation.13 | async-start | bytes 5898240 | tf_op jit(solution)/shard_map/reduce_scatter | solution.py:114
  314.8 35.6 %copy-start.91 = (f32[128]{0:T(128)S(1)}, f32[128]{0:T(128)}, u32[]{:S(2)}) copy-start(f32[128]{0:T(128)} %copy-done.90) | copy-start | bytes 1540
  314.8 35.6 %copy-start.93 = (f32[128]{0:T(128)S(1)}, f32[128]{0:T(128)}, u32[]{:S(2)}) copy-start(f32[128]{0:T(128)} %copy-done.92) | copy-start | bytes 1540
  389.0 63.9 %all-to-all-start.4 = ((f32[32,2,1536]{2,1,0:T(2,128)}), f32[32,2,1536]{2,1,0:T(2,128)S(1)}, u32[]{:S(2)}, u32[]{:S(2)}) async-start(f32[32,2,1536]{2,1,0:T(2,128)} %broadcast_in_dim.8), calls=%async_computation.7 | async-start | bytes 786432 | tf_op jit(solution)/shard_map/all_to_all | solution.py:51
  392.7 64.0 %collective-permute-start.2 = (bf16[1,3,32,1536]{3,2,1,0:T(8,128)(2,1)S(1)}, bf16[1,3,32,1536]{3,2,1,0:T(8,128)(2,1)S(1)}, u32[]{:S(2)}, u32[]{:S(2)}) collective-permute-start(bf16[1,3,32,1536]{3,2,1,0:T(8,128)(2,1)S(1)} %get-tuple-element.120), channel_id=1, source_target_pairs={{0,1},{1,2},{2,3},{4,5},{5,6},{6,7},{8,9},{9,10},{10,11},{12,13},{... | collective-permute-start | bytes 884744 | tf_op jit(solution)/shard_map/ppermute | solution.py:25
  394.9 61.9 %collective-permute-start.3 = (bf16[1,3,32,1536]{3,2,1,0:T(8,128)(2,1)S(1)}, bf16[1,3,32,1536]{3,2,1,0:T(8,128)(2,1)S(1)}, u32[]{:S(2)}, u32[]{:S(2)}) collective-permute-start(bf16[1,3,32,1536]{3,2,1,0:T(8,128)(2,1)S(1)} %get-tuple-element.121), channel_id=1, source_target_pairs={{1,0},{2,1},{3,2},{5,4},{6,5},{7,6},{9,8},{10,9},{11,10},{13,12},{... | collective-permute-start | bytes 884744 | tf_op jit(solution)/shard_map/ppermute | solution.py:26
  452.8 13.0 %all-to-all-start.2 = ((bf16[4,96,768]{2,1,0:T(8,128)(2,1)}), bf16[4,96,768]{2,1,0:T(8,128)(2,1)S(1)}, u32[]{:S(2)}, u32[]{:S(2)}) async-start(bf16[4,96,768]{2,1,0:T(8,128)(2,1)} %bitcast.20), calls=%async_computation.5 | async-start | bytes 1179648 | tf_op jit(solution)/shard_map/all_to_all | solution.py:116
  465.8 15.5 %all-to-all-start.1 = ((bf16[4,96,768]{2,1,0:T(8,128)(2,1)}), bf16[4,96,768]{2,1,0:T(8,128)(2,1)S(1)}, u32[]{:S(2)}, u32[]{:S(2)}) async-start(bf16[4,96,768]{2,1,0:T(8,128)(2,1)} %bitcast.120), calls=%async_computation.4 | async-start | bytes 1179648 | tf_op jit(solution)/shard_map/all_to_all | solution.py:115
  (79 other events, 899.8 us)
Sparse Core Ops, SparseCore 0:
  11.0 92.0 all-gather.5
  105.6 39.1 all-gather.3
  213.0 43.7 reduce-scatter.3
  259.7 32.2 all-gather.7
  304.1 46.2 reduce-scatter.5
  352.6 97.8 reduce-scatter.7

commit v7 on v5

--- a/solution.py
+++ b/solution.py
@@ -57,13 +57,12 @@
     scenes, strip, across, width = feature_maps.shape
     cells = scenes * strip * across
     hid_axes = ("fsdp", "rows")
-    up_mine = lax.all_to_all(w_up, "rows", 1, 0, tiled=True)
-    down_mine = lax.all_to_all(w_down, "rows", 0, 1, tiled=True)
-    both = lax.all_gather(jnp.stack([up_mine, down_mine.T]), "dp", axis=1, tiled=True)
-    up_loc, down_t = both[0], both[1]
+    up_loc = lax.all_to_all(w_up, "rows", 1, 0, tiled=True)
+    up_loc = lax.all_gather(up_loc, "dp", axis=0, tiled=True)
+    down_loc = lax.all_to_all(w_down, "rows", 0, 1, tiled=True)
+    down_loc = lax.all_gather(down_loc, "dp", axis=1, tiled=True)
     cotan = d_out.reshape(cells, width).astype(jnp.float32)
     back = (cotan * layer_scale).astype(jnp.bfloat16)
-    back_all = lax.all_gather(back, hid_axes, axis=0, tiled=True)
     rimmed = padded_2(feature_maps, (("rows", 1),), 3)
     padded = jnp.pad(rimmed.astype(jnp.float32), ((0, 0), (0, 0), (3, 3), (0, 0)))
     filtered = jnp.zeros(feature_maps.shape, jnp.float32)
@@ -81,12 +80,11 @@
     rstd = lax.rsqrt(variance + norm_eps)
     normed = center * rstd
     scaled = (normed * norm_gain).astype(jnp.bfloat16)
-    gathered = lax.all_gather(scaled, hid_axes, axis=0, tiled=True)
+    pair = lax.all_gather(jnp.stack([scaled, back]), hid_axes, axis=1, tiled=True)
+    gathered, back_all = pair[0], pair[1]
     hidden = jnp.dot(gathered, up_loc, preferred_element_type=jnp.float32)
     active = gelu_exact(hidden).astype(jnp.bfloat16)
-    mlp_terms = lax.dot_general(
-        active, down_t, contract_cols, preferred_element_type=jnp.float32
-    )
+    mlp_terms = jnp.dot(active, down_loc, preferred_element_type=jnp.float32)
     branch = lax.psum_scatter(
         mlp_terms.astype(jnp.bfloat16), hid_axes, scatter_dimension=0, tiled=True
     ).astype(jnp.float32)
@@ -96,7 +94,9 @@
     down_part_t = lax.dot_general(
         back_all, active, contract_rows, preferred_element_type=jnp.float32
     )
-    slope_in = jnp.dot(back_all, down_t, preferred_element_type=jnp.float32)
+    slope_in = lax.dot_general(
+        back_all, down_loc, contract_cols, preferred_element_type=jnp.float32
+    )
     hidden_grad = (slope_in * gelu_slope(hidden)).astype(jnp.bfloat16)
     up_part = lax.dot_general(
         gathered, hidden_grad, contract_rows, preferred_element_type=jnp.float32

time: 460 us -> 418 us (0.909)
  waiting for transfers between devices: 280 us -> 233 us
  blocking collectives: 42.1 us -> 56.7 us
  starting transfers between devices: 24.5 us -> 18.2 us
  local copies, waits for them, and re-layouts: 24.4 us -> 18.6 us
    all_gather x3, waiting for transfers between devices: 129 us -> 104 us  [the longest x1 46.8 us: body(): lax.all_gather(jnp.stack([scaled, back]), hid_axes, axis=1, tiled=True)]
    reduce_scatter x1, waiting for transfers between devices: 44.8 us -> 20.5 us  [body(): lax.psum_scatter(mlp_terms.astype(jnp.bfloat16), hid_axes, scatter_dimens...]
    all_to_all x1 -> x2, blocking collectives: 14.9 us -> 29.5 us  [the longest x1 15.8 us: body(): down_loc = lax.all_to_all(w_down, 'rows', 0, 1, tiled=True)]
    reduce_scatter x1, waiting for transfers between devices: 34.3 us -> 47.3 us  [body(): lax.psum_scatter(norm_terms.astype(jnp.bfloat16), hid_axes, scatter_dimen...]
    all_to_all x1 -> x0, waiting for transfers between devices: 11.3 us -> none  [body(): up_mine = lax.all_to_all(w_up, 'rows', 1, 0, tiled=True)]
    all_to_all x1 -> x0, starting transfers between devices: 6.13 us -> none  [body(): up_mine = lax.all_to_all(w_up, 'rows', 1, 0, tiled=True)]
  transfers between devices with their start and end apart: 14 -> 13, of which waited for: 8 -> 8; matrix products, arithmetic and copies ran while one was open for 10% -> 19% of each run, Pallas kernels for 0% -> 0%
where the time goes in v7:
time: 418 us; the launch traced here: 414 us
  waiting for transfers between devices  233 us (56%)
  blocking collectives  56.7 us (14%)
  other arithmetic  36.6 us (9%)
  matrix products  34.5 us (8%)
  local copies, waits for them, and re-layouts  18.6 us (4%)
  starting transfers between devices  18.2 us (4%)
  between operations  15.9 us (4%)
    reduce_scatter x1, waiting for transfers between devices, body(): lax.psum_scatter(grad_parts, 'dp', scatter_dimension=1, tiled=True)  54.2 us
    reduce_scatter x1, waiting for transfers between devices, body(): lax.psum_scatter(norm_terms.astype(jnp.bfloat16), hid_axes, scatter_dimen...  47.3 us
    all_gather x1, waiting for transfers between devices, body(): lax.all_gather(jnp.stack([scaled, back]), hid_axes, axis=1, tiled=True)  46.8 us
    all_gather x1, waiting for transfers between devices, body(): down_loc = lax.all_gather(down_loc, 'dp', axis=1, tiled=True)  44.6 us
    all_to_all x1, blocking collectives, small_sums(): lax.all_to_all(packed.reshape(devices, per, width), every, 0, 0, tiled=True)  27.2 us
    reduce_scatter x1, waiting for transfers between devices, body(): lax.psum_scatter(mlp_terms.astype(jnp.bfloat16), hid_axes, scatter_dimens...  20.5 us
    all_to_all x1, blocking collectives, body(): down_loc = lax.all_to_all(w_down, 'rows', 0, 1, tiled=True)  15.8 us
    all_to_all x1, blocking collectives, body(): up_loc = lax.all_to_all(w_up, 'rows', 1, 0, tiled=True)  13.7 us
  transfers between devices with their start and end apart: 13, of which 8 were waited for; matrix products, arithmetic and copies ran while one was open for 19% of the time, Pallas kernels for 0%

profile of v7, /device:TPU:0, one launch (start us, length us, event | category | flops | bytes accessed | tf_op | source)
XLA Modules:
  0.0 413.6 jit_solution(12665234852482637166)
XLA Ops:
  8.4 13.7 %all_to_all.74 = bf16[96,4,768]{2,0,1:T(8,128)(2,1)} all-to-all(bf16[96,4,768]{2,0,1:T(8,128)(2,1)S(1)} %bitcast.133), channel_id=1, replica_groups=mesh['dp'=4,'fsdp'=2,'rows'=4] {'rows'}, dimensions={1} | all-to-all | bytes 1179648 | tf_op jit(solution)/shard_map/all_to_all | solution.py:60
  22.2 1.7 collective-permute-start
  23.9 1.3 collective-permute-start.1
  27.8 9.5 %fusion.118 = (f32[4,32]{1,0:T(4,128)S(1)}, f32[1,4,32,1536]{3,2,1,0:T(8,128)S(1)}) fusion(f32[1536]{0:T(1024)S(1)} %get-tuple-element.108, f32[1536]{0:T(1024)S(1)} %get-tuple-element.109, f32[1536]{0:T(1024)S(1)} %get-tuple-element.62, f32[1536]{0:T(1024)S(1)} %get-tuple-element.63, f32[1,10,32,1536]{3,2,1,0:T(8,128)S(1)} %maximum_convert_fusion, ...), kind=kLoop, calls=%fused_computation.338 | loop fusion | flops 19267456 | bytes 8641024 | tf_op jit(solution)/shard_map/reduce_sum | solution.py:77
  41.0 1.3 rsqrt.12
  45.3 15.8 %all_to_all.75 = bf16[4,768,96]{1,2,0:T(8,128)(2,1)} all-to-all(bf16[4,768,96]{1,2,0:T(8,128)(2,1)S(1)} %bitcast.134), channel_id=1, replica_groups=mesh['dp'=4,'fsdp'=2,'rows'=4] {'rows'}, dimensions={0} | all-to-all | bytes 1179648 | tf_op jit(solution)/shard_map/all_to_all | solution.py:62
  61.2 12.3 %all-gather.6.cloned.1.call-done = bf16[1536,768]{1,0:T(8,128)(2,1)} async-done(((bf16[384,768]{1,0:T(8,128)(2,1)}), bf16[1536,768]{1,0:T(8,128)(2,1)}) %all-gather.6.cloned.1.call-update) | async-done | bytes 2359312 | tf_op jit(solution)/shard_map/all_gather | solution.py:61
  73.5 46.8 %all-gather.4.cloned.1.call-done = bf16[2,1024,1536]{2,1,0:T(8,128)(2,1)} async-done(((bf16[2,128,1536]{2,1,0:T(8,128)(2,1)}), bf16[2,1024,1536]{2,1,0:T(8,128)(2,1)}) %all-gather.4.cloned.1.call-update) | async-done | bytes 6291472 | tf_op jit(solution)/shard_map/all_gather | solution.py:83
  120.3 7.5 %multiply_convert_fusion = (bf16[1024,768]{1,0:T(8,128)(2,1)}, f32[1024,768]{1,0:T(8,128)}) fusion(bf16[1536,768]{1,0:T(8,128)(2,1)} %all-gather.6.cloned.1.call-done, bf16[2,1024,1536]{2,1,0:T(8,128)(2,1)} %all-gather.4.cloned.1.call-done), kind=kOutput, calls=%fused_computation.98 | convolution fusion | flops 2419851264 | bytes 10223616 | tf_op jit(solution)/shard_map/dot_general | solution.py:85
  127.8 44.6 %all-gather.8.cloned.1.call-done = bf16[768,1536]{0,1:T(8,128)(2,1)} async-done(((bf16[768,384]{0,1:T(8,128)(2,1)}), bf16[768,1536]{0,1:T(8,128)(2,1)}) %all-gather.8.cloned.1.call-update) | async-done | bytes 2359312 | tf_op jit(solution)/shard_map/all_gather | solution.py:63
  172.4 6.5 %convolution_convert_fusion.1 = bf16[1024,1536]{1,0:T(8,128)(2,1)} fusion(bf16[1024,768]{1,0:T(8,128)(2,1)} %get-tuple-element.121, bf16[768,1536]{0,1:T(8,128)(2,1)} %all-gather.8.cloned.1.call-done), kind=kOutput, calls=%fused_computation.87 | convolution fusion | flops 2417491968 | bytes 7077888 | tf_op jit(solution)/shard_map/dot_general | solution.py:87
  179.1 6.8 %fusion.5 = bf16[1024,768]{1,0:T(8,128)(2,1)S(1)} fusion(f32[1024,768]{1,0:T(8,128)} %get-tuple-element.122, bf16[768,1536]{0,1:T(8,128)(2,1)} %all-gather.8.cloned.1.call-done, bf16[2,1024,1536]{2,1,0:T(8,128)(2,1)} %all-gather.4.cloned.1.call-done), kind=kOutput, calls=%fused_computation.95 | convolution fusion | flops 2423783424 | bytes 10223616 | tf_op jit(solution)/shard_map/dot_general | solution.py:97
  187.1 4.1 convolution_convert_fusion
  191.2 5.2 %fusion.7 = bf16[1,1536,768]{2,1,0:T(8,128)(2,1)S(1)} fusion(bf16[1024,768]{1,0:T(8,128)(2,1)} %get-tuple-element.121, bf16[2,1024,1536]{2,1,0:T(8,128)(2,1)} %all-gather.4.cloned.1.call-done), kind=kOutput, calls=%fused_computation.101 | convolution fusion | flops 2417098752 | bytes 7077888 | tf_op jit(solution)/shard_map/dot_general | solution.py:94
  196.4 4.6 %fusion.6 = bf16[1,1536,768]{2,1,0:T(8,128)(2,1)S(1)} fusion(bf16[1024,768]{1,0:T(8,128)(2,1)S(1)} %copy-done.75, bf16[2,1024,1536]{2,1,0:T(8,128)(2,1)} %all-gather.4.cloned.1.call-done), kind=kOutput, calls=%fused_computation.100 | convolution fusion | flops 2417098752 | bytes 7077888 | tf_op jit(solution)/shard_map/dot_general | solution.py:101
  201.0 2.5 pad_maximum_fusion
  203.6 20.5 %reduce-scatter.4.cloned.1.call-done = bf16[128,1536]{1,0:T(8,128)(2,1)} async-done(((bf16[1024,1536]{1,0:T(8,128)(2,1)}), bf16[128,1536]{1,0:T(8,128)(2,1)}) %reduce-scatter.4.cloned.1.call-update) | async-done | bytes 393232 | tf_op jit(solution)/shard_map/reduce_scatter | solution.py:88
  224.1 1.9 fusion.15
  226.6 47.3 %reduce-scatter.6.cloned.1.call-done = bf16[128,1536]{1,0:T(8,128)(2,1)} async-done(((bf16[1024,1536]{1,0:T(8,128)(2,1)}), bf16[128,1536]{1,0:T(8,128)(2,1)}) %reduce-scatter.6.cloned.1.call-update) | async-done | bytes 393232 | tf_op jit(solution)/shard_map/reduce_scatter | solution.py:107
  273.9 1.4 fusion.19
  276.0 3.6 multiply_reduce_fusion.1
  279.8 2.0 multiply_reduce_fusion
  284.3 27.2 %all_to_all.76 = f32[32,2,1536]{2,1,0:T(2,128)S(1)} all-to-all(f32[32,2,1536]{2,1,0:T(2,128)S(1)} %reshape.467), channel_id=1, replica_groups=mesh['dp'=4,'fsdp'=2,'rows'=4] {'dp','fsdp','rows'}, dimensions={0} | all-to-all | bytes 786432 | tf_op jit(solution)/shard_map/all_to_all | solution.py:49
  312.5 3.7 all-to-all-start.5
  316.4 2.2 collective-permute-start.2
  318.5 1.3 collective-permute-start.3
  319.8 54.2 %reduce-scatter.8.cloned.1.call-done = bf16[2,384,768]{2,1,0:T(8,128)(2,1)} async-done(((bf16[2,1536,768]{2,1,0:T(8,128)(2,1)}), bf16[2,384,768]{2,1,0:T(8,128)(2,1)}) %reduce-scatter.8.cloned.1.call-update) | async-done | bytes 1179664 | tf_op jit(solution)/shard_map/reduce_scatter | solution.py:111
  374.0 2.3 fusion.119
  376.3 4.2 %all-to-all-start.3 = ((bf16[4,96,768]{2,1,0:T(8,128)(2,1)}), bf16[4,96,768]{2,1,0:T(8,128)(2,1)}, u32[]{:S(2)}, u32[]{:S(2)}) async-start(bf16[4,96,768]{2,1,0:T(8,128)(2,1)} %bitcast.17), calls=%async_computation.6 | async-start | bytes 1179648 | tf_op jit(solution)/shard_map/all_to_all | solution.py:113
  383.5 6.7 %all-to-all-done.3 = bf16[4,96,768]{2,1,0:T(8,128)(2,1)} async-done(((bf16[4,96,768]{2,1,0:T(8,128)(2,1)}), bf16[4,96,768]{2,1,0:T(8,128)(2,1)}, u32[]{:S(2)}, u32[]{:S(2)}) %all-to-all-start.3) | async-done | bytes 589856 | tf_op jit(solution)/shard_map/all_to_all | solution.py:113
  390.1 3.5 all-to-all-start.2
  393.9 7.7 %fusion.107 = bf16[1,4,32,1536]{3,2,1,0:T(8,128)(2,1)} fusion(f32[1,10,32,1536]{3,2,1,0:T(8,128)S(1)} %maximum_convert_fusion.1, f32[1536]{0:T(1024)S(1)} %copy-done.24, f32[1536]{0:T(1024)S(1)} %copy-done.26, f32[1536]{0:T(1024)S(1)} %copy-done.30, f32[1536]{0:T(1024)S(1)} %copy-done.32, f32[1536]{0:T(1024)S(1)} %copy-done.34, f32[1536]{0:T(1024)S(1)} %copy-done.36, ...), kind=kLoop, calls=%fused_computation.209 | loop fusion | flops 19660800 | bytes 8611840 | tf_op jit(solution)/shard_map/convert_element_type | solution.py:138
  (254 shorter events, 24.1 us)
Async XLA Ops:
  7.2 15.0 %copy-start = (bf16[1,4,32,1536]{3,2,1,0:T(8,128)(2,1)S(1)}, bf16[1,4,32,1536]{3,2,1,0:T(8,128)(2,1)}, u32[]{:S(2)}) copy-start(bf16[1,4,32,1536]{3,2,1,0:T(8,128)(2,1)} %param.7) | copy-start | bytes 1179652
  7.2 18.0 %copy-start.5 = (f32[7,7,1536]{2,1,0:T(8,128)S(1)}, f32[7,7,1536]{2,1,0:T(8,128)}, u32[]{:S(2)}) copy-start(f32[7,7,1536]{2,1,0:T(8,128)} %param.8) | copy-start | bytes 903172
  7.2 66.3 %all-gather.6.cloned.1.call-start = ((), (), s32[]{:S(2)}) async-start(), calls=%async_computation.10 | async-start | bytes 2949120 | tf_op jit(solution)/shard_map/all_gather | solution.py:61
  22.1 98.2 %all-gather.4.cloned.1.call-start = ((), (), s32[]{:S(2)}) async-start(), calls=%async_computation.9 | async-start | bytes 7077888 | tf_op jit(solution)/shard_map/all_gather | solution.py:83
  22.2 4.8 %collective-permute-start = (bf16[1,3,32,1536]{3,2,1,0:T(8,128)(2,1)S(1)}, bf16[1,3,32,1536]{3,2,1,0:T(8,128)(2,1)S(1)}, u32[]{:S(2)}, u32[]{:S(2)}) collective-permute-start(bf16[1,3,32,1536]{3,2,1,0:T(8,128)(2,1)S(1)} %get-tuple-element.119), channel_id=1, source_target_pairs={{0,1},{1,2},{2,3},{4,5},{5,6},{6,7},{8,9},{9,10},{10,11},{12,13},{... | collective-permute-start | bytes 884744 | tf_op jit(solution)/shard_map/ppermute | solution.py:25
  23.9 3.7 collective-permute-start.1
  27.7 14.5 %copy-start.1 = (bf16[1,4,32,1536]{3,2,1,0:T(8,128)(2,1)S(1)}, bf16[1,4,32,1536]{3,2,1,0:T(8,128)(2,1)}, u32[]{:S(2)}) copy-start(bf16[1,4,32,1536]{3,2,1,0:T(8,128)(2,1)} %param.13) | copy-start | bytes 1179652
  27.8 14.5 %copy-start.6 = (f32[1536]{0:T(1024)S(1)}, f32[1536]{0:T(1024)}, u32[]{:S(2)}) copy-start(f32[1536]{0:T(1024)} %param.9) | copy-start | bytes 18436
  44.2 128.2 %all-gather.8.cloned.1.call-start = ((), (), s32[]{:S(2)}) async-start(), calls=%async_computation.11 | async-start | bytes 2949120 | tf_op jit(solution)/shard_map/all_gather | solution.py:63
  61.2 162.9 %reduce-scatter.4.cloned.1.call-start = ((), (), s32[]{:S(2)}) async-start(), calls=%async_computation.12 | async-start | bytes 3538944 | tf_op jit(solution)/shard_map/reduce_scatter | solution.py:88
  178.9 95.0 %reduce-scatter.6.cloned.1.call-start = ((), (), s32[]{:S(2)}) async-start(), calls=%async_computation.13 | async-start | bytes 3538944 | tf_op jit(solution)/shard_map/reduce_scatter | solution.py:107
  191.2 182.8 %reduce-scatter.8.cloned.1.call-start = ((), (), s32[]{:S(2)}) async-start(), calls=%async_computation.14 | async-start | bytes 5898240 | tf_op jit(solution)/shard_map/reduce_scatter | solution.py:111
  312.5 63.9 %all-to-all-start.5 = ((f32[32,2,1536]{2,1,0:T(2,128)}), f32[32,2,1536]{2,1,0:T(2,128)S(1)}, u32[]{:S(2)}, u32[]{:S(2)}) async-start(f32[32,2,1536]{2,1,0:T(2,128)} %broadcast_in_dim.8), calls=%async_computation.8 | async-start | bytes 786432 | tf_op jit(solution)/shard_map/all_to_all | solution.py:51
  316.4 64.5 %collective-permute-start.2 = (bf16[1,3,32,1536]{3,2,1,0:T(8,128)(2,1)S(1)}, bf16[1,3,32,1536]{3,2,1,0:T(8,128)(2,1)S(1)}, u32[]{:S(2)}, u32[]{:S(2)}) collective-permute-start(bf16[1,3,32,1536]{3,2,1,0:T(8,128)(2,1)S(1)} %get-tuple-element.117), channel_id=1, source_target_pairs={{0,1},{1,2},{2,3},{4,5},{5,6},{6,7},{8,9},{9,10},{10,11},{12,13},{... | collective-permute-start | bytes 884744 | tf_op jit(solution)/shard_map/ppermute | solution.py:25
  318.5 62.3 %collective-permute-start.3 = (bf16[1,3,32,1536]{3,2,1,0:T(8,128)(2,1)S(1)}, bf16[1,3,32,1536]{3,2,1,0:T(8,128)(2,1)S(1)}, u32[]{:S(2)}, u32[]{:S(2)}) collective-permute-start(bf16[1,3,32,1536]{3,2,1,0:T(8,128)(2,1)S(1)} %get-tuple-element.118), channel_id=1, source_target_pairs={{1,0},{2,1},{3,2},{5,4},{6,5},{7,6},{9,8},{10,9},{11,10},{13,12},{... | collective-permute-start | bytes 884744 | tf_op jit(solution)/shard_map/ppermute | solution.py:26
  376.3 13.8 %all-to-all-start.3 = ((bf16[4,96,768]{2,1,0:T(8,128)(2,1)}), bf16[4,96,768]{2,1,0:T(8,128)(2,1)}, u32[]{:S(2)}, u32[]{:S(2)}) async-start(bf16[4,96,768]{2,1,0:T(8,128)(2,1)} %bitcast.17), calls=%async_computation.6 | async-start | bytes 1179648 | tf_op jit(solution)/shard_map/all_to_all | solution.py:113
  380.5 13.1 %copy-start.2 = (bf16[1,4,32,1536]{3,2,1,0:T(8,128)(2,1)S(1)}, bf16[1,4,32,1536]{3,2,1,0:T(8,128)(2,1)}, u32[]{:S(2)}) copy-start(bf16[1,4,32,1536]{3,2,1,0:T(8,128)(2,1)} %param.13) | copy-start | bytes 1179652
  380.5 13.1 %copy-start.8 = (f32[1536]{0:T(1024)S(1)}, f32[1536]{0:T(1024)}, u32[]{:S(2)}) copy-start(f32[1536]{0:T(1024)} %copy-done.7) | copy-start | bytes 18436
  380.5 13.1 %copy-start.10 = (f32[1536]{0:T(1024)S(1)}, f32[1536]{0:T(1024)}, u32[]{:S(2)}) copy-start(f32[1536]{0:T(1024)} %copy-done.9) | copy-start | bytes 18436
  380.5 13.1 %copy-start.12 = (f32[1536]{0:T(1024)S(1)}, f32[1536]{0:T(1024)}, u32[]{:S(2)}) copy-start(f32[1536]{0:T(1024)} %copy-done.11) | copy-start | bytes 18436
  380.5 13.1 %copy-start.14 = (f32[1536]{0:T(1024)S(1)}, f32[1536]{0:T(1024)}, u32[]{:S(2)}) copy-start(f32[1536]{0:T(1024)} %copy-done.13) | copy-start | bytes 18436
  380.6 13.1 %copy-start.16 = (f32[1536]{0:T(1024)S(1)}, f32[1536]{0:T(1024)}, u32[]{:S(2)}) copy-start(f32[1536]{0:T(1024)} %copy-done.15) | copy-start | bytes 18436
  380.6 13.1 %copy-start.18 = (f32[1536]{0:T(1024)S(1)}, f32[1536]{0:T(1024)}, u32[]{:S(2)}) copy-start(f32[1536]{0:T(1024)} %copy-done.17) | copy-start | bytes 18436
  380.6 13.1 %copy-start.20 = (f32[1536]{0:T(1024)S(1)}, f32[1536]{0:T(1024)}, u32[]{:S(2)}) copy-start(f32[1536]{0:T(1024)} %copy-done.19) | copy-start | bytes 18436
  380.6 13.1 %copy-start.22 = (f32[1536]{0:T(1024)S(1)}, f32[1536]{0:T(1024)}, u32[]{:S(2)}) copy-start(f32[1536]{0:T(1024)} %copy-done.21) | copy-start | bytes 18436
  380.6 13.1 %copy-start.24 = (f32[1536]{0:T(1024)S(1)}, f32[1536]{0:T(1024)}, u32[]{:S(2)}) copy-start(f32[1536]{0:T(1024)} %copy-done.23) | copy-start | bytes 18436
  380.6 13.1 %copy-start.26 = (f32[1536]{0:T(1024)S(1)}, f32[1536]{0:T(1024)}, u32[]{:S(2)}) copy-start(f32[1536]{0:T(1024)} %copy-done.25) | copy-start | bytes 18436
  380.6 13.1 %copy-start.28 = (f32[1536]{0:T(1024)S(1)}, f32[1536]{0:T(1024)}, u32[]{:S(2)}) copy-start(f32[1536]{0:T(1024)} %copy-done.27) | copy-start | bytes 18436
  380.6 13.1 %copy-start.30 = (f32[1536]{0:T(1024)S(1)}, f32[1536]{0:T(1024)}, u32[]{:S(2)}) copy-start(f32[1536]{0:T(1024)} %copy-done.29) | copy-start | bytes 18436
  380.6 13.1 %copy-start.32 = (f32[1536]{0:T(1024)S(1)}, f32[1536]{0:T(1024)}, u32[]{:S(2)}) copy-start(f32[1536]{0:T(1024)} %copy-done.31) | copy-start | bytes 18436
  380.6 13.1 %copy-start.34 = (f32[1536]{0:T(1024)S(1)}, f32[1536]{0:T(1024)}, u32[]{:S(2)}) copy-start(f32[1536]{0:T(1024)} %copy-done.33) | copy-start | bytes 18436
  390.1 15.4 %all-to-all-start.2 = ((bf16[4,96,768]{2,1,0:T(8,128)(2,1)}), bf16[4,96,768]{2,1,0:T(8,128)(2,1)S(1)}, u32[]{:S(2)}, u32[]{:S(2)}) async-start(bf16[4,96,768]{2,1,0:T(8,128)(2,1)} %bitcast.15), calls=%async_computation.5 | async-start | bytes 1179648 | tf_op jit(solution)/shard_map/all_to_all | solution.py:112
  (57 other events, 605.7 us)
Sparse Core Ops, SparseCore 0:
  22.2 51.1 all-gather.5
  75.9 44.3 all-gather.3
  121.9 50.4 all-gather.7
  179.0 45.0 reduce-scatter.3
  227.7 46.2 reduce-scatter.5
  276.1 97.8 reduce-scatter.7

commit v8 on v5

--- a/solution.py
+++ b/solution.py
@@ -63,7 +63,6 @@
     up_loc, down_t = both[0], both[1]
     cotan = d_out.reshape(cells, width).astype(jnp.float32)
     back = (cotan * layer_scale).astype(jnp.bfloat16)
-    back_all = lax.all_gather(back, hid_axes, axis=0, tiled=True)
     rimmed = padded_2(feature_maps, (("rows", 1),), 3)
     padded = jnp.pad(rimmed.astype(jnp.float32), ((0, 0), (0, 0), (3, 3), (0, 0)))
     filtered = jnp.zeros(feature_maps.shape, jnp.float32)
@@ -81,18 +80,13 @@
     rstd = lax.rsqrt(variance + norm_eps)
     normed = center * rstd
     scaled = (normed * norm_gain).astype(jnp.bfloat16)
-    gathered = lax.all_gather(scaled, hid_axes, axis=0, tiled=True)
+    pair = lax.all_gather(jnp.stack([scaled, back]), hid_axes, axis=1, tiled=True)
+    gathered, back_all = pair[0], pair[1]
     hidden = jnp.dot(gathered, up_loc, preferred_element_type=jnp.float32)
     active = gelu_exact(hidden).astype(jnp.bfloat16)
     mlp_terms = lax.dot_general(
         active, down_t, contract_cols, preferred_element_type=jnp.float32
     )
-    branch = lax.psum_scatter(
-        mlp_terms.astype(jnp.bfloat16), hid_axes, scatter_dimension=0, tiled=True
-    ).astype(jnp.float32)
-    resid = feature_maps.reshape(cells, width).astype(jnp.float32)
-    result = (resid + layer_scale * branch).astype(jnp.bfloat16).reshape(feature_maps.shape)
-    scale_part = jnp.sum(cotan * branch, axis=0)
     down_part_t = lax.dot_general(
         back_all, active, contract_rows, preferred_element_type=jnp.float32
     )
@@ -104,9 +98,16 @@
     norm_terms = lax.dot_general(
         hidden_grad, up_loc, contract_cols, preferred_element_type=jnp.float32
     )
-    norm_grad = lax.psum_scatter(
-        norm_terms.astype(jnp.bfloat16), hid_axes, scatter_dimension=0, tiled=True
+    sums = lax.psum_scatter(
+        jnp.stack([mlp_terms, norm_terms]).astype(jnp.bfloat16),
+        hid_axes,
+        scatter_dimension=1,
+        tiled=True,
     ).astype(jnp.float32)
+    branch, norm_grad = sums[0], sums[1]
+    resid = feature_maps.reshape(cells, width).astype(jnp.float32)
+    result = (resid + layer_scale * branch).astype(jnp.bfloat16).reshape(feature_maps.shape)
+    scale_part = jnp.sum(cotan * branch, axis=0)
     grad_parts = jnp.stack([up_part, down_part_t]).astype(jnp.bfloat16)
     grad_sums = lax.psum_scatter(grad_parts, "dp", scatter_dimension=1, tiled=True)
     grad_up = lax.all_to_all(grad_sums[0], "rows", 0, 1, tiled=True).astype(jnp.float32)

time: 460 us -> 414 us (0.900)
  blocking collectives: 42.1 us -> 11.9 us
  matrix products: 31.7 us -> 24.5 us
  local copies, waits for them, and re-layouts: 24.4 us -> 18.5 us
    all_to_all x1 -> x0, blocking collectives: 27.3 us -> none  [small_sums(): lax.all_to_all(packed.reshape(devices, per, width), every, 0, 0, tiled=True)]
    reduce_scatter x2 -> x1, waiting for transfers between devices: 79.1 us -> 58.8 us  [body(): lax.psum_scatter(jnp.stack([mlp_terms, norm_terms]).astype(jnp.bfloat16),...]
    all_gather x1, waiting for transfers between devices: 92.2 us -> 73.1 us  [body(): lax.all_gather(jnp.stack([up_mine, down_mine.T]), 'dp', axis=1, tiled=True)]
    reduce_scatter x1, waiting for transfers between devices: 54.3 us -> 72.1 us  [body(): lax.psum_scatter(grad_parts, 'dp', scatter_dimension=1, tiled=True)]
    all_gather x2 -> x1, waiting for transfers between devices: 37.1 us -> 46.5 us  [body(): lax.all_gather(jnp.stack([scaled, back]), hid_axes, axis=1, tiled=True)]
    all_to_all x0 -> x1, waiting for transfers between devices: none -> 8.85 us  [small_sums(): lax.all_to_all(packed.reshape(devices, per, width), every, 0, 0, tiled=True)]
  transfers between devices with their start and end apart: 14 -> 13, of which waited for: 8 -> 9; matrix products, arithmetic and copies ran while one was open for 10% -> 14% of each run, Pallas kernels for 0% -> 0%
where the time goes in v8:
time: 414 us; the launch traced here: 413 us
  waiting for transfers between devices  277 us (67%)
  other arithmetic  40.3 us (10%)
  starting transfers between devices  26 us (6%)
  matrix products  24.5 us (6%)
  local copies, waits for them, and re-layouts  18.5 us (4%)
  between operations  15.7 us (4%)
  blocking collectives  11.9 us (3%)
    all_gather x1, waiting for transfers between devices, body(): lax.all_gather(jnp.stack([up_mine, down_mine.T]), 'dp', axis=1, tiled=True)  73.1 us
    reduce_scatter x1, waiting for transfers between devices, body(): lax.psum_scatter(grad_parts, 'dp', scatter_dimension=1, tiled=True)  72.1 us
    reduce_scatter x1, waiting for transfers between devices, body(): lax.psum_scatter(jnp.stack([mlp_terms, norm_terms]).astype(jnp.bfloat16),...  58.8 us
    all_gather x1, waiting for transfers between devices, body(): lax.all_gather(jnp.stack([scaled, back]), hid_axes, axis=1, tiled=True)  46.5 us
    all_to_all x1, blocking collectives, body(): down_mine = lax.all_to_all(w_down, 'rows', 0, 1, tiled=True)  11.9 us
    all_to_all x1, waiting for transfers between devices, body(): up_mine = lax.all_to_all(w_up, 'rows', 1, 0, tiled=True)  9.49 us
    reduce_sum x1, other arithmetic, body(): average = jnp.mean(flat, axis=-1, keepdims=True)  9.44 us
    all_to_all x1, waiting for transfers between devices, small_sums(): lax.all_to_all(packed.reshape(devices, per, width), every, 0, 0, tiled=True)  8.85 us
  transfers between devices with their start and end apart: 13, of which 9 were waited for; matrix products, arithmetic and copies ran while one was open for 14% of the time, Pallas kernels for 0%

profile of v8, /device:TPU:0, one launch (start us, length us, event | category | flops | bytes accessed | tf_op | source)
XLA Modules:
  0.0 413.4 jit_solution(14937305217825392730)
XLA Ops:
  7.2 2.0 copy.43
  9.2 4.2 %all-to-all-start = ((bf16[96,4,768]{2,0,1:T(8,128)(2,1)}), bf16[96,4,768]{2,0,1:T(8,128)(2,1)S(1)}, u32[]{:S(2)}, u32[]{:S(2)}) async-start(bf16[96,4,768]{2,0,1:T(8,128)(2,1)} %bitcast.102), calls=%async_computation | async-start | bytes 1179648 | tf_op jit(solution)/shard_map/all_to_all | solution.py:60
  13.5 9.5 %all-to-all-done = bf16[96,4,768]{2,0,1:T(8,128)(2,1)S(1)} async-done(((bf16[96,4,768]{2,0,1:T(8,128)(2,1)}), bf16[96,4,768]{2,0,1:T(8,128)(2,1)S(1)}, u32[]{:S(2)}, u32[]{:S(2)}) %all-to-all-start) | async-done | bytes 589856 | tf_op jit(solution)/shard_map/all_to_all | solution.py:60
  22.9 11.9 %all_to_all.71 = bf16[4,768,96]{1,2,0:T(8,128)(2,1)S(1)} all-to-all(bf16[4,768,96]{1,2,0:T(8,128)(2,1)S(1)} %bitcast.105), channel_id=1, replica_groups=mesh['dp'=4,'fsdp'=2,'rows'=4] {'rows'}, dimensions={0} | all-to-all | bytes 1179648 | tf_op jit(solution)/shard_map/all_to_all | solution.py:61
  36.1 1.7 collective-permute-start
  41.7 9.4 %fusion.112 = (f32[4,32]{1,0:T(4,128)S(1)}, f32[1,4,32,1536]{3,2,1,0:T(8,128)S(1)}) fusion(f32[1536]{0:T(1024)S(1)} %get-tuple-element.109, f32[1536]{0:T(1024)S(1)} %get-tuple-element.110, f32[1536]{0:T(1024)S(1)} %get-tuple-element.63, f32[1536]{0:T(1024)S(1)} %get-tuple-element.64, f32[1,10,32,1536]{3,2,1,0:T(8,128)S(1)} %maximum_convert_fusion, ...), kind=kLoop, calls=%fused_computation.339 | loop fusion | flops 19267456 | bytes 8641024 | tf_op jit(solution)/shard_map/reduce_sum | solution.py:77
  53.4 73.1 %all-gather.5.cloned.1.call-done = bf16[2,1536,768]{2,1,0:T(8,128)(2,1)} async-done(((bf16[2,384,768]{2,1,0:T(8,128)(2,1)}), bf16[2,1536,768]{2,1,0:T(8,128)(2,1)}) %all-gather.5.cloned.1.call-update) | async-done | bytes 4718608 | tf_op jit(solution)/shard_map/all_gather | solution.py:62
  126.5 46.5 %all-gather.3.cloned.1.call-done = bf16[2,1024,1536]{2,1,0:T(8,128)(2,1)} async-done(((bf16[2,128,1536]{2,1,0:T(8,128)(2,1)}), bf16[2,1024,1536]{2,1,0:T(8,128)(2,1)}) %all-gather.3.cloned.1.call-update) | async-done | bytes 6291472 | tf_op jit(solution)/shard_map/all_gather | solution.py:83
  173.0 5.5 %multiply_convert_fusion = (bf16[1024,768]{1,0:T(8,128)(2,1)S(1)}, f32[1024,768]{1,0:T(8,128)S(1)}) fusion(bf16[2,1536,768]{2,1,0:T(8,128)(2,1)} %all-gather.5.cloned.1.call-done, bf16[2,1024,1536]{2,1,0:T(8,128)(2,1)} %all-gather.3.cloned.1.call-done), kind=kOutput, calls=%fused_computation.101 | convolution fusion | flops 2419851264 | bytes 10223616 | tf_op jit(solution)/shard_map/dot_general | solution.py:85
  178.8 3.1 fusion.7
  181.9 3.0 fusion.8
  184.9 3.0 fusion.9
  187.9 2.6 pad_maximum_fusion.1
  190.6 4.9 %fusion = bf16[1,1024,1536]{2,1,0:T(8,128)(2,1)S(1)} fusion(bf16[1024,768]{1,0:T(8,128)(2,1)} %copy-done.89, bf16[2,1536,768]{2,1,0:T(8,128)(2,1)} %all-gather.5.cloned.1.call-done), kind=kOutput, calls=%fused_computation.91 | convolution fusion | flops 2417491968 | bytes 7077888 | tf_op jit(solution)/shard_map/dot_general | solution.py:87
  195.5 5.1 %fusion.1 = bf16[1,1024,1536]{2,1,0:T(8,128)(2,1)S(1)} fusion(bf16[1024,768]{1,0:T(8,128)(2,1)S(1)} %copy-done.91, bf16[2,1536,768]{2,1,0:T(8,128)(2,1)} %all-gather.5.cloned.1.call-done), kind=kOutput, calls=%fused_computation.92 | convolution fusion | flops 2417491968 | bytes 7077888 | tf_op jit(solution)/shard_map/dot_general | solution.py:98
  200.6 3.2 pad_maximum_fusion
  203.9 72.1 %reduce-scatter.5.cloned.1.call-done = bf16[2,384,768]{2,1,0:T(8,128)(2,1)} async-done(((bf16[2,1536,768]{2,1,0:T(8,128)(2,1)}), bf16[2,384,768]{2,1,0:T(8,128)(2,1)}) %reduce-scatter.5.cloned.1.call-update) | async-done | bytes 1179664 | tf_op jit(solution)/shard_map/reduce_scatter | solution.py:112
  276.0 2.3 fusion.113
  278.3 4.4 %all-to-all-start.2 = ((bf16[4,96,768]{2,1,0:T(8,128)(2,1)}), bf16[4,96,768]{2,1,0:T(8,128)(2,1)}, u32[]{:S(2)}, u32[]{:S(2)}) async-start(bf16[4,96,768]{2,1,0:T(8,128)(2,1)} %bitcast.20), calls=%async_computation.4 | async-start | bytes 1179648 | tf_op jit(solution)/shard_map/all_to_all | solution.py:113
  282.7 58.8 %reduce-scatter.3.cloned.1.call-done = bf16[2,128,1536]{2,1,0:T(8,128)(2,1)} async-done(((bf16[2,1024,1536]{2,1,0:T(8,128)(2,1)}), bf16[2,128,1536]{2,1,0:T(8,128)(2,1)}) %reduce-scatter.3.cloned.1.call-update) | async-done | bytes 786448 | tf_op jit(solution)/shard_map/reduce_scatter | solution.py:101
  342.9 2.1 fusion.106
  349.6 2.4 multiply_reduce_fusion
  352.0 2.0 multiply_reduce_fusion.18
  354.4 1.4 multiply_reduce_fusion.36
  357.8 4.6 %all-to-all-start.4 = ((f32[32,2,1536]{2,1,0:T(2,128)}), f32[32,2,1536]{2,1,0:T(2,128)S(1)}, u32[]{:S(2)}, u32[]{:S(2)}) async-start(f32[32,2,1536]{2,1,0:T(2,128)} %reshape.555), calls=%async_computation.6 | async-start | bytes 786432 | tf_op jit(solution)/shard_map/all_to_all | solution.py:49
  363.3 2.2 collective-permute-start.2
  366.7 8.9 %all-to-all-done.4 = f32[32,2,1536]{2,1,0:T(2,128)S(1)} async-done(((f32[32,2,1536]{2,1,0:T(2,128)}), f32[32,2,1536]{2,1,0:T(2,128)S(1)}, u32[]{:S(2)}, u32[]{:S(2)}) %all-to-all-start.4) | async-done | bytes 393248 | tf_op jit(solution)/shard_map/all_to_all | solution.py:49
  375.6 3.5 all-to-all-start.3
  383.2 5.3 %all-to-all-done.3 = bf16[4,96,768]{2,1,0:T(8,128)(2,1)S(1)} async-done(((bf16[4,96,768]{2,1,0:T(8,128)(2,1)}), bf16[4,96,768]{2,1,0:T(8,128)(2,1)S(1)}, u32[]{:S(2)}, u32[]{:S(2)}) %all-to-all-start.3) | async-done | bytes 589856 | tf_op jit(solution)/shard_map/all_to_all | solution.py:114
  389.4 2.6 all-to-all-start.5
  392.3 7.7 %fusion.99 = bf16[1,4,32,1536]{3,2,1,0:T(8,128)(2,1)} fusion(f32[1,10,32,1536]{3,2,1,0:T(8,128)S(1)} %maximum_convert_fusion.1, f32[1536]{0:T(1024)S(1)} %copy-done.28, f32[1536]{0:T(1024)S(1)} %copy-done.30, f32[1536]{0:T(1024)S(1)} %copy-done.34, f32[1536]{0:T(1024)S(1)} %copy-done.36, f32[1536]{0:T(1024)S(1)} %copy-done.38, f32[1536]{0:T(1024)S(1)} %copy-done.40, ...), kind=kLoop, calls=%fused_computation.201 | loop fusion | flops 19660800 | bytes 8611840 | tf_op jit(solution)/shard_map/convert_element_type | solution.py:139
  403.5 1.7 all-to-all-done.5
  (286 shorter events, 27.2 us)
Async XLA Ops:
  9.2 13.8 %all-to-all-start = ((bf16[96,4,768]{2,0,1:T(8,128)(2,1)}), bf16[96,4,768]{2,0,1:T(8,128)(2,1)S(1)}, u32[]{:S(2)}, u32[]{:S(2)}) async-start(bf16[96,4,768]{2,0,1:T(8,128)(2,1)} %bitcast.102), calls=%async_computation | async-start | bytes 1179648 | tf_op jit(solution)/shard_map/all_to_all | solution.py:60
  13.4 113.1 %all-gather.5.cloned.1.call-start = ((), (), s32[]{:S(2)}) async-start(), calls=%async_computation.9 | async-start | bytes 5898240 | tf_op jit(solution)/shard_map/all_gather | solution.py:62
  13.4 22.6 %copy-start.1 = (bf16[1,4,32,1536]{3,2,1,0:T(8,128)(2,1)S(1)}, bf16[1,4,32,1536]{3,2,1,0:T(8,128)(2,1)}, u32[]{:S(2)}) copy-start(bf16[1,4,32,1536]{3,2,1,0:T(8,128)(2,1)} %param.7) | copy-start | bytes 1179652
  36.0 137.0 %all-gather.3.cloned.1.call-start = ((), (), s32[]{:S(2)}) async-start(), calls=%async_computation.8 | async-start | bytes 7077888 | tf_op jit(solution)/shard_map/all_gather | solution.py:83
  36.1 4.8 %collective-permute-start = (bf16[1,3,32,1536]{3,2,1,0:T(8,128)(2,1)S(1)}, bf16[1,3,32,1536]{3,2,1,0:T(8,128)(2,1)S(1)}, u32[]{:S(2)}, u32[]{:S(2)}) collective-permute-start(bf16[1,3,32,1536]{3,2,1,0:T(8,128)(2,1)S(1)} %get-tuple-element.121), channel_id=1, source_target_pairs={{0,1},{1,2},{2,3},{4,5},{5,6},{6,7},{8,9},{9,10},{10,11},{12,13},{... | collective-permute-start | bytes 884744 | tf_op jit(solution)/shard_map/ppermute | solution.py:25
  37.8 3.7 collective-permute-start.1
  51.8 126.7 %copy-start.81 = (f32[4,32]{1,0:T(4,128)}, f32[4,32]{1,0:T(4,128)S(1)}, u32[]{:S(2)}) copy-start(f32[4,32]{1,0:T(4,128)S(1)} %add_rsqrt_fusion) | copy-start | bytes 1540
  52.0 126.6 %copy-start.86 = (f32[128]{0:T(128)}, f32[128]{0:T(128)S(1)}, u32[]{:S(2)}) copy-start(f32[128]{0:T(128)S(1)} %rsqrt.13) | copy-start | bytes 1540
  53.2 222.8 %reduce-scatter.5.cloned.1.call-start = ((), (), s32[]{:S(2)}) async-start(), calls=%async_computation.11 | async-start | bytes 5898240 | tf_op jit(solution)/shard_map/reduce_scatter | solution.py:112
  190.5 150.9 %reduce-scatter.3.cloned.1.call-start = ((), (), s32[]{:S(2)}) async-start(), calls=%async_computation.10 | async-start | bytes 7077888 | tf_op jit(solution)/shard_map/reduce_scatter | solution.py:101
  278.3 79.5 %all-to-all-start.2 = ((bf16[4,96,768]{2,1,0:T(8,128)(2,1)}), bf16[4,96,768]{2,1,0:T(8,128)(2,1)}, u32[]{:S(2)}, u32[]{:S(2)}) async-start(bf16[4,96,768]{2,1,0:T(8,128)(2,1)} %bitcast.20), calls=%async_computation.4 | async-start | bytes 1179648 | tf_op jit(solution)/shard_map/all_to_all | solution.py:113
  356.8 22.3 %copy-start.2 = (bf16[1,4,32,1536]{3,2,1,0:T(8,128)(2,1)S(1)}, bf16[1,4,32,1536]{3,2,1,0:T(8,128)(2,1)}, u32[]{:S(2)}) copy-start(bf16[1,4,32,1536]{3,2,1,0:T(8,128)(2,1)} %param.7) | copy-start | bytes 1179652
  356.8 22.3 %copy-start.5 = (f32[1,128,1536]{2,1,0:T(8,128)S(1)}, f32[1,128,1536]{2,1,0:T(8,128)}, u32[]{:S(2)}) copy-start(f32[1,128,1536]{2,1,0:T(8,128)} %get-tuple-element.118) | copy-start | bytes 2359300
  356.8 22.3 %copy-start.76 = (f32[1536]{0:T(1024)S(1)}, f32[1536]{0:T(1024)}, u32[]{:S(2)}) copy-start(f32[1536]{0:T(1024)} %param.12) | copy-start | bytes 18436
  357.8 17.8 %all-to-all-start.4 = ((f32[32,2,1536]{2,1,0:T(2,128)}), f32[32,2,1536]{2,1,0:T(2,128)S(1)}, u32[]{:S(2)}, u32[]{:S(2)}) async-start(f32[32,2,1536]{2,1,0:T(2,128)} %reshape.555), calls=%async_computation.6 | async-start | bytes 786432 | tf_op jit(solution)/shard_map/all_to_all | solution.py:49
  363.3 16.9 %collective-permute-start.2 = (bf16[1,3,32,1536]{3,2,1,0:T(8,128)(2,1)}, bf16[1,3,32,1536]{3,2,1,0:T(8,128)(2,1)S(1)}, u32[]{:S(2)}, u32[]{:S(2)}) collective-permute-start(bf16[1,3,32,1536]{3,2,1,0:T(8,128)(2,1)} %get-tuple-element.119), channel_id=1, source_target_pairs={{0,1},{1,2},{2,3},{4,5},{5,6},{6,7},{8,9},{9,10},{10,11},{12,13},{... | collective-permute-start | bytes 884744 | tf_op jit(solution)/shard_map/ppermute | solution.py:25
  365.4 15.5 %collective-permute-start.3 = (bf16[1,3,32,1536]{3,2,1,0:T(8,128)(2,1)}, bf16[1,3,32,1536]{3,2,1,0:T(8,128)(2,1)}, u32[]{:S(2)}, u32[]{:S(2)}) collective-permute-start(bf16[1,3,32,1536]{3,2,1,0:T(8,128)(2,1)} %get-tuple-element.120), channel_id=1, source_target_pairs={{1,0},{2,1},{3,2},{5,4},{6,5},{7,6},{9,8},{10,9},{11,10},{13,12},{... | collective-permute-start | bytes 884744 | tf_op jit(solution)/shard_map/ppermute | solution.py:26
  375.6 13.0 %all-to-all-start.3 = ((bf16[4,96,768]{2,1,0:T(8,128)(2,1)}), bf16[4,96,768]{2,1,0:T(8,128)(2,1)S(1)}, u32[]{:S(2)}, u32[]{:S(2)}) async-start(bf16[4,96,768]{2,1,0:T(8,128)(2,1)} %bitcast.22), calls=%async_computation.5 | async-start | bytes 1179648 | tf_op jit(solution)/shard_map/all_to_all | solution.py:114
  380.0 12.1 %copy-start.18 = (f32[1536]{0:T(1024)S(1)}, f32[1536]{0:T(1024)}, u32[]{:S(2)}) copy-start(f32[1536]{0:T(1024)} %copy-done.17) | copy-start | bytes 18436
  380.0 12.1 %copy-start.20 = (f32[1536]{0:T(1024)S(1)}, f32[1536]{0:T(1024)}, u32[]{:S(2)}) copy-start(f32[1536]{0:T(1024)} %copy-done.19) | copy-start | bytes 18436
  380.0 12.1 %copy-start.22 = (f32[1536]{0:T(1024)S(1)}, f32[1536]{0:T(1024)}, u32[]{:S(2)}) copy-start(f32[1536]{0:T(1024)} %copy-done.21) | copy-start | bytes 18436
  380.0 12.1 %copy-start.24 = (f32[1536]{0:T(1024)S(1)}, f32[1536]{0:T(1024)}, u32[]{:S(2)}) copy-start(f32[1536]{0:T(1024)} %copy-done.23) | copy-start | bytes 18436
  380.0 12.1 %copy-start.26 = (f32[1536]{0:T(1024)S(1)}, f32[1536]{0:T(1024)}, u32[]{:S(2)}) copy-start(f32[1536]{0:T(1024)} %copy-done.25) | copy-start | bytes 18436
  380.0 12.1 %copy-start.28 = (f32[1536]{0:T(1024)S(1)}, f32[1536]{0:T(1024)}, u32[]{:S(2)}) copy-start(f32[1536]{0:T(1024)} %copy-done.27) | copy-start | bytes 18436
  380.0 12.1 %copy-start.30 = (f32[1536]{0:T(1024)S(1)}, f32[1536]{0:T(1024)}, u32[]{:S(2)}) copy-start(f32[1536]{0:T(1024)} %copy-done.29) | copy-start | bytes 18436
  380.0 12.1 %copy-start.32 = (f32[1536]{0:T(1024)S(1)}, f32[1536]{0:T(1024)}, u32[]{:S(2)}) copy-start(f32[1536]{0:T(1024)} %copy-done.31) | copy-start | bytes 18436
  380.0 12.1 %copy-start.34 = (f32[1536]{0:T(1024)S(1)}, f32[1536]{0:T(1024)}, u32[]{:S(2)}) copy-start(f32[1536]{0:T(1024)} %copy-done.33) | copy-start | bytes 18436
  380.0 12.1 %copy-start.36 = (f32[1536]{0:T(1024)S(1)}, f32[1536]{0:T(1024)}, u32[]{:S(2)}) copy-start(f32[1536]{0:T(1024)} %copy-done.35) | copy-start | bytes 18436
  380.1 12.1 %copy-start.38 = (f32[1536]{0:T(1024)S(1)}, f32[1536]{0:T(1024)}, u32[]{:S(2)}) copy-start(f32[1536]{0:T(1024)} %copy-done.37) | copy-start | bytes 18436
  380.1 12.1 %copy-start.40 = (f32[1536]{0:T(1024)S(1)}, f32[1536]{0:T(1024)}, u32[]{:S(2)}) copy-start(f32[1536]{0:T(1024)} %copy-done.39) | copy-start | bytes 18436
  380.1 12.1 %copy-start.42 = (f32[1536]{0:T(1024)S(1)}, f32[1536]{0:T(1024)}, u32[]{:S(2)}) copy-start(f32[1536]{0:T(1024)} %copy-done.41) | copy-start | bytes 18436
  389.4 15.8 %all-to-all-start.5 = ((f32[32,2,1536]{2,1,0:T(2,128)}), f32[32,2,1536]{2,1,0:T(2,128)S(1)}, u32[]{:S(2)}, u32[]{:S(2)}) async-start(f32[32,2,1536]{2,1,0:T(2,128)} %broadcast_in_dim.8), calls=%async_computation.7 | async-start | bytes 786432 | tf_op jit(solution)/shard_map/all_to_all | solution.py:51
  (73 other events, 690.5 us)
Sparse Core Ops, SparseCore 0:
  36.1 90.3 all-gather.4
  129.0 43.9 all-gather.2
  190.7 85.2 reduce-scatter.4
  279.2 62.2 reduce-scatter.2

commit v9 on v8

--- a/solution.py
+++ b/solution.py
@@ -57,9 +57,8 @@
     scenes, strip, across, width = feature_maps.shape
     cells = scenes * strip * across
     hid_axes = ("fsdp", "rows")
-    up_mine = lax.all_to_all(w_up, "rows", 1, 0, tiled=True)
-    down_mine = lax.all_to_all(w_down, "rows", 0, 1, tiled=True)
-    both = lax.all_gather(jnp.stack([up_mine, down_mine.T]), "dp", axis=1, tiled=True)
+    mine = lax.all_to_all(jnp.stack([w_up, w_down.T]), "rows", 2, 1, tiled=True)
+    both = lax.all_gather(mine, "dp", axis=1, tiled=True)
     up_loc, down_t = both[0], both[1]
     cotan = d_out.reshape(cells, width).astype(jnp.float32)
     back = (cotan * layer_scale).astype(jnp.bfloat16)
@@ -110,8 +109,6 @@
     scale_part = jnp.sum(cotan * branch, axis=0)
     grad_parts = jnp.stack([up_part, down_part_t]).astype(jnp.bfloat16)
     grad_sums = lax.psum_scatter(grad_parts, "dp", scatter_dimension=1, tiled=True)
-    grad_up = lax.all_to_all(grad_sums[0], "rows", 0, 1, tiled=True).astype(jnp.float32)
-    grad_down = lax.all_to_all(grad_sums[1], "rows", 0, 1, tiled=True).T.astype(jnp.float32)
     gain_part = jnp.sum(norm_grad * normed, axis=0)
     scaled_grad = norm_grad * norm_gain
     conv_grad = rstd * (
@@ -138,6 +135,11 @@
     kernel_part = jnp.stack(kernel_rows).reshape(KS, KS, width)
     grad_x = (d_out.astype(jnp.float32) + back_conv).astype(jnp.bfloat16)
     grad_kernel, grad_gain, grad_scale = small_sums(kernel_part, gain_part, scale_part, width)
+    grad_sums, grad_x, grad_kernel, grad_gain, grad_scale = lax.optimization_barrier(
+        (grad_sums, grad_x, grad_kernel, grad_gain, grad_scale)
+    )
+    grad_up = lax.all_to_all(grad_sums[0], "rows", 0, 1, tiled=True).astype(jnp.float32)
+    grad_down = lax.all_to_all(grad_sums[1], "rows", 0, 1, tiled=True).T.astype(jnp.float32)
     return (result, grad_x, grad_up, grad_down, grad_kernel, grad_gain, grad_scale)
 
 

time: 414 us -> 392 us (0.947)
  waiting for transfers between devices: 277 us -> 232 us
  blocking collectives: 11.9 us -> 36.2 us
  starting transfers between devices: 26 us -> 20.8 us
    reduce_scatter x1, waiting for transfers between devices: 72.1 us -> 24.5 us  [body(): lax.psum_scatter(grad_parts, 'dp', scatter_dimension=1, tiled=True)]
    all_to_all x1 -> x2, blocking collectives: 11.9 us -> 36.2 us  [the longest x1 24.1 us: body(): mine = lax.all_to_all(jnp.stack([w_up, w_down.T]), 'rows', 2, 1, tiled=True)]
    all_to_all x2 -> x0, waiting for transfers between devices: 14.8 us -> none  [the longest x1 9.49 us: body(): up_mine = lax.all_to_all(w_up, 'rows', 1, 0, tiled=True)]
    all_to_all x1, waiting for transfers between devices: 1.74 us -> 15.3 us  [small_sums(): lax.all_to_all(spread, every, 0, 0, tiled=True)]
    reduce_scatter x1, waiting for transfers between devices: 58.8 us -> 49.1 us  [body(): lax.psum_scatter(jnp.stack([mlp_terms, norm_terms]).astype(jnp.bfloat16),...]
    all_to_all x2 -> x0, starting transfers between devices: 7.71 us -> none  [the longest x1 4.24 us: body(): up_mine = lax.all_to_all(w_up, 'rows', 1, 0, tiled=True)]
    all_to_all x1, waiting for transfers between devices: 0.01 us -> 7.41 us  [body(): lax.all_to_all(grad_sums[0], 'rows', 0, 1, tiled=True).astype(jnp.float32)]
    all_to_all x1, waiting for transfers between devices: 8.85 us -> 13.2 us  [small_sums(): lax.all_to_all(packed.reshape(devices, per, width), every, 0, 0, tiled=True)]
  transfers between devices with their start and end apart: 13 -> 11, of which waited for: 9 -> 9; matrix products, arithmetic and copies ran while one was open for 14% -> 14% of each run, Pallas kernels for 0% -> 0%
where the time goes in v9:
time: 392 us; the launch traced here: 389 us
  waiting for transfers between devices  232 us (59%)
  other arithmetic  38 us (10%)
  blocking collectives  36.2 us (9%)
  matrix products  24.2 us (6%)
  local copies, waits for them, and re-layouts  21.4 us (5%)
  starting transfers between devices  20.8 us (5%)
  between operations  15.9 us (4%)
    all_gather x1, waiting for transfers between devices, body(): both = lax.all_gather(mine, 'dp', axis=1, tiled=True)  72.4 us
    reduce_scatter x1, waiting for transfers between devices, body(): lax.psum_scatter(jnp.stack([mlp_terms, norm_terms]).astype(jnp.bfloat16),...  49.1 us
    all_gather x1, waiting for transfers between devices, body(): lax.all_gather(jnp.stack([scaled, back]), hid_axes, axis=1, tiled=True)  46.5 us
    reduce_scatter x1, waiting for transfers between devices, body(): lax.psum_scatter(grad_parts, 'dp', scatter_dimension=1, tiled=True)  24.5 us
    all_to_all x1, blocking collectives, body(): mine = lax.all_to_all(jnp.stack([w_up, w_down.T]), 'rows', 2, 1, tiled=True)  24.1 us
    all_to_all x1, waiting for transfers between devices, small_sums(): lax.all_to_all(spread, every, 0, 0, tiled=True)  15.3 us
    all_to_all x1, waiting for transfers between devices, small_sums(): lax.all_to_all(packed.reshape(devices, per, width), every, 0, 0, tiled=True)  13.2 us
    all_to_all x1, blocking collectives, body(): lax.all_to_all(grad_sums[1], 'rows', 0, 1, tiled=True).T.astype(jnp.float32)  12.1 us
  transfers between devices with their start and end apart: 11, of which 9 were waited for; matrix products, arithmetic and copies ran while one was open for 14% of the time, Pallas kernels for 0%

profile of v9, /device:TPU:0, one launch (start us, length us, event | category | flops | bytes accessed | tf_op | source)
XLA Modules:
  0.0 388.8 jit_solution(14751080558201865920)
XLA Ops:
  8.6 2.0 copy.37
  10.6 24.1 %all_to_all.54 = bf16[2,96,3072]{1,0,2:T(2,128)(2,1)S(1)} all-to-all(bf16[2,96,3072]{1,0,2:T(2,128)(2,1)S(1)} %copy.37), channel_id=1, replica_groups=mesh['dp'=4,'fsdp'=2,'rows'=4] {'rows'}, dimensions={2} | all-to-all | bytes 2359296 | tf_op jit(solution)/shard_map/all_to_all | solution.py:60
  34.7 1.5 copy.43
  43.1 9.5 %fusion.112 = (f32[4,32]{1,0:T(4,128)S(1)}, f32[1,4,32,1536]{3,2,1,0:T(8,128)S(1)}) fusion(f32[1536]{0:T(1024)S(1)} %get-tuple-element.119, f32[1536]{0:T(1024)S(1)} %get-tuple-element.120, f32[1536]{0:T(1024)S(1)} %get-tuple-element.73, f32[1536]{0:T(1024)S(1)} %get-tuple-element.74, f32[1,10,32,1536]{3,2,1,0:T(8,128)S(1)} %maximum_convert_fusion, ...), kind=kLoop, calls=%fused_computation.337 | loop fusion | flops 19267456 | bytes 8641024 | tf_op jit(solution)/shard_map/reduce_sum | solution.py:76
  54.9 72.4 %all-gather.5.cloned.1.call-done = bf16[2,1536,768]{2,1,0:T(8,128)(2,1)} async-done(((bf16[2,384,768]{2,1,0:T(8,128)(2,1)}), bf16[2,1536,768]{2,1,0:T(8,128)(2,1)}) %all-gather.5.cloned.1.call-update) | async-done | bytes 4718608 | tf_op jit(solution)/shard_map/all_gather | solution.py:61
  127.3 46.5 %all-gather.3.cloned.1.call-done = bf16[2,1024,1536]{2,1,0:T(8,128)(2,1)} async-done(((bf16[2,128,1536]{2,1,0:T(8,128)(2,1)}), bf16[2,1024,1536]{2,1,0:T(8,128)(2,1)}) %all-gather.3.cloned.1.call-update) | async-done | bytes 6291472 | tf_op jit(solution)/shard_map/all_gather | solution.py:82
  173.8 5.5 %multiply_convert_fusion = (bf16[1024,768]{1,0:T(8,128)(2,1)S(1)}, f32[1024,768]{1,0:T(8,128)S(1)}) fusion(bf16[2,1536,768]{2,1,0:T(8,128)(2,1)} %all-gather.5.cloned.1.call-done, bf16[2,1024,1536]{2,1,0:T(8,128)(2,1)} %all-gather.3.cloned.1.call-done), kind=kOutput, calls=%fused_computation.101 | convolution fusion | flops 2419851264 | bytes 10223616 | tf_op jit(solution)/shard_map/dot_general | solution.py:84
  179.6 3.1 fusion.7
  182.7 2.9 fusion
  185.6 2.9 fusion.1
  188.5 3.2 pad_maximum_fusion
  192.0 5.1 %fusion.8 = bf16[1,1536,768]{2,1,0:T(8,128)(2,1)S(1)} fusion(bf16[1024,768]{1,0:T(8,128)(2,1)} %copy-done.102, bf16[2,1024,1536]{2,1,0:T(8,128)(2,1)} %all-gather.3.cloned.1.call-done), kind=kOutput, calls=%fused_computation.103 | convolution fusion | flops 2417098752 | bytes 7077888 | tf_op jit(solution)/shard_map/dot_general | solution.py:94
  197.2 4.6 %fusion.9 = bf16[1,1536,768]{2,1,0:T(8,128)(2,1)S(1)} fusion(bf16[1024,768]{1,0:T(8,128)(2,1)S(1)} %copy-done.101, bf16[2,1024,1536]{2,1,0:T(8,128)(2,1)} %all-gather.3.cloned.1.call-done), kind=kOutput, calls=%fused_computation.104 | convolution fusion | flops 2417098752 | bytes 7077888 | tf_op jit(solution)/shard_map/dot_general | solution.py:89
  201.8 2.8 pad_maximum_fusion.1
  204.6 49.1 %reduce-scatter.3.cloned.1.call-done = bf16[2,128,1536]{2,1,0:T(8,128)(2,1)} async-done(((bf16[2,1024,1536]{2,1,0:T(8,128)(2,1)}), bf16[2,128,1536]{2,1,0:T(8,128)(2,1)}) %reduce-scatter.3.cloned.1.call-update) | async-done | bytes 786448 | tf_op jit(solution)/shard_map/reduce_scatter | solution.py:100
  255.1 2.1 fusion.106
  264.4 2.4 multiply_reduce_fusion
  267.0 2.0 multiply_reduce_fusion.18
  269.1 1.4 multiply_reduce_fusion.36
  272.5 4.6 %all-to-all-start.1 = ((f32[32,2,1536]{2,1,0:T(2,128)}), f32[32,2,1536]{2,1,0:T(2,128)S(1)}, u32[]{:S(2)}, u32[]{:S(2)}) async-start(f32[32,2,1536]{2,1,0:T(2,128)} %reshape.548), calls=%async_computation.3 | async-start | bytes 786432 | tf_op jit(solution)/shard_map/all_to_all | solution.py:49
  277.5 2.3 collective-permute-start.2
  279.8 1.6 collective-permute-start.3
  281.4 3.0 collective-permute-done.3
  284.6 13.2 %all-to-all-done.1 = f32[32,2,1536]{2,1,0:T(2,128)S(1)} async-done(((f32[32,2,1536]{2,1,0:T(2,128)}), f32[32,2,1536]{2,1,0:T(2,128)S(1)}, u32[]{:S(2)}, u32[]{:S(2)}) %all-to-all-start.1) | async-done | bytes 393248 | tf_op jit(solution)/shard_map/all_to_all | solution.py:49
  298.8 5.6 %all-to-all-start.2 = ((f32[32,2,1536]{2,1,0:T(2,128)}), f32[32,2,1536]{2,1,0:T(2,128)S(1)}, u32[]{:S(2)}, u32[]{:S(2)}) async-start(f32[32,2,1536]{2,1,0:T(2,128)} %broadcast_in_dim.8), calls=%async_computation.4 | async-start | bytes 786432 | tf_op jit(solution)/shard_map/all_to_all | solution.py:51
  304.8 7.4 %fusion.99 = bf16[1,4,32,1536]{3,2,1,0:T(8,128)(2,1)} fusion(f32[1,10,32,1536]{3,2,1,0:T(8,128)S(1)} %maximum_convert_fusion.1, f32[1536]{0:T(1024)S(1)} %copy-done.25, f32[1536]{0:T(1024)S(1)} %copy-done.27, f32[1536]{0:T(1024)S(1)} %copy-done.31, f32[1536]{0:T(1024)S(1)} %copy-done.33, f32[1536]{0:T(1024)S(1)} %copy-done.35, f32[1536]{0:T(1024)S(1)} %copy-done.37, ...), kind=kLoop, calls=%fused_computation.201 | loop fusion | flops 19660800 | bytes 8640512 | tf_op jit(solution)/shard_map/convert_element_type | solution.py:136
  312.2 15.3 %all-to-all-done.2 = f32[32,2,1536]{2,1,0:T(2,128)S(1)} async-done(((f32[32,2,1536]{2,1,0:T(2,128)}), f32[32,2,1536]{2,1,0:T(2,128)S(1)}, u32[]{:S(2)}, u32[]{:S(2)}) %all-to-all-start.2) | async-done | bytes 393248 | tf_op jit(solution)/shard_map/all_to_all | solution.py:51
  329.3 24.5 %reduce-scatter.5.cloned.1.call-done = bf16[2,384,768]{2,1,0:T(8,128)(2,1)} async-done(((bf16[2,1536,768]{2,1,0:T(8,128)(2,1)}), bf16[2,384,768]{2,1,0:T(8,128)(2,1)}) %reduce-scatter.5.cloned.1.call-update) | async-done | bytes 1179664 | tf_op jit(solution)/shard_map/reduce_scatter | solution.py:111
  353.9 2.1 fusion.113
  356.0 12.1 %all_to_all.55 = bf16[4,96,768]{2,1,0:T(8,128)(2,1)S(1)} all-to-all(bf16[4,96,768]{2,1,0:T(8,128)(2,1)S(1)} %bitcast.97), channel_id=1, replica_groups=mesh['dp'=4,'fsdp'=2,'rows'=4] {'rows'}, dimensions={0} | all-to-all | bytes 1179648 | tf_op jit(solution)/shard_map/all_to_all | solution.py:142
  368.0 3.5 all-to-all-start.3
  373.6 7.4 %all-to-all-done.3 = bf16[4,96,768]{2,1,0:T(8,128)(2,1)S(1)} async-done(((bf16[4,96,768]{2,1,0:T(8,128)(2,1)}), bf16[4,96,768]{2,1,0:T(8,128)(2,1)S(1)}, u32[]{:S(2)}, u32[]{:S(2)}) %all-to-all-start.3) | async-done | bytes 589856 | tf_op jit(solution)/shard_map/all_to_all | solution.py:141
  (306 shorter events, 27.2 us)
Async XLA Ops:
  7.2 120.1 %all-gather.5.cloned.1.call-start = ((), (), s32[]{:S(2)}) async-start(), calls=%async_computation.8 | async-start | bytes 5898240 | tf_op jit(solution)/shard_map/all_gather | solution.py:61
  37.4 136.4 %all-gather.3.cloned.1.call-start = ((), (), s32[]{:S(2)}) async-start(), calls=%async_computation.7 | async-start | bytes 7077888 | tf_op jit(solution)/shard_map/all_gather | solution.py:82
  37.5 4.5 %collective-permute-start = (bf16[1,3,32,1536]{3,2,1,0:T(8,128)(2,1)S(1)}, bf16[1,3,32,1536]{3,2,1,0:T(8,128)(2,1)S(1)}, u32[]{:S(2)}, u32[]{:S(2)}) collective-permute-start(bf16[1,3,32,1536]{3,2,1,0:T(8,128)(2,1)S(1)} %get-tuple-element.131), channel_id=1, source_target_pairs={{0,1},{1,2},{2,3},{4,5},{5,6},{6,7},{8,9},{9,10},{10,11},{12,13},{... | collective-permute-start | bytes 884744 | tf_op jit(solution)/shard_map/ppermute | solution.py:25
  38.9 4.0 %collective-permute-start.1 = (bf16[1,3,32,1536]{3,2,1,0:T(8,128)(2,1)S(1)}, bf16[1,3,32,1536]{3,2,1,0:T(8,128)(2,1)S(1)}, u32[]{:S(2)}, u32[]{:S(2)}) collective-permute-start(bf16[1,3,32,1536]{3,2,1,0:T(8,128)(2,1)S(1)} %get-tuple-element.132), channel_id=1, source_target_pairs={{1,0},{2,1},{3,2},{5,4},{6,5},{7,6},{9,8},{10,9},{11,10},{13,12},{... | collective-permute-start | bytes 884744 | tf_op jit(solution)/shard_map/ppermute | solution.py:26
  53.0 126.2 %copy-start.96 = (f32[128]{0:T(128)}, f32[128]{0:T(128)S(1)}, u32[]{:S(2)}) copy-start(f32[128]{0:T(128)S(1)} %div.19) | copy-start | bytes 1540
  53.3 126.0 %copy-start.92 = (f32[4,32]{1,0:T(4,128)}, f32[4,32]{1,0:T(4,128)S(1)}, u32[]{:S(2)}) copy-start(f32[4,32]{1,0:T(4,128)S(1)} %add_rsqrt_fusion) | copy-start | bytes 1540
  53.4 125.9 %copy-start.97 = (f32[128]{0:T(128)}, f32[128]{0:T(128)S(1)}, u32[]{:S(2)}) copy-start(f32[128]{0:T(128)S(1)} %rsqrt.13) | copy-start | bytes 1540
  54.6 199.0 %reduce-scatter.3.cloned.1.call-start = ((), (), s32[]{:S(2)}) async-start(), calls=%async_computation.9 | async-start | bytes 7077888 | tf_op jit(solution)/shard_map/reduce_scatter | solution.py:100
  191.8 162.1 %reduce-scatter.5.cloned.1.call-start = ((), (), s32[]{:S(2)}) async-start(), calls=%async_computation.10 | async-start | bytes 5898240 | tf_op jit(solution)/shard_map/reduce_scatter | solution.py:111
  272.5 25.3 %all-to-all-start.1 = ((f32[32,2,1536]{2,1,0:T(2,128)}), f32[32,2,1536]{2,1,0:T(2,128)S(1)}, u32[]{:S(2)}, u32[]{:S(2)}) async-start(f32[32,2,1536]{2,1,0:T(2,128)} %reshape.548), calls=%async_computation.3 | async-start | bytes 786432 | tf_op jit(solution)/shard_map/all_to_all | solution.py:49
  277.1 27.3 %copy-start.4 = (bf16[1,4,32,1536]{3,2,1,0:T(8,128)(2,1)S(1)}, bf16[1,4,32,1536]{3,2,1,0:T(8,128)(2,1)}, u32[]{:S(2)}) copy-start(bf16[1,4,32,1536]{3,2,1,0:T(8,128)(2,1)} %param.13) | copy-start | bytes 1179652
  277.1 27.3 %copy-start.9 = (f32[1536]{0:T(1024)S(1)}, f32[1536]{0:T(1024)}, u32[]{:S(2)}) copy-start(f32[1536]{0:T(1024)} %copy-done.8) | copy-start | bytes 18436
  277.1 27.3 %copy-start.11 = (f32[1536]{0:T(1024)S(1)}, f32[1536]{0:T(1024)}, u32[]{:S(2)}) copy-start(f32[1536]{0:T(1024)} %copy-done.10) | copy-start | bytes 18436
  277.1 27.3 %copy-start.13 = (f32[1536]{0:T(1024)S(1)}, f32[1536]{0:T(1024)}, u32[]{:S(2)}) copy-start(f32[1536]{0:T(1024)} %copy-done.12) | copy-start | bytes 18436
  277.2 27.3 %copy-start.15 = (f32[1536]{0:T(1024)S(1)}, f32[1536]{0:T(1024)}, u32[]{:S(2)}) copy-start(f32[1536]{0:T(1024)} %copy-done.14) | copy-start | bytes 18436
  277.2 27.3 %copy-start.17 = (f32[1536]{0:T(1024)S(1)}, f32[1536]{0:T(1024)}, u32[]{:S(2)}) copy-start(f32[1536]{0:T(1024)} %copy-done.16) | copy-start | bytes 18436
  277.2 27.3 %copy-start.19 = (f32[1536]{0:T(1024)S(1)}, f32[1536]{0:T(1024)}, u32[]{:S(2)}) copy-start(f32[1536]{0:T(1024)} %copy-done.18) | copy-start | bytes 18436
  277.2 27.3 %copy-start.21 = (f32[1536]{0:T(1024)S(1)}, f32[1536]{0:T(1024)}, u32[]{:S(2)}) copy-start(f32[1536]{0:T(1024)} %copy-done.20) | copy-start | bytes 18436
  277.2 27.3 %copy-start.23 = (f32[1536]{0:T(1024)S(1)}, f32[1536]{0:T(1024)}, u32[]{:S(2)}) copy-start(f32[1536]{0:T(1024)} %copy-done.22) | copy-start | bytes 18436
  277.2 27.3 %copy-start.25 = (f32[1536]{0:T(1024)S(1)}, f32[1536]{0:T(1024)}, u32[]{:S(2)}) copy-start(f32[1536]{0:T(1024)} %copy-done.24) | copy-start | bytes 18436
  277.2 27.3 %copy-start.27 = (f32[1536]{0:T(1024)S(1)}, f32[1536]{0:T(1024)}, u32[]{:S(2)}) copy-start(f32[1536]{0:T(1024)} %copy-done.26) | copy-start | bytes 18436
  277.2 27.3 %copy-start.29 = (f32[1536]{0:T(1024)S(1)}, f32[1536]{0:T(1024)}, u32[]{:S(2)}) copy-start(f32[1536]{0:T(1024)} %copy-done.28) | copy-start | bytes 18436
  277.2 27.3 %copy-start.31 = (f32[1536]{0:T(1024)S(1)}, f32[1536]{0:T(1024)}, u32[]{:S(2)}) copy-start(f32[1536]{0:T(1024)} %copy-done.30) | copy-start | bytes 18436
  277.2 27.3 %copy-start.33 = (f32[1536]{0:T(1024)S(1)}, f32[1536]{0:T(1024)}, u32[]{:S(2)}) copy-start(f32[1536]{0:T(1024)} %copy-done.32) | copy-start | bytes 18436
  277.3 27.3 %copy-start.35 = (f32[1536]{0:T(1024)S(1)}, f32[1536]{0:T(1024)}, u32[]{:S(2)}) copy-start(f32[1536]{0:T(1024)} %copy-done.34) | copy-start | bytes 18436
  277.5 3.9 collective-permute-start.2
  279.8 4.6 %collective-permute-start.3 = (bf16[1,3,32,1536]{3,2,1,0:T(8,128)(2,1)S(1)}, bf16[1,3,32,1536]{3,2,1,0:T(8,128)(2,1)S(1)}, u32[]{:S(2)}, u32[]{:S(2)}) collective-permute-start(bf16[1,3,32,1536]{3,2,1,0:T(8,128)(2,1)S(1)} %get-tuple-element.130), channel_id=1, source_target_pairs={{1,0},{2,1},{3,2},{5,4},{6,5},{7,6},{9,8},{10,9},{11,10},{13,12},{... | collective-permute-start | bytes 884744 | tf_op jit(solution)/shard_map/ppermute | solution.py:26
  298.8 28.8 %all-to-all-start.2 = ((f32[32,2,1536]{2,1,0:T(2,128)}), f32[32,2,1536]{2,1,0:T(2,128)S(1)}, u32[]{:S(2)}, u32[]{:S(2)}) async-start(f32[32,2,1536]{2,1,0:T(2,128)} %broadcast_in_dim.8), calls=%async_computation.4 | async-start | bytes 786432 | tf_op jit(solution)/shard_map/all_to_all | solution.py:51
  328.7 42.9 %copy-start.2 = (bf16[1,4,32,1536]{3,2,1,0:T(8,128)(2,1)S(1)}, bf16[1,4,32,1536]{3,2,1,0:T(8,128)(2,1)}, u32[]{:S(2)}) copy-start(bf16[1,4,32,1536]{3,2,1,0:T(8,128)(2,1)} %param.7) | copy-start | bytes 1179652
  328.7 42.9 %copy-start.5 = (f32[1,128,1536]{2,1,0:T(8,128)S(1)}, f32[1,128,1536]{2,1,0:T(8,128)}, u32[]{:S(2)}) copy-start(f32[1,128,1536]{2,1,0:T(8,128)} %get-tuple-element.128) | copy-start | bytes 2359300
  328.7 42.9 %copy-start.87 = (f32[1536]{0:T(1024)S(1)}, f32[1536]{0:T(1024)}, u32[]{:S(2)}) copy-start(f32[1536]{0:T(1024)} %param.12) | copy-start | bytes 18436
  368.0 13.0 %all-to-all-start.3 = ((bf16[4,96,768]{2,1,0:T(8,128)(2,1)}), bf16[4,96,768]{2,1,0:T(8,128)(2,1)S(1)}, u32[]{:S(2)}, u32[]{:S(2)}) async-start(bf16[4,96,768]{2,1,0:T(8,128)(2,1)} %bitcast.22), calls=%async_computation.5 | async-start | bytes 1179648 | tf_op jit(solution)/shard_map/all_to_all | solution.py:141
  (82 other events, 1222.0 us)
Sparse Core Ops, SparseCore 0:
  37.5 89.6 all-gather.4
  129.7 43.9 all-gather.2
  191.9 61.7 reduce-scatter.2
  255.9 97.8 reduce-scatter.4

commit v10 on v9

--- a/solution.py
+++ b/solution.py
@@ -57,8 +57,14 @@
     scenes, strip, across, width = feature_maps.shape
     cells = scenes * strip * across
     hid_axes = ("fsdp", "rows")
-    mine = lax.all_to_all(jnp.stack([w_up, w_down.T]), "rows", 2, 1, tiled=True)
-    both = lax.all_gather(mine, "dp", axis=1, tiled=True)
+    dp_size, row_size = lax.axis_size("dp"), lax.axis_size("rows")
+    block_c, hid_f = w_up.shape
+    sub = hid_f // row_size
+    pieces = jnp.stack([w_up, w_down.T]).reshape(2, block_c, row_size, sub).transpose(0, 2, 1, 3)
+    pieces = jnp.broadcast_to(pieces[:, None], (2, dp_size, row_size, block_c, sub))
+    pieces = pieces.reshape(2, dp_size * row_size, block_c, sub)
+    both = lax.all_to_all(pieces, ("dp", "rows"), 1, 1, tiled=True)
+    both = both.reshape(2, dp_size * row_size * block_c, sub)
     up_loc, down_t = both[0], both[1]
     cotan = d_out.reshape(cells, width).astype(jnp.float32)
     back = (cotan * layer_scale).astype(jnp.bfloat16)
@@ -138,8 +144,8 @@
     grad_sums, grad_x, grad_kernel, grad_gain, grad_scale = lax.optimization_barrier(
         (grad_sums, grad_x, grad_kernel, grad_gain, grad_scale)
     )
-    grad_up = lax.all_to_all(grad_sums[0], "rows", 0, 1, tiled=True).astype(jnp.float32)
-    grad_down = lax.all_to_all(grad_sums[1], "rows", 0, 1, tiled=True).T.astype(jnp.float32)
+    grad_sums = lax.all_to_all(grad_sums, "rows", 1, 2, tiled=True).astype(jnp.float32)
+    grad_up, grad_down = grad_sums[0], grad_sums[1].T
     return (result, grad_x, grad_up, grad_down, grad_kernel, grad_gain, grad_scale)
 
 

time: 392 us -> 375 us (0.957)
  waiting for transfers between devices: 232 us -> 121 us
  blocking collectives: 36.2 us -> 113 us
  local copies, waits for them, and re-layouts: 21.4 us -> 35.3 us
    all_to_all x2 -> x1, blocking collectives: 36.2 us -> 113 us  [body(): both = lax.all_to_all(pieces, ('dp', 'rows'), 1, 1, tiled=True)]
    all_gather x1 -> x0, waiting for transfers between devices: 72.4 us -> none  [body(): both = lax.all_gather(mine, 'dp', axis=1, tiled=True)]
    all_gather x1, waiting for transfers between devices: 46.5 us -> 0.01 us  [body(): lax.all_gather(jnp.stack([scaled, back]), hid_axes, axis=1, tiled=True)]
    all_to_all x1, waiting for transfers between devices: 7.41 us -> 15 us  [body(): lax.all_to_all(grad_sums, 'rows', 1, 2, tiled=True).astype(jnp.float32)]
    slice x3, local copies, waits for them, and re-layouts: 1.41 us -> 5.44 us  [body(): dw_kernel[row_off, col_off]]
  transfers between devices with their start and end apart: 11 -> 10, of which waited for: 9 -> 6; matrix products, arithmetic and copies ran while one was open for 14% -> 15% of each run, Pallas kernels for 0% -> 0%
where the time goes in v10:
time: 375 us; the launch traced here: 371 us
  waiting for transfers between devices  121 us (32%)
  blocking collectives  113 us (30%)
  other arithmetic  40.1 us (11%)
  local copies, waits for them, and re-layouts  35.3 us (9%)
  matrix products  24.7 us (7%)
  starting transfers between devices  21.3 us (6%)
  between operations  15.8 us (4%)
    all_to_all x1, blocking collectives, body(): both = lax.all_to_all(pieces, ('dp', 'rows'), 1, 1, tiled=True)  113 us
    reduce_scatter x1, waiting for transfers between devices, body(): lax.psum_scatter(jnp.stack([mlp_terms, norm_terms]).astype(jnp.bfloat16),...  49.5 us
    reduce_scatter x1, waiting for transfers between devices, body(): lax.psum_scatter(grad_parts, 'dp', scatter_dimension=1, tiled=True)  24.6 us
    all_to_all x1, waiting for transfers between devices, small_sums(): lax.all_to_all(spread, every, 0, 0, tiled=True)  15.3 us
    all_to_all x1, waiting for transfers between devices, body(): lax.all_to_all(grad_sums, 'rows', 1, 2, tiled=True).astype(jnp.float32)  15 us
    all_to_all x1, waiting for transfers between devices, small_sums(): lax.all_to_all(packed.reshape(devices, per, width), every, 0, 0, tiled=True)  13.3 us
    reduce_sum x1, other arithmetic, body(): average = jnp.mean(flat, axis=-1, keepdims=True)  9.44 us
  transfers between devices with their start and end apart: 10, of which 6 were waited for; matrix products, arithmetic and copies ran while one was open for 15% of the time, Pallas kernels for 0%

profile of v10, /device:TPU:0, one launch (start us, length us, event | category | flops | bytes accessed | tf_op | source)
XLA Modules:
  0.0 370.7 jit_solution(10288674371595409943)
XLA Ops:
  8.3 2.4 collective-permute-start
  15.4 2.3 slice_reduce_fusion.49
  19.0 9.4 %fusion.112 = (f32[4,32]{1,0:T(4,128)S(1)}, f32[1,4,32,1536]{3,2,1,0:T(8,128)S(1)}) fusion(f32[1536]{0:T(1024)S(1)} %get-tuple-element.119, f32[1536]{0:T(1024)S(1)} %get-tuple-element.120, f32[1536]{0:T(1024)S(1)} %get-tuple-element.73, f32[1536]{0:T(1024)S(1)} %get-tuple-element.74, f32[1,10,32,1536]{3,2,1,0:T(8,128)S(1)} %maximum_convert_fusion, ...), kind=kLoop, calls=%fused_computation.334 | loop fusion | flops 19267456 | bytes 8641024 | tf_op jit(solution)/shard_map/reduce_sum | solution.py:82
  30.6 1.8 stack.186
  32.4 2.5 stack.187
  34.8 1.9 maximum_bitcast_fusion
  37.5 112.6 %all_to_all.24 = bf16[2,16,96,768]{3,2,0,1:T(8,128)(2,1)S(1)} all-to-all(bf16[2,16,96,768]{3,2,0,1:T(8,128)(2,1)S(1)} %bitcast.83), channel_id=1, replica_groups=mesh['dp'=4,'fsdp'=2,'rows'=4] {'dp','rows'}, dimensions={1} | all-to-all | bytes 9437184 | tf_op jit(solution)/shard_map/all_to_all | solution.py:66
  150.1 2.4 fusion.113
  152.5 5.2 %multiply_convert_fusion = (bf16[1024,768]{1,0:T(8,128)(2,1)S(1)}, f32[1024,768]{1,0:T(8,128)S(1)}) fusion(bf16[1536,768]{1,0:T(8,128)(2,1)} %bitcast.89, bf16[2,1024,1536]{2,1,0:T(8,128)(2,1)} %all-gather.2.cloned.1.call-done), kind=kOutput, calls=%fused_computation.101 | convolution fusion | flops 2419851264 | bytes 10223616 | tf_op jit(solution)/shard_map/dot_general | solution.py:90
  157.8 2.9 fusion
  161.1 3.5 fusion.7
  165.7 2.9 fusion.1
  168.6 3.2 pad_maximum_fusion
  171.9 5.1 %fusion.9 = bf16[1,1536,768]{2,1,0:T(8,128)(2,1)S(1)} fusion(bf16[1024,768]{1,0:T(8,128)(2,1)} %copy-done.99, bf16[2,1024,1536]{2,1,0:T(8,128)(2,1)} %all-gather.2.cloned.1.call-done), kind=kOutput, calls=%fused_computation.104 | convolution fusion | flops 2417098752 | bytes 7077888 | tf_op jit(solution)/shard_map/dot_general | solution.py:95
  177.0 5.1 %fusion.8 = bf16[1,1536,768]{2,1,0:T(8,128)(2,1)S(1)} fusion(bf16[1024,768]{1,0:T(8,128)(2,1)S(1)} %copy-done.101, bf16[2,1024,1536]{2,1,0:T(8,128)(2,1)} %all-gather.2.cloned.1.call-done), kind=kOutput, calls=%fused_computation.103 | convolution fusion | flops 2417098752 | bytes 7077888 | tf_op jit(solution)/shard_map/dot_general | solution.py:100
  182.1 2.7 pad_maximum_fusion.1
  184.8 49.5 %reduce-scatter.3.cloned.1.call-done = bf16[2,128,1536]{2,1,0:T(8,128)(2,1)} async-done(((bf16[2,1024,1536]{2,1,0:T(8,128)(2,1)}), bf16[2,128,1536]{2,1,0:T(8,128)(2,1)}) %reduce-scatter.3.cloned.1.call-update) | async-done | bytes 786448 | tf_op jit(solution)/shard_map/reduce_scatter | solution.py:106
  235.8 2.1 fusion.106
  245.1 2.4 multiply_reduce_fusion
  247.7 2.0 multiply_reduce_fusion.18
  253.2 4.6 %all-to-all-start.1 = ((f32[32,2,1536]{2,1,0:T(2,128)}), f32[32,2,1536]{2,1,0:T(2,128)S(1)}, u32[]{:S(2)}, u32[]{:S(2)}) async-start(f32[32,2,1536]{2,1,0:T(2,128)} %reshape.558), calls=%async_computation.3 | async-start | bytes 786432 | tf_op jit(solution)/shard_map/all_to_all | solution.py:49
  258.2 2.3 collective-permute-start.2
  262.1 3.1 collective-permute-done.3
  265.3 13.3 %all-to-all-done.1 = f32[32,2,1536]{2,1,0:T(2,128)S(1)} async-done(((f32[32,2,1536]{2,1,0:T(2,128)}), f32[32,2,1536]{2,1,0:T(2,128)S(1)}, u32[]{:S(2)}, u32[]{:S(2)}) %all-to-all-start.1) | async-done | bytes 393248 | tf_op jit(solution)/shard_map/all_to_all | solution.py:49
  279.6 5.6 %all-to-all-start.2 = ((f32[32,2,1536]{2,1,0:T(2,128)}), f32[32,2,1536]{2,1,0:T(2,128)S(1)}, u32[]{:S(2)}, u32[]{:S(2)}) async-start(f32[32,2,1536]{2,1,0:T(2,128)} %broadcast_in_dim.11), calls=%async_computation.4 | async-start | bytes 786432 | tf_op jit(solution)/shard_map/all_to_all | solution.py:51
  285.6 7.4 %fusion.99 = bf16[1,4,32,1536]{3,2,1,0:T(8,128)(2,1)} fusion(f32[1,10,32,1536]{3,2,1,0:T(8,128)S(1)} %maximum_convert_fusion.1, f32[1536]{0:T(1024)S(1)} %copy-done.25, f32[1536]{0:T(1024)S(1)} %copy-done.27, f32[1536]{0:T(1024)S(1)} %copy-done.31, f32[1536]{0:T(1024)S(1)} %copy-done.33, f32[1536]{0:T(1024)S(1)} %copy-done.35, f32[1536]{0:T(1024)S(1)} %copy-done.37, ...), kind=kLoop, calls=%fused_computation.198 | loop fusion | flops 19660800 | bytes 8640512 | tf_op jit(solution)/shard_map/convert_element_type | solution.py:142
  293.0 15.3 %all-to-all-done.2 = f32[32,2,1536]{2,1,0:T(2,128)S(1)} async-done(((f32[32,2,1536]{2,1,0:T(2,128)}), f32[32,2,1536]{2,1,0:T(2,128)S(1)}, u32[]{:S(2)}, u32[]{:S(2)}) %all-to-all-start.2) | async-done | bytes 393248 | tf_op jit(solution)/shard_map/all_to_all | solution.py:51
  310.1 24.6 %reduce-scatter.5.cloned.1.call-done = bf16[2,384,768]{2,1,0:T(8,128)(2,1)} async-done(((bf16[2,1536,768]{2,1,0:T(8,128)(2,1)}), bf16[2,384,768]{2,1,0:T(8,128)(2,1)}) %reduce-scatter.5.cloned.1.call-update) | async-done | bytes 1179664 | tf_op jit(solution)/shard_map/reduce_scatter | solution.py:117
  334.7 3.5 copy.27
  338.2 3.5 all-to-all-start.3
  342.6 15.0 %all-to-all-done.3 = bf16[2,384,768]{2,0,1:T(2,128)(2,1)S(1)} async-done(((bf16[2,384,768]{2,0,1:T(2,128)(2,1)}), bf16[2,384,768]{2,0,1:T(2,128)(2,1)S(1)}, u32[]{:S(2)}, u32[]{:S(2)}) %all-to-all-start.3) | async-done | bytes 1179680 | tf_op jit(solution)/shard_map/all_to_all | solution.py:147
  358.4 1.8 fusion.114
  (304 shorter events, 32.9 us)
Async XLA Ops:
  7.2 145.3 %all-gather.2.cloned.1.call-start = ((), (), s32[]{:S(2)}) async-start(), calls=%async_computation.6 | async-start | bytes 7077888 | tf_op jit(solution)/shard_map/all_gather | solution.py:88
  8.3 9.5 %collective-permute-start = (bf16[1,3,32,1536]{3,2,1,0:T(8,128)(2,1)S(1)}, bf16[1,3,32,1536]{3,2,1,0:T(8,128)(2,1)S(1)}, u32[]{:S(2)}, u32[]{:S(2)}) collective-permute-start(bf16[1,3,32,1536]{3,2,1,0:T(8,128)(2,1)S(1)} %get-tuple-element.133), channel_id=1, source_target_pairs={{0,1},{1,2},{2,3},{4,5},{5,6},{6,7},{8,9},{9,10},{10,11},{12,13},{... | collective-permute-start | bytes 884744 | tf_op jit(solution)/shard_map/ppermute | solution.py:25
  10.7 7.1 %collective-permute-start.1 = (bf16[1,3,32,1536]{3,2,1,0:T(8,128)(2,1)S(1)}, bf16[1,3,32,1536]{3,2,1,0:T(8,128)(2,1)S(1)}, u32[]{:S(2)}, u32[]{:S(2)}) collective-permute-start(bf16[1,3,32,1536]{3,2,1,0:T(8,128)(2,1)S(1)} %get-tuple-element.134), channel_id=1, source_target_pairs={{1,0},{2,1},{3,2},{5,4},{6,5},{7,6},{9,8},{10,9},{11,10},{13,12},{... | collective-permute-start | bytes 884744 | tf_op jit(solution)/shard_map/ppermute | solution.py:26
  30.5 203.8 %reduce-scatter.3.cloned.1.call-start = ((), (), s32[]{:S(2)}) async-start(), calls=%async_computation.7 | async-start | bytes 7077888 | tf_op jit(solution)/shard_map/reduce_scatter | solution.py:106
  171.8 162.9 %reduce-scatter.5.cloned.1.call-start = ((), (), s32[]{:S(2)}) async-start(), calls=%async_computation.8 | async-start | bytes 5898240 | tf_op jit(solution)/shard_map/reduce_scatter | solution.py:117
  253.2 25.4 %all-to-all-start.1 = ((f32[32,2,1536]{2,1,0:T(2,128)}), f32[32,2,1536]{2,1,0:T(2,128)S(1)}, u32[]{:S(2)}, u32[]{:S(2)}) async-start(f32[32,2,1536]{2,1,0:T(2,128)} %reshape.558), calls=%async_computation.3 | async-start | bytes 786432 | tf_op jit(solution)/shard_map/all_to_all | solution.py:49
  257.8 27.4 %copy-start.3 = (bf16[1,4,32,1536]{3,2,1,0:T(8,128)(2,1)S(1)}, bf16[1,4,32,1536]{3,2,1,0:T(8,128)(2,1)}, u32[]{:S(2)}) copy-start(bf16[1,4,32,1536]{3,2,1,0:T(8,128)(2,1)} %param.13) | copy-start | bytes 1179652
  257.8 27.4 %copy-start.9 = (f32[1536]{0:T(1024)S(1)}, f32[1536]{0:T(1024)}, u32[]{:S(2)}) copy-start(f32[1536]{0:T(1024)} %copy-done.8) | copy-start | bytes 18436
  257.9 27.4 %copy-start.11 = (f32[1536]{0:T(1024)S(1)}, f32[1536]{0:T(1024)}, u32[]{:S(2)}) copy-start(f32[1536]{0:T(1024)} %copy-done.10) | copy-start | bytes 18436
  257.9 27.4 %copy-start.13 = (f32[1536]{0:T(1024)S(1)}, f32[1536]{0:T(1024)}, u32[]{:S(2)}) copy-start(f32[1536]{0:T(1024)} %copy-done.12) | copy-start | bytes 18436
  257.9 27.4 %copy-start.15 = (f32[1536]{0:T(1024)S(1)}, f32[1536]{0:T(1024)}, u32[]{:S(2)}) copy-start(f32[1536]{0:T(1024)} %copy-done.14) | copy-start | bytes 18436
  257.9 27.4 %copy-start.17 = (f32[1536]{0:T(1024)S(1)}, f32[1536]{0:T(1024)}, u32[]{:S(2)}) copy-start(f32[1536]{0:T(1024)} %copy-done.16) | copy-start | bytes 18436
  257.9 27.4 %copy-start.19 = (f32[1536]{0:T(1024)S(1)}, f32[1536]{0:T(1024)}, u32[]{:S(2)}) copy-start(f32[1536]{0:T(1024)} %copy-done.18) | copy-start | bytes 18436
  257.9 27.4 %copy-start.21 = (f32[1536]{0:T(1024)S(1)}, f32[1536]{0:T(1024)}, u32[]{:S(2)}) copy-start(f32[1536]{0:T(1024)} %copy-done.20) | copy-start | bytes 18436
  257.9 27.4 %copy-start.23 = (f32[1536]{0:T(1024)S(1)}, f32[1536]{0:T(1024)}, u32[]{:S(2)}) copy-start(f32[1536]{0:T(1024)} %copy-done.22) | copy-start | bytes 18436
  257.9 27.4 %copy-start.25 = (f32[1536]{0:T(1024)S(1)}, f32[1536]{0:T(1024)}, u32[]{:S(2)}) copy-start(f32[1536]{0:T(1024)} %copy-done.24) | copy-start | bytes 18436
  257.9 27.4 %copy-start.27 = (f32[1536]{0:T(1024)S(1)}, f32[1536]{0:T(1024)}, u32[]{:S(2)}) copy-start(f32[1536]{0:T(1024)} %copy-done.26) | copy-start | bytes 18436
  257.9 27.4 %copy-start.29 = (f32[1536]{0:T(1024)S(1)}, f32[1536]{0:T(1024)}, u32[]{:S(2)}) copy-start(f32[1536]{0:T(1024)} %copy-done.28) | copy-start | bytes 18436
  258.0 27.4 %copy-start.31 = (f32[1536]{0:T(1024)S(1)}, f32[1536]{0:T(1024)}, u32[]{:S(2)}) copy-start(f32[1536]{0:T(1024)} %copy-done.30) | copy-start | bytes 18436
  258.0 27.4 %copy-start.33 = (f32[1536]{0:T(1024)S(1)}, f32[1536]{0:T(1024)}, u32[]{:S(2)}) copy-start(f32[1536]{0:T(1024)} %copy-done.32) | copy-start | bytes 18436
  258.0 27.4 %copy-start.35 = (f32[1536]{0:T(1024)S(1)}, f32[1536]{0:T(1024)}, u32[]{:S(2)}) copy-start(f32[1536]{0:T(1024)} %copy-done.34) | copy-start | bytes 18436
  258.0 27.4 %copy-start.37 = (f32[1536]{0:T(1024)S(1)}, f32[1536]{0:T(1024)}, u32[]{:S(2)}) copy-start(f32[1536]{0:T(1024)} %copy-done.36) | copy-start | bytes 18436
  258.0 27.4 %copy-start.39 = (f32[1536]{0:T(1024)S(1)}, f32[1536]{0:T(1024)}, u32[]{:S(2)}) copy-start(f32[1536]{0:T(1024)} %copy-done.38) | copy-start | bytes 18436
  258.0 27.4 %copy-start.41 = (f32[1536]{0:T(1024)S(1)}, f32[1536]{0:T(1024)}, u32[]{:S(2)}) copy-start(f32[1536]{0:T(1024)} %copy-done.40) | copy-start | bytes 18436
  258.0 27.4 %copy-start.43 = (f32[1536]{0:T(1024)S(1)}, f32[1536]{0:T(1024)}, u32[]{:S(2)}) copy-start(f32[1536]{0:T(1024)} %copy-done.42) | copy-start | bytes 18436
  258.2 3.8 %collective-permute-start.2 = (bf16[1,3,32,1536]{3,2,1,0:T(8,128)(2,1)S(1)}, bf16[1,3,32,1536]{3,2,1,0:T(8,128)(2,1)S(1)}, u32[]{:S(2)}, u32[]{:S(2)}) collective-permute-start(bf16[1,3,32,1536]{3,2,1,0:T(8,128)(2,1)S(1)} %get-tuple-element.131), channel_id=1, source_target_pairs={{0,1},{1,2},{2,3},{4,5},{5,6},{6,7},{8,9},{9,10},{10,11},{12,13},{... | collective-permute-start | bytes 884744 | tf_op jit(solution)/shard_map/ppermute | solution.py:25
  260.5 4.6 %collective-permute-start.3 = (bf16[1,3,32,1536]{3,2,1,0:T(8,128)(2,1)S(1)}, bf16[1,3,32,1536]{3,2,1,0:T(8,128)(2,1)S(1)}, u32[]{:S(2)}, u32[]{:S(2)}) collective-permute-start(bf16[1,3,32,1536]{3,2,1,0:T(8,128)(2,1)S(1)} %get-tuple-element.132), channel_id=1, source_target_pairs={{1,0},{2,1},{3,2},{5,4},{6,5},{7,6},{9,8},{10,9},{11,10},{13,12},{... | collective-permute-start | bytes 884744 | tf_op jit(solution)/shard_map/ppermute | solution.py:26
  279.6 28.8 %all-to-all-start.2 = ((f32[32,2,1536]{2,1,0:T(2,128)}), f32[32,2,1536]{2,1,0:T(2,128)S(1)}, u32[]{:S(2)}, u32[]{:S(2)}) async-start(f32[32,2,1536]{2,1,0:T(2,128)} %broadcast_in_dim.11), calls=%async_computation.4 | async-start | bytes 786432 | tf_op jit(solution)/shard_map/all_to_all | solution.py:51
  309.4 32.3 %copy-start.1 = (bf16[1,4,32,1536]{3,2,1,0:T(8,128)(2,1)S(1)}, bf16[1,4,32,1536]{3,2,1,0:T(8,128)(2,1)}, u32[]{:S(2)}) copy-start(bf16[1,4,32,1536]{3,2,1,0:T(8,128)(2,1)} %param.7) | copy-start | bytes 1179652
  309.4 32.3 %copy-start.4 = (f32[1,128,1536]{2,1,0:T(8,128)S(1)}, f32[1,128,1536]{2,1,0:T(8,128)}, u32[]{:S(2)}) copy-start(f32[1,128,1536]{2,1,0:T(8,128)} %get-tuple-element.130) | copy-start | bytes 2359300
  309.4 32.3 %copy-start.87 = (f32[1536]{0:T(1024)S(1)}, f32[1536]{0:T(1024)}, u32[]{:S(2)}) copy-start(f32[1536]{0:T(1024)} %param.12) | copy-start | bytes 18436
  338.2 19.4 %all-to-all-start.3 = ((bf16[2,384,768]{2,0,1:T(2,128)(2,1)}), bf16[2,384,768]{2,0,1:T(2,128)(2,1)S(1)}, u32[]{:S(2)}, u32[]{:S(2)}) async-start(bf16[2,384,768]{2,0,1:T(2,128)(2,1)} %copy.27), calls=%async_computation.5 | async-start | bytes 2359296 | tf_op jit(solution)/shard_map/all_to_all | solution.py:147
  (80 other events, 1175.3 us)
Sparse Core Ops, SparseCore 0:
  30.6 82.8 all-gather.1
  171.9 62.3 reduce-scatter.2
  236.8 97.8 reduce-scatter.4

commit v11 on v10

--- a/solution.py
+++ b/solution.py
@@ -92,23 +92,24 @@
     mlp_terms = lax.dot_general(
         active, down_t, contract_cols, preferred_element_type=jnp.float32
     )
+    slope_in = jnp.dot(back_all, down_t, preferred_element_type=jnp.float32)
+    hidden_grad = (slope_in * gelu_slope(hidden)).astype(jnp.bfloat16)
+    norm_terms = lax.dot_general(
+        hidden_grad, up_loc, contract_cols, preferred_element_type=jnp.float32
+    )
+    to_sum = jnp.stack([mlp_terms, norm_terms]).astype(jnp.bfloat16)
+    to_sum, gathered, back_all, active, hidden_grad = lax.optimization_barrier(
+        (to_sum, gathered, back_all, active, hidden_grad)
+    )
+    sums = lax.psum_scatter(to_sum, hid_axes, scatter_dimension=1, tiled=True).astype(
+        jnp.float32
+    )
     down_part_t = lax.dot_general(
         back_all, active, contract_rows, preferred_element_type=jnp.float32
     )
-    slope_in = jnp.dot(back_all, down_t, preferred_element_type=jnp.float32)
-    hidden_grad = (slope_in * gelu_slope(hidden)).astype(jnp.bfloat16)
     up_part = lax.dot_general(
         gathered, hidden_grad, contract_rows, preferred_element_type=jnp.float32
     )
-    norm_terms = lax.dot_general(
-        hidden_grad, up_loc, contract_cols, preferred_element_type=jnp.float32
-    )
-    sums = lax.psum_scatter(
-        jnp.stack([mlp_terms, norm_terms]).astype(jnp.bfloat16),
-        hid_axes,
-        scatter_dimension=1,
-        tiled=True,
-    ).astype(jnp.float32)
     branch, norm_grad = sums[0], sums[1]
     resid = feature_maps.reshape(cells, width).astype(jnp.float32)
     result = (resid + layer_scale * branch).astype(jnp.bfloat16).reshape(feature_maps.shape)

time: 375 us -> 379 us (1.011)
  local copies, waits for them, and re-layouts: 35.3 us -> 40.2 us
    squeeze x0 -> x1, local copies, waits for them, and re-layouts: none -> 5.86 us  [body(): gathered, back_all = (pair[0], pair[1])]
where the time goes in v11:
time: 379 us; the launch traced here: 376 us
  waiting for transfers between devices  123 us (32%)
  blocking collectives  113 us (30%)
  local copies, waits for them, and re-layouts  40.2 us (11%)
  other arithmetic  40.1 us (11%)
  matrix products  22.6 us (6%)
  starting transfers between devices  21.6 us (6%)
  between operations  15.9 us (4%)
    all_to_all x1, blocking collectives, body(): both = lax.all_to_all(pieces, ('dp', 'rows'), 1, 1, tiled=True)  113 us
    reduce_scatter x1, waiting for transfers between devices, body(): lax.psum_scatter(to_sum, hid_axes, scatter_dimension=1, tiled=True)  51.4 us
    reduce_scatter x1, waiting for transfers between devices, body(): lax.psum_scatter(grad_parts, 'dp', scatter_dimension=1, tiled=True)  24.6 us
    all_to_all x1, waiting for transfers between devices, small_sums(): lax.all_to_all(spread, every, 0, 0, tiled=True)  15.1 us
    all_to_all x1, waiting for transfers between devices, body(): lax.all_to_all(grad_sums, 'rows', 1, 2, tiled=True).astype(jnp.float32)  15 us
    all_to_all x1, waiting for transfers between devices, small_sums(): lax.all_to_all(packed.reshape(devices, per, width), every, 0, 0, tiled=True)  13.3 us
    reduce_sum x1, other arithmetic, body(): average = jnp.mean(flat, axis=-1, keepdims=True)  9.44 us
  transfers between devices with their start and end apart: 10, of which 6 were waited for; matrix products, arithmetic and copies ran while one was open for 15% of the time, Pallas kernels for 0%

profile of v11, /device:TPU:0, one launch (start us, length us, event | category | flops | bytes accessed | tf_op | source)
XLA Modules:
  0.0 375.6 jit_solution(6789784241697802138)
XLA Ops:
  8.3 2.4 collective-permute-start
  13.4 1.8 slice_reduce_fusion.50
  15.4 2.5 slice_reduce_fusion.49
  19.1 9.4 %fusion.111 = (f32[4,32]{1,0:T(4,128)S(1)}, f32[1,4,32,1536]{3,2,1,0:T(8,128)S(1)}) fusion(f32[1536]{0:T(1024)S(1)} %get-tuple-element.129, f32[1536]{0:T(1024)S(1)} %get-tuple-element.130, f32[1536]{0:T(1024)S(1)} %get-tuple-element.83, f32[1536]{0:T(1024)S(1)} %get-tuple-element.84, f32[1,10,32,1536]{3,2,1,0:T(8,128)S(1)} %maximum_convert_fusion, ...), kind=kLoop, calls=%fused_computation.333 | loop fusion | flops 19267456 | bytes 8641024 | tf_op jit(solution)/shard_map/reduce_sum | solution.py:82
  32.5 2.5 stack.187
  35.0 1.9 maximum_bitcast_fusion
  37.6 112.6 %all_to_all.24 = bf16[2,16,96,768]{3,2,0,1:T(8,128)(2,1)S(1)} all-to-all(bf16[2,16,96,768]{3,2,0,1:T(8,128)(2,1)S(1)} %bitcast.81), channel_id=1, replica_groups=mesh['dp'=4,'fsdp'=2,'rows'=4] {'dp','rows'}, dimensions={1} | all-to-all | bytes 9437184 | tf_op jit(solution)/shard_map/all_to_all | solution.py:66
  150.2 2.4 fusion.112
  152.6 5.2 %multiply_convert_fusion = (bf16[1024,768]{1,0:T(8,128)(2,1)S(1)}, f32[1024,768]{1,0:T(8,128)S(1)}) fusion(bf16[1536,768]{1,0:T(8,128)(2,1)} %bitcast.87, bf16[2,1024,1536]{2,1,0:T(8,128)(2,1)} %all-gather.2.cloned.1.call-done), kind=kOutput, calls=%fused_computation.101 | convolution fusion | flops 2419851264 | bytes 10223616 | tf_op jit(solution)/shard_map/dot_general | solution.py:90
  157.9 2.9 fusion
  161.2 3.5 fusion.7
  164.7 2.9 fusion.1
  167.6 3.2 pad_maximum_fusion
  170.8 5.9 %slice_bitcast_fusion = (bf16[1024,1536]{1,0:T(8,128)(2,1)}, bf16[1024,1536]{1,0:T(8,128)(2,1)}) fusion(bf16[2,1024,1536]{2,1,0:T(8,128)(2,1)} %all-gather.2.cloned.1.call-done), kind=kLoop, calls=%fused_computation.99 | loop fusion | bytes 12582912 | tf_op jit(solution)/shard_map/squeeze | solution.py:89
  177.0 5.2 %fusion.8 = bf16[1,1536,768]{2,1,0:T(8,128)(2,1)S(1)} fusion(bf16[1024,1536]{1,0:T(8,128)(2,1)} %get-tuple-element.18, bf16[1024,768]{1,0:T(8,128)(2,1)} %copy-done.102), kind=kOutput, calls=%fused_computation.103 | convolution fusion | flops 2417098752 | bytes 7077888 | tf_op jit(solution)/shard_map/dot_general | solution.py:110
  182.2 3.0 fusion.9
  185.2 2.7 pad_maximum_fusion.1
  187.9 51.4 %reduce-scatter.3.cloned.1.call-done = bf16[2,128,1536]{2,1,0:T(8,128)(2,1)} async-done(((bf16[2,1024,1536]{2,1,0:T(8,128)(2,1)}), bf16[2,128,1536]{2,1,0:T(8,128)(2,1)}) %reduce-scatter.3.cloned.1.call-update) | async-done | bytes 786448 | tf_op jit(solution)/shard_map/reduce_scatter | solution.py:104
  240.7 2.1 fusion.104
  250.0 2.4 multiply_reduce_fusion
  252.6 2.0 multiply_reduce_fusion.18
  258.1 4.6 %all-to-all-start.1 = ((f32[32,2,1536]{2,1,0:T(2,128)}), f32[32,2,1536]{2,1,0:T(2,128)S(1)}, u32[]{:S(2)}, u32[]{:S(2)}) async-start(f32[32,2,1536]{2,1,0:T(2,128)} %reshape.558), calls=%async_computation.3 | async-start | bytes 786432 | tf_op jit(solution)/shard_map/all_to_all | solution.py:49
  263.1 2.3 collective-permute-start.2
  266.8 3.3 collective-permute-done.3
  270.2 13.3 %all-to-all-done.1 = f32[32,2,1536]{2,1,0:T(2,128)S(1)} async-done(((f32[32,2,1536]{2,1,0:T(2,128)}), f32[32,2,1536]{2,1,0:T(2,128)S(1)}, u32[]{:S(2)}, u32[]{:S(2)}) %all-to-all-start.1) | async-done | bytes 393248 | tf_op jit(solution)/shard_map/all_to_all | solution.py:49
  284.5 5.9 %all-to-all-start.2 = ((f32[32,2,1536]{2,1,0:T(2,128)}), f32[32,2,1536]{2,1,0:T(2,128)S(1)}, u32[]{:S(2)}, u32[]{:S(2)}) async-start(f32[32,2,1536]{2,1,0:T(2,128)} %broadcast_in_dim.11), calls=%async_computation.4 | async-start | bytes 786432 | tf_op jit(solution)/shard_map/all_to_all | solution.py:51
  290.8 7.4 %fusion.97 = bf16[1,4,32,1536]{3,2,1,0:T(8,128)(2,1)} fusion(f32[1,10,32,1536]{3,2,1,0:T(8,128)S(1)} %maximum_convert_fusion.1, f32[1536]{0:T(1024)S(1)} %copy-done.27, f32[1536]{0:T(1024)S(1)} %copy-done.29, f32[1536]{0:T(1024)S(1)} %copy-done.33, f32[1536]{0:T(1024)S(1)} %copy-done.35, f32[1536]{0:T(1024)S(1)} %copy-done.37, f32[1536]{0:T(1024)S(1)} %copy-done.39, ...), kind=kLoop, calls=%fused_computation.196 | loop fusion | flops 19660800 | bytes 8640512 | tf_op jit(solution)/shard_map/convert_element_type | solution.py:143
  298.2 15.1 %all-to-all-done.2 = f32[32,2,1536]{2,1,0:T(2,128)S(1)} async-done(((f32[32,2,1536]{2,1,0:T(2,128)}), f32[32,2,1536]{2,1,0:T(2,128)S(1)}, u32[]{:S(2)}, u32[]{:S(2)}) %all-to-all-start.2) | async-done | bytes 393248 | tf_op jit(solution)/shard_map/all_to_all | solution.py:51
  315.0 24.6 %reduce-scatter.5.cloned.1.call-done = bf16[2,384,768]{2,1,0:T(8,128)(2,1)} async-done(((bf16[2,1536,768]{2,1,0:T(8,128)(2,1)}), bf16[2,384,768]{2,1,0:T(8,128)(2,1)}) %reduce-scatter.5.cloned.1.call-update) | async-done | bytes 1179664 | tf_op jit(solution)/shard_map/reduce_scatter | solution.py:118
  339.6 3.5 copy.27
  343.1 3.5 all-to-all-start.3
  347.5 15.0 %all-to-all-done.3 = bf16[2,384,768]{2,0,1:T(2,128)(2,1)S(1)} async-done(((bf16[2,384,768]{2,0,1:T(2,128)(2,1)}), bf16[2,384,768]{2,0,1:T(2,128)(2,1)S(1)}, u32[]{:S(2)}, u32[]{:S(2)}) %all-to-all-start.3) | async-done | bytes 1179680 | tf_op jit(solution)/shard_map/all_to_all | solution.py:148
  (307 shorter events, 33.6 us)
Async XLA Ops:
  7.2 145.5 %all-gather.2.cloned.1.call-start = ((), (), s32[]{:S(2)}) async-start(), calls=%async_computation.6 | async-start | bytes 7077888 | tf_op jit(solution)/shard_map/all_gather | solution.py:88
  8.3 9.6 %collective-permute-start = (bf16[1,3,32,1536]{3,2,1,0:T(8,128)(2,1)S(1)}, bf16[1,3,32,1536]{3,2,1,0:T(8,128)(2,1)S(1)}, u32[]{:S(2)}, u32[]{:S(2)}) collective-permute-start(bf16[1,3,32,1536]{3,2,1,0:T(8,128)(2,1)S(1)} %get-tuple-element.145), channel_id=1, source_target_pairs={{0,1},{1,2},{2,3},{4,5},{5,6},{6,7},{8,9},{9,10},{10,11},{12,13},{... | collective-permute-start | bytes 884744 | tf_op jit(solution)/shard_map/ppermute | solution.py:25
  10.7 7.2 %collective-permute-start.1 = (bf16[1,3,32,1536]{3,2,1,0:T(8,128)(2,1)S(1)}, bf16[1,3,32,1536]{3,2,1,0:T(8,128)(2,1)S(1)}, u32[]{:S(2)}, u32[]{:S(2)}) collective-permute-start(bf16[1,3,32,1536]{3,2,1,0:T(8,128)(2,1)S(1)} %get-tuple-element.146), channel_id=1, source_target_pairs={{1,0},{2,1},{3,2},{5,4},{6,5},{7,6},{9,8},{10,9},{11,10},{13,12},{... | collective-permute-start | bytes 884744 | tf_op jit(solution)/shard_map/ppermute | solution.py:26
  30.7 208.6 %reduce-scatter.3.cloned.1.call-start = ((), (), s32[]{:S(2)}) async-start(), calls=%async_computation.7 | async-start | bytes 7077888 | tf_op jit(solution)/shard_map/reduce_scatter | solution.py:104
  176.7 162.9 %reduce-scatter.5.cloned.1.call-start = ((), (), s32[]{:S(2)}) async-start(), calls=%async_computation.8 | async-start | bytes 5898240 | tf_op jit(solution)/shard_map/reduce_scatter | solution.py:118
  258.1 25.4 %all-to-all-start.1 = ((f32[32,2,1536]{2,1,0:T(2,128)}), f32[32,2,1536]{2,1,0:T(2,128)S(1)}, u32[]{:S(2)}, u32[]{:S(2)}) async-start(f32[32,2,1536]{2,1,0:T(2,128)} %reshape.558), calls=%async_computation.3 | async-start | bytes 786432 | tf_op jit(solution)/shard_map/all_to_all | solution.py:49
  262.7 27.7 %copy-start.4 = (bf16[1,4,32,1536]{3,2,1,0:T(8,128)(2,1)S(1)}, bf16[1,4,32,1536]{3,2,1,0:T(8,128)(2,1)}, u32[]{:S(2)}) copy-start(bf16[1,4,32,1536]{3,2,1,0:T(8,128)(2,1)} %param.13) | copy-start | bytes 1179652
  262.8 27.7 %copy-start.11 = (f32[1536]{0:T(1024)S(1)}, f32[1536]{0:T(1024)}, u32[]{:S(2)}) copy-start(f32[1536]{0:T(1024)} %copy-done.10) | copy-start | bytes 18436
  262.8 27.7 %copy-start.13 = (f32[1536]{0:T(1024)S(1)}, f32[1536]{0:T(1024)}, u32[]{:S(2)}) copy-start(f32[1536]{0:T(1024)} %copy-done.12) | copy-start | bytes 18436
  262.8 27.7 %copy-start.15 = (f32[1536]{0:T(1024)S(1)}, f32[1536]{0:T(1024)}, u32[]{:S(2)}) copy-start(f32[1536]{0:T(1024)} %copy-done.14) | copy-start | bytes 18436
  262.8 27.7 %copy-start.17 = (f32[1536]{0:T(1024)S(1)}, f32[1536]{0:T(1024)}, u32[]{:S(2)}) copy-start(f32[1536]{0:T(1024)} %copy-done.16) | copy-start | bytes 18436
  262.8 27.7 %copy-start.19 = (f32[1536]{0:T(1024)S(1)}, f32[1536]{0:T(1024)}, u32[]{:S(2)}) copy-start(f32[1536]{0:T(1024)} %copy-done.18) | copy-start | bytes 18436
  262.8 27.7 %copy-start.21 = (f32[1536]{0:T(1024)S(1)}, f32[1536]{0:T(1024)}, u32[]{:S(2)}) copy-start(f32[1536]{0:T(1024)} %copy-done.20) | copy-start | bytes 18436
  262.8 27.7 %copy-start.23 = (f32[1536]{0:T(1024)S(1)}, f32[1536]{0:T(1024)}, u32[]{:S(2)}) copy-start(f32[1536]{0:T(1024)} %copy-done.22) | copy-start | bytes 18436
  262.8 27.7 %copy-start.25 = (f32[1536]{0:T(1024)S(1)}, f32[1536]{0:T(1024)}, u32[]{:S(2)}) copy-start(f32[1536]{0:T(1024)} %copy-done.24) | copy-start | bytes 18436
  262.8 27.7 %copy-start.27 = (f32[1536]{0:T(1024)S(1)}, f32[1536]{0:T(1024)}, u32[]{:S(2)}) copy-start(f32[1536]{0:T(1024)} %copy-done.26) | copy-start | bytes 18436
  262.8 27.7 %copy-start.29 = (f32[1536]{0:T(1024)S(1)}, f32[1536]{0:T(1024)}, u32[]{:S(2)}) copy-start(f32[1536]{0:T(1024)} %copy-done.28) | copy-start | bytes 18436
  262.9 27.7 %copy-start.31 = (f32[1536]{0:T(1024)S(1)}, f32[1536]{0:T(1024)}, u32[]{:S(2)}) copy-start(f32[1536]{0:T(1024)} %copy-done.30) | copy-start | bytes 18436
  262.9 27.7 %copy-start.33 = (f32[1536]{0:T(1024)S(1)}, f32[1536]{0:T(1024)}, u32[]{:S(2)}) copy-start(f32[1536]{0:T(1024)} %copy-done.32) | copy-start | bytes 18436
  262.9 27.7 %copy-start.35 = (f32[1536]{0:T(1024)S(1)}, f32[1536]{0:T(1024)}, u32[]{:S(2)}) copy-start(f32[1536]{0:T(1024)} %copy-done.34) | copy-start | bytes 18436
  262.9 27.7 %copy-start.37 = (f32[1536]{0:T(1024)S(1)}, f32[1536]{0:T(1024)}, u32[]{:S(2)}) copy-start(f32[1536]{0:T(1024)} %copy-done.36) | copy-start | bytes 18436
  262.9 27.7 %copy-start.39 = (f32[1536]{0:T(1024)S(1)}, f32[1536]{0:T(1024)}, u32[]{:S(2)}) copy-start(f32[1536]{0:T(1024)} %copy-done.38) | copy-start | bytes 18436
  262.9 27.7 %copy-start.41 = (f32[1536]{0:T(1024)S(1)}, f32[1536]{0:T(1024)}, u32[]{:S(2)}) copy-start(f32[1536]{0:T(1024)} %copy-done.40) | copy-start | bytes 18436
  262.9 27.7 %copy-start.43 = (f32[1536]{0:T(1024)S(1)}, f32[1536]{0:T(1024)}, u32[]{:S(2)}) copy-start(f32[1536]{0:T(1024)} %copy-done.42) | copy-start | bytes 18436
  262.9 27.7 %copy-start.45 = (f32[1536]{0:T(1024)S(1)}, f32[1536]{0:T(1024)}, u32[]{:S(2)}) copy-start(f32[1536]{0:T(1024)} %copy-done.44) | copy-start | bytes 18436
  263.1 3.6 collective-permute-start.2
  265.5 4.6 %collective-permute-start.3 = (bf16[1,3,32,1536]{3,2,1,0:T(8,128)(2,1)S(1)}, bf16[1,3,32,1536]{3,2,1,0:T(8,128)(2,1)S(1)}, u32[]{:S(2)}, u32[]{:S(2)}) collective-permute-start(bf16[1,3,32,1536]{3,2,1,0:T(8,128)(2,1)S(1)} %get-tuple-element.144), channel_id=1, source_target_pairs={{1,0},{2,1},{3,2},{5,4},{6,5},{7,6},{9,8},{10,9},{11,10},{13,12},{... | collective-permute-start | bytes 884744 | tf_op jit(solution)/shard_map/ppermute | solution.py:26
  284.5 28.8 %all-to-all-start.2 = ((f32[32,2,1536]{2,1,0:T(2,128)}), f32[32,2,1536]{2,1,0:T(2,128)S(1)}, u32[]{:S(2)}, u32[]{:S(2)}) async-start(f32[32,2,1536]{2,1,0:T(2,128)} %broadcast_in_dim.11), calls=%async_computation.4 | async-start | bytes 786432 | tf_op jit(solution)/shard_map/all_to_all | solution.py:51
  314.4 32.3 %copy-start.2 = (bf16[1,4,32,1536]{3,2,1,0:T(8,128)(2,1)S(1)}, bf16[1,4,32,1536]{3,2,1,0:T(8,128)(2,1)}, u32[]{:S(2)}) copy-start(bf16[1,4,32,1536]{3,2,1,0:T(8,128)(2,1)} %param.7) | copy-start | bytes 1179652
  314.4 32.3 %copy-start.5 = (f32[1,128,1536]{2,1,0:T(8,128)S(1)}, f32[1,128,1536]{2,1,0:T(8,128)}, u32[]{:S(2)}) copy-start(f32[1,128,1536]{2,1,0:T(8,128)} %get-tuple-element.142) | copy-start | bytes 2359300
  314.4 32.3 %copy-start.89 = (f32[1536]{0:T(1024)S(1)}, f32[1536]{0:T(1024)}, u32[]{:S(2)}) copy-start(f32[1536]{0:T(1024)} %param.12) | copy-start | bytes 18436
  343.1 19.4 %all-to-all-start.3 = ((bf16[2,384,768]{2,0,1:T(2,128)(2,1)}), bf16[2,384,768]{2,0,1:T(2,128)(2,1)S(1)}, u32[]{:S(2)}, u32[]{:S(2)}) async-start(bf16[2,384,768]{2,0,1:T(2,128)(2,1)} %copy.27), calls=%async_computation.5 | async-start | bytes 2359296 | tf_op jit(solution)/shard_map/all_to_all | solution.py:148
  (81 other events, 1192.0 us)
Sparse Core Ops, SparseCore 0:
  30.8 82.8 all-gather.1
  176.8 62.3 reduce-scatter.2
  241.7 97.8 reduce-scatter.4

commit v12 on v10

--- a/solution.py
+++ b/solution.py
@@ -140,10 +140,10 @@
             )
     kernel_part = jnp.stack(kernel_rows).reshape(KS, KS, width)
     grad_x = (d_out.astype(jnp.float32) + back_conv).astype(jnp.bfloat16)
+    grad_sums, grad_x, kernel_part, gain_part, scale_part = lax.optimization_barrier(
+        (grad_sums, grad_x, kernel_part, gain_part, scale_part)
+    )
     grad_kernel, grad_gain, grad_scale = small_sums(kernel_part, gain_part, scale_part, width)
-    grad_sums, grad_x, grad_kernel, grad_gain, grad_scale = lax.optimization_barrier(
-        (grad_sums, grad_x, grad_kernel, grad_gain, grad_scale)
-    )
     grad_sums = lax.all_to_all(grad_sums, "rows", 1, 2, tiled=True).astype(jnp.float32)
     grad_up, grad_down = grad_sums[0], grad_sums[1].T
     return (result, grad_x, grad_up, grad_down, grad_kernel, grad_gain, grad_scale)

time: 375 us -> 388 us (1.035)
  local copies, waits for them, and re-layouts: 35.3 us -> 47.8 us
  waiting for transfers between devices: 121 us -> 128 us
    reduce_scatter x1, waiting for transfers between devices: 24.6 us -> 46 us  [body(): lax.psum_scatter(grad_parts, 'dp', scatter_dimension=1, tiled=True)]
    another operation x49 -> x50, local copies, waits for them, and re-layouts: 0.31 us -> 15 us  [body(): kernel_part = jnp.stack(kernel_rows).reshape(KS, KS, width)]
    all_to_all x1, waiting for transfers between devices: 15.3 us -> 5.39 us  [small_sums(): lax.all_to_all(spread, every, 0, 0, tiled=True)]
  transfers between devices with their start and end apart: 10 -> 10, of which waited for: 6 -> 5; matrix products, arithmetic and copies ran while one was open for 15% -> 19% of each run, Pallas kernels for 0% -> 0%
where the time goes in v12:
time: 388 us; the launch traced here: 387 us
  waiting for transfers between devices  128 us (33%)
  blocking collectives  113 us (29%)
  local copies, waits for them, and re-layouts  47.8 us (12%)
  other arithmetic  40.2 us (10%)
  matrix products  24.5 us (6%)
  starting transfers between devices  18.8 us (5%)
  between operations  15.7 us (4%)
    all_to_all x1, blocking collectives, body(): both = lax.all_to_all(pieces, ('dp', 'rows'), 1, 1, tiled=True)  113 us
    reduce_scatter x1, waiting for transfers between devices, body(): lax.psum_scatter(jnp.stack([mlp_terms, norm_terms]).astype(jnp.bfloat16),...  49.5 us
    reduce_scatter x1, waiting for transfers between devices, body(): lax.psum_scatter(grad_parts, 'dp', scatter_dimension=1, tiled=True)  46 us
    all_to_all x1, waiting for transfers between devices, body(): lax.all_to_all(grad_sums, 'rows', 1, 2, tiled=True).astype(jnp.float32)  15.7 us
    another operation x50, local copies, waits for them, and re-layouts, body(): kernel_part = jnp.stack(kernel_rows).reshape(KS, KS, width)  15 us
    all_to_all x1, waiting for transfers between devices, small_sums(): lax.all_to_all(packed.reshape(devices, per, width), every, 0, 0, tiled=True)  10.9 us
    reduce_sum x1, other arithmetic, body(): average = jnp.mean(flat, axis=-1, keepdims=True)  9.44 us
  transfers between devices with their start and end apart: 10, of which 5 were waited for; matrix products, arithmetic and copies ran while one was open for 19% of the time, Pallas kernels for 0%

profile of v12, /device:TPU:0, one launch (start us, length us, event | category | flops | bytes accessed | tf_op | source)
XLA Modules:
  0.0 387.2 jit_solution(11659370900414596236)
XLA Ops:
  8.3 2.4 collective-permute-start
  15.4 2.3 slice_reduce_fusion.49
  19.0 9.4 %fusion.112 = (f32[4,32]{1,0:T(4,128)S(1)}, f32[1,4,32,1536]{3,2,1,0:T(8,128)S(1)}) fusion(f32[1536]{0:T(1024)S(1)} %get-tuple-element.119, f32[1536]{0:T(1024)S(1)} %get-tuple-element.120, f32[1536]{0:T(1024)S(1)} %get-tuple-element.73, f32[1536]{0:T(1024)S(1)} %get-tuple-element.74, f32[1,10,32,1536]{3,2,1,0:T(8,128)S(1)} %maximum_convert_fusion, ...), kind=kLoop, calls=%fused_computation.337 | loop fusion | flops 19267456 | bytes 8641024 | tf_op jit(solution)/shard_map/reduce_sum | solution.py:82
  30.6 1.8 stack.189
  32.4 2.5 stack.190
  34.9 1.9 maximum_bitcast_fusion
  37.5 112.6 %all_to_all.24 = bf16[2,16,96,768]{3,2,0,1:T(8,128)(2,1)S(1)} all-to-all(bf16[2,16,96,768]{3,2,0,1:T(8,128)(2,1)S(1)} %bitcast.83), channel_id=1, replica_groups=mesh['dp'=4,'fsdp'=2,'rows'=4] {'dp','rows'}, dimensions={1} | all-to-all | bytes 9437184 | tf_op jit(solution)/shard_map/all_to_all | solution.py:66
  150.1 2.4 fusion.113
  152.5 5.2 %multiply_convert_fusion = (bf16[1024,768]{1,0:T(8,128)(2,1)S(1)}, f32[1024,768]{1,0:T(8,128)S(1)}) fusion(bf16[1536,768]{1,0:T(8,128)(2,1)} %bitcast.89, bf16[2,1024,1536]{2,1,0:T(8,128)(2,1)} %all-gather.2.cloned.1.call-done), kind=kOutput, calls=%fused_computation.101 | convolution fusion | flops 2419851264 | bytes 10223616 | tf_op jit(solution)/shard_map/dot_general | solution.py:90
  157.8 2.9 fusion
  161.1 3.5 fusion.7
  165.7 2.9 fusion.1
  168.6 3.2 pad_maximum_fusion
  172.1 5.1 %fusion.9 = bf16[1,1536,768]{2,1,0:T(8,128)(2,1)S(1)} fusion(bf16[1024,768]{1,0:T(8,128)(2,1)} %copy-done.98, bf16[2,1024,1536]{2,1,0:T(8,128)(2,1)} %all-gather.2.cloned.1.call-done), kind=kOutput, calls=%fused_computation.104 | convolution fusion | flops 2417098752 | bytes 7077888 | tf_op jit(solution)/shard_map/dot_general | solution.py:95
  177.3 4.9 %fusion.8 = bf16[1,1536,768]{2,1,0:T(8,128)(2,1)S(1)} fusion(bf16[1024,768]{1,0:T(8,128)(2,1)S(1)} %copy-done.100, bf16[2,1024,1536]{2,1,0:T(8,128)(2,1)} %all-gather.2.cloned.1.call-done), kind=kOutput, calls=%fused_computation.103 | convolution fusion | flops 2417098752 | bytes 7077888 | tf_op jit(solution)/shard_map/dot_general | solution.py:100
  182.2 2.7 pad_maximum_fusion.1
  184.9 49.5 %reduce-scatter.3.cloned.1.call-done = bf16[2,128,1536]{2,1,0:T(8,128)(2,1)} async-done(((bf16[2,1024,1536]{2,1,0:T(8,128)(2,1)}), bf16[2,128,1536]{2,1,0:T(8,128)(2,1)}) %reduce-scatter.3.cloned.1.call-update) | async-done | bytes 786448 | tf_op jit(solution)/shard_map/reduce_scatter | solution.py:106
  235.8 2.1 fusion.106
  243.1 2.4 multiply_reduce_fusion
  256.2 2.0 multiply_reduce_fusion.18
  258.9 1.8 collective-permute-start.2
  264.5 3.5 stack.247
  268.6 7.5 %fusion.99 = bf16[1,4,32,1536]{3,2,1,0:T(8,128)(2,1)} fusion(f32[1,10,32,1536]{3,2,1,0:T(8,128)S(1)} %maximum_convert_fusion.1, f32[1536]{0:T(1024)S(1)} %copy-done.26, f32[1536]{0:T(1024)S(1)} %copy-done.28, f32[1536]{0:T(1024)S(1)} %copy-done.32, f32[1536]{0:T(1024)S(1)} %copy-done.34, f32[1536]{0:T(1024)S(1)} %copy-done.36, f32[1536]{0:T(1024)S(1)} %copy-done.38, ...), kind=kLoop, calls=%fused_computation.198 | loop fusion | flops 19660800 | bytes 8640512 | tf_op jit(solution)/shard_map/convert_element_type | solution.py:142
  276.1 46.0 %reduce-scatter.5.cloned.1.call-done = bf16[2,384,768]{2,1,0:T(8,128)(2,1)} async-done(((bf16[2,1536,768]{2,1,0:T(8,128)(2,1)}), bf16[2,384,768]{2,1,0:T(8,128)(2,1)}) %reduce-scatter.5.cloned.1.call-update) | async-done | bytes 1179664 | tf_op jit(solution)/shard_map/reduce_scatter | solution.py:117
  324.7 5.1 %all-to-all-start.2 = ((f32[32,2,1536]{2,1,0:T(2,128)}), f32[32,2,1536]{2,1,0:T(2,128)S(1)}, u32[]{:S(2)}, u32[]{:S(2)}) async-start(f32[32,2,1536]{2,1,0:T(2,128)} %reshape.566), calls=%async_computation.4 | async-start | bytes 786432 | tf_op jit(solution)/shard_map/all_to_all | solution.py:49
  329.8 2.2 copy.26
  332.0 10.9 %all-to-all-done.2 = f32[32,2,1536]{2,1,0:T(2,128)S(1)} async-done(((f32[32,2,1536]{2,1,0:T(2,128)}), f32[32,2,1536]{2,1,0:T(2,128)S(1)}, u32[]{:S(2)}, u32[]{:S(2)}) %all-to-all-start.2) | async-done | bytes 393248 | tf_op jit(solution)/shard_map/all_to_all | solution.py:49
  342.9 3.5 all-to-all-start.1
  346.6 15.7 %all-to-all-done.1 = bf16[2,384,768]{2,0,1:T(2,128)(2,1)S(1)} async-done(((bf16[2,384,768]{2,0,1:T(2,128)(2,1)}), bf16[2,384,768]{2,0,1:T(2,128)(2,1)S(1)}, u32[]{:S(2)}, u32[]{:S(2)}) %all-to-all-start.1) | async-done | bytes 1179680 | tf_op jit(solution)/shard_map/all_to_all | solution.py:147
  363.1 2.9 all-to-all-start.3
  367.7 1.8 fusion.114
  373.5 5.4 %all-to-all-done.3 = f32[32,2,1536]{2,1,0:T(2,128)S(1)} async-done(((f32[32,2,1536]{2,1,0:T(2,128)}), f32[32,2,1536]{2,1,0:T(2,128)S(1)}, u32[]{:S(2)}, u32[]{:S(2)}) %all-to-all-start.3) | async-done | bytes 393248 | tf_op jit(solution)/shard_map/all_to_all | solution.py:51
  (304 shorter events, 43.5 us)
Async XLA Ops:
  7.2 145.3 %all-gather.2.cloned.1.call-start = ((), (), s32[]{:S(2)}) async-start(), calls=%async_computation.6 | async-start | bytes 7077888 | tf_op jit(solution)/shard_map/all_gather | solution.py:88
  8.3 9.5 %collective-permute-start = (bf16[1,3,32,1536]{3,2,1,0:T(8,128)(2,1)S(1)}, bf16[1,3,32,1536]{3,2,1,0:T(8,128)(2,1)S(1)}, u32[]{:S(2)}, u32[]{:S(2)}) collective-permute-start(bf16[1,3,32,1536]{3,2,1,0:T(8,128)(2,1)S(1)} %get-tuple-element.133), channel_id=1, source_target_pairs={{0,1},{1,2},{2,3},{4,5},{5,6},{6,7},{8,9},{9,10},{10,11},{12,13},{... | collective-permute-start | bytes 884744 | tf_op jit(solution)/shard_map/ppermute | solution.py:25
  10.7 7.1 %collective-permute-start.1 = (bf16[1,3,32,1536]{3,2,1,0:T(8,128)(2,1)S(1)}, bf16[1,3,32,1536]{3,2,1,0:T(8,128)(2,1)S(1)}, u32[]{:S(2)}, u32[]{:S(2)}) collective-permute-start(bf16[1,3,32,1536]{3,2,1,0:T(8,128)(2,1)S(1)} %get-tuple-element.134), channel_id=1, source_target_pairs={{1,0},{2,1},{3,2},{5,4},{6,5},{7,6},{9,8},{10,9},{11,10},{13,12},{... | collective-permute-start | bytes 884744 | tf_op jit(solution)/shard_map/ppermute | solution.py:26
  13.4 15.1 %copy-start.9 = (f32[1536]{0:T(1024)}, f32[1536]{0:T(1024)S(1)}, u32[]{:S(2)}) copy-start(f32[1536]{0:T(1024)S(1)} %get-tuple-element.111) | copy-start | bytes 18436
  13.4 15.1 %copy-start.11 = (f32[1536]{0:T(1024)}, f32[1536]{0:T(1024)S(1)}, u32[]{:S(2)}) copy-start(f32[1536]{0:T(1024)S(1)} %get-tuple-element.112) | copy-start | bytes 18436
  13.4 15.1 %copy-start.13 = (f32[1536]{0:T(1024)}, f32[1536]{0:T(1024)S(1)}, u32[]{:S(2)}) copy-start(f32[1536]{0:T(1024)S(1)} %get-tuple-element.113) | copy-start | bytes 18436
  13.4 15.1 %copy-start.15 = (f32[1536]{0:T(1024)}, f32[1536]{0:T(1024)S(1)}, u32[]{:S(2)}) copy-start(f32[1536]{0:T(1024)S(1)} %get-tuple-element.114) | copy-start | bytes 18436
  13.4 15.1 %copy-start.17 = (f32[1536]{0:T(1024)}, f32[1536]{0:T(1024)S(1)}, u32[]{:S(2)}) copy-start(f32[1536]{0:T(1024)S(1)} %get-tuple-element.115) | copy-start | bytes 18436
  13.4 15.1 %copy-start.19 = (f32[1536]{0:T(1024)}, f32[1536]{0:T(1024)S(1)}, u32[]{:S(2)}) copy-start(f32[1536]{0:T(1024)S(1)} %get-tuple-element.116) | copy-start | bytes 18436
  13.4 15.1 %copy-start.21 = (f32[1536]{0:T(1024)}, f32[1536]{0:T(1024)S(1)}, u32[]{:S(2)}) copy-start(f32[1536]{0:T(1024)S(1)} %get-tuple-element.117) | copy-start | bytes 18436
  13.4 15.1 %copy-start.23 = (f32[1536]{0:T(1024)}, f32[1536]{0:T(1024)S(1)}, u32[]{:S(2)}) copy-start(f32[1536]{0:T(1024)S(1)} %get-tuple-element.118) | copy-start | bytes 18436
  13.5 15.1 %copy-start.25 = (f32[1536]{0:T(1024)}, f32[1536]{0:T(1024)S(1)}, u32[]{:S(2)}) copy-start(f32[1536]{0:T(1024)S(1)} %get-tuple-element.119) | copy-start | bytes 18436
  13.5 15.1 %copy-start.27 = (f32[1536]{0:T(1024)}, f32[1536]{0:T(1024)S(1)}, u32[]{:S(2)}) copy-start(f32[1536]{0:T(1024)S(1)} %get-tuple-element.120) | copy-start | bytes 18436
  15.2 13.3 %copy-start.29 = (f32[1536]{0:T(1024)}, f32[1536]{0:T(1024)S(1)}, u32[]{:S(2)}) copy-start(f32[1536]{0:T(1024)S(1)} %get-tuple-element.72) | copy-start | bytes 18436
  15.2 13.3 %copy-start.31 = (f32[1536]{0:T(1024)}, f32[1536]{0:T(1024)S(1)}, u32[]{:S(2)}) copy-start(f32[1536]{0:T(1024)S(1)} %get-tuple-element.73) | copy-start | bytes 18436
  15.2 13.3 %copy-start.33 = (f32[1536]{0:T(1024)}, f32[1536]{0:T(1024)S(1)}, u32[]{:S(2)}) copy-start(f32[1536]{0:T(1024)S(1)} %get-tuple-element.74) | copy-start | bytes 18436
  15.2 13.3 %copy-start.35 = (f32[1536]{0:T(1024)}, f32[1536]{0:T(1024)S(1)}, u32[]{:S(2)}) copy-start(f32[1536]{0:T(1024)S(1)} %get-tuple-element.75) | copy-start | bytes 18436
  15.2 13.3 %copy-start.37 = (f32[1536]{0:T(1024)}, f32[1536]{0:T(1024)S(1)}, u32[]{:S(2)}) copy-start(f32[1536]{0:T(1024)S(1)} %get-tuple-element.76) | copy-start | bytes 18436
  15.3 13.3 %copy-start.39 = (f32[1536]{0:T(1024)}, f32[1536]{0:T(1024)S(1)}, u32[]{:S(2)}) copy-start(f32[1536]{0:T(1024)S(1)} %get-tuple-element.77) | copy-start | bytes 18436
  15.3 13.3 %copy-start.41 = (f32[1536]{0:T(1024)}, f32[1536]{0:T(1024)S(1)}, u32[]{:S(2)}) copy-start(f32[1536]{0:T(1024)S(1)} %get-tuple-element.78) | copy-start | bytes 18436
  15.3 13.3 %copy-start.43 = (f32[1536]{0:T(1024)}, f32[1536]{0:T(1024)S(1)}, u32[]{:S(2)}) copy-start(f32[1536]{0:T(1024)S(1)} %get-tuple-element.79) | copy-start | bytes 18436
  15.3 13.3 %copy-start.45 = (f32[1536]{0:T(1024)}, f32[1536]{0:T(1024)S(1)}, u32[]{:S(2)}) copy-start(f32[1536]{0:T(1024)S(1)} %get-tuple-element.80) | copy-start | bytes 18436
  30.5 203.8 %reduce-scatter.3.cloned.1.call-start = ((), (), s32[]{:S(2)}) async-start(), calls=%async_computation.7 | async-start | bytes 7077888 | tf_op jit(solution)/shard_map/reduce_scatter | solution.py:106
  171.8 150.3 %reduce-scatter.5.cloned.1.call-start = ((), (), s32[]{:S(2)}) async-start(), calls=%async_computation.8 | async-start | bytes 5898240 | tf_op jit(solution)/shard_map/reduce_scatter | solution.py:117
  258.9 9.2 %collective-permute-start.2 = (bf16[1,3,32,1536]{3,2,1,0:T(8,128)(2,1)S(1)}, bf16[1,3,32,1536]{3,2,1,0:T(8,128)(2,1)S(1)}, u32[]{:S(2)}, u32[]{:S(2)}) collective-permute-start(bf16[1,3,32,1536]{3,2,1,0:T(8,128)(2,1)S(1)} %get-tuple-element.131), channel_id=1, source_target_pairs={{0,1},{1,2},{2,3},{4,5},{5,6},{6,7},{8,9},{9,10},{10,11},{12,13},{... | collective-permute-start | bytes 884744 | tf_op jit(solution)/shard_map/ppermute | solution.py:25
  260.7 7.4 %collective-permute-start.3 = (bf16[1,3,32,1536]{3,2,1,0:T(8,128)(2,1)S(1)}, bf16[1,3,32,1536]{3,2,1,0:T(8,128)(2,1)S(1)}, u32[]{:S(2)}, u32[]{:S(2)}) collective-permute-start(bf16[1,3,32,1536]{3,2,1,0:T(8,128)(2,1)S(1)} %get-tuple-element.132), channel_id=1, source_target_pairs={{1,0},{2,1},{3,2},{5,4},{6,5},{7,6},{9,8},{10,9},{11,10},{13,12},{... | collective-permute-start | bytes 884744 | tf_op jit(solution)/shard_map/ppermute | solution.py:26
  324.7 18.3 %all-to-all-start.2 = ((f32[32,2,1536]{2,1,0:T(2,128)}), f32[32,2,1536]{2,1,0:T(2,128)S(1)}, u32[]{:S(2)}, u32[]{:S(2)}) async-start(f32[32,2,1536]{2,1,0:T(2,128)} %reshape.566), calls=%async_computation.4 | async-start | bytes 786432 | tf_op jit(solution)/shard_map/all_to_all | solution.py:49
  332.0 34.1 %copy-start.1 = (bf16[1,4,32,1536]{3,2,1,0:T(8,128)(2,1)S(1)}, bf16[1,4,32,1536]{3,2,1,0:T(8,128)(2,1)}, u32[]{:S(2)}) copy-start(bf16[1,4,32,1536]{3,2,1,0:T(8,128)(2,1)} %param.7) | copy-start | bytes 1179652
  332.0 34.1 %copy-start.4 = (f32[1,128,1536]{2,1,0:T(8,128)S(1)}, f32[1,128,1536]{2,1,0:T(8,128)}, u32[]{:S(2)}) copy-start(f32[1,128,1536]{2,1,0:T(8,128)} %get-tuple-element.130) | copy-start | bytes 2359300
  332.0 34.1 %copy-start.88 = (f32[1536]{0:T(1024)S(1)}, f32[1536]{0:T(1024)}, u32[]{:S(2)}) copy-start(f32[1536]{0:T(1024)} %param.12) | copy-start | bytes 18436
  342.9 19.4 %all-to-all-start.1 = ((bf16[2,384,768]{2,0,1:T(2,128)(2,1)}), bf16[2,384,768]{2,0,1:T(2,128)(2,1)S(1)}, u32[]{:S(2)}, u32[]{:S(2)}) async-start(bf16[2,384,768]{2,0,1:T(2,128)(2,1)} %copy.26), calls=%async_computation.3 | async-start | bytes 2359296 | tf_op jit(solution)/shard_map/all_to_all | solution.py:147
  363.1 15.8 %all-to-all-start.3 = ((f32[32,2,1536]{2,1,0:T(2,128)}), f32[32,2,1536]{2,1,0:T(2,128)S(1)}, u32[]{:S(2)}, u32[]{:S(2)}) async-start(f32[32,2,1536]{2,1,0:T(2,128)} %broadcast_in_dim.11), calls=%async_computation.5 | async-start | bytes 786432 | tf_op jit(solution)/shard_map/all_to_all | solution.py:51
  (79 other events, 509.1 us)
Sparse Core Ops, SparseCore 0:
  30.6 82.8 all-gather.1
  171.9 62.3 reduce-scatter.2
  236.8 85.2 reduce-scatter.4

commit v13 on v10

--- a/solution.py
+++ b/solution.py
@@ -60,12 +60,13 @@
     dp_size, row_size = lax.axis_size("dp"), lax.axis_size("rows")
     block_c, hid_f = w_up.shape
     sub = hid_f // row_size
-    pieces = jnp.stack([w_up, w_down.T]).reshape(2, block_c, row_size, sub).transpose(0, 2, 1, 3)
-    pieces = jnp.broadcast_to(pieces[:, None], (2, dp_size, row_size, block_c, sub))
-    pieces = pieces.reshape(2, dp_size * row_size, block_c, sub)
-    both = lax.all_to_all(pieces, ("dp", "rows"), 1, 1, tiled=True)
-    both = both.reshape(2, dp_size * row_size * block_c, sub)
-    up_loc, down_t = both[0], both[1]
+    pieces = w_up.reshape(block_c, row_size, sub).transpose(1, 0, 2)
+    pieces = jnp.broadcast_to(pieces[None], (dp_size, row_size, block_c, sub))
+    pieces = pieces.reshape(dp_size * row_size, block_c, sub)
+    up_loc = lax.all_to_all(pieces, ("dp", "rows"), 0, 0, tiled=True)
+    up_loc = up_loc.reshape(dp_size * row_size * block_c, sub)
+    down_loc = lax.all_to_all(w_down, "rows", 0, 1, tiled=True)
+    down_loc = lax.all_gather(down_loc, "dp", axis=1, tiled=True)
     cotan = d_out.reshape(cells, width).astype(jnp.float32)
     back = (cotan * layer_scale).astype(jnp.bfloat16)
     rimmed = padded_2(feature_maps, (("rows", 1),), 3)
@@ -89,13 +90,13 @@
     gathered, back_all = pair[0], pair[1]
     hidden = jnp.dot(gathered, up_loc, preferred_element_type=jnp.float32)
     active = gelu_exact(hidden).astype(jnp.bfloat16)
-    mlp_terms = lax.dot_general(
-        active, down_t, contract_cols, preferred_element_type=jnp.float32
-    )
+    mlp_terms = jnp.dot(active, down_loc, preferred_element_type=jnp.float32)
     down_part_t = lax.dot_general(
         back_all, active, contract_rows, preferred_element_type=jnp.float32
     )
-    slope_in = jnp.dot(back_all, down_t, preferred_element_type=jnp.float32)
+    slope_in = lax.dot_general(
+        back_all, down_loc, contract_cols, preferred_element_type=jnp.float32
+    )
     hidden_grad = (slope_in * gelu_slope(hidden)).astype(jnp.bfloat16)
     up_part = lax.dot_general(
         gathered, hidden_grad, contract_rows, preferred_element_type=jnp.float32

time: 375 us -> 373 us (level)
  blocking collectives: 113 us -> 0 us
  waiting for transfers between devices: 121 us -> 215 us
  starting transfers between devices: 21.3 us -> 33.3 us
  matrix products: 24.7 us -> 32.3 us
    all_to_all x1 -> x0, blocking collectives: 113 us -> none  [body(): both = lax.all_to_all(pieces, ('dp', 'rows'), 1, 1, tiled=True)]
    all_to_all x0 -> x2, waiting for transfers between devices: none -> 51.9 us  [the longest x1 44.9 us: body(): up_loc = lax.all_to_all(pieces, ('dp', 'rows'), 0, 0, tiled=True)]
    all_gather x0 -> x1, waiting for transfers between devices: none -> 43.3 us  [body(): down_loc = lax.all_gather(down_loc, 'dp', axis=1, tiled=True)]
    all_to_all x0 -> x2, starting transfers between devices: none -> 11.4 us  [the longest x1 6.13 us: body(): down_loc = lax.all_to_all(w_down, 'rows', 0, 1, tiled=True)]
    another operation x2 -> x0, local copies, waits for them, and re-layouts: 4.24 us -> none  [body(): jnp.stack([w_up, w_down.T]).reshape(2, block_c, row_size, sub)]
  transfers between devices with their start and end apart: 10 -> 13, of which waited for: 6 -> 9; matrix products, arithmetic and copies ran while one was open for 15% -> 17% of each run, Pallas kernels for 0% -> 0%
where the time goes in v13:
time: 373 us; the launch traced here: 369 us
  waiting for transfers between devices  215 us (58%)
  other arithmetic  38.1 us (10%)
  local copies, waits for them, and re-layouts  34.9 us (9%)
  starting transfers between devices  33.3 us (9%)
  matrix products  32.3 us (9%)
  between operations  15.8 us (4%)
    reduce_scatter x1, waiting for transfers between devices, body(): lax.psum_scatter(jnp.stack([mlp_terms, norm_terms]).astype(jnp.bfloat16),...  47.6 us
    all_to_all x1, waiting for transfers between devices, body(): up_loc = lax.all_to_all(pieces, ('dp', 'rows'), 0, 0, tiled=True)  44.9 us
    all_gather x1, waiting for transfers between devices, body(): down_loc = lax.all_gather(down_loc, 'dp', axis=1, tiled=True)  43.3 us
    reduce_scatter x1, waiting for transfers between devices, body(): lax.psum_scatter(grad_parts, 'dp', scatter_dimension=1, tiled=True)  24.5 us
    all_to_all x1, waiting for transfers between devices, small_sums(): lax.all_to_all(spread, every, 0, 0, tiled=True)  15.3 us
    all_to_all x1, waiting for transfers between devices, body(): lax.all_to_all(grad_sums, 'rows', 1, 2, tiled=True).astype(jnp.float32)  15 us
    all_to_all x1, waiting for transfers between devices, small_sums(): lax.all_to_all(packed.reshape(devices, per, width), every, 0, 0, tiled=True)  13.2 us
    reduce_sum x1, other arithmetic, body(): average = jnp.mean(flat, axis=-1, keepdims=True)  9.44 us
  transfers between devices with their start and end apart: 13, of which 9 were waited for; matrix products, arithmetic and copies ran while one was open for 17% of the time, Pallas kernels for 0%

profile of v13, /device:TPU:0, one launch (start us, length us, event | category | flops | bytes accessed | tf_op | source)
XLA Modules:
  0.0 369.0 jit_solution(16988529015988435468)
XLA Ops:
  8.3 2.4 collective-permute-start
  15.4 2.3 slice_reduce_fusion.49
  19.0 9.4 %fusion.112 = (f32[4,32]{1,0:T(4,128)S(1)}, f32[1,4,32,1536]{3,2,1,0:T(8,128)S(1)}) fusion(f32[1536]{0:T(1024)S(1)} %get-tuple-element.119, f32[1536]{0:T(1024)S(1)} %get-tuple-element.120, f32[1536]{0:T(1024)S(1)} %get-tuple-element.73, f32[1536]{0:T(1024)S(1)} %get-tuple-element.74, f32[1,10,32,1536]{3,2,1,0:T(8,128)S(1)} %maximum_convert_fusion, ...), kind=kLoop, calls=%fused_computation.334 | loop fusion | flops 19267456 | bytes 8641024 | tf_op jit(solution)/shard_map/reduce_sum | solution.py:83
  31.7 6.1 %all-to-all-start.1 = ((bf16[4,768,96]{1,2,0:T(8,128)(2,1)}), bf16[4,768,96]{1,2,0:T(8,128)(2,1)S(1)}, u32[]{:S(2)}, u32[]{:S(2)}) async-start(bf16[4,768,96]{1,2,0:T(8,128)(2,1)} %bitcast.94), calls=%async_computation.1 | async-start | bytes 1179648 | tf_op jit(solution)/shard_map/all_to_all | solution.py:68
  37.8 2.5 reshape.555
  42.3 7.0 %all-to-all-done.1 = bf16[4,768,96]{1,2,0:T(8,128)(2,1)S(1)} async-done(((bf16[4,768,96]{1,2,0:T(8,128)(2,1)}), bf16[4,768,96]{1,2,0:T(8,128)(2,1)S(1)}, u32[]{:S(2)}, u32[]{:S(2)}) %all-to-all-start.1) | async-done | bytes 589856 | tf_op jit(solution)/shard_map/all_to_all | solution.py:68
  49.3 2.9 broadcast_in_dim.8
  52.2 5.3 %all-to-all-start = ((bf16[16,96,768]{2,1,0:T(8,128)(2,1)}), bf16[16,96,768]{2,1,0:T(8,128)(2,1)}, u32[]{:S(2)}, u32[]{:S(2)}) async-start(bf16[16,96,768]{2,1,0:T(8,128)(2,1)} %bitcast.87), calls=%async_computation | async-start | bytes 4718592 | tf_op jit(solution)/shard_map/all_to_all | solution.py:66
  58.5 44.9 %all-to-all-done = bf16[16,96,768]{2,1,0:T(8,128)(2,1)} async-done(((bf16[16,96,768]{2,1,0:T(8,128)(2,1)}), bf16[16,96,768]{2,1,0:T(8,128)(2,1)}, u32[]{:S(2)}, u32[]{:S(2)}) %all-to-all-start) | async-done | bytes 2359328 | tf_op jit(solution)/shard_map/all_to_all | solution.py:66
  103.4 7.4 %multiply_convert_fusion = (bf16[1024,768]{1,0:T(8,128)(2,1)}, f32[1024,768]{1,0:T(8,128)}) fusion(bf16[1536,768]{1,0:T(8,128)(2,1)} %bitcast.5, bf16[2,1024,1536]{2,1,0:T(8,128)(2,1)} %all-gather.3.cloned.1.call-done), kind=kOutput, calls=%fused_computation.101 | convolution fusion | flops 2419851264 | bytes 10223616 | tf_op jit(solution)/shard_map/dot_general | solution.py:91
  110.8 43.3 %all-gather.5.cloned.1.call-done = bf16[768,1536]{0,1:T(8,128)(2,1)} async-done(((bf16[768,384]{0,1:T(8,128)(2,1)}), bf16[768,1536]{0,1:T(8,128)(2,1)}) %all-gather.5.cloned.1.call-update) | async-done | bytes 2359312 | tf_op jit(solution)/shard_map/all_gather | solution.py:69
  154.1 6.6 %fusion.7 = bf16[1024,768]{1,0:T(8,128)(2,1)S(1)} fusion(f32[1024,768]{1,0:T(8,128)} %get-tuple-element.134, bf16[768,1536]{0,1:T(8,128)(2,1)} %all-gather.5.cloned.1.call-done, bf16[2,1024,1536]{2,1,0:T(8,128)(2,1)} %all-gather.3.cloned.1.call-done), kind=kOutput, calls=%fused_computation.98 | convolution fusion | flops 2423783424 | bytes 10223616 | tf_op jit(solution)/shard_map/dot_general | solution.py:97
  160.8 5.1 %fusion.1 = bf16[1,1024,1536]{2,1,0:T(8,128)(2,1)S(1)} fusion(bf16[1024,768]{1,0:T(8,128)(2,1)S(1)} %fusion.7, bf16[1536,768]{1,0:T(8,128)(2,1)} %bitcast.5), kind=kOutput, calls=%fused_computation.92 | convolution fusion | flops 2417491968 | bytes 7077888 | tf_op jit(solution)/shard_map/dot_general | solution.py:104
  165.9 2.9 fusion
  168.8 3.2 pad_maximum_fusion
  172.3 5.1 %fusion.9 = bf16[1,1536,768]{2,1,0:T(8,128)(2,1)S(1)} fusion(bf16[1024,768]{1,0:T(8,128)(2,1)} %get-tuple-element.133, bf16[2,1024,1536]{2,1,0:T(8,128)(2,1)} %all-gather.3.cloned.1.call-done), kind=kOutput, calls=%fused_computation.104 | convolution fusion | flops 2417098752 | bytes 7077888 | tf_op jit(solution)/shard_map/dot_general | solution.py:94
  177.5 5.0 %fusion.8 = bf16[1,1536,768]{2,1,0:T(8,128)(2,1)S(1)} fusion(bf16[1024,768]{1,0:T(8,128)(2,1)S(1)} %copy-done.101, bf16[2,1024,1536]{2,1,0:T(8,128)(2,1)} %all-gather.3.cloned.1.call-done), kind=kOutput, calls=%fused_computation.103 | convolution fusion | flops 2417098752 | bytes 7077888 | tf_op jit(solution)/shard_map/dot_general | solution.py:101
  182.5 2.6 pad_maximum_fusion.1
  185.2 47.6 %reduce-scatter.3.cloned.1.call-done = bf16[2,128,1536]{2,1,0:T(8,128)(2,1)} async-done(((bf16[2,1024,1536]{2,1,0:T(8,128)(2,1)}), bf16[2,128,1536]{2,1,0:T(8,128)(2,1)}) %reduce-scatter.3.cloned.1.call-update) | async-done | bytes 786448 | tf_op jit(solution)/shard_map/reduce_scatter | solution.py:107
  234.1 2.1 fusion.106
  243.5 2.4 multiply_reduce_fusion
  251.6 4.6 %all-to-all-start.2 = ((f32[32,2,1536]{2,1,0:T(2,128)}), f32[32,2,1536]{2,1,0:T(2,128)S(1)}, u32[]{:S(2)}, u32[]{:S(2)}) async-start(f32[32,2,1536]{2,1,0:T(2,128)} %reshape.559), calls=%async_computation.4 | async-start | bytes 786432 | tf_op jit(solution)/shard_map/all_to_all | solution.py:49
  256.6 2.3 collective-permute-start.2
  260.5 3.0 collective-permute-done.3
  263.7 13.2 %all-to-all-done.2 = f32[32,2,1536]{2,1,0:T(2,128)S(1)} async-done(((f32[32,2,1536]{2,1,0:T(2,128)}), f32[32,2,1536]{2,1,0:T(2,128)S(1)}, u32[]{:S(2)}, u32[]{:S(2)}) %all-to-all-start.2) | async-done | bytes 393248 | tf_op jit(solution)/shard_map/all_to_all | solution.py:49
  277.9 5.7 %all-to-all-start.3 = ((f32[32,2,1536]{2,1,0:T(2,128)}), f32[32,2,1536]{2,1,0:T(2,128)S(1)}, u32[]{:S(2)}, u32[]{:S(2)}) async-start(f32[32,2,1536]{2,1,0:T(2,128)} %broadcast_in_dim.11), calls=%async_computation.5 | async-start | bytes 786432 | tf_op jit(solution)/shard_map/all_to_all | solution.py:51
  284.0 7.4 %fusion.99 = bf16[1,4,32,1536]{3,2,1,0:T(8,128)(2,1)} fusion(f32[1,10,32,1536]{3,2,1,0:T(8,128)S(1)} %maximum_convert_fusion.1, f32[1536]{0:T(1024)S(1)} %copy-done.25, f32[1536]{0:T(1024)S(1)} %copy-done.27, f32[1536]{0:T(1024)S(1)} %copy-done.31, f32[1536]{0:T(1024)S(1)} %copy-done.33, f32[1536]{0:T(1024)S(1)} %copy-done.35, f32[1536]{0:T(1024)S(1)} %copy-done.37, ...), kind=kLoop, calls=%fused_computation.197 | loop fusion | flops 19660800 | bytes 8640512 | tf_op jit(solution)/shard_map/convert_element_type | solution.py:143
  291.4 15.3 %all-to-all-done.3 = f32[32,2,1536]{2,1,0:T(2,128)S(1)} async-done(((f32[32,2,1536]{2,1,0:T(2,128)}), f32[32,2,1536]{2,1,0:T(2,128)S(1)}, u32[]{:S(2)}, u32[]{:S(2)}) %all-to-all-start.3) | async-done | bytes 393248 | tf_op jit(solution)/shard_map/all_to_all | solution.py:51
  308.4 24.5 %reduce-scatter.5.cloned.1.call-done = bf16[2,384,768]{2,1,0:T(8,128)(2,1)} async-done(((bf16[2,1536,768]{2,1,0:T(8,128)(2,1)}), bf16[2,384,768]{2,1,0:T(8,128)(2,1)}) %reduce-scatter.5.cloned.1.call-update) | async-done | bytes 1179664 | tf_op jit(solution)/shard_map/reduce_scatter | solution.py:118
  333.0 3.5 copy.37
  336.4 3.5 all-to-all-start.4
  340.9 15.0 %all-to-all-done.4 = bf16[2,384,768]{2,0,1:T(2,128)(2,1)S(1)} async-done(((bf16[2,384,768]{2,0,1:T(2,128)(2,1)}), bf16[2,384,768]{2,0,1:T(2,128)(2,1)S(1)}, u32[]{:S(2)}, u32[]{:S(2)}) %all-to-all-start.4) | async-done | bytes 1179680 | tf_op jit(solution)/shard_map/all_to_all | solution.py:148
  (308 shorter events, 38.8 us)
Async XLA Ops:
  7.2 96.2 %all-gather.3.cloned.1.call-start = ((), (), s32[]{:S(2)}) async-start(), calls=%async_computation.7 | async-start | bytes 7077888 | tf_op jit(solution)/shard_map/all_gather | solution.py:89
  8.3 9.5 %collective-permute-start = (bf16[1,3,32,1536]{3,2,1,0:T(8,128)(2,1)S(1)}, bf16[1,3,32,1536]{3,2,1,0:T(8,128)(2,1)S(1)}, u32[]{:S(2)}, u32[]{:S(2)}) collective-permute-start(bf16[1,3,32,1536]{3,2,1,0:T(8,128)(2,1)S(1)} %get-tuple-element.131), channel_id=1, source_target_pairs={{0,1},{1,2},{2,3},{4,5},{5,6},{6,7},{8,9},{9,10},{10,11},{12,13},{... | collective-permute-start | bytes 884744 | tf_op jit(solution)/shard_map/ppermute | solution.py:25
  10.7 7.1 %collective-permute-start.1 = (bf16[1,3,32,1536]{3,2,1,0:T(8,128)(2,1)S(1)}, bf16[1,3,32,1536]{3,2,1,0:T(8,128)(2,1)S(1)}, u32[]{:S(2)}, u32[]{:S(2)}) collective-permute-start(bf16[1,3,32,1536]{3,2,1,0:T(8,128)(2,1)S(1)} %get-tuple-element.132), channel_id=1, source_target_pairs={{1,0},{2,1},{3,2},{5,4},{6,5},{7,6},{9,8},{10,9},{11,10},{13,12},{... | collective-permute-start | bytes 884744 | tf_op jit(solution)/shard_map/ppermute | solution.py:26
  31.7 17.6 %all-to-all-start.1 = ((bf16[4,768,96]{1,2,0:T(8,128)(2,1)}), bf16[4,768,96]{1,2,0:T(8,128)(2,1)S(1)}, u32[]{:S(2)}, u32[]{:S(2)}) async-start(bf16[4,768,96]{1,2,0:T(8,128)(2,1)} %bitcast.94), calls=%async_computation.1 | async-start | bytes 1179648 | tf_op jit(solution)/shard_map/all_to_all | solution.py:68
  52.2 51.2 %all-to-all-start = ((bf16[16,96,768]{2,1,0:T(8,128)(2,1)}), bf16[16,96,768]{2,1,0:T(8,128)(2,1)}, u32[]{:S(2)}, u32[]{:S(2)}) async-start(bf16[16,96,768]{2,1,0:T(8,128)(2,1)} %bitcast.87), calls=%async_computation | async-start | bytes 4718592 | tf_op jit(solution)/shard_map/all_to_all | solution.py:66
  57.5 96.6 %all-gather.5.cloned.1.call-start = ((), (), s32[]{:S(2)}) async-start(), calls=%async_computation.8 | async-start | bytes 2949120 | tf_op jit(solution)/shard_map/all_gather | solution.py:69
  58.2 174.5 %reduce-scatter.3.cloned.1.call-start = ((), (), s32[]{:S(2)}) async-start(), calls=%async_computation.9 | async-start | bytes 7077888 | tf_op jit(solution)/shard_map/reduce_scatter | solution.py:107
  172.1 160.9 %reduce-scatter.5.cloned.1.call-start = ((), (), s32[]{:S(2)}) async-start(), calls=%async_computation.10 | async-start | bytes 5898240 | tf_op jit(solution)/shard_map/reduce_scatter | solution.py:118
  251.6 25.3 %all-to-all-start.2 = ((f32[32,2,1536]{2,1,0:T(2,128)}), f32[32,2,1536]{2,1,0:T(2,128)S(1)}, u32[]{:S(2)}, u32[]{:S(2)}) async-start(f32[32,2,1536]{2,1,0:T(2,128)} %reshape.559), calls=%async_computation.4 | async-start | bytes 786432 | tf_op jit(solution)/shard_map/all_to_all | solution.py:49
  256.2 27.3 %copy-start.3 = (bf16[1,4,32,1536]{3,2,1,0:T(8,128)(2,1)S(1)}, bf16[1,4,32,1536]{3,2,1,0:T(8,128)(2,1)}, u32[]{:S(2)}) copy-start(bf16[1,4,32,1536]{3,2,1,0:T(8,128)(2,1)} %param.13) | copy-start | bytes 1179652
  256.2 27.3 %copy-start.9 = (f32[1536]{0:T(1024)S(1)}, f32[1536]{0:T(1024)}, u32[]{:S(2)}) copy-start(f32[1536]{0:T(1024)} %copy-done.8) | copy-start | bytes 18436
  256.3 27.3 %copy-start.11 = (f32[1536]{0:T(1024)S(1)}, f32[1536]{0:T(1024)}, u32[]{:S(2)}) copy-start(f32[1536]{0:T(1024)} %copy-done.10) | copy-start | bytes 18436
  256.3 27.3 %copy-start.13 = (f32[1536]{0:T(1024)S(1)}, f32[1536]{0:T(1024)}, u32[]{:S(2)}) copy-start(f32[1536]{0:T(1024)} %copy-done.12) | copy-start | bytes 18436
  256.3 27.3 %copy-start.15 = (f32[1536]{0:T(1024)S(1)}, f32[1536]{0:T(1024)}, u32[]{:S(2)}) copy-start(f32[1536]{0:T(1024)} %copy-done.14) | copy-start | bytes 18436
  256.3 27.3 %copy-start.17 = (f32[1536]{0:T(1024)S(1)}, f32[1536]{0:T(1024)}, u32[]{:S(2)}) copy-start(f32[1536]{0:T(1024)} %copy-done.16) | copy-start | bytes 18436
  256.3 27.3 %copy-start.19 = (f32[1536]{0:T(1024)S(1)}, f32[1536]{0:T(1024)}, u32[]{:S(2)}) copy-start(f32[1536]{0:T(1024)} %copy-done.18) | copy-start | bytes 18436
  256.3 27.3 %copy-start.21 = (f32[1536]{0:T(1024)S(1)}, f32[1536]{0:T(1024)}, u32[]{:S(2)}) copy-start(f32[1536]{0:T(1024)} %copy-done.20) | copy-start | bytes 18436
  256.3 27.3 %copy-start.23 = (f32[1536]{0:T(1024)S(1)}, f32[1536]{0:T(1024)}, u32[]{:S(2)}) copy-start(f32[1536]{0:T(1024)} %copy-done.22) | copy-start | bytes 18436
  256.3 27.3 %copy-start.25 = (f32[1536]{0:T(1024)S(1)}, f32[1536]{0:T(1024)}, u32[]{:S(2)}) copy-start(f32[1536]{0:T(1024)} %copy-done.24) | copy-start | bytes 18436
  256.3 27.3 %copy-start.27 = (f32[1536]{0:T(1024)S(1)}, f32[1536]{0:T(1024)}, u32[]{:S(2)}) copy-start(f32[1536]{0:T(1024)} %copy-done.26) | copy-start | bytes 18436
  256.3 27.3 %copy-start.29 = (f32[1536]{0:T(1024)S(1)}, f32[1536]{0:T(1024)}, u32[]{:S(2)}) copy-start(f32[1536]{0:T(1024)} %copy-done.28) | copy-start | bytes 18436
  256.4 27.3 %copy-start.31 = (f32[1536]{0:T(1024)S(1)}, f32[1536]{0:T(1024)}, u32[]{:S(2)}) copy-start(f32[1536]{0:T(1024)} %copy-done.30) | copy-start | bytes 18436
  256.4 27.3 %copy-start.33 = (f32[1536]{0:T(1024)S(1)}, f32[1536]{0:T(1024)}, u32[]{:S(2)}) copy-start(f32[1536]{0:T(1024)} %copy-done.32) | copy-start | bytes 18436
  256.4 27.3 %copy-start.35 = (f32[1536]{0:T(1024)S(1)}, f32[1536]{0:T(1024)}, u32[]{:S(2)}) copy-start(f32[1536]{0:T(1024)} %copy-done.34) | copy-start | bytes 18436
  256.4 27.3 %copy-start.37 = (f32[1536]{0:T(1024)S(1)}, f32[1536]{0:T(1024)}, u32[]{:S(2)}) copy-start(f32[1536]{0:T(1024)} %copy-done.36) | copy-start | bytes 18436
  256.6 3.9 %collective-permute-start.2 = (bf16[1,3,32,1536]{3,2,1,0:T(8,128)(2,1)S(1)}, bf16[1,3,32,1536]{3,2,1,0:T(8,128)(2,1)S(1)}, u32[]{:S(2)}, u32[]{:S(2)}) collective-permute-start(bf16[1,3,32,1536]{3,2,1,0:T(8,128)(2,1)S(1)} %get-tuple-element.129), channel_id=1, source_target_pairs={{0,1},{1,2},{2,3},{4,5},{5,6},{6,7},{8,9},{9,10},{10,11},{12,13},{... | collective-permute-start | bytes 884744 | tf_op jit(solution)/shard_map/ppermute | solution.py:25
  258.9 4.6 %collective-permute-start.3 = (bf16[1,3,32,1536]{3,2,1,0:T(8,128)(2,1)S(1)}, bf16[1,3,32,1536]{3,2,1,0:T(8,128)(2,1)S(1)}, u32[]{:S(2)}, u32[]{:S(2)}) collective-permute-start(bf16[1,3,32,1536]{3,2,1,0:T(8,128)(2,1)S(1)} %get-tuple-element.130), channel_id=1, source_target_pairs={{1,0},{2,1},{3,2},{5,4},{6,5},{7,6},{9,8},{10,9},{11,10},{13,12},{... | collective-permute-start | bytes 884744 | tf_op jit(solution)/shard_map/ppermute | solution.py:26
  277.9 28.8 %all-to-all-start.3 = ((f32[32,2,1536]{2,1,0:T(2,128)}), f32[32,2,1536]{2,1,0:T(2,128)S(1)}, u32[]{:S(2)}, u32[]{:S(2)}) async-start(f32[32,2,1536]{2,1,0:T(2,128)} %broadcast_in_dim.11), calls=%async_computation.5 | async-start | bytes 786432 | tf_op jit(solution)/shard_map/all_to_all | solution.py:51
  307.8 32.2 %copy-start.1 = (bf16[1,4,32,1536]{3,2,1,0:T(8,128)(2,1)S(1)}, bf16[1,4,32,1536]{3,2,1,0:T(8,128)(2,1)}, u32[]{:S(2)}) copy-start(bf16[1,4,32,1536]{3,2,1,0:T(8,128)(2,1)} %param.7) | copy-start | bytes 1179652
  307.8 32.2 %copy-start.4 = (f32[1,128,1536]{2,1,0:T(8,128)S(1)}, f32[1,128,1536]{2,1,0:T(8,128)}, u32[]{:S(2)}) copy-start(f32[1,128,1536]{2,1,0:T(8,128)} %get-tuple-element.128) | copy-start | bytes 2359300
  307.8 32.2 %copy-start.87 = (f32[1536]{0:T(1024)S(1)}, f32[1536]{0:T(1024)}, u32[]{:S(2)}) copy-start(f32[1536]{0:T(1024)} %param.12) | copy-start | bytes 18436
  336.4 19.4 %all-to-all-start.4 = ((bf16[2,384,768]{2,0,1:T(2,128)(2,1)}), bf16[2,384,768]{2,0,1:T(2,128)(2,1)S(1)}, u32[]{:S(2)}, u32[]{:S(2)}) async-start(bf16[2,384,768]{2,0,1:T(2,128)(2,1)} %copy.37), calls=%async_computation.6 | async-start | bytes 2359296 | tf_op jit(solution)/shard_map/all_to_all | solution.py:148
  (83 other events, 1257.2 us)
Sparse Core Ops, SparseCore 0:
  30.6 67.5 all-gather.2
  100.4 53.6 all-gather.4
  172.2 60.5 reduce-scatter.2
  235.0 97.8 reduce-scatter.4

commit v14 on v13

--- a/solution.py
+++ b/solution.py
@@ -114,8 +114,12 @@
     resid = feature_maps.reshape(cells, width).astype(jnp.float32)
     result = (resid + layer_scale * branch).astype(jnp.bfloat16).reshape(feature_maps.shape)
     scale_part = jnp.sum(cotan * branch, axis=0)
-    grad_parts = jnp.stack([up_part, down_part_t]).astype(jnp.bfloat16)
-    grad_sums = lax.psum_scatter(grad_parts, "dp", scatter_dimension=1, tiled=True)
+    down_blocks = down_part_t.astype(jnp.bfloat16).reshape(dp_size, -1, sub)
+    down_sum = lax.all_to_all(down_blocks, "dp", 0, 0, tiled=True).astype(jnp.float32).sum(0)
+    up_sum = lax.psum_scatter(
+        up_part.astype(jnp.bfloat16), "dp", scatter_dimension=0, tiled=True
+    ).astype(jnp.float32)
+    grad_sums = jnp.stack([up_sum, down_sum])
     gain_part = jnp.sum(norm_grad * normed, axis=0)
     scaled_grad = norm_grad * norm_gain
     conv_grad = rstd * (

time: 373 us -> 365 us (0.979)
  waiting for transfers between devices: 215 us -> 198 us
  other arithmetic: 38.1 us -> 42.2 us
    reduce_scatter x1, waiting for transfers between devices: 47.6 us -> 0.01 us  [body(): lax.psum_scatter(jnp.stack([mlp_terms, norm_terms]).astype(jnp.bfloat16),...]
    all_to_all x0 -> x1, waiting for transfers between devices: none -> 46.8 us  [body(): lax.all_to_all(down_blocks, 'dp', 0, 0, tiled=True).astype(jnp.float32)]
    all_to_all x1, waiting for transfers between devices: 13.2 us -> 0.01 us  [small_sums(): lax.all_to_all(packed.reshape(devices, per, width), every, 0, 0, tiled=True)]
    all_to_all x1, waiting for transfers between devices: 15 us -> 27.6 us  [body(): lax.all_to_all(grad_sums, 'rows', 1, 2, tiled=True).astype(jnp.float32)]
    all_to_all x1, waiting for transfers between devices: 15.3 us -> 4.93 us  [small_sums(): lax.all_to_all(spread, every, 0, 0, tiled=True)]
    all_to_all x0 -> x1, starting transfers between devices: none -> 4.54 us  [body(): lax.all_to_all(down_blocks, 'dp', 0, 0, tiled=True).astype(jnp.float32)]
  transfers between devices with their start and end apart: 13 -> 14, of which waited for: 9 -> 7; matrix products, arithmetic and copies ran while one was open for 17% -> 19% of each run, Pallas kernels for 0% -> 0%
where the time goes in v14:
time: 365 us; the launch traced here: 364 us
  waiting for transfers between devices  198 us (54%)
  other arithmetic  42.2 us (12%)
  local copies, waits for them, and re-layouts  36.3 us (10%)
  starting transfers between devices  36 us (10%)
  matrix products  35.6 us (10%)
  between operations  15.4 us (4%)
    all_to_all x1, waiting for transfers between devices, body(): lax.all_to_all(down_blocks, 'dp', 0, 0, tiled=True).astype(jnp.float32)  46.8 us
    all_to_all x1, waiting for transfers between devices, body(): up_loc = lax.all_to_all(pieces, ('dp', 'rows'), 0, 0, tiled=True)  44.9 us
    all_gather x1, waiting for transfers between devices, body(): down_loc = lax.all_gather(down_loc, 'dp', axis=1, tiled=True)  43.2 us
    all_to_all x1, waiting for transfers between devices, body(): lax.all_to_all(grad_sums, 'rows', 1, 2, tiled=True).astype(jnp.float32)  27.6 us
    reduce_scatter x1, waiting for transfers between devices, body(): lax.psum_scatter(up_part.astype(jnp.bfloat16), 'dp', scatter_dimension=0,...  22.9 us
    reduce_sum x1, other arithmetic, body(): average = jnp.mean(flat, axis=-1, keepdims=True)  9.44 us
    convert_element_type x1, other arithmetic, body(): grad_x = (d_out.astype(jnp.float32) + back_conv).astype(jnp.bfloat16)  7.84 us
    dot_general x1, matrix products, body(): hidden = jnp.dot(gathered, up_loc, preferred_element_type=jnp.float32)  7.49 us
  transfers between devices with their start and end apart: 14, of which 7 were waited for; matrix products, arithmetic and copies ran while one was open for 19% of the time, Pallas kernels for 0%

profile of v14, /device:TPU:0, one launch (start us, length us, event | category | flops | bytes accessed | tf_op | source)
XLA Modules:
  0.0 363.7 jit_solution(3533473465423472678)
XLA Ops:
  8.3 2.4 collective-permute-start
  15.4 2.5 slice_reduce_fusion.49
  19.1 9.4 %fusion.110 = (f32[4,32]{1,0:T(4,128)S(1)}, f32[1,4,32,1536]{3,2,1,0:T(8,128)S(1)}) fusion(f32[1536]{0:T(1024)S(1)} %get-tuple-element.119, f32[1536]{0:T(1024)S(1)} %get-tuple-element.120, f32[1536]{0:T(1024)S(1)} %get-tuple-element.73, f32[1536]{0:T(1024)S(1)} %get-tuple-element.74, f32[1,10,32,1536]{3,2,1,0:T(8,128)S(1)} %maximum_convert_fusion, ...), kind=kLoop, calls=%fused_computation.333 | loop fusion | flops 19267456 | bytes 8641024 | tf_op jit(solution)/shard_map/reduce_sum | solution.py:83
  31.8 6.1 %all-to-all-start.1 = ((bf16[4,768,96]{1,2,0:T(8,128)(2,1)}), bf16[4,768,96]{1,2,0:T(8,128)(2,1)S(1)}, u32[]{:S(2)}, u32[]{:S(2)}) async-start(bf16[4,768,96]{1,2,0:T(8,128)(2,1)} %bitcast.96), calls=%async_computation.1 | async-start | bytes 1179648 | tf_op jit(solution)/shard_map/all_to_all | solution.py:68
  38.0 2.5 reshape.555
  42.4 7.0 %all-to-all-done.1 = bf16[4,768,96]{1,2,0:T(8,128)(2,1)S(1)} async-done(((bf16[4,768,96]{1,2,0:T(8,128)(2,1)}), bf16[4,768,96]{1,2,0:T(8,128)(2,1)S(1)}, u32[]{:S(2)}, u32[]{:S(2)}) %all-to-all-start.1) | async-done | bytes 589856 | tf_op jit(solution)/shard_map/all_to_all | solution.py:68
  49.4 2.9 broadcast_in_dim.8
  52.3 5.3 %all-to-all-start = ((bf16[16,96,768]{2,1,0:T(8,128)(2,1)}), bf16[16,96,768]{2,1,0:T(8,128)(2,1)}, u32[]{:S(2)}, u32[]{:S(2)}) async-start(bf16[16,96,768]{2,1,0:T(8,128)(2,1)} %bitcast.87), calls=%async_computation | async-start | bytes 4718592 | tf_op jit(solution)/shard_map/all_to_all | solution.py:66
  58.6 44.9 %all-to-all-done = bf16[16,96,768]{2,1,0:T(8,128)(2,1)} async-done(((bf16[16,96,768]{2,1,0:T(8,128)(2,1)}), bf16[16,96,768]{2,1,0:T(8,128)(2,1)}, u32[]{:S(2)}, u32[]{:S(2)}) %all-to-all-start) | async-done | bytes 2359328 | tf_op jit(solution)/shard_map/all_to_all | solution.py:66
  103.5 7.5 %multiply_convert_fusion = (bf16[1024,768]{1,0:T(8,128)(2,1)}, f32[1024,768]{1,0:T(8,128)}) fusion(bf16[1536,768]{1,0:T(8,128)(2,1)} %bitcast.5, bf16[2,1024,1536]{2,1,0:T(8,128)(2,1)} %all-gather.3.cloned.1.call-done), kind=kOutput, calls=%fused_computation.101 | convolution fusion | flops 2419851264 | bytes 10223616 | tf_op jit(solution)/shard_map/dot_general | solution.py:91
  111.0 43.2 %all-gather.5.cloned.1.call-done = bf16[768,1536]{0,1:T(8,128)(2,1)} async-done(((bf16[768,384]{0,1:T(8,128)(2,1)}), bf16[768,1536]{0,1:T(8,128)(2,1)}) %all-gather.5.cloned.1.call-update) | async-done | bytes 2359312 | tf_op jit(solution)/shard_map/all_gather | solution.py:69
  154.2 6.6 %fusion.7 = bf16[1024,768]{1,0:T(8,128)(2,1)S(1)} fusion(f32[1024,768]{1,0:T(8,128)} %get-tuple-element.134, bf16[768,1536]{0,1:T(8,128)(2,1)} %all-gather.5.cloned.1.call-done, bf16[2,1024,1536]{2,1,0:T(8,128)(2,1)} %all-gather.3.cloned.1.call-done), kind=kOutput, calls=%fused_computation.98 | convolution fusion | flops 2423783424 | bytes 10223616 | tf_op jit(solution)/shard_map/dot_general | solution.py:97
  160.9 5.1 %fusion.1 = bf16[1,1024,1536]{2,1,0:T(8,128)(2,1)S(1)} fusion(bf16[1024,768]{1,0:T(8,128)(2,1)S(1)} %fusion.7, bf16[1536,768]{1,0:T(8,128)(2,1)} %bitcast.5), kind=kOutput, calls=%fused_computation.92 | convolution fusion | flops 2417491968 | bytes 7077888 | tf_op jit(solution)/shard_map/dot_general | solution.py:104
  166.1 2.9 fusion
  169.0 3.2 pad_maximum_fusion
  172.2 6.4 %convolution_convert_fusion.2 = bf16[1536,768]{1,0:T(8,128)(2,1)} fusion(bf16[1024,768]{1,0:T(8,128)(2,1)} %get-tuple-element.133, bf16[2,1024,1536]{2,1,0:T(8,128)(2,1)} %all-gather.3.cloned.1.call-done), kind=kOutput, calls=%fused_computation.89 | convolution fusion | flops 2417098752 | bytes 7077888 | tf_op jit(solution)/shard_map/dot_general | solution.py:94
  178.6 4.5 %all-to-all-start.2 = ((bf16[4,384,768]{2,1,0:T(8,128)(2,1)}), bf16[4,384,768]{2,1,0:T(8,128)(2,1)}, u32[]{:S(2)}, u32[]{:S(2)}) async-start(bf16[4,384,768]{2,1,0:T(8,128)(2,1)} %bitcast.94), calls=%async_computation.4 | async-start | bytes 4718592 | tf_op jit(solution)/shard_map/all_to_all | solution.py:118
  183.5 7.0 %convolution_convert_fusion.3 = bf16[1536,768]{1,0:T(8,128)(2,1)} fusion(bf16[1024,768]{1,0:T(8,128)(2,1)} %copy-done.74, bf16[2,1024,1536]{2,1,0:T(8,128)(2,1)} %all-gather.3.cloned.1.call-done), kind=kOutput, calls=%fused_computation.90 | convolution fusion | flops 2417098752 | bytes 7077888 | tf_op jit(solution)/shard_map/dot_general | solution.py:101
  190.5 46.8 %all-to-all-done.2 = bf16[4,384,768]{2,1,0:T(8,128)(2,1)} async-done(((bf16[4,384,768]{2,1,0:T(8,128)(2,1)}), bf16[4,384,768]{2,1,0:T(8,128)(2,1)}, u32[]{:S(2)}, u32[]{:S(2)}) %all-to-all-start.2) | async-done | bytes 2359328 | tf_op jit(solution)/shard_map/all_to_all | solution.py:118
  237.3 3.1 convert_reduce_fusion
  242.0 2.1 fusion.104
  251.4 2.4 multiply_reduce_fusion
  254.0 2.0 multiply_reduce_fusion.18
  259.5 3.5 all-to-all-start.3
  263.0 2.2 collective-permute-start.2
  266.5 22.9 %reduce-scatter.5.cloned.1.call-done = bf16[384,768]{1,0:T(8,128)(2,1)} async-done(((bf16[1536,768]{1,0:T(8,128)(2,1)}), bf16[384,768]{1,0:T(8,128)(2,1)}) %reduce-scatter.5.cloned.1.call-update) | async-done | bytes 589840 | tf_op jit(solution)/shard_map/reduce_scatter | solution.py:119
  294.5 5.1 %all-to-all-start.4 = ((f32[32,2,1536]{2,1,0:T(2,128)}), f32[32,2,1536]{2,1,0:T(2,128)S(1)}, u32[]{:S(2)}, u32[]{:S(2)}) async-start(f32[32,2,1536]{2,1,0:T(2,128)} %broadcast_in_dim.11), calls=%async_computation.6 | async-start | bytes 786432 | tf_op jit(solution)/shard_map/all_to_all | solution.py:51
  299.8 7.8 %fusion.97 = bf16[1,4,32,1536]{3,2,1,0:T(8,128)(2,1)} fusion(f32[1,10,32,1536]{3,2,1,0:T(8,128)S(1)} %maximum_convert_fusion.1, f32[1536]{0:T(1024)S(1)} %copy-done.26, f32[1536]{0:T(1024)S(1)} %copy-done.28, f32[1536]{0:T(1024)S(1)} %copy-done.32, f32[1536]{0:T(1024)S(1)} %copy-done.34, f32[1536]{0:T(1024)} %copy-done.35, f32[1536]{0:T(1024)} %copy-done.36, ...), kind=kLoop, calls=%fused_computation.195 | loop fusion | flops 19660800 | bytes 8587264 | tf_op jit(solution)/shard_map/convert_element_type | solution.py:147
  307.6 4.9 %all-to-all-done.4 = f32[32,2,1536]{2,1,0:T(2,128)S(1)} async-done(((f32[32,2,1536]{2,1,0:T(2,128)}), f32[32,2,1536]{2,1,0:T(2,128)S(1)}, u32[]{:S(2)}, u32[]{:S(2)}) %all-to-all-start.4) | async-done | bytes 393248 | tf_op jit(solution)/shard_map/all_to_all | solution.py:51
  314.3 4.9 %copy.37 = f32[2,384,768]{2,0,1:T(2,128)} copy(f32[2,384,768]{2,1,0:T(8,128)} %pad_maximum_fusion.1) | data formatting | bytes 4718592 | tf_op jit(solution)/shard_map/optimization_barrier | solution.py:149
  319.2 3.8 %all-to-all-start.5 = ((f32[2,384,768]{2,0,1:T(2,128)}), f32[2,384,768]{2,0,1:T(2,128)S(1)}, u32[]{:S(2)}, u32[]{:S(2)}) async-start(f32[2,384,768]{2,0,1:T(2,128)} %copy.37), calls=%async_computation.7 | async-start | bytes 4718592 | tf_op jit(solution)/shard_map/all_to_all | solution.py:152
  323.8 27.6 %all-to-all-done.5 = f32[2,384,768]{2,0,1:T(2,128)S(1)} async-done(((f32[2,384,768]{2,0,1:T(2,128)}), f32[2,384,768]{2,0,1:T(2,128)S(1)}, u32[]{:S(2)}, u32[]{:S(2)}) %all-to-all-start.5) | async-done | bytes 2359328 | tf_op jit(solution)/shard_map/all_to_all | solution.py:152
  (259 shorter events, 39.7 us)
Async XLA Ops:
  7.2 96.3 %all-gather.3.cloned.1.call-start = ((), (), s32[]{:S(2)}) async-start(), calls=%async_computation.8 | async-start | bytes 7077888 | tf_op jit(solution)/shard_map/all_gather | solution.py:89
  8.3 9.6 %collective-permute-start = (bf16[1,3,32,1536]{3,2,1,0:T(8,128)(2,1)S(1)}, bf16[1,3,32,1536]{3,2,1,0:T(8,128)(2,1)S(1)}, u32[]{:S(2)}, u32[]{:S(2)}) collective-permute-start(bf16[1,3,32,1536]{3,2,1,0:T(8,128)(2,1)S(1)} %get-tuple-element.131), channel_id=1, source_target_pairs={{0,1},{1,2},{2,3},{4,5},{5,6},{6,7},{8,9},{9,10},{10,11},{12,13},{... | collective-permute-start | bytes 884744 | tf_op jit(solution)/shard_map/ppermute | solution.py:25
  10.7 7.2 %collective-permute-start.1 = (bf16[1,3,32,1536]{3,2,1,0:T(8,128)(2,1)S(1)}, bf16[1,3,32,1536]{3,2,1,0:T(8,128)(2,1)S(1)}, u32[]{:S(2)}, u32[]{:S(2)}) collective-permute-start(bf16[1,3,32,1536]{3,2,1,0:T(8,128)(2,1)S(1)} %get-tuple-element.132), channel_id=1, source_target_pairs={{1,0},{2,1},{3,2},{5,4},{6,5},{7,6},{9,8},{10,9},{11,10},{13,12},{... | collective-permute-start | bytes 884744 | tf_op jit(solution)/shard_map/ppermute | solution.py:26
  13.3 15.3 %copy-start.9 = (f32[1536]{0:T(1024)}, f32[1536]{0:T(1024)S(1)}, u32[]{:S(2)}) copy-start(f32[1536]{0:T(1024)S(1)} %get-tuple-element.111) | copy-start | bytes 18436
  13.3 15.3 %copy-start.11 = (f32[1536]{0:T(1024)}, f32[1536]{0:T(1024)S(1)}, u32[]{:S(2)}) copy-start(f32[1536]{0:T(1024)S(1)} %get-tuple-element.112) | copy-start | bytes 18436
  13.3 15.3 %copy-start.13 = (f32[1536]{0:T(1024)}, f32[1536]{0:T(1024)S(1)}, u32[]{:S(2)}) copy-start(f32[1536]{0:T(1024)S(1)} %get-tuple-element.113) | copy-start | bytes 18436
  13.3 15.3 %copy-start.15 = (f32[1536]{0:T(1024)}, f32[1536]{0:T(1024)S(1)}, u32[]{:S(2)}) copy-start(f32[1536]{0:T(1024)S(1)} %get-tuple-element.114) | copy-start | bytes 18436
  13.3 15.3 %copy-start.17 = (f32[1536]{0:T(1024)}, f32[1536]{0:T(1024)S(1)}, u32[]{:S(2)}) copy-start(f32[1536]{0:T(1024)S(1)} %get-tuple-element.115) | copy-start | bytes 18436
  13.3 15.3 %copy-start.19 = (f32[1536]{0:T(1024)}, f32[1536]{0:T(1024)S(1)}, u32[]{:S(2)}) copy-start(f32[1536]{0:T(1024)S(1)} %get-tuple-element.116) | copy-start | bytes 18436
  13.3 15.3 %copy-start.21 = (f32[1536]{0:T(1024)}, f32[1536]{0:T(1024)S(1)}, u32[]{:S(2)}) copy-start(f32[1536]{0:T(1024)S(1)} %get-tuple-element.117) | copy-start | bytes 18436
  13.3 15.3 %copy-start.23 = (f32[1536]{0:T(1024)}, f32[1536]{0:T(1024)S(1)}, u32[]{:S(2)}) copy-start(f32[1536]{0:T(1024)S(1)} %get-tuple-element.118) | copy-start | bytes 18436
  13.3 15.3 %copy-start.25 = (f32[1536]{0:T(1024)}, f32[1536]{0:T(1024)S(1)}, u32[]{:S(2)}) copy-start(f32[1536]{0:T(1024)S(1)} %get-tuple-element.119) | copy-start | bytes 18436
  13.4 15.3 %copy-start.27 = (f32[1536]{0:T(1024)}, f32[1536]{0:T(1024)S(1)}, u32[]{:S(2)}) copy-start(f32[1536]{0:T(1024)S(1)} %get-tuple-element.120) | copy-start | bytes 18436
  15.2 13.5 %copy-start.29 = (f32[1536]{0:T(1024)}, f32[1536]{0:T(1024)S(1)}, u32[]{:S(2)}) copy-start(f32[1536]{0:T(1024)S(1)} %get-tuple-element.72) | copy-start | bytes 18436
  15.2 13.5 %copy-start.31 = (f32[1536]{0:T(1024)}, f32[1536]{0:T(1024)S(1)}, u32[]{:S(2)}) copy-start(f32[1536]{0:T(1024)S(1)} %get-tuple-element.73) | copy-start | bytes 18436
  15.2 13.5 %copy-start.33 = (f32[1536]{0:T(1024)}, f32[1536]{0:T(1024)S(1)}, u32[]{:S(2)}) copy-start(f32[1536]{0:T(1024)S(1)} %get-tuple-element.74) | copy-start | bytes 18436
  15.2 13.5 %copy-start.35 = (f32[1536]{0:T(1024)}, f32[1536]{0:T(1024)S(1)}, u32[]{:S(2)}) copy-start(f32[1536]{0:T(1024)S(1)} %get-tuple-element.75) | copy-start | bytes 18436
  15.2 13.5 %copy-start.36 = (f32[1536]{0:T(1024)}, f32[1536]{0:T(1024)S(1)}, u32[]{:S(2)}) copy-start(f32[1536]{0:T(1024)S(1)} %get-tuple-element.76) | copy-start | bytes 18436
  15.3 13.5 %copy-start.37 = (f32[1536]{0:T(1024)}, f32[1536]{0:T(1024)S(1)}, u32[]{:S(2)}) copy-start(f32[1536]{0:T(1024)S(1)} %get-tuple-element.77) | copy-start | bytes 18436
  15.3 13.5 %copy-start.38 = (f32[1536]{0:T(1024)}, f32[1536]{0:T(1024)S(1)}, u32[]{:S(2)}) copy-start(f32[1536]{0:T(1024)S(1)} %get-tuple-element.78) | copy-start | bytes 18436
  31.8 17.6 %all-to-all-start.1 = ((bf16[4,768,96]{1,2,0:T(8,128)(2,1)}), bf16[4,768,96]{1,2,0:T(8,128)(2,1)S(1)}, u32[]{:S(2)}, u32[]{:S(2)}) async-start(bf16[4,768,96]{1,2,0:T(8,128)(2,1)} %bitcast.96), calls=%async_computation.1 | async-start | bytes 1179648 | tf_op jit(solution)/shard_map/all_to_all | solution.py:68
  52.3 51.2 %all-to-all-start = ((bf16[16,96,768]{2,1,0:T(8,128)(2,1)}), bf16[16,96,768]{2,1,0:T(8,128)(2,1)}, u32[]{:S(2)}, u32[]{:S(2)}) async-start(bf16[16,96,768]{2,1,0:T(8,128)(2,1)} %bitcast.87), calls=%async_computation | async-start | bytes 4718592 | tf_op jit(solution)/shard_map/all_to_all | solution.py:66
  57.6 96.6 %all-gather.5.cloned.1.call-start = ((), (), s32[]{:S(2)}) async-start(), calls=%async_computation.9 | async-start | bytes 2949120 | tf_op jit(solution)/shard_map/all_gather | solution.py:69
  58.4 182.0 %reduce-scatter.3.cloned.1.call-start = ((), (), s32[]{:S(2)}) async-start(), calls=%async_computation.10 | async-start | bytes 7077888 | tf_op jit(solution)/shard_map/reduce_scatter | solution.py:107
  178.6 58.7 %all-to-all-start.2 = ((bf16[4,384,768]{2,1,0:T(8,128)(2,1)}), bf16[4,384,768]{2,1,0:T(8,128)(2,1)}, u32[]{:S(2)}, u32[]{:S(2)}) async-start(bf16[4,384,768]{2,1,0:T(8,128)(2,1)} %bitcast.94), calls=%async_computation.4 | async-start | bytes 4718592 | tf_op jit(solution)/shard_map/all_to_all | solution.py:118
  183.2 106.3 %reduce-scatter.5.cloned.1.call-start = ((), (), s32[]{:S(2)}) async-start(), calls=%async_computation.11 | async-start | bytes 2949120 | tf_op jit(solution)/shard_map/reduce_scatter | solution.py:119
  258.5 32.1 %copy-start.2 = (f32[384,768]{1,0:T(8,128)S(1)}, f32[384,768]{1,0:T(8,128)}, u32[]{:S(2)}) copy-start(f32[384,768]{1,0:T(8,128)} %convert_reduce_fusion) | copy-start | bytes 3538948
  259.5 34.0 %all-to-all-start.3 = ((f32[32,2,1536]{2,1,0:T(2,128)}), f32[32,2,1536]{2,1,0:T(2,128)S(1)}, u32[]{:S(2)}, u32[]{:S(2)}) async-start(f32[32,2,1536]{2,1,0:T(2,128)} %reshape.560), calls=%async_computation.5 | async-start | bytes 786432 | tf_op jit(solution)/shard_map/all_to_all | solution.py:49
  263.0 29.2 %collective-permute-start.2 = (bf16[1,3,32,1536]{3,2,1,0:T(8,128)(2,1)S(1)}, bf16[1,3,32,1536]{3,2,1,0:T(8,128)(2,1)S(1)}, u32[]{:S(2)}, u32[]{:S(2)}) collective-permute-start(bf16[1,3,32,1536]{3,2,1,0:T(8,128)(2,1)S(1)} %get-tuple-element.129), channel_id=1, source_target_pairs={{0,1},{1,2},{2,3},{4,5},{5,6},{6,7},{8,9},{9,10},{10,11},{12,13},{... | collective-permute-start | bytes 884744 | tf_op jit(solution)/shard_map/ppermute | solution.py:25
  265.2 27.1 %collective-permute-start.3 = (bf16[1,3,32,1536]{3,2,1,0:T(8,128)(2,1)S(1)}, bf16[1,3,32,1536]{3,2,1,0:T(8,128)(2,1)}, u32[]{:S(2)}, u32[]{:S(2)}) collective-permute-start(bf16[1,3,32,1536]{3,2,1,0:T(8,128)(2,1)S(1)} %get-tuple-element.130), channel_id=1, source_target_pairs={{1,0},{2,1},{3,2},{5,4},{6,5},{7,6},{9,8},{10,9},{11,10},{13,12},{... | collective-permute-start | bytes 884744 | tf_op jit(solution)/shard_map/ppermute | solution.py:26
  294.5 18.0 %all-to-all-start.4 = ((f32[32,2,1536]{2,1,0:T(2,128)}), f32[32,2,1536]{2,1,0:T(2,128)S(1)}, u32[]{:S(2)}, u32[]{:S(2)}) async-start(f32[32,2,1536]{2,1,0:T(2,128)} %broadcast_in_dim.11), calls=%async_computation.6 | async-start | bytes 786432 | tf_op jit(solution)/shard_map/all_to_all | solution.py:51
  319.2 32.2 %all-to-all-start.5 = ((f32[2,384,768]{2,0,1:T(2,128)}), f32[2,384,768]{2,0,1:T(2,128)S(1)}, u32[]{:S(2)}, u32[]{:S(2)}) async-start(f32[2,384,768]{2,0,1:T(2,128)} %copy.37), calls=%async_computation.7 | async-start | bytes 4718592 | tf_op jit(solution)/shard_map/all_to_all | solution.py:152
  (58 other events, 470.3 us)
Sparse Core Ops, SparseCore 0:
  30.8 67.5 all-gather.2
  100.6 53.6 all-gather.4
  172.3 60.5 reduce-scatter.2
  235.2 54.2 reduce-scatter.4

commit v15 on v14

--- a/solution.py
+++ b/solution.py
@@ -118,8 +118,8 @@
     down_sum = lax.all_to_all(down_blocks, "dp", 0, 0, tiled=True).astype(jnp.float32).sum(0)
     up_sum = lax.psum_scatter(
         up_part.astype(jnp.bfloat16), "dp", scatter_dimension=0, tiled=True
-    ).astype(jnp.float32)
-    grad_sums = jnp.stack([up_sum, down_sum])
+    )
+    grad_sums = jnp.stack([up_sum, down_sum.astype(jnp.bfloat16)])
     gain_part = jnp.sum(norm_grad * normed, axis=0)
     scaled_grad = norm_grad * norm_gain
     conv_grad = rstd * (

time: 365 us -> 357 us (0.978); the launches traced: 364 us -> 350 us
  waiting for transfers between devices: 198 us -> 184 us
    all_to_all x1, waiting for transfers between devices: 46.8 us -> 0.01 us  [body(): lax.all_to_all(down_blocks, 'dp', 0, 0, tiled=True).astype(jnp.float32)]
    reduce_scatter x1, waiting for transfers between devices: 0.01 us -> 42.4 us  [body(): lax.psum_scatter(jnp.stack([mlp_terms, norm_terms]).astype(jnp.bfloat16),...]
    all_to_all x1, waiting for transfers between devices: 27.6 us -> 13.8 us  [body(): lax.all_to_all(grad_sums, 'rows', 1, 2, tiled=True).astype(jnp.float32)]
    reduce_scatter x1, waiting for transfers between devices: 22.9 us -> 27.5 us  [body(): lax.psum_scatter(up_part.astype(jnp.bfloat16), 'dp', scatter_dimension=0,...]
  transfers between devices with their start and end apart: 14 -> 14, of which waited for: 7 -> 7; matrix products, arithmetic and copies ran while one was open for 19% -> 20% of each run, Pallas kernels for 0% -> 0%
where the time goes in v15:
time: 357 us; the launch traced here: 350 us
  waiting for transfers between devices  184 us (52%)
  other arithmetic  43 us (12%)
  starting transfers between devices  37 us (10%)
  matrix products  35.8 us (10%)
  local copies, waits for them, and re-layouts  34.4 us (10%)
  between operations  15.4 us (4%)
    all_to_all x1, waiting for transfers between devices, body(): up_loc = lax.all_to_all(pieces, ('dp', 'rows'), 0, 0, tiled=True)  44.6 us
    all_gather x1, waiting for transfers between devices, body(): down_loc = lax.all_gather(down_loc, 'dp', axis=1, tiled=True)  43.2 us
    reduce_scatter x1, waiting for transfers between devices, body(): lax.psum_scatter(jnp.stack([mlp_terms, norm_terms]).astype(jnp.bfloat16),...  42.4 us
    reduce_scatter x1, waiting for transfers between devices, body(): lax.psum_scatter(up_part.astype(jnp.bfloat16), 'dp', scatter_dimension=0,...  27.5 us
    all_to_all x1, waiting for transfers between devices, body(): lax.all_to_all(grad_sums, 'rows', 1, 2, tiled=True).astype(jnp.float32)  13.8 us
    reduce_sum x1, other arithmetic, body(): average = jnp.mean(flat, axis=-1, keepdims=True)  9.44 us
    convert_element_type x1, other arithmetic, body(): grad_x = (d_out.astype(jnp.float32) + back_conv).astype(jnp.bfloat16)  8.33 us
    dot_general x1, matrix products, body(): hidden = jnp.dot(gathered, up_loc, preferred_element_type=jnp.float32)  7.49 us
  transfers between devices with their start and end apart: 14, of which 7 were waited for; matrix products, arithmetic and copies ran while one was open for 20% of the time, Pallas kernels for 0%

profile of v15, /device:TPU:0, one launch (start us, length us, event | category | flops | bytes accessed | tf_op | source)
XLA Modules:
  0.0 349.8 jit_solution(6042365886521894993)
XLA Ops:
  8.3 2.4 collective-permute-start
  15.4 2.5 slice_reduce_fusion.49
  19.2 9.4 %fusion.110 = (f32[4,32]{1,0:T(4,128)S(1)}, f32[1,4,32,1536]{3,2,1,0:T(8,128)S(1)}) fusion(f32[1536]{0:T(1024)S(1)} %get-tuple-element.119, f32[1536]{0:T(1024)S(1)} %get-tuple-element.120, f32[1536]{0:T(1024)S(1)} %get-tuple-element.73, f32[1536]{0:T(1024)S(1)} %get-tuple-element.74, f32[1,10,32,1536]{3,2,1,0:T(8,128)S(1)} %maximum_convert_fusion, ...), kind=kLoop, calls=%fused_computation.332 | loop fusion | flops 19267456 | bytes 8641024 | tf_op jit(solution)/shard_map/reduce_sum | solution.py:83
  31.9 6.1 %all-to-all-start.1 = ((bf16[4,768,96]{1,2,0:T(8,128)(2,1)}), bf16[4,768,96]{1,2,0:T(8,128)(2,1)S(1)}, u32[]{:S(2)}, u32[]{:S(2)}) async-start(bf16[4,768,96]{1,2,0:T(8,128)(2,1)} %bitcast.94), calls=%async_computation.1 | async-start | bytes 1179648 | tf_op jit(solution)/shard_map/all_to_all | solution.py:68
  38.0 2.5 reshape.558
  42.5 7.0 %all-to-all-done.1 = bf16[4,768,96]{1,2,0:T(8,128)(2,1)S(1)} async-done(((bf16[4,768,96]{1,2,0:T(8,128)(2,1)}), bf16[4,768,96]{1,2,0:T(8,128)(2,1)S(1)}, u32[]{:S(2)}, u32[]{:S(2)}) %all-to-all-start.1) | async-done | bytes 589856 | tf_op jit(solution)/shard_map/all_to_all | solution.py:68
  49.5 2.9 broadcast_in_dim.8
  52.4 5.3 %all-to-all-start = ((bf16[16,96,768]{2,1,0:T(8,128)(2,1)}), bf16[16,96,768]{2,1,0:T(8,128)(2,1)}, u32[]{:S(2)}, u32[]{:S(2)}) async-start(bf16[16,96,768]{2,1,0:T(8,128)(2,1)} %bitcast.86), calls=%async_computation | async-start | bytes 4718592 | tf_op jit(solution)/shard_map/all_to_all | solution.py:66
  59.0 44.6 %all-to-all-done = bf16[16,96,768]{2,1,0:T(8,128)(2,1)} async-done(((bf16[16,96,768]{2,1,0:T(8,128)(2,1)}), bf16[16,96,768]{2,1,0:T(8,128)(2,1)}, u32[]{:S(2)}, u32[]{:S(2)}) %all-to-all-start) | async-done | bytes 2359328 | tf_op jit(solution)/shard_map/all_to_all | solution.py:66
  103.6 7.5 %multiply_convert_fusion = (bf16[1024,768]{1,0:T(8,128)(2,1)}, f32[1024,768]{1,0:T(8,128)}) fusion(bf16[1536,768]{1,0:T(8,128)(2,1)} %bitcast.5, bf16[2,1024,1536]{2,1,0:T(8,128)(2,1)} %all-gather.3.cloned.1.call-done), kind=kOutput, calls=%fused_computation.100 | convolution fusion | flops 2419851264 | bytes 10223616 | tf_op jit(solution)/shard_map/dot_general | solution.py:91
  111.1 43.2 %all-gather.5.cloned.1.call-done = bf16[768,1536]{0,1:T(8,128)(2,1)} async-done(((bf16[768,384]{0,1:T(8,128)(2,1)}), bf16[768,1536]{0,1:T(8,128)(2,1)}) %all-gather.5.cloned.1.call-update) | async-done | bytes 2359312 | tf_op jit(solution)/shard_map/all_gather | solution.py:69
  154.3 6.6 %fusion.7 = bf16[1024,768]{1,0:T(8,128)(2,1)S(1)} fusion(f32[1024,768]{1,0:T(8,128)} %get-tuple-element.134, bf16[768,1536]{0,1:T(8,128)(2,1)} %all-gather.5.cloned.1.call-done, bf16[2,1024,1536]{2,1,0:T(8,128)(2,1)} %all-gather.3.cloned.1.call-done), kind=kOutput, calls=%fused_computation.97 | convolution fusion | flops 2423783424 | bytes 10223616 | tf_op jit(solution)/shard_map/dot_general | solution.py:97
  161.0 5.1 %fusion.1 = bf16[1,1024,1536]{2,1,0:T(8,128)(2,1)S(1)} fusion(bf16[1024,768]{1,0:T(8,128)(2,1)S(1)} %fusion.7, bf16[1536,768]{1,0:T(8,128)(2,1)} %bitcast.5), kind=kOutput, calls=%fused_computation.91 | convolution fusion | flops 2417491968 | bytes 7077888 | tf_op jit(solution)/shard_map/dot_general | solution.py:104
  166.1 2.9 fusion
  169.1 3.2 pad_maximum_fusion
  172.5 6.5 %convolution_convert_fusion.3 = bf16[1536,768]{1,0:T(8,128)(2,1)} fusion(bf16[1024,768]{1,0:T(8,128)(2,1)} %copy-done.61, bf16[2,1024,1536]{2,1,0:T(8,128)(2,1)} %all-gather.3.cloned.1.call-done), kind=kOutput, calls=%fused_computation.89 | convolution fusion | flops 2417098752 | bytes 7077888 | tf_op jit(solution)/shard_map/dot_general | solution.py:101
  179.0 7.1 %convolution_convert_fusion.2 = bf16[1536,768]{1,0:T(8,128)(2,1)} fusion(bf16[1024,768]{1,0:T(8,128)(2,1)} %get-tuple-element.133, bf16[2,1024,1536]{2,1,0:T(8,128)(2,1)} %all-gather.3.cloned.1.call-done), kind=kOutput, calls=%fused_computation.88 | convolution fusion | flops 2417098752 | bytes 7077888 | tf_op jit(solution)/shard_map/dot_general | solution.py:94
  186.1 4.5 %all-to-all-start.2 = ((bf16[4,384,768]{2,1,0:T(8,128)(2,1)}), bf16[4,384,768]{2,1,0:T(8,128)(2,1)}, u32[]{:S(2)}, u32[]{:S(2)}) async-start(bf16[4,384,768]{2,1,0:T(8,128)(2,1)} %bitcast.92), calls=%async_computation.4 | async-start | bytes 4718592 | tf_op jit(solution)/shard_map/all_to_all | solution.py:118
  190.6 42.4 %reduce-scatter.3.cloned.1.call-done = bf16[2,128,1536]{2,1,0:T(8,128)(2,1)} async-done(((bf16[2,1024,1536]{2,1,0:T(8,128)(2,1)}), bf16[2,128,1536]{2,1,0:T(8,128)(2,1)}) %reduce-scatter.3.cloned.1.call-update) | async-done | bytes 786448 | tf_op jit(solution)/shard_map/reduce_scatter | solution.py:107
  234.4 2.1 fusion.104
  243.7 2.4 multiply_reduce_fusion
  246.3 2.0 multiply_reduce_fusion.18
  251.8 4.7 %all-to-all-start.3 = ((f32[32,2,1536]{2,1,0:T(2,128)}), f32[32,2,1536]{2,1,0:T(2,128)}, u32[]{:S(2)}, u32[]{:S(2)}) async-start(f32[32,2,1536]{2,1,0:T(2,128)} %reshape.563), calls=%async_computation.5 | async-start | bytes 786432 | tf_op jit(solution)/shard_map/all_to_all | solution.py:49
  256.6 2.1 collective-permute-start.2
  260.2 2.3 reduce_sum.518
  262.5 27.5 %reduce-scatter.5.cloned.1.call-done = bf16[384,768]{1,0:T(8,128)(2,1)} async-done(((bf16[1536,768]{1,0:T(8,128)(2,1)}), bf16[384,768]{1,0:T(8,128)(2,1)}) %reduce-scatter.5.cloned.1.call-update) | async-done | bytes 589840 | tf_op jit(solution)/shard_map/reduce_scatter | solution.py:119
  295.2 4.8 %all-to-all-start.4 = ((f32[32,2,1536]{2,1,0:T(2,128)}), f32[32,2,1536]{2,1,0:T(2,128)S(1)}, u32[]{:S(2)}, u32[]{:S(2)}) async-start(f32[32,2,1536]{2,1,0:T(2,128)} %broadcast_in_dim.11), calls=%async_computation.6 | async-start | bytes 786432 | tf_op jit(solution)/shard_map/all_to_all | solution.py:51
  300.0 8.3 %fusion.97 = bf16[1,4,32,1536]{3,2,1,0:T(8,128)(2,1)} fusion(f32[1,10,32,1536]{3,2,1,0:T(8,128)S(1)} %maximum_convert_fusion.1, f32[1536]{0:T(1024)} %copy-done.16, f32[1536]{0:T(1024)} %copy-done.17, f32[1536]{0:T(1024)} %copy-done.19, f32[1536]{0:T(1024)} %copy-done.20, f32[1536]{0:T(1024)} %copy-done.21, f32[1536]{0:T(1024)} %copy-done.22, ...), kind=kLoop, calls=%fused_computation.195 | loop fusion | flops 19660800 | bytes 8562688 | tf_op jit(solution)/shard_map/convert_element_type | solution.py:147
  308.3 4.8 %all-to-all-done.4 = f32[32,2,1536]{2,1,0:T(2,128)S(1)} async-done(((f32[32,2,1536]{2,1,0:T(2,128)}), f32[32,2,1536]{2,1,0:T(2,128)S(1)}, u32[]{:S(2)}, u32[]{:S(2)}) %all-to-all-start.4) | async-done | bytes 393248 | tf_op jit(solution)/shard_map/all_to_all | solution.py:51
  314.9 2.2 copy.37
  317.1 3.5 %all-to-all-start.5 = ((bf16[2,384,768]{2,0,1:T(2,128)(2,1)}), bf16[2,384,768]{2,0,1:T(2,128)(2,1)S(1)}, u32[]{:S(2)}, u32[]{:S(2)}) async-start(bf16[2,384,768]{2,0,1:T(2,128)(2,1)} %copy.37), calls=%async_computation.7 | async-start | bytes 2359296 | tf_op jit(solution)/shard_map/all_to_all | solution.py:152
  322.6 13.8 %all-to-all-done.5 = bf16[2,384,768]{2,0,1:T(2,128)(2,1)S(1)} async-done(((bf16[2,384,768]{2,0,1:T(2,128)(2,1)}), bf16[2,384,768]{2,0,1:T(2,128)(2,1)S(1)}, u32[]{:S(2)}, u32[]{:S(2)}) %all-to-all-start.5) | async-done | bytes 1179680 | tf_op jit(solution)/shard_map/all_to_all | solution.py:152
  (231 shorter events, 41.9 us)
Async XLA Ops:
  7.2 96.4 %all-gather.3.cloned.1.call-start = ((), (), s32[]{:S(2)}) async-start(), calls=%async_computation.8 | async-start | bytes 7077888 | tf_op jit(solution)/shard_map/all_gather | solution.py:89
  8.3 9.7 %collective-permute-start = (bf16[1,3,32,1536]{3,2,1,0:T(8,128)(2,1)S(1)}, bf16[1,3,32,1536]{3,2,1,0:T(8,128)(2,1)S(1)}, u32[]{:S(2)}, u32[]{:S(2)}) collective-permute-start(bf16[1,3,32,1536]{3,2,1,0:T(8,128)(2,1)S(1)} %get-tuple-element.131), channel_id=1, source_target_pairs={{0,1},{1,2},{2,3},{4,5},{5,6},{6,7},{8,9},{9,10},{10,11},{12,13},{... | collective-permute-start | bytes 884744 | tf_op jit(solution)/shard_map/ppermute | solution.py:25
  10.7 7.3 %collective-permute-start.1 = (bf16[1,3,32,1536]{3,2,1,0:T(8,128)(2,1)S(1)}, bf16[1,3,32,1536]{3,2,1,0:T(8,128)(2,1)S(1)}, u32[]{:S(2)}, u32[]{:S(2)}) collective-permute-start(bf16[1,3,32,1536]{3,2,1,0:T(8,128)(2,1)S(1)} %get-tuple-element.132), channel_id=1, source_target_pairs={{1,0},{2,1},{3,2},{5,4},{6,5},{7,6},{9,8},{10,9},{11,10},{13,12},{... | collective-permute-start | bytes 884744 | tf_op jit(solution)/shard_map/ppermute | solution.py:26
  13.4 15.3 %copy-start.7 = (f32[1536]{0:T(1024)}, f32[1536]{0:T(1024)S(1)}, u32[]{:S(2)}) copy-start(f32[1536]{0:T(1024)S(1)} %get-tuple-element.111) | copy-start | bytes 18436
  13.4 15.3 %copy-start.9 = (f32[1536]{0:T(1024)}, f32[1536]{0:T(1024)S(1)}, u32[]{:S(2)}) copy-start(f32[1536]{0:T(1024)S(1)} %get-tuple-element.112) | copy-start | bytes 18436
  13.4 15.3 %copy-start.10 = (f32[1536]{0:T(1024)}, f32[1536]{0:T(1024)S(1)}, u32[]{:S(2)}) copy-start(f32[1536]{0:T(1024)S(1)} %get-tuple-element.113) | copy-start | bytes 18436
  13.4 15.3 %copy-start.11 = (f32[1536]{0:T(1024)}, f32[1536]{0:T(1024)S(1)}, u32[]{:S(2)}) copy-start(f32[1536]{0:T(1024)S(1)} %get-tuple-element.114) | copy-start | bytes 18436
  13.4 15.3 %copy-start.12 = (f32[1536]{0:T(1024)}, f32[1536]{0:T(1024)S(1)}, u32[]{:S(2)}) copy-start(f32[1536]{0:T(1024)S(1)} %get-tuple-element.115) | copy-start | bytes 18436
  13.4 15.3 %copy-start.13 = (f32[1536]{0:T(1024)}, f32[1536]{0:T(1024)S(1)}, u32[]{:S(2)}) copy-start(f32[1536]{0:T(1024)S(1)} %get-tuple-element.116) | copy-start | bytes 18436
  13.4 15.3 %copy-start.14 = (f32[1536]{0:T(1024)}, f32[1536]{0:T(1024)S(1)}, u32[]{:S(2)}) copy-start(f32[1536]{0:T(1024)S(1)} %get-tuple-element.117) | copy-start | bytes 18436
  13.4 15.3 %copy-start.15 = (f32[1536]{0:T(1024)}, f32[1536]{0:T(1024)S(1)}, u32[]{:S(2)}) copy-start(f32[1536]{0:T(1024)S(1)} %get-tuple-element.118) | copy-start | bytes 18436
  13.5 15.3 %copy-start.16 = (f32[1536]{0:T(1024)}, f32[1536]{0:T(1024)S(1)}, u32[]{:S(2)}) copy-start(f32[1536]{0:T(1024)S(1)} %get-tuple-element.119) | copy-start | bytes 18436
  13.5 15.3 %copy-start.17 = (f32[1536]{0:T(1024)}, f32[1536]{0:T(1024)S(1)}, u32[]{:S(2)}) copy-start(f32[1536]{0:T(1024)S(1)} %get-tuple-element.120) | copy-start | bytes 18436
  15.2 13.5 %copy-start.18 = (f32[1536]{0:T(1024)}, f32[1536]{0:T(1024)S(1)}, u32[]{:S(2)}) copy-start(f32[1536]{0:T(1024)S(1)} %get-tuple-element.72) | copy-start | bytes 18436
  15.3 13.5 %copy-start.19 = (f32[1536]{0:T(1024)}, f32[1536]{0:T(1024)S(1)}, u32[]{:S(2)}) copy-start(f32[1536]{0:T(1024)S(1)} %get-tuple-element.73) | copy-start | bytes 18436
  15.3 13.5 %copy-start.20 = (f32[1536]{0:T(1024)}, f32[1536]{0:T(1024)S(1)}, u32[]{:S(2)}) copy-start(f32[1536]{0:T(1024)S(1)} %get-tuple-element.74) | copy-start | bytes 18436
  15.3 13.5 %copy-start.21 = (f32[1536]{0:T(1024)}, f32[1536]{0:T(1024)S(1)}, u32[]{:S(2)}) copy-start(f32[1536]{0:T(1024)S(1)} %get-tuple-element.75) | copy-start | bytes 18436
  15.3 13.5 %copy-start.22 = (f32[1536]{0:T(1024)}, f32[1536]{0:T(1024)S(1)}, u32[]{:S(2)}) copy-start(f32[1536]{0:T(1024)S(1)} %get-tuple-element.76) | copy-start | bytes 18436
  15.3 13.5 %copy-start.23 = (f32[1536]{0:T(1024)}, f32[1536]{0:T(1024)S(1)}, u32[]{:S(2)}) copy-start(f32[1536]{0:T(1024)S(1)} %get-tuple-element.77) | copy-start | bytes 18436
  15.3 13.5 %copy-start.24 = (f32[1536]{0:T(1024)}, f32[1536]{0:T(1024)S(1)}, u32[]{:S(2)}) copy-start(f32[1536]{0:T(1024)S(1)} %get-tuple-element.78) | copy-start | bytes 18436
  15.3 13.5 %copy-start.25 = (f32[1536]{0:T(1024)}, f32[1536]{0:T(1024)S(1)}, u32[]{:S(2)}) copy-start(f32[1536]{0:T(1024)S(1)} %get-tuple-element.79) | copy-start | bytes 18436
  31.9 17.6 %all-to-all-start.1 = ((bf16[4,768,96]{1,2,0:T(8,128)(2,1)}), bf16[4,768,96]{1,2,0:T(8,128)(2,1)S(1)}, u32[]{:S(2)}, u32[]{:S(2)}) async-start(bf16[4,768,96]{1,2,0:T(8,128)(2,1)} %bitcast.94), calls=%async_computation.1 | async-start | bytes 1179648 | tf_op jit(solution)/shard_map/all_to_all | solution.py:68
  52.4 51.2 %all-to-all-start = ((bf16[16,96,768]{2,1,0:T(8,128)(2,1)}), bf16[16,96,768]{2,1,0:T(8,128)(2,1)}, u32[]{:S(2)}, u32[]{:S(2)}) async-start(bf16[16,96,768]{2,1,0:T(8,128)(2,1)} %bitcast.86), calls=%async_computation | async-start | bytes 4718592 | tf_op jit(solution)/shard_map/all_to_all | solution.py:66
  57.7 96.6 %all-gather.5.cloned.1.call-start = ((), (), s32[]{:S(2)}) async-start(), calls=%async_computation.9 | async-start | bytes 2949120 | tf_op jit(solution)/shard_map/all_gather | solution.py:69
  58.5 174.5 %reduce-scatter.3.cloned.1.call-start = ((), (), s32[]{:S(2)}) async-start(), calls=%async_computation.10 | async-start | bytes 7077888 | tf_op jit(solution)/shard_map/reduce_scatter | solution.py:107
  172.3 117.8 %reduce-scatter.5.cloned.1.call-start = ((), (), s32[]{:S(2)}) async-start(), calls=%async_computation.11 | async-start | bytes 2949120 | tf_op jit(solution)/shard_map/reduce_scatter | solution.py:119
  186.1 65.7 %all-to-all-start.2 = ((bf16[4,384,768]{2,1,0:T(8,128)(2,1)}), bf16[4,384,768]{2,1,0:T(8,128)(2,1)}, u32[]{:S(2)}, u32[]{:S(2)}) async-start(bf16[4,384,768]{2,1,0:T(8,128)(2,1)} %bitcast.92), calls=%async_computation.4 | async-start | bytes 4718592 | tf_op jit(solution)/shard_map/all_to_all | solution.py:118
  251.8 41.4 %all-to-all-start.3 = ((f32[32,2,1536]{2,1,0:T(2,128)}), f32[32,2,1536]{2,1,0:T(2,128)}, u32[]{:S(2)}, u32[]{:S(2)}) async-start(f32[32,2,1536]{2,1,0:T(2,128)} %reshape.563), calls=%async_computation.5 | async-start | bytes 786432 | tf_op jit(solution)/shard_map/all_to_all | solution.py:49
  256.6 34.7 %collective-permute-start.2 = (bf16[1,3,32,1536]{3,2,1,0:T(8,128)(2,1)S(1)}, bf16[1,3,32,1536]{3,2,1,0:T(8,128)(2,1)S(1)}, u32[]{:S(2)}, u32[]{:S(2)}) collective-permute-start(bf16[1,3,32,1536]{3,2,1,0:T(8,128)(2,1)S(1)} %get-tuple-element.129), channel_id=1, source_target_pairs={{0,1},{1,2},{2,3},{4,5},{5,6},{6,7},{8,9},{9,10},{10,11},{12,13},{... | collective-permute-start | bytes 884744 | tf_op jit(solution)/shard_map/ppermute | solution.py:25
  258.7 33.3 %collective-permute-start.3 = (bf16[1,3,32,1536]{3,2,1,0:T(8,128)(2,1)S(1)}, bf16[1,3,32,1536]{3,2,1,0:T(8,128)(2,1)}, u32[]{:S(2)}, u32[]{:S(2)}) collective-permute-start(bf16[1,3,32,1536]{3,2,1,0:T(8,128)(2,1)S(1)} %get-tuple-element.130), channel_id=1, source_target_pairs={{1,0},{2,1},{3,2},{5,4},{6,5},{7,6},{9,8},{10,9},{11,10},{13,12},{... | collective-permute-start | bytes 884744 | tf_op jit(solution)/shard_map/ppermute | solution.py:26
  295.2 18.0 %all-to-all-start.4 = ((f32[32,2,1536]{2,1,0:T(2,128)}), f32[32,2,1536]{2,1,0:T(2,128)S(1)}, u32[]{:S(2)}, u32[]{:S(2)}) async-start(f32[32,2,1536]{2,1,0:T(2,128)} %broadcast_in_dim.11), calls=%async_computation.6 | async-start | bytes 786432 | tf_op jit(solution)/shard_map/all_to_all | solution.py:51
  317.1 19.4 %all-to-all-start.5 = ((bf16[2,384,768]{2,0,1:T(2,128)(2,1)}), bf16[2,384,768]{2,0,1:T(2,128)(2,1)S(1)}, u32[]{:S(2)}, u32[]{:S(2)}) async-start(bf16[2,384,768]{2,0,1:T(2,128)(2,1)} %copy.37), calls=%async_computation.7 | async-start | bytes 2359296 | tf_op jit(solution)/shard_map/all_to_all | solution.py:152
  (44 other events, 361.5 us)
Sparse Core Ops, SparseCore 0:
  30.9 67.5 all-gather.2
  100.6 53.6 all-gather.4
  172.4 60.5 reduce-scatter.2
  235.3 54.7 reduce-scatter.4

commit v16 on v13

--- a/solution.py
+++ b/solution.py
@@ -114,8 +114,15 @@
     resid = feature_maps.reshape(cells, width).astype(jnp.float32)
     result = (resid + layer_scale * branch).astype(jnp.bfloat16).reshape(feature_maps.shape)
     scale_part = jnp.sum(cotan * branch, axis=0)
-    grad_parts = jnp.stack([up_part, down_part_t]).astype(jnp.bfloat16)
-    grad_sums = lax.psum_scatter(grad_parts, "dp", scatter_dimension=1, tiled=True)
+    def rows_first(part):
+        part = part.astype(jnp.bfloat16).reshape(dp_size, row_size, block_c, sub)
+        part = lax.all_to_all(part, "rows", 1, 3, tiled=True)
+        return part.reshape(dp_size, block_c, row_size * sub)
+
+    down_sum = lax.all_to_all(rows_first(down_part_t), "dp", 0, 0, tiled=True)
+    down_sum = down_sum.astype(jnp.float32).sum(0)
+    up_sum = lax.psum_scatter(rows_first(up_part), "dp", scatter_dimension=0, tiled=True)
+    grad_sums = (up_sum.reshape(block_c, row_size * sub), down_sum)
     gain_part = jnp.sum(norm_grad * normed, axis=0)
     scaled_grad = norm_grad * norm_gain
     conv_grad = rstd * (
@@ -145,8 +152,7 @@
     grad_sums, grad_x, grad_kernel, grad_gain, grad_scale = lax.optimization_barrier(
         (grad_sums, grad_x, grad_kernel, grad_gain, grad_scale)
     )
-    grad_sums = lax.all_to_all(grad_sums, "rows", 1, 2, tiled=True).astype(jnp.float32)
-    grad_up, grad_down = grad_sums[0], grad_sums[1].T
+    grad_up, grad_down = grad_sums[0].astype(jnp.float32), grad_sums[1].T
     return (result, grad_x, grad_up, grad_down, grad_kernel, grad_gain, grad_scale)
 
 

time: 373 us -> 432 us (1.16)
  waiting for transfers between devices: 215 us -> 253 us
  local copies, waits for them, and re-layouts: 34.9 us -> 49.3 us
  starting transfers between devices: 33.3 us -> 39.3 us
    all_to_all x1 -> x3, waiting for transfers between devices: 15 us -> 144 us  [the longest x1 81.4 us: body(): down_sum = lax.all_to_all(rows_first(down_part_t), 'dp', 0, 0, tiled=True)]
    reduce_scatter x1, waiting for transfers between devices: 47.6 us -> 0.01 us  [body(): lax.psum_scatter(jnp.stack([mlp_terms, norm_terms]).astype(jnp.bfloat16),...]
    reduce_scatter x1, waiting for transfers between devices: 24.5 us -> 0.01 us  [body(): lax.psum_scatter(rows_first(up_part), 'dp', scatter_dimension=0, tiled=True)]
    reshape x0 -> x4, local copies, waits for them, and re-layouts: none -> 13.8 us  [the longest x2 10.6 us: rows_first(): return part.reshape(dp_size, block_c, row_size * sub)]
    all_to_all x1, waiting for transfers between devices: 15.3 us -> 5.08 us  [small_sums(): lax.all_to_all(spread, every, 0, 0, tiled=True)]
    all_to_all x1 -> x3, starting transfers between devices: 3.53 us -> 13.8 us  [the longest x2 9.27 us: rows_first(): part = lax.all_to_all(part, 'rows', 1, 3, tiled=True)]
    all_to_all x0 -> x2, local copies, waits for them, and re-layouts: none -> 9.77 us  [rows_first(): part = lax.all_to_all(part, 'rows', 1, 3, tiled=True)]
    all_to_all x1, waiting for transfers between devices: 13.2 us -> 6.31 us  [small_sums(): lax.all_to_all(packed.reshape(devices, per, width), every, 0, 0, tiled=True)]
  transfers between devices with their start and end apart: 13 -> 15, of which waited for: 9 -> 9; matrix products, arithmetic and copies ran while one was open for 17% -> 20% of each run, Pallas kernels for 0% -> 0%
where the time goes in v16:
time: 432 us; the launch traced here: 431 us
  waiting for transfers between devices  253 us (59%)
  local copies, waits for them, and re-layouts  49.3 us (11%)
  other arithmetic  40 us (9%)
  starting transfers between devices  39.3 us (9%)
  matrix products  32.7 us (8%)
  between operations  15.8 us (4%)
    all_to_all x1, waiting for transfers between devices, body(): down_sum = lax.all_to_all(rows_first(down_part_t), 'dp', 0, 0, tiled=True)  81.4 us
    all_to_all x2, waiting for transfers between devices, rows_first(): part = lax.all_to_all(part, 'rows', 1, 3, tiled=True)  62.6 us
    all_to_all x1, waiting for transfers between devices, body(): up_loc = lax.all_to_all(pieces, ('dp', 'rows'), 0, 0, tiled=True)  44.9 us
    all_gather x1, waiting for transfers between devices, body(): down_loc = lax.all_gather(down_loc, 'dp', axis=1, tiled=True)  43.3 us
    reshape x2, local copies, waits for them, and re-layouts, rows_first(): return part.reshape(dp_size, block_c, row_size * sub)  10.6 us
    all_to_all x2, local copies, waits for them, and re-layouts, rows_first(): part = lax.all_to_all(part, 'rows', 1, 3, tiled=True)  9.77 us
    reduce_sum x1, other arithmetic, body(): average = jnp.mean(flat, axis=-1, keepdims=True)  9.44 us
    all_to_all x2, starting transfers between devices, rows_first(): part = lax.all_to_all(part, 'rows', 1, 3, tiled=True)  9.27 us
  transfers between devices with their start and end apart: 15, of which 9 were waited for; matrix products, arithmetic and copies ran while one was open for 20% of the time, Pallas kernels for 0%

profile of v16, /device:TPU:0, one launch (start us, length us, event | category | flops | bytes accessed | tf_op | source)
XLA Modules:
  0.0 430.5 jit_solution(13287643251108786847)
XLA Ops:
  15.4 2.5 slice_reduce_fusion.49
  19.2 9.4 %fusion.110 = (f32[4,32]{1,0:T(4,128)S(1)}, f32[1,4,32,1536]{3,2,1,0:T(8,128)S(1)}) fusion(f32[1536]{0:T(1024)S(1)} %get-tuple-element.121, f32[1536]{0:T(1024)S(1)} %get-tuple-element.122, f32[1536]{0:T(1024)S(1)} %get-tuple-element.75, f32[1536]{0:T(1024)S(1)} %get-tuple-element.76, f32[1,10,32,1536]{3,2,1,0:T(8,128)S(1)} %maximum_convert_fusion, ...), kind=kLoop, calls=%fused_computation.331 | loop fusion | flops 19267456 | bytes 8641024 | tf_op jit(solution)/shard_map/reduce_sum | solution.py:83
  31.9 6.1 %all-to-all-start.1 = ((bf16[4,768,96]{1,2,0:T(8,128)(2,1)}), bf16[4,768,96]{1,2,0:T(8,128)(2,1)S(1)}, u32[]{:S(2)}, u32[]{:S(2)}) async-start(bf16[4,768,96]{1,2,0:T(8,128)(2,1)} %bitcast.91), calls=%async_computation.1 | async-start | bytes 1179648 | tf_op jit(solution)/shard_map/all_to_all | solution.py:68
  38.0 2.5 reshape.565
  42.4 7.0 %all-to-all-done.1 = bf16[4,768,96]{1,2,0:T(8,128)(2,1)S(1)} async-done(((bf16[4,768,96]{1,2,0:T(8,128)(2,1)}), bf16[4,768,96]{1,2,0:T(8,128)(2,1)S(1)}, u32[]{:S(2)}, u32[]{:S(2)}) %all-to-all-start.1) | async-done | bytes 589856 | tf_op jit(solution)/shard_map/all_to_all | solution.py:68
  49.5 2.9 broadcast_in_dim.8
  52.4 5.3 %all-to-all-start = ((bf16[16,96,768]{2,1,0:T(8,128)(2,1)}), bf16[16,96,768]{2,1,0:T(8,128)(2,1)}, u32[]{:S(2)}, u32[]{:S(2)}) async-start(bf16[16,96,768]{2,1,0:T(8,128)(2,1)} %bitcast.85), calls=%async_computation | async-start | bytes 4718592 | tf_op jit(solution)/shard_map/all_to_all | solution.py:66
  58.7 44.9 %all-to-all-done = bf16[16,96,768]{2,1,0:T(8,128)(2,1)} async-done(((bf16[16,96,768]{2,1,0:T(8,128)(2,1)}), bf16[16,96,768]{2,1,0:T(8,128)(2,1)}, u32[]{:S(2)}, u32[]{:S(2)}) %all-to-all-start) | async-done | bytes 2359328 | tf_op jit(solution)/shard_map/all_to_all | solution.py:66
  103.6 7.4 %multiply_convert_fusion = (bf16[1024,768]{1,0:T(8,128)(2,1)}, f32[1024,768]{1,0:T(8,128)}) fusion(bf16[1536,768]{1,0:T(8,128)(2,1)} %bitcast.5, bf16[2,1024,1536]{2,1,0:T(8,128)(2,1)} %all-gather.3.cloned.1.call-done), kind=kOutput, calls=%fused_computation.101 | convolution fusion | flops 2419851264 | bytes 10223616 | tf_op jit(solution)/shard_map/dot_general | solution.py:91
  111.0 43.3 %all-gather.5.cloned.1.call-done = bf16[768,1536]{0,1:T(8,128)(2,1)} async-done(((bf16[768,384]{0,1:T(8,128)(2,1)}), bf16[768,1536]{0,1:T(8,128)(2,1)}) %all-gather.5.cloned.1.call-update) | async-done | bytes 2359312 | tf_op jit(solution)/shard_map/all_gather | solution.py:69
  154.3 6.6 %fusion.7 = bf16[1024,768]{1,0:T(8,128)(2,1)S(1)} fusion(f32[1024,768]{1,0:T(8,128)} %get-tuple-element.134, bf16[768,1536]{0,1:T(8,128)(2,1)} %all-gather.5.cloned.1.call-done, bf16[2,1024,1536]{2,1,0:T(8,128)(2,1)} %all-gather.3.cloned.1.call-done), kind=kOutput, calls=%fused_computation.98 | convolution fusion | flops 2423783424 | bytes 10223616 | tf_op jit(solution)/shard_map/dot_general | solution.py:97
  161.0 5.1 %fusion.1 = bf16[1,1024,1536]{2,1,0:T(8,128)(2,1)S(1)} fusion(bf16[1024,768]{1,0:T(8,128)(2,1)S(1)} %fusion.7, bf16[1536,768]{1,0:T(8,128)(2,1)} %bitcast.5), kind=kOutput, calls=%fused_computation.92 | convolution fusion | flops 2417491968 | bytes 7077888 | tf_op jit(solution)/shard_map/dot_general | solution.py:104
  166.1 2.9 fusion
  169.0 3.2 pad_maximum_fusion
  172.3 5.0 %convolution_convert_fusion.2 = bf16[1536,768]{1,0:T(8,128)(2,1)S(1)} fusion(bf16[1024,768]{1,0:T(8,128)(2,1)} %get-tuple-element.133, bf16[2,1024,1536]{2,1,0:T(8,128)(2,1)} %all-gather.3.cloned.1.call-done), kind=kOutput, calls=%fused_computation.89 | convolution fusion | flops 2417098752 | bytes 7077888 | tf_op jit(solution)/shard_map/dot_general | solution.py:94
  178.9 4.8 %all-to-all-start.3 = ((bf16[4,4,96,768]{3,2,0,1:T(8,128)(2,1)}), bf16[4,4,96,768]{3,2,0,1:T(8,128)(2,1)}, u32[]{:S(2)}, u32[]{:S(2)}) async-start(bf16[4,4,96,768]{3,2,0,1:T(8,128)(2,1)} %copy.44), calls=%async_computation.5 | async-start | bytes 4718592 | tf_op jit(solution)/shard_map/all_to_all | solution.py:119
  183.7 5.5 %convolution_convert_fusion.3 = bf16[1536,768]{1,0:T(8,128)(2,1)S(1)} fusion(bf16[1024,768]{1,0:T(8,128)(2,1)} %copy-done.99, bf16[2,1024,1536]{2,1,0:T(8,128)(2,1)} %all-gather.3.cloned.1.call-done), kind=kOutput, calls=%fused_computation.90 | convolution fusion | flops 2417098752 | bytes 7077888 | tf_op jit(solution)/shard_map/dot_general | solution.py:101
  190.8 35.9 %all-to-all-done.3 = bf16[4,4,96,768]{3,2,0,1:T(8,128)(2,1)} async-done(((bf16[4,4,96,768]{3,2,0,1:T(8,128)(2,1)}), bf16[4,4,96,768]{3,2,0,1:T(8,128)(2,1)}, u32[]{:S(2)}, u32[]{:S(2)}) %all-to-all-start.3) | async-done | bytes 2359328 | tf_op jit(solution)/shard_map/all_to_all | solution.py:119
  226.6 4.5 %all-to-all-start.2 = ((bf16[4,4,96,768]{3,2,0,1:T(8,128)(2,1)}), bf16[4,4,96,768]{3,2,0,1:T(8,128)(2,1)}, u32[]{:S(2)}, u32[]{:S(2)}) async-start(bf16[4,4,96,768]{3,2,0,1:T(8,128)(2,1)} %copy.42), calls=%async_computation.3 | async-start | bytes 4718592 | tf_op jit(solution)/shard_map/all_to_all | solution.py:119
  231.2 4.9 %copy.45 = bf16[4,1,96,4,768]{4,3,2,0,1:T(4,128)(2,1)} copy(bf16[4,1,96,4,768]{4,2,0,3,1:T(8,128)(2,1)} %bitcast.18) | data formatting | bytes 4718592 | tf_op jit(solution)/shard_map/all_to_all | solution.py:119
  236.1 5.3 %reshape.572 = bf16[4,96,3072]{2,1,0:T(8,128)(2,1)} reshape(bf16[4,1,96,4,768]{4,3,2,0,1:T(4,128)(2,1)} %copy.45) | data formatting | bytes 4718592 | tf_op jit(solution)/shard_map/reshape | solution.py:120
  241.4 26.8 %all-to-all-done.2 = bf16[4,4,96,768]{3,2,0,1:T(8,128)(2,1)} async-done(((bf16[4,4,96,768]{3,2,0,1:T(8,128)(2,1)}), bf16[4,4,96,768]{3,2,0,1:T(8,128)(2,1)}, u32[]{:S(2)}, u32[]{:S(2)}) %all-to-all-start.2) | async-done | bytes 2359328 | tf_op jit(solution)/shard_map/all_to_all | solution.py:119
  268.1 4.5 %all-to-all-start.4 = ((bf16[4,96,3072]{2,1,0:T(8,128)(2,1)}), bf16[4,96,3072]{2,1,0:T(8,128)(2,1)}, u32[]{:S(2)}, u32[]{:S(2)}) async-start(bf16[4,96,3072]{2,1,0:T(8,128)(2,1)} %reshape.572), calls=%async_computation.6 | async-start | bytes 4718592 | tf_op jit(solution)/shard_map/all_to_all | solution.py:122
  273.0 4.9 %copy.43 = bf16[4,1,96,4,768]{4,3,2,0,1:T(4,128)(2,1)} copy(bf16[4,1,96,4,768]{4,2,0,3,1:T(8,128)(2,1)} %bitcast.14) | data formatting | bytes 4718592 | tf_op jit(solution)/shard_map/all_to_all | solution.py:119
  277.8 5.3 %reshape.569 = bf16[4,96,3072]{2,1,0:T(8,128)(2,1)} reshape(bf16[4,1,96,4,768]{4,3,2,0,1:T(4,128)(2,1)} %copy.43) | data formatting | bytes 4718592 | tf_op jit(solution)/shard_map/reshape | solution.py:120
  283.2 81.4 %all-to-all-done.4 = bf16[4,96,3072]{2,1,0:T(8,128)(2,1)} async-done(((bf16[4,96,3072]{2,1,0:T(8,128)(2,1)}), bf16[4,96,3072]{2,1,0:T(8,128)(2,1)}, u32[]{:S(2)}, u32[]{:S(2)}) %all-to-all-start.4) | async-done | bytes 2359328 | tf_op jit(solution)/shard_map/all_to_all | solution.py:122
  364.5 3.2 convert_reduce_fusion
  386.5 2.6 all-to-all-start.5
  396.0 6.3 %all-to-all-done.5 = f32[32,2,1536]{2,1,0:T(2,128)S(1)} async-done(((f32[32,2,1536]{2,1,0:T(2,128)}), f32[32,2,1536]{2,1,0:T(2,128)S(1)}, u32[]{:S(2)}, u32[]{:S(2)}) %all-to-all-start.5) | async-done | bytes 393248 | tf_op jit(solution)/shard_map/all_to_all | solution.py:49
  403.3 3.9 all-to-all-start.6
  407.6 7.4 %fusion.97 = bf16[1,4,32,1536]{3,2,1,0:T(8,128)(2,1)} fusion(f32[1,10,32,1536]{3,2,1,0:T(8,128)S(1)} %maximum_convert_fusion.1, f32[1536]{0:T(1024)S(1)} %copy-done.25, f32[1536]{0:T(1024)S(1)} %copy-done.27, f32[1536]{0:T(1024)S(1)} %copy-done.31, f32[1536]{0:T(1024)S(1)} %copy-done.33, f32[1536]{0:T(1024)S(1)} %copy-done.35, f32[1536]{0:T(1024)S(1)} %copy-done.37, ...), kind=kLoop, calls=%fused_computation.194 | loop fusion | flops 19660800 | bytes 8640512 | tf_op jit(solution)/shard_map/convert_element_type | solution.py:150
  415.0 5.1 %all-to-all-done.6 = f32[32,2,1536]{2,1,0:T(2,128)S(1)} async-done(((f32[32,2,1536]{2,1,0:T(2,128)}), f32[32,2,1536]{2,1,0:T(2,128)S(1)}, u32[]{:S(2)}, u32[]{:S(2)}) %all-to-all-start.6) | async-done | bytes 393248 | tf_op jit(solution)/shard_map/all_to_all | solution.py:51
  (310 shorter events, 48.2 us)
Async XLA Ops:
  7.2 96.4 %all-gather.3.cloned.1.call-start = ((), (), s32[]{:S(2)}) async-start(), calls=%async_computation.9 | async-start | bytes 7077888 | tf_op jit(solution)/shard_map/all_gather | solution.py:89
  8.3 9.7 %collective-permute-start = (bf16[1,3,32,1536]{3,2,1,0:T(8,128)(2,1)S(1)}, bf16[1,3,32,1536]{3,2,1,0:T(8,128)(2,1)S(1)}, u32[]{:S(2)}, u32[]{:S(2)}) collective-permute-start(bf16[1,3,32,1536]{3,2,1,0:T(8,128)(2,1)S(1)} %get-tuple-element.131), channel_id=1, source_target_pairs={{0,1},{1,2},{2,3},{4,5},{5,6},{6,7},{8,9},{9,10},{10,11},{12,13},{... | collective-permute-start | bytes 884744 | tf_op jit(solution)/shard_map/ppermute | solution.py:25
  10.7 7.3 %collective-permute-start.1 = (bf16[1,3,32,1536]{3,2,1,0:T(8,128)(2,1)S(1)}, bf16[1,3,32,1536]{3,2,1,0:T(8,128)(2,1)S(1)}, u32[]{:S(2)}, u32[]{:S(2)}) collective-permute-start(bf16[1,3,32,1536]{3,2,1,0:T(8,128)(2,1)S(1)} %get-tuple-element.132), channel_id=1, source_target_pairs={{1,0},{2,1},{3,2},{5,4},{6,5},{7,6},{9,8},{10,9},{11,10},{13,12},{... | collective-permute-start | bytes 884744 | tf_op jit(solution)/shard_map/ppermute | solution.py:26
  13.4 15.3 %copy-start.8 = (f32[1536]{0:T(1024)}, f32[1536]{0:T(1024)S(1)}, u32[]{:S(2)}) copy-start(f32[1536]{0:T(1024)S(1)} %get-tuple-element.113) | copy-start | bytes 18436
  13.4 15.3 %copy-start.10 = (f32[1536]{0:T(1024)}, f32[1536]{0:T(1024)S(1)}, u32[]{:S(2)}) copy-start(f32[1536]{0:T(1024)S(1)} %get-tuple-element.114) | copy-start | bytes 18436
  13.4 15.3 %copy-start.12 = (f32[1536]{0:T(1024)}, f32[1536]{0:T(1024)S(1)}, u32[]{:S(2)}) copy-start(f32[1536]{0:T(1024)S(1)} %get-tuple-element.115) | copy-start | bytes 18436
  13.4 15.3 %copy-start.14 = (f32[1536]{0:T(1024)}, f32[1536]{0:T(1024)S(1)}, u32[]{:S(2)}) copy-start(f32[1536]{0:T(1024)S(1)} %get-tuple-element.116) | copy-start | bytes 18436
  13.4 15.3 %copy-start.16 = (f32[1536]{0:T(1024)}, f32[1536]{0:T(1024)S(1)}, u32[]{:S(2)}) copy-start(f32[1536]{0:T(1024)S(1)} %get-tuple-element.117) | copy-start | bytes 18436
  13.4 15.3 %copy-start.18 = (f32[1536]{0:T(1024)}, f32[1536]{0:T(1024)S(1)}, u32[]{:S(2)}) copy-start(f32[1536]{0:T(1024)S(1)} %get-tuple-element.118) | copy-start | bytes 18436
  13.4 15.3 %copy-start.20 = (f32[1536]{0:T(1024)}, f32[1536]{0:T(1024)S(1)}, u32[]{:S(2)}) copy-start(f32[1536]{0:T(1024)S(1)} %get-tuple-element.119) | copy-start | bytes 18436
  13.4 15.3 %copy-start.22 = (f32[1536]{0:T(1024)}, f32[1536]{0:T(1024)S(1)}, u32[]{:S(2)}) copy-start(f32[1536]{0:T(1024)S(1)} %get-tuple-element.120) | copy-start | bytes 18436
  13.5 15.3 %copy-start.24 = (f32[1536]{0:T(1024)}, f32[1536]{0:T(1024)S(1)}, u32[]{:S(2)}) copy-start(f32[1536]{0:T(1024)S(1)} %get-tuple-element.121) | copy-start | bytes 18436
  13.5 15.3 %copy-start.26 = (f32[1536]{0:T(1024)}, f32[1536]{0:T(1024)S(1)}, u32[]{:S(2)}) copy-start(f32[1536]{0:T(1024)S(1)} %get-tuple-element.122) | copy-start | bytes 18436
  31.9 17.6 %all-to-all-start.1 = ((bf16[4,768,96]{1,2,0:T(8,128)(2,1)}), bf16[4,768,96]{1,2,0:T(8,128)(2,1)S(1)}, u32[]{:S(2)}, u32[]{:S(2)}) async-start(bf16[4,768,96]{1,2,0:T(8,128)(2,1)} %bitcast.91), calls=%async_computation.1 | async-start | bytes 1179648 | tf_op jit(solution)/shard_map/all_to_all | solution.py:68
  52.4 51.2 %all-to-all-start = ((bf16[16,96,768]{2,1,0:T(8,128)(2,1)}), bf16[16,96,768]{2,1,0:T(8,128)(2,1)}, u32[]{:S(2)}, u32[]{:S(2)}) async-start(bf16[16,96,768]{2,1,0:T(8,128)(2,1)} %bitcast.85), calls=%async_computation | async-start | bytes 4718592 | tf_op jit(solution)/shard_map/all_to_all | solution.py:66
  57.7 96.6 %all-gather.5.cloned.1.call-start = ((), (), s32[]{:S(2)}) async-start(), calls=%async_computation.10 | async-start | bytes 2949120 | tf_op jit(solution)/shard_map/all_gather | solution.py:69
  58.4 309.3 %reduce-scatter.3.cloned.1.call-start = ((), (), s32[]{:S(2)}) async-start(), calls=%async_computation.11 | async-start | bytes 7077888 | tf_op jit(solution)/shard_map/reduce_scatter | solution.py:107
  178.9 47.8 %all-to-all-start.3 = ((bf16[4,4,96,768]{3,2,0,1:T(8,128)(2,1)}), bf16[4,4,96,768]{3,2,0,1:T(8,128)(2,1)}, u32[]{:S(2)}, u32[]{:S(2)}) async-start(bf16[4,4,96,768]{3,2,0,1:T(8,128)(2,1)} %copy.44), calls=%async_computation.5 | async-start | bytes 4718592 | tf_op jit(solution)/shard_map/all_to_all | solution.py:119
  226.6 41.5 %all-to-all-start.2 = ((bf16[4,4,96,768]{3,2,0,1:T(8,128)(2,1)}), bf16[4,4,96,768]{3,2,0,1:T(8,128)(2,1)}, u32[]{:S(2)}, u32[]{:S(2)}) async-start(bf16[4,4,96,768]{3,2,0,1:T(8,128)(2,1)} %copy.42), calls=%async_computation.3 | async-start | bytes 4718592 | tf_op jit(solution)/shard_map/all_to_all | solution.py:119
  268.1 96.4 %all-to-all-start.4 = ((bf16[4,96,3072]{2,1,0:T(8,128)(2,1)}), bf16[4,96,3072]{2,1,0:T(8,128)(2,1)}, u32[]{:S(2)}, u32[]{:S(2)}) async-start(bf16[4,96,3072]{2,1,0:T(8,128)(2,1)} %reshape.572), calls=%async_computation.6 | async-start | bytes 4718592 | tf_op jit(solution)/shard_map/all_to_all | solution.py:122
  272.7 149.1 %reduce-scatter.5.cloned.1.call-start = ((), (), s32[]{:S(2)}) async-start(), calls=%async_computation.12 | async-start | bytes 2949120 | tf_op jit(solution)/shard_map/reduce_scatter | solution.py:124
  386.5 15.8 %all-to-all-start.5 = ((f32[32,2,1536]{2,1,0:T(2,128)}), f32[32,2,1536]{2,1,0:T(2,128)S(1)}, u32[]{:S(2)}, u32[]{:S(2)}) async-start(f32[32,2,1536]{2,1,0:T(2,128)} %reshape.574), calls=%async_computation.7 | async-start | bytes 786432 | tf_op jit(solution)/shard_map/all_to_all | solution.py:49
  389.2 4.6 %collective-permute-start.2 = (bf16[1,3,32,1536]{3,2,1,0:T(8,128)(2,1)S(1)}, bf16[1,3,32,1536]{3,2,1,0:T(8,128)(2,1)S(1)}, u32[]{:S(2)}, u32[]{:S(2)}) collective-permute-start(bf16[1,3,32,1536]{3,2,1,0:T(8,128)(2,1)S(1)} %get-tuple-element.129), channel_id=1, source_target_pairs={{0,1},{1,2},{2,3},{4,5},{5,6},{6,7},{8,9},{9,10},{10,11},{12,13},{... | collective-permute-start | bytes 884744 | tf_op jit(solution)/shard_map/ppermute | solution.py:25
  391.2 4.6 %collective-permute-start.3 = (bf16[1,3,32,1536]{3,2,1,0:T(8,128)(2,1)S(1)}, bf16[1,3,32,1536]{3,2,1,0:T(8,128)(2,1)S(1)}, u32[]{:S(2)}, u32[]{:S(2)}) collective-permute-start(bf16[1,3,32,1536]{3,2,1,0:T(8,128)(2,1)S(1)} %get-tuple-element.130), channel_id=1, source_target_pairs={{1,0},{2,1},{3,2},{5,4},{6,5},{7,6},{9,8},{10,9},{11,10},{13,12},{... | collective-permute-start | bytes 884744 | tf_op jit(solution)/shard_map/ppermute | solution.py:26
  393.4 13.9 %copy-start.15 = (f32[1536]{0:T(1024)S(1)}, f32[1536]{0:T(1024)}, u32[]{:S(2)}) copy-start(f32[1536]{0:T(1024)} %copy-done.14) | copy-start | bytes 18436
  393.4 13.9 %copy-start.17 = (f32[1536]{0:T(1024)S(1)}, f32[1536]{0:T(1024)}, u32[]{:S(2)}) copy-start(f32[1536]{0:T(1024)} %copy-done.16) | copy-start | bytes 18436
  393.4 13.9 %copy-start.19 = (f32[1536]{0:T(1024)S(1)}, f32[1536]{0:T(1024)}, u32[]{:S(2)}) copy-start(f32[1536]{0:T(1024)} %copy-done.18) | copy-start | bytes 18436
  393.4 13.9 %copy-start.21 = (f32[1536]{0:T(1024)S(1)}, f32[1536]{0:T(1024)}, u32[]{:S(2)}) copy-start(f32[1536]{0:T(1024)} %copy-done.20) | copy-start | bytes 18436
  393.4 13.9 %copy-start.23 = (f32[1536]{0:T(1024)S(1)}, f32[1536]{0:T(1024)}, u32[]{:S(2)}) copy-start(f32[1536]{0:T(1024)} %copy-done.22) | copy-start | bytes 18436
  393.4 13.9 %copy-start.25 = (f32[1536]{0:T(1024)S(1)}, f32[1536]{0:T(1024)}, u32[]{:S(2)}) copy-start(f32[1536]{0:T(1024)} %copy-done.24) | copy-start | bytes 18436
  393.4 13.9 %copy-start.27 = (f32[1536]{0:T(1024)S(1)}, f32[1536]{0:T(1024)}, u32[]{:S(2)}) copy-start(f32[1536]{0:T(1024)} %copy-done.26) | copy-start | bytes 18436
  403.3 16.8 %all-to-all-start.6 = ((f32[32,2,1536]{2,1,0:T(2,128)}), f32[32,2,1536]{2,1,0:T(2,128)S(1)}, u32[]{:S(2)}, u32[]{:S(2)}) async-start(f32[32,2,1536]{2,1,0:T(2,128)} %broadcast_in_dim.11), calls=%async_computation.8 | async-start | bytes 786432 | tf_op jit(solution)/shard_map/all_to_all | solution.py:51
  (84 other events, 930.3 us)
Sparse Core Ops, SparseCore 0:
  30.9 67.5 all-gather.2
  100.6 53.6 all-gather.4
  172.4 81.4 reduce-scatter.2
  283.3 79.8 reduce-scatter.4

commit v17 on v13

--- a/solution.py
+++ b/solution.py
@@ -114,8 +114,9 @@
     resid = feature_maps.reshape(cells, width).astype(jnp.float32)
     result = (resid + layer_scale * branch).astype(jnp.bfloat16).reshape(feature_maps.shape)
     scale_part = jnp.sum(cotan * branch, axis=0)
-    grad_parts = jnp.stack([up_part, down_part_t]).astype(jnp.bfloat16)
-    grad_sums = lax.psum_scatter(grad_parts, "dp", scatter_dimension=1, tiled=True)
+    blocks = jnp.stack([up_part, down_part_t]).astype(jnp.bfloat16).reshape(2, dp_size, -1, sub)
+    grad_sums = lax.all_to_all(blocks, "dp", 1, 1, tiled=True).astype(jnp.float32).sum(1)
+    grad_sums = grad_sums.astype(jnp.bfloat16)
     gain_part = jnp.sum(norm_grad * normed, axis=0)
     scaled_grad = norm_grad * norm_gain
     conv_grad = rstd * (

time: 373 us -> 374 us (level)
  waiting for transfers between devices: 215 us -> 206 us
  other arithmetic: 38.1 us -> 44.7 us
  local copies, waits for them, and re-layouts: 34.9 us -> 40.9 us
    all_to_all x0 -> x1, waiting for transfers between devices: none -> 43 us  [body(): lax.all_to_all(blocks, 'dp', 1, 1, tiled=True).astype(jnp.float32).sum(1)]
    reduce_scatter x1 -> x0, waiting for transfers between devices: 24.5 us -> none  [body(): lax.psum_scatter(grad_parts, 'dp', scatter_dimension=1, tiled=True)]
    all_to_all x1, waiting for transfers between devices: 15.3 us -> 4.84 us  [small_sums(): lax.all_to_all(spread, every, 0, 0, tiled=True)]
    all_to_all x1, waiting for transfers between devices: 13.2 us -> 4.07 us  [small_sums(): lax.all_to_all(packed.reshape(devices, per, width), every, 0, 0, tiled=True)]
    all_to_all x0 -> x1, starting transfers between devices: none -> 4.98 us  [body(): lax.all_to_all(blocks, 'dp', 1, 1, tiled=True).astype(jnp.float32).sum(1)]
    reduce_scatter x1, waiting for transfers between devices: 47.6 us -> 43.4 us  [body(): lax.psum_scatter(jnp.stack([mlp_terms, norm_terms]).astype(jnp.bfloat16),...]
where the time goes in v17:
time: 374 us; the launch traced here: 372 us
  waiting for transfers between devices  206 us (55%)
  other arithmetic  44.7 us (12%)
  local copies, waits for them, and re-layouts  40.9 us (11%)
  starting transfers between devices  37 us (10%)
  matrix products  28.6 us (8%)
  between operations  15.4 us (4%)
    all_to_all x1, waiting for transfers between devices, body(): up_loc = lax.all_to_all(pieces, ('dp', 'rows'), 0, 0, tiled=True)  44.9 us
    all_gather x1, waiting for transfers between devices, body(): down_loc = lax.all_gather(down_loc, 'dp', axis=1, tiled=True)  44.3 us
    reduce_scatter x1, waiting for transfers between devices, body(): lax.psum_scatter(jnp.stack([mlp_terms, norm_terms]).astype(jnp.bfloat16),...  43.4 us
    all_to_all x1, waiting for transfers between devices, body(): lax.all_to_all(blocks, 'dp', 1, 1, tiled=True).astype(jnp.float32).sum(1)  43 us
    all_to_all x1, waiting for transfers between devices, body(): lax.all_to_all(grad_sums, 'rows', 1, 2, tiled=True).astype(jnp.float32)  13.8 us
    reduce_sum x1, other arithmetic, body(): average = jnp.mean(flat, axis=-1, keepdims=True)  8.54 us
    convert_element_type x1, other arithmetic, body(): grad_x = (d_out.astype(jnp.float32) + back_conv).astype(jnp.bfloat16)  8.33 us
    dot_general x1, matrix products, body(): hidden = jnp.dot(gathered, up_loc, preferred_element_type=jnp.float32)  7.63 us
  transfers between devices with their start and end apart: 13, of which 9 were waited for; matrix products, arithmetic and copies ran while one was open for 17% of the time, Pallas kernels for 0%

profile of v17, /device:TPU:0, one launch (start us, length us, event | category | flops | bytes accessed | tf_op | source)
XLA Modules:
  0.0 372.3 jit_solution(11304591414220803026)
XLA Ops:
  8.4 2.4 collective-permute-start
  17.7 8.5 %fusion.114 = (f32[4,32]{1,0:T(4,128)S(1)}, f32[1,4,32,1536]{3,2,1,0:T(8,128)S(1)}) fusion(f32[1536]{0:T(1024)S(1)} %copy-done.18, f32[1536]{0:T(1024)S(1)} %copy-done.19, f32[1536]{0:T(1024)S(1)} %get-tuple-element.73, f32[1536]{0:T(1024)S(1)} %get-tuple-element.74, f32[1,10,32,1536]{3,2,1,0:T(8,128)S(1)} %maximum_convert_fusion, ...), kind=kLoop, calls=%fused_computation.332 | loop fusion | flops 19267456 | bytes 8659456 | tf_op jit(solution)/shard_map/reduce_sum | solution.py:83
  36.2 6.3 %all-to-all-start.1 = ((bf16[4,768,96]{1,2,0:T(8,128)(2,1)}), bf16[4,768,96]{1,2,0:T(8,128)(2,1)S(1)}, u32[]{:S(2)}, u32[]{:S(2)}) async-start(bf16[4,768,96]{1,2,0:T(8,128)(2,1)} %bitcast.101), calls=%async_computation.1 | async-start | bytes 1179648 | tf_op jit(solution)/shard_map/all_to_all | solution.py:68
  42.6 2.5 reshape.574
  47.0 6.6 %all-to-all-done.1 = bf16[4,768,96]{1,2,0:T(8,128)(2,1)S(1)} async-done(((bf16[4,768,96]{1,2,0:T(8,128)(2,1)}), bf16[4,768,96]{1,2,0:T(8,128)(2,1)S(1)}, u32[]{:S(2)}, u32[]{:S(2)}) %all-to-all-start.1) | async-done | bytes 589856 | tf_op jit(solution)/shard_map/all_to_all | solution.py:68
  53.6 2.9 broadcast_in_dim.8
  56.5 6.0 %all-to-all-start = ((bf16[16,96,768]{2,1,0:T(8,128)(2,1)}), bf16[16,96,768]{2,1,0:T(8,128)(2,1)}, u32[]{:S(2)}, u32[]{:S(2)}) async-start(bf16[16,96,768]{2,1,0:T(8,128)(2,1)} %bitcast.91), calls=%async_computation | async-start | bytes 4718592 | tf_op jit(solution)/shard_map/all_to_all | solution.py:66
  63.6 44.9 %all-to-all-done = bf16[16,96,768]{2,1,0:T(8,128)(2,1)} async-done(((bf16[16,96,768]{2,1,0:T(8,128)(2,1)}), bf16[16,96,768]{2,1,0:T(8,128)(2,1)}, u32[]{:S(2)}, u32[]{:S(2)}) %all-to-all-start) | async-done | bytes 2359328 | tf_op jit(solution)/shard_map/all_to_all | solution.py:66
  108.5 7.6 %multiply_convert_fusion = (bf16[1024,768]{1,0:T(8,128)(2,1)}, f32[1024,768]{1,0:T(8,128)}) fusion(bf16[1536,768]{1,0:T(8,128)(2,1)} %bitcast.5, bf16[2,1024,1536]{1,2,0:T(8,128)(2,1)} %all-gather.3.cloned.1.call-done), kind=kOutput, calls=%fused_computation.101 | convolution fusion | flops 2419851264 | bytes 10223616 | tf_op jit(solution)/shard_map/dot_general | solution.py:91
  116.1 44.3 %all-gather.5.cloned.1.call-done = bf16[768,1536]{0,1:T(8,128)(2,1)} async-done(((bf16[768,384]{0,1:T(8,128)(2,1)}), bf16[768,1536]{0,1:T(8,128)(2,1)}) %all-gather.5.cloned.1.call-update) | async-done | bytes 2359312 | tf_op jit(solution)/shard_map/all_gather | solution.py:69
  160.4 7.0 %fusion.7 = bf16[1024,768]{1,0:T(8,128)(2,1)S(1)} fusion(f32[1024,768]{1,0:T(8,128)} %get-tuple-element.136, bf16[768,1536]{0,1:T(8,128)(2,1)} %all-gather.5.cloned.1.call-done, bf16[2,1024,1536]{1,2,0:T(8,128)(2,1)} %all-gather.3.cloned.1.call-done), kind=kOutput, calls=%fused_computation.96 | convolution fusion | flops 2423783424 | bytes 10223616 | tf_op jit(solution)/shard_map/dot_general | solution.py:97
  167.5 5.5 %fusion.1 = bf16[1,1024,1536]{2,1,0:T(8,128)(2,1)S(1)} fusion(bf16[1024,768]{1,0:T(8,128)(2,1)S(1)} %fusion.7, bf16[1536,768]{1,0:T(8,128)(2,1)} %bitcast.5), kind=kOutput, calls=%fused_computation.90 | convolution fusion | flops 2417491968 | bytes 7077888 | tf_op jit(solution)/shard_map/dot_general | solution.py:104
  173.0 2.9 fusion
  175.9 3.2 pad_maximum_fusion
  179.1 3.7 fusion.115
  182.8 2.8 convert_bitcast_fusion.2
  185.6 2.8 convert_bitcast_fusion.1
  188.9 2.6 copy.56
  191.5 5.0 %all-to-all-start.2 = ((bf16[2,4,384,768]{3,2,0,1:T(8,128)(2,1)}), bf16[2,4,384,768]{3,2,0,1:T(8,128)(2,1)}, u32[]{:S(2)}, u32[]{:S(2)}) async-start(bf16[2,4,384,768]{3,2,0,1:T(8,128)(2,1)} %copy.56), calls=%async_computation.3 | async-start | bytes 9437184 | tf_op jit(solution)/shard_map/all_to_all | solution.py:118
  196.5 43.4 %reduce-scatter.2.cloned.1.call-done = bf16[2,128,1536]{2,1,0:T(8,128)(2,1)} async-done(((bf16[2,1024,1536]{2,1,0:T(8,128)(2,1)}), bf16[2,128,1536]{2,1,0:T(8,128)(2,1)}) %reduce-scatter.2.cloned.1.call-update) | async-done | bytes 786448 | tf_op jit(solution)/shard_map/reduce_scatter | solution.py:107
  250.1 2.4 multiply_reduce_fusion
  258.2 43.0 %all-to-all-done.2 = bf16[2,4,384,768]{3,2,0,1:T(8,128)(2,1)} async-done(((bf16[2,4,384,768]{3,2,0,1:T(8,128)(2,1)}), bf16[2,4,384,768]{3,2,0,1:T(8,128)(2,1)}, u32[]{:S(2)}, u32[]{:S(2)}) %all-to-all-start.2) | async-done | bytes 4718624 | tf_op jit(solution)/shard_map/all_to_all | solution.py:118
  301.2 3.8 %all-to-all-start.3 = ((f32[32,2,1536]{2,1,0:T(2,128)}), f32[32,2,1536]{2,1,0:T(2,128)}, u32[]{:S(2)}, u32[]{:S(2)}) async-start(f32[32,2,1536]{2,1,0:T(2,128)} %reshape.580), calls=%async_computation.4 | async-start | bytes 786432 | tf_op jit(solution)/shard_map/all_to_all | solution.py:49
  305.0 2.1 collective-permute-start.2
  308.7 3.4 reduce_sum.518
  314.1 4.1 %all-to-all-done.3 = f32[32,2,1536]{2,1,0:T(2,128)} async-done(((f32[32,2,1536]{2,1,0:T(2,128)}), f32[32,2,1536]{2,1,0:T(2,128)}, u32[]{:S(2)}, u32[]{:S(2)}) %all-to-all-start.3) | async-done | bytes 393248 | tf_op jit(solution)/shard_map/all_to_all | solution.py:49
  320.1 4.7 %all-to-all-start.4 = ((f32[32,2,1536]{2,1,0:T(2,128)}), f32[32,2,1536]{2,1,0:T(2,128)S(1)}, u32[]{:S(2)}, u32[]{:S(2)}) async-start(f32[32,2,1536]{2,1,0:T(2,128)} %broadcast_in_dim.11), calls=%async_computation.5 | async-start | bytes 786432 | tf_op jit(solution)/shard_map/all_to_all | solution.py:51
  324.9 8.3 %fusion.103 = bf16[1,4,32,1536]{3,2,1,0:T(8,128)(2,1)} fusion(f32[1,10,32,1536]{3,2,1,0:T(8,128)S(1)} %maximum_convert_fusion.1, f32[1536]{0:T(1024)} %get-tuple-element.119, f32[1536]{0:T(1024)} %get-tuple-element.120, f32[1536]{0:T(1024)} %copy-done.21, f32[1536]{0:T(1024)} %copy-done.22, f32[1536]{0:T(1024)} %copy-done.23, f32[1536]{0:T(1024)} %copy-done.24, ...), kind=kLoop, calls=%fused_computation.197 | loop fusion | flops 19660800 | bytes 8562688 | tf_op jit(solution)/shard_map/convert_element_type | solution.py:144
  333.2 4.8 %all-to-all-done.4 = f32[32,2,1536]{2,1,0:T(2,128)S(1)} async-done(((f32[32,2,1536]{2,1,0:T(2,128)}), f32[32,2,1536]{2,1,0:T(2,128)S(1)}, u32[]{:S(2)}, u32[]{:S(2)}) %all-to-all-start.4) | async-done | bytes 393248 | tf_op jit(solution)/shard_map/all_to_all | solution.py:51
  339.7 2.2 copy.58
  342.0 3.5 all-to-all-start.5
  347.5 13.8 %all-to-all-done.5 = bf16[2,384,768]{2,0,1:T(2,128)(2,1)S(1)} async-done(((bf16[2,384,768]{2,0,1:T(2,128)(2,1)}), bf16[2,384,768]{2,0,1:T(2,128)(2,1)S(1)}, u32[]{:S(2)}, u32[]{:S(2)}) %all-to-all-start.5) | async-done | bytes 1179680 | tf_op jit(solution)/shard_map/all_to_all | solution.py:149
  (249 shorter events, 49.9 us)
Async XLA Ops:
  7.2 101.3 %all-gather.3.cloned.1.call-start = ((), (), s32[]{:S(2)}) async-start(), calls=%async_computation.7 | async-start | bytes 7077888 | tf_op jit(solution)/shard_map/all_gather | solution.py:89
  8.4 8.0 %collective-permute-start = (bf16[1,3,32,1536]{3,2,1,0:T(8,128)(2,1)S(1)}, bf16[1,3,32,1536]{3,2,1,0:T(8,128)(2,1)S(1)}, u32[]{:S(2)}, u32[]{:S(2)}) collective-permute-start(bf16[1,3,32,1536]{3,2,1,0:T(8,128)(2,1)S(1)} %get-tuple-element.133), channel_id=1, source_target_pairs={{0,1},{1,2},{2,3},{4,5},{5,6},{6,7},{8,9},{9,10},{10,11},{12,13},{... | collective-permute-start | bytes 884744 | tf_op jit(solution)/shard_map/ppermute | solution.py:25
  10.8 5.7 %collective-permute-start.1 = (bf16[1,3,32,1536]{3,2,1,0:T(8,128)(2,1)S(1)}, bf16[1,3,32,1536]{3,2,1,0:T(8,128)(2,1)}, u32[]{:S(2)}, u32[]{:S(2)}) collective-permute-start(bf16[1,3,32,1536]{3,2,1,0:T(8,128)(2,1)S(1)} %get-tuple-element.134), channel_id=1, source_target_pairs={{1,0},{2,1},{3,2},{5,4},{6,5},{7,6},{9,8},{10,9},{11,10},{13,12},{... | collective-permute-start | bytes 884744 | tf_op jit(solution)/shard_map/ppermute | solution.py:26
  15.7 10.6 %copy-start.20 = (f32[1536]{0:T(1024)}, f32[1536]{0:T(1024)S(1)}, u32[]{:S(2)}) copy-start(f32[1536]{0:T(1024)S(1)} %get-tuple-element.72) | copy-start | bytes 18436
  15.7 10.6 %copy-start.21 = (f32[1536]{0:T(1024)}, f32[1536]{0:T(1024)S(1)}, u32[]{:S(2)}) copy-start(f32[1536]{0:T(1024)S(1)} %get-tuple-element.73) | copy-start | bytes 18436
  15.7 10.6 %copy-start.22 = (f32[1536]{0:T(1024)}, f32[1536]{0:T(1024)S(1)}, u32[]{:S(2)}) copy-start(f32[1536]{0:T(1024)S(1)} %get-tuple-element.74) | copy-start | bytes 18436
  15.7 10.6 %copy-start.23 = (f32[1536]{0:T(1024)}, f32[1536]{0:T(1024)S(1)}, u32[]{:S(2)}) copy-start(f32[1536]{0:T(1024)S(1)} %get-tuple-element.75) | copy-start | bytes 18436
  15.7 10.6 %copy-start.24 = (f32[1536]{0:T(1024)}, f32[1536]{0:T(1024)S(1)}, u32[]{:S(2)}) copy-start(f32[1536]{0:T(1024)S(1)} %get-tuple-element.76) | copy-start | bytes 18436
  15.8 10.6 %copy-start.25 = (f32[1536]{0:T(1024)}, f32[1536]{0:T(1024)S(1)}, u32[]{:S(2)}) copy-start(f32[1536]{0:T(1024)S(1)} %get-tuple-element.77) | copy-start | bytes 18436
  15.8 10.6 %copy-start.26 = (f32[1536]{0:T(1024)}, f32[1536]{0:T(1024)S(1)}, u32[]{:S(2)}) copy-start(f32[1536]{0:T(1024)S(1)} %get-tuple-element.78) | copy-start | bytes 18436
  15.8 10.6 %copy-start.27 = (f32[1536]{0:T(1024)}, f32[1536]{0:T(1024)S(1)}, u32[]{:S(2)}) copy-start(f32[1536]{0:T(1024)S(1)} %get-tuple-element.79) | copy-start | bytes 18436
  15.8 10.6 %copy-start.28 = (f32[1536]{0:T(1024)}, f32[1536]{0:T(1024)S(1)}, u32[]{:S(2)}) copy-start(f32[1536]{0:T(1024)S(1)} %get-tuple-element.80) | copy-start | bytes 18436
  15.8 10.6 %copy-start.29 = (f32[1536]{0:T(1024)}, f32[1536]{0:T(1024)S(1)}, u32[]{:S(2)}) copy-start(f32[1536]{0:T(1024)S(1)} %get-tuple-element.81) | copy-start | bytes 18436
  15.8 10.6 %copy-start.30 = (f32[1536]{0:T(1024)}, f32[1536]{0:T(1024)S(1)}, u32[]{:S(2)}) copy-start(f32[1536]{0:T(1024)S(1)} %get-tuple-element.82) | copy-start | bytes 18436
  15.8 10.6 %copy-start.31 = (f32[1536]{0:T(1024)}, f32[1536]{0:T(1024)S(1)}, u32[]{:S(2)}) copy-start(f32[1536]{0:T(1024)S(1)} %get-tuple-element.83) | copy-start | bytes 18436
  15.8 10.6 %copy-start.32 = (f32[1536]{0:T(1024)}, f32[1536]{0:T(1024)S(1)}, u32[]{:S(2)}) copy-start(f32[1536]{0:T(1024)S(1)} %get-tuple-element.84) | copy-start | bytes 18436
  15.8 10.6 %copy-start.33 = (f32[1536]{0:T(1024)}, f32[1536]{0:T(1024)S(1)}, u32[]{:S(2)}) copy-start(f32[1536]{0:T(1024)S(1)} %get-tuple-element.85) | copy-start | bytes 18436
  15.8 10.6 %copy-start.34 = (f32[1536]{0:T(1024)}, f32[1536]{0:T(1024)S(1)}, u32[]{:S(2)}) copy-start(f32[1536]{0:T(1024)S(1)} %get-tuple-element.86) | copy-start | bytes 18436
  15.9 10.6 %copy-start.35 = (f32[1536]{0:T(1024)}, f32[1536]{0:T(1024)S(1)}, u32[]{:S(2)}) copy-start(f32[1536]{0:T(1024)S(1)} %get-tuple-element.87) | copy-start | bytes 18436
  15.9 10.6 %copy-start.36 = (f32[1536]{0:T(1024)}, f32[1536]{0:T(1024)S(1)}, u32[]{:S(2)}) copy-start(f32[1536]{0:T(1024)S(1)} %get-tuple-element.88) | copy-start | bytes 18436
  17.7 14.7 %copy-start.8 = (f32[1536]{0:T(1024)S(1)}, f32[1536]{0:T(1024)}, u32[]{:S(2)}) copy-start(f32[1536]{0:T(1024)} %param.9) | copy-start | bytes 18436
  36.2 17.4 %all-to-all-start.1 = ((bf16[4,768,96]{1,2,0:T(8,128)(2,1)}), bf16[4,768,96]{1,2,0:T(8,128)(2,1)S(1)}, u32[]{:S(2)}, u32[]{:S(2)}) async-start(bf16[4,768,96]{1,2,0:T(8,128)(2,1)} %bitcast.101), calls=%async_computation.1 | async-start | bytes 1179648 | tf_op jit(solution)/shard_map/all_to_all | solution.py:68
  56.5 51.9 %all-to-all-start = ((bf16[16,96,768]{2,1,0:T(8,128)(2,1)}), bf16[16,96,768]{2,1,0:T(8,128)(2,1)}, u32[]{:S(2)}, u32[]{:S(2)}) async-start(bf16[16,96,768]{2,1,0:T(8,128)(2,1)} %bitcast.91), calls=%async_computation | async-start | bytes 4718592 | tf_op jit(solution)/shard_map/all_to_all | solution.py:66
  62.6 97.8 %all-gather.5.cloned.1.call-start = ((), (), s32[]{:S(2)}) async-start(), calls=%async_computation.8 | async-start | bytes 2949120 | tf_op jit(solution)/shard_map/all_gather | solution.py:69
  63.3 176.5 %reduce-scatter.2.cloned.1.call-start = ((), (), s32[]{:S(2)}) async-start(), calls=%async_computation.9 | async-start | bytes 7077888 | tf_op jit(solution)/shard_map/reduce_scatter | solution.py:107
  191.5 109.7 %all-to-all-start.2 = ((bf16[2,4,384,768]{3,2,0,1:T(8,128)(2,1)}), bf16[2,4,384,768]{3,2,0,1:T(8,128)(2,1)}, u32[]{:S(2)}, u32[]{:S(2)}) async-start(bf16[2,4,384,768]{3,2,0,1:T(8,128)(2,1)} %copy.56), calls=%async_computation.3 | async-start | bytes 9437184 | tf_op jit(solution)/shard_map/all_to_all | solution.py:118
  301.2 16.9 %all-to-all-start.3 = ((f32[32,2,1536]{2,1,0:T(2,128)}), f32[32,2,1536]{2,1,0:T(2,128)}, u32[]{:S(2)}, u32[]{:S(2)}) async-start(f32[32,2,1536]{2,1,0:T(2,128)} %reshape.580), calls=%async_computation.4 | async-start | bytes 786432 | tf_op jit(solution)/shard_map/all_to_all | solution.py:49
  305.0 7.1 %collective-permute-start.2 = (bf16[1,3,32,1536]{3,2,1,0:T(8,128)(2,1)S(1)}, bf16[1,3,32,1536]{3,2,1,0:T(8,128)(2,1)S(1)}, u32[]{:S(2)}, u32[]{:S(2)}) collective-permute-start(bf16[1,3,32,1536]{3,2,1,0:T(8,128)(2,1)S(1)} %get-tuple-element.131), channel_id=1, source_target_pairs={{0,1},{1,2},{2,3},{4,5},{5,6},{6,7},{8,9},{9,10},{10,11},{12,13},{... | collective-permute-start | bytes 884744 | tf_op jit(solution)/shard_map/ppermute | solution.py:25
  307.1 5.7 %collective-permute-start.3 = (bf16[1,3,32,1536]{3,2,1,0:T(8,128)(2,1)S(1)}, bf16[1,3,32,1536]{3,2,1,0:T(8,128)(2,1)}, u32[]{:S(2)}, u32[]{:S(2)}) collective-permute-start(bf16[1,3,32,1536]{3,2,1,0:T(8,128)(2,1)S(1)} %get-tuple-element.132), channel_id=1, source_target_pairs={{1,0},{2,1},{3,2},{5,4},{6,5},{7,6},{9,8},{10,9},{11,10},{13,12},{... | collective-permute-start | bytes 884744 | tf_op jit(solution)/shard_map/ppermute | solution.py:26
  312.1 12.7 %copy-start.10 = (f32[1536]{0:T(1024)S(1)}, f32[1536]{0:T(1024)}, u32[]{:S(2)}) copy-start(f32[1536]{0:T(1024)} %get-tuple-element.111) | copy-start | bytes 18436
  320.1 17.9 %all-to-all-start.4 = ((f32[32,2,1536]{2,1,0:T(2,128)}), f32[32,2,1536]{2,1,0:T(2,128)S(1)}, u32[]{:S(2)}, u32[]{:S(2)}) async-start(f32[32,2,1536]{2,1,0:T(2,128)} %broadcast_in_dim.11), calls=%async_computation.5 | async-start | bytes 786432 | tf_op jit(solution)/shard_map/all_to_all | solution.py:51
  342.0 19.4 %all-to-all-start.5 = ((bf16[2,384,768]{2,0,1:T(2,128)(2,1)}), bf16[2,384,768]{2,0,1:T(2,128)(2,1)S(1)}, u32[]{:S(2)}, u32[]{:S(2)}) async-start(bf16[2,384,768]{2,0,1:T(2,128)(2,1)} %copy.58), calls=%async_computation.6 | async-start | bytes 2359296 | tf_op jit(solution)/shard_map/all_to_all | solution.py:149
  (51 other events, 320.1 us)
Sparse Core Ops, SparseCore 0:
  35.2 69.3 all-gather.2
  106.7 53.6 all-gather.4
  179.2 60.5 reduce-scatter.1

commit v18 on v15

--- a/solution.py
+++ b/solution.py
@@ -146,9 +146,6 @@
     kernel_part = jnp.stack(kernel_rows).reshape(KS, KS, width)
     grad_x = (d_out.astype(jnp.float32) + back_conv).astype(jnp.bfloat16)
     grad_kernel, grad_gain, grad_scale = small_sums(kernel_part, gain_part, scale_part, width)
-    grad_sums, grad_x, grad_kernel, grad_gain, grad_scale = lax.optimization_barrier(
-        (grad_sums, grad_x, grad_kernel, grad_gain, grad_scale)
-    )
     grad_sums = lax.all_to_all(grad_sums, "rows", 1, 2, tiled=True).astype(jnp.float32)
     grad_up, grad_down = grad_sums[0], grad_sums[1].T
     return (result, grad_x, grad_up, grad_down, grad_kernel, grad_gain, grad_scale)

time: 357 us -> 381 us (1.067); the launches traced: 350 us -> 380 us
  blocking collectives: 0 us -> 111 us
  waiting for transfers between devices: 184 us -> 124 us
  starting transfers between devices: 37 us -> 27.6 us
  other arithmetic: 43 us -> 38.3 us
  matrix products: 35.8 us -> 31.1 us
    all_to_all x0 -> x2, blocking collectives: none -> 111 us  [the longest x1 80 us: body(): lax.all_to_all(down_blocks, 'dp', 0, 0, tiled=True).astype(jnp.float32)]
    reduce_scatter x1, waiting for transfers between devices: 42.4 us -> 14.5 us  [body(): lax.psum_scatter(jnp.stack([mlp_terms, norm_terms]).astype(jnp.bfloat16),...]
    reduce_scatter x1, waiting for transfers between devices: 27.5 us -> 0.02 us  [body(): lax.psum_scatter(up_part.astype(jnp.bfloat16), 'dp', scatter_dimension=0,...]
    all_to_all x2 -> x0, waiting for transfers between devices: 13.8 us -> none  [the longest x1 13.8 us: body(): lax.all_to_all(grad_sums, 'rows', 1, 2, tiled=True).astype(jnp.float32)]
    all_to_all x2 -> x0, starting transfers between devices: 8.01 us -> none  [the longest x1 4.48 us: body(): lax.all_to_all(down_blocks, 'dp', 0, 0, tiled=True).astype(jnp.float32)]
    all_to_all x1, waiting for transfers between devices: 0.01 us -> 6.2 us  [small_sums(): lax.all_to_all(packed.reshape(devices, per, width), every, 0, 0, tiled=True)]
  transfers between devices with their start and end apart: 14 -> 12, of which waited for: 7 -> 7; matrix products, arithmetic and copies ran while one was open for 20% -> 15% of each run, Pallas kernels for 0% -> 0%
where the time goes in v18:
time: 381 us; the launch traced here: 380 us
  waiting for transfers between devices  124 us (33%)
  blocking collectives  111 us (29%)
  other arithmetic  38.3 us (10%)
  local copies, waits for them, and re-layouts  32.1 us (8%)
  matrix products  31.1 us (8%)
  starting transfers between devices  27.6 us (7%)
  between operations  15.8 us (4%)
    all_to_all x1, blocking collectives, body(): lax.all_to_all(down_blocks, 'dp', 0, 0, tiled=True).astype(jnp.float32)  80 us
    all_to_all x1, waiting for transfers between devices, body(): up_loc = lax.all_to_all(pieces, ('dp', 'rows'), 0, 0, tiled=True)  44.9 us
    all_gather x1, waiting for transfers between devices, body(): down_loc = lax.all_gather(down_loc, 'dp', axis=1, tiled=True)  43.2 us
    all_to_all x1, blocking collectives, body(): lax.all_to_all(grad_sums, 'rows', 1, 2, tiled=True).astype(jnp.float32)  31.2 us
    reduce_scatter x1, waiting for transfers between devices, body(): lax.psum_scatter(jnp.stack([mlp_terms, norm_terms]).astype(jnp.bfloat16),...  14.5 us
    reduce_sum x1, other arithmetic, body(): average = jnp.mean(flat, axis=-1, keepdims=True)  9.44 us
  transfers between devices with their start and end apart: 12, of which 7 were waited for; matrix products, arithmetic and copies ran while one was open for 15% of the time, Pallas kernels for 0%

profile of v18, /device:TPU:0, one launch (start us, length us, event | category | flops | bytes accessed | tf_op | source)
XLA Modules:
  0.0 379.9 jit_solution(15461107863779151266)
XLA Ops:
  8.3 2.4 collective-permute-start
  15.6 2.4 slice_reduce_fusion.49
  19.2 9.4 %fusion.110 = (f32[4,32]{1,0:T(4,128)S(1)}, f32[1,4,32,1536]{3,2,1,0:T(8,128)S(1)}) fusion(f32[1536]{0:T(1024)S(1)} %get-tuple-element.109, f32[1536]{0:T(1024)S(1)} %get-tuple-element.110, f32[1536]{0:T(1024)S(1)} %get-tuple-element.63, f32[1536]{0:T(1024)S(1)} %get-tuple-element.64, f32[1,10,32,1536]{3,2,1,0:T(8,128)S(1)} %maximum_convert_fusion, ...), kind=kLoop, calls=%fused_computation.332 | loop fusion | flops 19267456 | bytes 8641024 | tf_op jit(solution)/shard_map/reduce_sum | solution.py:83
  31.9 6.1 %all-to-all-start.1 = ((bf16[4,768,96]{1,2,0:T(8,128)(2,1)}), bf16[4,768,96]{1,2,0:T(8,128)(2,1)S(1)}, u32[]{:S(2)}, u32[]{:S(2)}) async-start(bf16[4,768,96]{1,2,0:T(8,128)(2,1)} %bitcast.94), calls=%async_computation.1 | async-start | bytes 1179648 | tf_op jit(solution)/shard_map/all_to_all | solution.py:68
  38.1 2.5 reshape.558
  40.5 1.9 copy.34
  42.5 7.1 %all-to-all-done.1 = bf16[4,768,96]{1,2,0:T(8,128)(2,1)S(1)} async-done(((bf16[4,768,96]{1,2,0:T(8,128)(2,1)}), bf16[4,768,96]{1,2,0:T(8,128)(2,1)S(1)}, u32[]{:S(2)}, u32[]{:S(2)}) %all-to-all-start.1) | async-done | bytes 589856 | tf_op jit(solution)/shard_map/all_to_all | solution.py:68
  49.5 3.0 broadcast_in_dim.8
  52.5 5.3 %all-to-all-start = ((bf16[16,96,768]{2,1,0:T(8,128)(2,1)}), bf16[16,96,768]{2,1,0:T(8,128)(2,1)}, u32[]{:S(2)}, u32[]{:S(2)}) async-start(bf16[16,96,768]{2,1,0:T(8,128)(2,1)} %bitcast.86), calls=%async_computation | async-start | bytes 4718592 | tf_op jit(solution)/shard_map/all_to_all | solution.py:66
  58.8 44.9 %all-to-all-done = bf16[16,96,768]{2,1,0:T(8,128)(2,1)} async-done(((bf16[16,96,768]{2,1,0:T(8,128)(2,1)}), bf16[16,96,768]{2,1,0:T(8,128)(2,1)}, u32[]{:S(2)}, u32[]{:S(2)}) %all-to-all-start) | async-done | bytes 2359328 | tf_op jit(solution)/shard_map/all_to_all | solution.py:66
  103.7 7.5 %multiply_convert_fusion = (bf16[1024,768]{1,0:T(8,128)(2,1)}, f32[1024,768]{1,0:T(8,128)}) fusion(bf16[1536,768]{1,0:T(8,128)(2,1)} %bitcast.5, bf16[2,1024,1536]{2,1,0:T(8,128)(2,1)} %all-gather.3.cloned.1.call-done), kind=kOutput, calls=%fused_computation.100 | convolution fusion | flops 2419851264 | bytes 10223616 | tf_op jit(solution)/shard_map/dot_general | solution.py:91
  111.2 43.2 %all-gather.5.cloned.1.call-done = bf16[768,1536]{0,1:T(8,128)(2,1)} async-done(((bf16[768,384]{0,1:T(8,128)(2,1)}), bf16[768,1536]{0,1:T(8,128)(2,1)}) %all-gather.5.cloned.1.call-update) | async-done | bytes 2359312 | tf_op jit(solution)/shard_map/all_gather | solution.py:69
  154.4 6.8 %fusion.7 = bf16[1024,768]{1,0:T(8,128)(2,1)S(1)} fusion(f32[1024,768]{1,0:T(8,128)} %get-tuple-element.124, bf16[768,1536]{0,1:T(8,128)(2,1)} %all-gather.5.cloned.1.call-done, bf16[2,1024,1536]{2,1,0:T(8,128)(2,1)} %all-gather.3.cloned.1.call-done), kind=kOutput, calls=%fused_computation.97 | convolution fusion | flops 2423783424 | bytes 10223616 | tf_op jit(solution)/shard_map/dot_general | solution.py:97
  162.3 3.9 %convolution_convert_fusion.3 = bf16[1536,768]{1,0:T(8,128)(2,1)} fusion(bf16[1024,768]{1,0:T(8,128)(2,1)S(1)} %fusion.7, bf16[2,1024,1536]{2,1,0:T(8,128)(2,1)S(1)} %copy-done.98), kind=kOutput, calls=%fused_computation.89 | convolution fusion | flops 2417098752 | bytes 7077888 | tf_op jit(solution)/shard_map/dot_general | solution.py:101
  166.6 4.9 %fusion.1 = bf16[1,1024,1536]{2,1,0:T(8,128)(2,1)S(1)} fusion(bf16[1024,768]{1,0:T(8,128)(2,1)} %copy-done.101, bf16[1536,768]{1,0:T(8,128)(2,1)} %bitcast.5), kind=kOutput, calls=%fused_computation.91 | convolution fusion | flops 2417491968 | bytes 7077888 | tf_op jit(solution)/shard_map/dot_general | solution.py:104
  171.6 2.9 fusion
  174.5 3.2 pad_maximum_fusion
  177.7 5.1 %convolution_convert_fusion.2 = bf16[1536,768]{1,0:T(8,128)(2,1)S(1)} fusion(bf16[1024,768]{1,0:T(8,128)(2,1)} %get-tuple-element.123, bf16[2,1024,1536]{2,1,0:T(8,128)(2,1)} %all-gather.3.cloned.1.call-done), kind=kOutput, calls=%fused_computation.88 | convolution fusion | flops 2417098752 | bytes 7077888 | tf_op jit(solution)/shard_map/dot_general | solution.py:94
  182.7 80.0 %all_to_all.48 = bf16[4,384,768]{2,1,0:T(8,128)(2,1)} all-to-all(bf16[4,384,768]{2,1,0:T(8,128)(2,1)S(1)} %bitcast.92), channel_id=1, replica_groups=mesh['dp'=4,'fsdp'=2,'rows'=4] {'dp'}, dimensions={0} | all-to-all | bytes 4718592 | tf_op jit(solution)/shard_map/all_to_all | solution.py:118
  262.8 2.3 reduce_sum.520
  267.5 31.2 %all_to_all.49 = bf16[2,384,768]{2,0,1:T(2,128)(2,1)S(1)} all-to-all(bf16[2,384,768]{2,0,1:T(2,128)(2,1)S(1)} %copy.36), channel_id=1, replica_groups=mesh['dp'=4,'fsdp'=2,'rows'=4] {'rows'}, dimensions={1} | all-to-all | bytes 2359296 | tf_op jit(solution)/shard_map/all_to_all | solution.py:149
  305.3 14.5 %reduce-scatter.3.cloned.1.call-done = bf16[2,128,1536]{2,1,0:T(8,128)(2,1)} async-done(((bf16[2,1024,1536]{2,1,0:T(8,128)(2,1)}), bf16[2,128,1536]{2,1,0:T(8,128)(2,1)}) %reduce-scatter.3.cloned.1.call-update) | async-done | bytes 786448 | tf_op jit(solution)/shard_map/reduce_scatter | solution.py:107
  321.2 2.1 fusion.104
  328.0 2.4 multiply_reduce_fusion
  331.8 2.0 multiply_reduce_fusion.18
  336.1 4.6 %all-to-all-start.4 = ((f32[32,2,1536]{2,1,0:T(2,128)}), f32[32,2,1536]{2,1,0:T(2,128)S(1)}, u32[]{:S(2)}, u32[]{:S(2)}) async-start(f32[32,2,1536]{2,1,0:T(2,128)} %reshape.563), calls=%async_computation.6 | async-start | bytes 786432 | tf_op jit(solution)/shard_map/all_to_all | solution.py:49
  340.8 2.2 collective-permute-start.2
  345.5 2.0 collective-permute-done.3
  347.7 6.2 %all-to-all-done.4 = f32[32,2,1536]{2,1,0:T(2,128)S(1)} async-done(((f32[32,2,1536]{2,1,0:T(2,128)}), f32[32,2,1536]{2,1,0:T(2,128)S(1)}, u32[]{:S(2)}, u32[]{:S(2)}) %all-to-all-start.4) | async-done | bytes 393248 | tf_op jit(solution)/shard_map/all_to_all | solution.py:49
  354.9 3.9 %all-to-all-start.5 = ((f32[32,2,1536]{2,1,0:T(2,128)}), f32[32,2,1536]{2,1,0:T(2,128)S(1)}, u32[]{:S(2)}, u32[]{:S(2)}) async-start(f32[32,2,1536]{2,1,0:T(2,128)} %broadcast_in_dim.11), calls=%async_computation.7 | async-start | bytes 786432 | tf_op jit(solution)/shard_map/all_to_all | solution.py:51
  359.2 7.4 %fusion.97 = bf16[1,4,32,1536]{3,2,1,0:T(8,128)(2,1)} fusion(f32[1,10,32,1536]{3,2,1,0:T(8,128)S(1)} %maximum_convert_fusion.1, f32[1536]{0:T(1024)S(1)} %copy-done.25, f32[1536]{0:T(1024)S(1)} %copy-done.27, f32[1536]{0:T(1024)S(1)} %copy-done.31, f32[1536]{0:T(1024)S(1)} %copy-done.33, f32[1536]{0:T(1024)S(1)} %copy-done.35, f32[1536]{0:T(1024)S(1)} %copy-done.37, ...), kind=kLoop, calls=%fused_computation.195 | loop fusion | flops 19660800 | bytes 8640512 | tf_op jit(solution)/shard_map/convert_element_type | solution.py:147
  366.6 5.1 %all-to-all-done.5 = f32[32,2,1536]{2,1,0:T(2,128)S(1)} async-done(((f32[32,2,1536]{2,1,0:T(2,128)}), f32[32,2,1536]{2,1,0:T(2,128)S(1)}, u32[]{:S(2)}, u32[]{:S(2)}) %all-to-all-start.5) | async-done | bytes 393248 | tf_op jit(solution)/shard_map/all_to_all | solution.py:51
  (309 shorter events, 35.7 us)
Async XLA Ops:
  7.2 96.5 %all-gather.3.cloned.1.call-start = ((), (), s32[]{:S(2)}) async-start(), calls=%async_computation.8 | async-start | bytes 7077888 | tf_op jit(solution)/shard_map/all_gather | solution.py:89
  8.3 9.7 %collective-permute-start = (bf16[1,3,32,1536]{3,2,1,0:T(8,128)(2,1)S(1)}, bf16[1,3,32,1536]{3,2,1,0:T(8,128)(2,1)S(1)}, u32[]{:S(2)}, u32[]{:S(2)}) collective-permute-start(bf16[1,3,32,1536]{3,2,1,0:T(8,128)(2,1)S(1)} %get-tuple-element.121), channel_id=1, source_target_pairs={{0,1},{1,2},{2,3},{4,5},{5,6},{6,7},{8,9},{9,10},{10,11},{12,13},{... | collective-permute-start | bytes 884744 | tf_op jit(solution)/shard_map/ppermute | solution.py:25
  10.7 7.3 %collective-permute-start.1 = (bf16[1,3,32,1536]{3,2,1,0:T(8,128)(2,1)S(1)}, bf16[1,3,32,1536]{3,2,1,0:T(8,128)(2,1)S(1)}, u32[]{:S(2)}, u32[]{:S(2)}) collective-permute-start(bf16[1,3,32,1536]{3,2,1,0:T(8,128)(2,1)S(1)} %get-tuple-element.122), channel_id=1, source_target_pairs={{1,0},{2,1},{3,2},{5,4},{6,5},{7,6},{9,8},{10,9},{11,10},{13,12},{... | collective-permute-start | bytes 884744 | tf_op jit(solution)/shard_map/ppermute | solution.py:26
  13.4 15.3 %copy-start.8 = (f32[1536]{0:T(1024)}, f32[1536]{0:T(1024)S(1)}, u32[]{:S(2)}) copy-start(f32[1536]{0:T(1024)S(1)} %get-tuple-element.101) | copy-start | bytes 18436
  13.4 15.3 %copy-start.10 = (f32[1536]{0:T(1024)}, f32[1536]{0:T(1024)S(1)}, u32[]{:S(2)}) copy-start(f32[1536]{0:T(1024)S(1)} %get-tuple-element.102) | copy-start | bytes 18436
  13.4 15.3 %copy-start.12 = (f32[1536]{0:T(1024)}, f32[1536]{0:T(1024)S(1)}, u32[]{:S(2)}) copy-start(f32[1536]{0:T(1024)S(1)} %get-tuple-element.103) | copy-start | bytes 18436
  13.4 15.3 %copy-start.14 = (f32[1536]{0:T(1024)}, f32[1536]{0:T(1024)S(1)}, u32[]{:S(2)}) copy-start(f32[1536]{0:T(1024)S(1)} %get-tuple-element.104) | copy-start | bytes 18436
  13.5 15.3 %copy-start.16 = (f32[1536]{0:T(1024)}, f32[1536]{0:T(1024)S(1)}, u32[]{:S(2)}) copy-start(f32[1536]{0:T(1024)S(1)} %get-tuple-element.105) | copy-start | bytes 18436
  13.5 15.3 %copy-start.18 = (f32[1536]{0:T(1024)}, f32[1536]{0:T(1024)S(1)}, u32[]{:S(2)}) copy-start(f32[1536]{0:T(1024)S(1)} %get-tuple-element.106) | copy-start | bytes 18436
  13.5 15.3 %copy-start.20 = (f32[1536]{0:T(1024)}, f32[1536]{0:T(1024)S(1)}, u32[]{:S(2)}) copy-start(f32[1536]{0:T(1024)S(1)} %get-tuple-element.107) | copy-start | bytes 18436
  13.5 15.3 %copy-start.22 = (f32[1536]{0:T(1024)}, f32[1536]{0:T(1024)S(1)}, u32[]{:S(2)}) copy-start(f32[1536]{0:T(1024)S(1)} %get-tuple-element.108) | copy-start | bytes 18436
  13.5 15.3 %copy-start.24 = (f32[1536]{0:T(1024)}, f32[1536]{0:T(1024)S(1)}, u32[]{:S(2)}) copy-start(f32[1536]{0:T(1024)S(1)} %get-tuple-element.109) | copy-start | bytes 18436
  13.5 15.3 %copy-start.26 = (f32[1536]{0:T(1024)}, f32[1536]{0:T(1024)S(1)}, u32[]{:S(2)}) copy-start(f32[1536]{0:T(1024)S(1)} %get-tuple-element.110) | copy-start | bytes 18436
  31.9 17.6 %all-to-all-start.1 = ((bf16[4,768,96]{1,2,0:T(8,128)(2,1)}), bf16[4,768,96]{1,2,0:T(8,128)(2,1)S(1)}, u32[]{:S(2)}, u32[]{:S(2)}) async-start(bf16[4,768,96]{1,2,0:T(8,128)(2,1)} %bitcast.94), calls=%async_computation.1 | async-start | bytes 1179648 | tf_op jit(solution)/shard_map/all_to_all | solution.py:68
  52.5 51.2 %all-to-all-start = ((bf16[16,96,768]{2,1,0:T(8,128)(2,1)}), bf16[16,96,768]{2,1,0:T(8,128)(2,1)}, u32[]{:S(2)}, u32[]{:S(2)}) async-start(bf16[16,96,768]{2,1,0:T(8,128)(2,1)} %bitcast.86), calls=%async_computation | async-start | bytes 4718592 | tf_op jit(solution)/shard_map/all_to_all | solution.py:66
  57.8 96.6 %all-gather.5.cloned.1.call-start = ((), (), s32[]{:S(2)}) async-start(), calls=%async_computation.9 | async-start | bytes 2949120 | tf_op jit(solution)/shard_map/all_gather | solution.py:69
  58.5 206.5 %reduce-scatter.5.cloned.1.call-start = ((), (), s32[]{:S(2)}) async-start(), calls=%async_computation.11 | async-start | bytes 2949120 | tf_op jit(solution)/shard_map/reduce_scatter | solution.py:119
  166.3 153.5 %reduce-scatter.3.cloned.1.call-start = ((), (), s32[]{:S(2)}) async-start(), calls=%async_computation.10 | async-start | bytes 7077888 | tf_op jit(solution)/shard_map/reduce_scatter | solution.py:107
  336.1 17.8 %all-to-all-start.4 = ((f32[32,2,1536]{2,1,0:T(2,128)}), f32[32,2,1536]{2,1,0:T(2,128)S(1)}, u32[]{:S(2)}, u32[]{:S(2)}) async-start(f32[32,2,1536]{2,1,0:T(2,128)} %reshape.563), calls=%async_computation.6 | async-start | bytes 786432 | tf_op jit(solution)/shard_map/all_to_all | solution.py:49
  340.8 4.7 %collective-permute-start.2 = (bf16[1,3,32,1536]{3,2,1,0:T(8,128)(2,1)S(1)}, bf16[1,3,32,1536]{3,2,1,0:T(8,128)(2,1)S(1)}, u32[]{:S(2)}, u32[]{:S(2)}) collective-permute-start(bf16[1,3,32,1536]{3,2,1,0:T(8,128)(2,1)S(1)} %get-tuple-element.119), channel_id=1, source_target_pairs={{0,1},{1,2},{2,3},{4,5},{5,6},{6,7},{8,9},{9,10},{10,11},{12,13},{... | collective-permute-start | bytes 884744 | tf_op jit(solution)/shard_map/ppermute | solution.py:25
  343.0 4.6 %collective-permute-start.3 = (bf16[1,3,32,1536]{3,2,1,0:T(8,128)(2,1)S(1)}, bf16[1,3,32,1536]{3,2,1,0:T(8,128)(2,1)S(1)}, u32[]{:S(2)}, u32[]{:S(2)}) collective-permute-start(bf16[1,3,32,1536]{3,2,1,0:T(8,128)(2,1)S(1)} %get-tuple-element.120), channel_id=1, source_target_pairs={{1,0},{2,1},{3,2},{5,4},{6,5},{7,6},{9,8},{10,9},{11,10},{13,12},{... | collective-permute-start | bytes 884744 | tf_op jit(solution)/shard_map/ppermute | solution.py:26
  345.1 13.7 %copy-start.15 = (f32[1536]{0:T(1024)S(1)}, f32[1536]{0:T(1024)}, u32[]{:S(2)}) copy-start(f32[1536]{0:T(1024)} %copy-done.14) | copy-start | bytes 18436
  345.2 13.7 %copy-start.17 = (f32[1536]{0:T(1024)S(1)}, f32[1536]{0:T(1024)}, u32[]{:S(2)}) copy-start(f32[1536]{0:T(1024)} %copy-done.16) | copy-start | bytes 18436
  345.2 13.7 %copy-start.19 = (f32[1536]{0:T(1024)S(1)}, f32[1536]{0:T(1024)}, u32[]{:S(2)}) copy-start(f32[1536]{0:T(1024)} %copy-done.18) | copy-start | bytes 18436
  345.2 13.7 %copy-start.21 = (f32[1536]{0:T(1024)S(1)}, f32[1536]{0:T(1024)}, u32[]{:S(2)}) copy-start(f32[1536]{0:T(1024)} %copy-done.20) | copy-start | bytes 18436
  345.2 13.7 %copy-start.23 = (f32[1536]{0:T(1024)S(1)}, f32[1536]{0:T(1024)}, u32[]{:S(2)}) copy-start(f32[1536]{0:T(1024)} %copy-done.22) | copy-start | bytes 18436
  345.2 13.7 %copy-start.25 = (f32[1536]{0:T(1024)S(1)}, f32[1536]{0:T(1024)}, u32[]{:S(2)}) copy-start(f32[1536]{0:T(1024)} %copy-done.24) | copy-start | bytes 18436
  345.2 13.7 %copy-start.27 = (f32[1536]{0:T(1024)S(1)}, f32[1536]{0:T(1024)}, u32[]{:S(2)}) copy-start(f32[1536]{0:T(1024)} %copy-done.26) | copy-start | bytes 18436
  345.2 13.7 %copy-start.29 = (f32[1536]{0:T(1024)S(1)}, f32[1536]{0:T(1024)}, u32[]{:S(2)}) copy-start(f32[1536]{0:T(1024)} %copy-done.28) | copy-start | bytes 18436
  345.2 13.7 %copy-start.31 = (f32[1536]{0:T(1024)S(1)}, f32[1536]{0:T(1024)}, u32[]{:S(2)}) copy-start(f32[1536]{0:T(1024)} %copy-done.30) | copy-start | bytes 18436
  345.2 13.7 %copy-start.33 = (f32[1536]{0:T(1024)S(1)}, f32[1536]{0:T(1024)}, u32[]{:S(2)}) copy-start(f32[1536]{0:T(1024)} %copy-done.32) | copy-start | bytes 18436
  354.9 16.8 %all-to-all-start.5 = ((f32[32,2,1536]{2,1,0:T(2,128)}), f32[32,2,1536]{2,1,0:T(2,128)S(1)}, u32[]{:S(2)}, u32[]{:S(2)}) async-start(f32[32,2,1536]{2,1,0:T(2,128)} %broadcast_in_dim.11), calls=%async_computation.7 | async-start | bytes 786432 | tf_op jit(solution)/shard_map/all_to_all | solution.py:51
  (82 other events, 885.9 us)
Sparse Core Ops, SparseCore 0:
  30.9 67.6 all-gather.2
  100.7 53.6 all-gather.4
  166.4 67.9 reduce-scatter.4
  237.6 82.1 reduce-scatter.2
